TPU v7x, 32 devices: a whole 2x2x4 slice. The times are simulated.
32 devices in a mesh: groups: 2 (over y), state: 4 (over z), input: 2 (over x), horizon: 2 (over core).
Axes of the slice: x: 2, y: 2, z: 4, core: 2. Of those that a mesh axis runs over, the one named last changes fastest.
Arguments:
- impulses: bfloat16 [4096, 8, 256], P(('state', 'horizon'), 'input', 'groups'), parts along dimension 2, may hold values from -6 to 6
- expectations: bfloat16 [4, 16, 4096], P('groups', None, ('state', 'horizon')), parts along dimension 0, may hold values from -0.09375 to 0.09375
- region_scale: float32 [32, 2], P('groups'), parts along dimension 0, may hold values from 0.125 to 1
- regions: int32 [32], P(('state', 'horizon')), may hold values from 0 to 15
- tiles: bfloat16 [32, 4, 128, 128], P(('state', 'horizon')), may hold values from -0.5 to 0.5
- offsets: int32 [32, 4], P(('state', 'horizon')), may hold values from -1 to 1, as said below
- counts: int32 [32], P(('state', 'horizon')), may hold values from 2 to 4, as said below
Outputs:
- jacobian: float32 [128, 4, 8, 128], P(('state', 'horizon'), 'groups', 'input'), parts along dimension 1
There are 2 independent parts, one for each index of `groups`. A program takes and returns all parts, laid end to end along the dimension named above; an argument that names none is the same for every part. Nothing has to cross between parts.
Inputs may be any that keep to these rules, and one draw needn't show every extreme that they name: tiles j >= counts[c] of block c are unused; some block uses all 4. `offsets`: tile 0 of every block reads the block below it (offset -1) and tile 1 the block above it (offset 1).
All inputs are finite; a program needn't handle non-finite values.
Results may differ from a plain program's by a relative error of at most 0.0065.
Values sent between devices are 32-bit elements; how exact they have to be, the bound alone decides.
No kernel may reach another device: no remote copies, remote signals or barrier semaphores. Data moves between devices by JAX's collectives and lax.ppermute only.
A program may use at most 64 MiB of HBM per device.

v0:
```python
import jax
import jax.numpy as jnp
from jax import lax
from jax.sharding import PartitionSpec as P


def with_halo(block, sides, width):
    for axis, dim in sides:
        count = lax.axis_size(axis)
        forward = [(i, i + 1) for i in range(count - 1)]
        backward = [(target, source) for source, target in forward]
        low = lax.ppermute(
            lax.slice_in_dim(block, block.shape[dim] - width, None, axis=dim), axis, forward
        )
        high = lax.ppermute(lax.slice_in_dim(block, 0, width, axis=dim), axis, backward)
        block = jnp.concatenate([low, block, high], axis=dim)
    return block


def diagonal_sums(news):
    rows = news.shape[0]
    width = news.shape[-1]
    total = news
    shift = 1
    while shift < rows:
        moved = lax.pad(
            total[: rows - shift, ..., : width - shift],
            jnp.zeros((), total.dtype),
            [(shift, 0, 0)] + [(0, 0, 0)] * (total.ndim - 2) + [(shift, 0, 0)],
        )
        total = total + moved
        shift *= 2
    return total


def split_product(rows_full, data_half):
    upper = rows_full.astype(jnp.bfloat16)
    remain = rows_full - upper.astype(jnp.float32)
    middle = remain.astype(jnp.bfloat16)
    lower = (remain - middle.astype(jnp.float32)).astype(jnp.bfloat16)
    total = jnp.dot(upper, data_half, preferred_element_type=jnp.float32)
    total = total + jnp.dot(middle, data_half, preferred_element_type=jnp.float32)
    return total + jnp.dot(lower, data_half, preferred_element_type=jnp.float32)


def pull_back(rows, masked, source, scaling):
    block_count = rows.shape[0]
    scaled = rows * scaling[:, None, None]
    contrib = jnp.einsum("cru,cjuv->cjrv", scaled, masked, precision=lax.Precision.HIGHEST)
    target = (
        source[:, :, None] == jnp.arange(block_count + 2, dtype=jnp.int32)[None, None, :]
    ).astype(jnp.float32)
    spread = jnp.einsum("cjb,cjrv->brv", target, contrib, precision=lax.Precision.HIGHEST)
    edges = jnp.stack([spread[0], spread[-1]], axis=0)
    arrived = with_halo(edges, ((("state", "horizon"), 0),), 1)
    inner = spread[1:-1]
    inner = inner.at[0].add(arrived[0])
    inner = inner.at[-1].add(arrived[3])
    return inner


def shards(impulses, expectations, region_scale, regions, tiles, offsets, counts):
    block_count, band_count, tile_size, _ = tiles.shape
    state_count, input_count, horizon = impulses.shape
    output_count, expect_rows, _ = expectations.shape
    region_total = region_scale.shape[0]
    width = input_count * horizon
    sections = horizon // expect_rows
    row_count = output_count * expect_rows
    onehot = (regions[:, None] == jnp.arange(region_total, dtype=jnp.int32)[None, :]).astype(
        jnp.float32
    )
    block_scale = jnp.dot(
        onehot, region_scale, precision=lax.Precision.HIGHEST, preferred_element_type=jnp.float32
    )
    weighted = (
        expectations.astype(jnp.float32).reshape(output_count, expect_rows, block_count, tile_size)
        * block_scale.T[:, None, :, None]
    )
    weighted_half = weighted.astype(jnp.bfloat16).reshape(row_count, state_count)
    in_use = jnp.arange(band_count, dtype=jnp.int32)[None, :] < counts[:, None]
    masked = jnp.where(in_use[:, :, None, None], tiles, jnp.zeros((), jnp.bfloat16)).astype(
        jnp.float32
    )
    scaling = lax.rsqrt(counts.astype(jnp.float32))
    source = jnp.arange(block_count, dtype=jnp.int32)[:, None] + 1 + offsets
    flat_start = impulses.reshape(state_count, width)
    pieces = []
    rows = (
        weighted_half.astype(jnp.float32)
        .reshape(row_count, block_count, tile_size)
        .transpose(1, 0, 2)
    )
    for section in range(sections):
        if section > 0:
            rows = pull_back(rows, masked, source, scaling)
            flat_rows = rows.transpose(1, 0, 2).reshape(row_count, state_count)
            product = split_product(flat_rows, flat_start)
        else:
            product = jnp.dot(weighted_half, flat_start, preferred_element_type=jnp.float32)
        pieces.append(
            product.reshape(output_count, expect_rows, input_count, horizon).transpose(1, 0, 2, 3)
        )
    partial_news = jnp.concatenate(pieces, axis=0)
    own_rows = horizon // lax.axis_size(("state", "horizon"))
    first_row = lax.axis_index(("state", "horizon")) * own_rows
    whole = lax.psum(partial_news, ("state", "horizon"))
    jacobian = diagonal_sums(whole)
    return lax.dynamic_slice_in_dim(jacobian, first_row, own_rows, 0)


def solution(mesh):
    return jax.shard_map(
        shards,
        mesh=mesh,
        in_specs=(
            P(("state", "horizon"), "input", "groups"),
            P("groups", None, ("state", "horizon")),
            P("groups", None),
            P(("state", "horizon")),
            P(("state", "horizon"), None, None, None),
            P(("state", "horizon"), None),
            P(("state", "horizon")),
        ),
        out_specs=P(("state", "horizon"), "groups", "input", None),
        check_vma=False,
    )
```

profile of v0, /device:TPU:0, one launch (start us, length us, event | category | flops | bytes accessed | tf_op | source)
XLA Modules:
  0.0 143.3 jit_solution(11071882634306471228)
XLA Ops:
  9.1 1.5 %fusion.49 = f32[4,4,128,32]{2,3,1,0:T(8,128)S(1)} fusion(bf16[4,4,128,128]{3,2,1,0:T(8,128)(2,1)} %param.39, pred[4,4]{1,0:T(4,128)(4,1)S(1)} %iota_compare_fusion.1, f32[4,32,128,1]{2,0,1,3:T(4,128)S(1)} %multiply_bitcast_fusion.6), kind=kOutput, calls=%fused_computation.81 | convolution fusion | flops 100925440 | bytes 851984 | tf_op jit(solution)/shard_map/cru,cjuv->cjrv/dot_general | solution.py:49
  11.2 2.4 %collective-permute-start = (f32[1,32,128]{2,0,1:T(1,128)S(1)}, f32[1,32,128]{2,0,1:T(1,128)S(1)}, u32[]{:S(2)}, u32[]{:S(2)}) collective-permute-start(f32[1,32,128]{2,0,1:T(1,128)S(1)} %get-tuple-element.186), channel_id=1, source_target_pairs={{0,1},{1,4},{4,5},{5,8},{8,9},{9,12},{12,13},{2,3},{3,6},{6,7},{7,... | collective-permute-start | bytes 49160 | tf_op jit(solution)/shard_map/ppermute | solution.py:12
  13.5 1.3 collective-permute-start.1
  16.2 2.6 %collective-permute-done.1 = f32[1,32,128]{2,0,1:T(1,128)S(1)} collective-permute-done((f32[1,32,128]{2,0,1:T(1,128)S(1)}, f32[1,32,128]{2,0,1:T(1,128)S(1)}, u32[]{:S(2)}, u32[]{:S(2)}) %collective-permute-start.1) | collective-permute-done | bytes 16416 | tf_op jit(solution)/shard_map/ppermute | solution.py:15
  21.5 4.4 %collective-permute-start.2 = (f32[1,32,128]{2,0,1:T(1,128)S(1)}, f32[1,32,128]{2,0,1:T(1,128)S(1)}, u32[]{:S(2)}, u32[]{:S(2)}) collective-permute-start(f32[1,32,128]{2,0,1:T(1,128)S(1)} %get-tuple-element.184), channel_id=1, source_target_pairs={{0,1},{1,4},{4,5},{5,8},{8,9},{9,12},{12,13},{2,3},{3,6},{6,7},{7,... | collective-permute-start | bytes 49160 | tf_op jit(solution)/shard_map/ppermute | solution.py:12
  25.9 1.3 collective-permute-start.3
  27.3 1.6 %collective-permute-done.3 = f32[1,32,128]{2,0,1:T(1,128)S(1)} collective-permute-done((f32[1,32,128]{2,0,1:T(1,128)S(1)}, f32[1,32,128]{2,0,1:T(1,128)S(1)}, u32[]{:S(2)}, u32[]{:S(2)}) %collective-permute-start.3) | collective-permute-done | bytes 16416 | tf_op jit(solution)/shard_map/ppermute | solution.py:15
  30.8 3.9 %collective-permute-start.4 = (f32[1,32,128]{2,0,1:T(1,128)S(1)}, f32[1,32,128]{2,0,1:T(1,128)S(1)}, u32[]{:S(2)}, u32[]{:S(2)}) collective-permute-start(f32[1,32,128]{2,0,1:T(1,128)S(1)} %get-tuple-element.182), channel_id=1, source_target_pairs={{0,1},{1,4},{4,5},{5,8},{8,9},{9,12},{12,13},{2,3},{3,6},{6,7},{7,... | collective-permute-start | bytes 49160 | tf_op jit(solution)/shard_map/ppermute | solution.py:12
  34.7 1.3 collective-permute-start.5
  36.2 1.6 %collective-permute-done.5 = f32[1,32,128]{2,0,1:T(1,128)S(1)} collective-permute-done((f32[1,32,128]{2,0,1:T(1,128)S(1)}, f32[1,32,128]{2,0,1:T(1,128)S(1)}, u32[]{:S(2)}, u32[]{:S(2)}) %collective-permute-start.5) | collective-permute-done | bytes 16416 | tf_op jit(solution)/shard_map/ppermute | solution.py:15
  39.7 3.9 %collective-permute-start.6 = (f32[1,32,128]{2,0,1:T(1,128)S(1)}, f32[1,32,128]{2,0,1:T(1,128)S(1)}, u32[]{:S(2)}, u32[]{:S(2)}) collective-permute-start(f32[1,32,128]{2,0,1:T(1,128)S(1)} %get-tuple-element.180), channel_id=1, source_target_pairs={{0,1},{1,4},{4,5},{5,8},{8,9},{9,12},{12,13},{2,3},{3,6},{6,7},{7,... | collective-permute-start | bytes 49160 | tf_op jit(solution)/shard_map/ppermute | solution.py:12
  43.6 1.3 collective-permute-start.7
  45.1 1.6 %collective-permute-done.7 = f32[1,32,128]{2,0,1:T(1,128)S(1)} collective-permute-done((f32[1,32,128]{2,0,1:T(1,128)S(1)}, f32[1,32,128]{2,0,1:T(1,128)S(1)}, u32[]{:S(2)}, u32[]{:S(2)}) %collective-permute-start.7) | collective-permute-done | bytes 16416 | tf_op jit(solution)/shard_map/ppermute | solution.py:15
  48.5 3.9 %collective-permute-start.8 = (f32[1,32,128]{2,0,1:T(1,128)S(1)}, f32[1,32,128]{2,0,1:T(1,128)S(1)}, u32[]{:S(2)}, u32[]{:S(2)}) collective-permute-start(f32[1,32,128]{2,0,1:T(1,128)S(1)} %get-tuple-element.178), channel_id=1, source_target_pairs={{0,1},{1,4},{4,5},{5,8},{8,9},{9,12},{12,13},{2,3},{3,6},{6,7},{7,... | collective-permute-start | bytes 49160 | tf_op jit(solution)/shard_map/ppermute | solution.py:12
  52.4 1.3 collective-permute-start.9
  53.9 1.6 %collective-permute-done.9 = f32[1,32,128]{2,0,1:T(1,128)S(1)} collective-permute-done((f32[1,32,128]{2,0,1:T(1,128)S(1)}, f32[1,32,128]{2,0,1:T(1,128)S(1)}, u32[]{:S(2)}, u32[]{:S(2)}) %collective-permute-start.9) | collective-permute-done | bytes 16416 | tf_op jit(solution)/shard_map/ppermute | solution.py:15
  57.4 3.9 %collective-permute-start.10 = (f32[1,32,128]{2,0,1:T(1,128)S(1)}, f32[1,32,128]{2,0,1:T(1,128)S(1)}, u32[]{:S(2)}, u32[]{:S(2)}) collective-permute-start(f32[1,32,128]{2,0,1:T(1,128)S(1)} %get-tuple-element.176), channel_id=1, source_target_pairs={{0,1},{1,4},{4,5},{5,8},{8,9},{9,12},{12,13},{2,3},{3,6},{6,7},{7,... | collective-permute-start | bytes 49160 | tf_op jit(solution)/shard_map/ppermute | solution.py:12
  61.3 1.3 collective-permute-start.11
  62.8 1.6 %collective-permute-done.11 = f32[1,32,128]{2,0,1:T(1,128)S(1)} collective-permute-done((f32[1,32,128]{2,0,1:T(1,128)S(1)}, f32[1,32,128]{2,0,1:T(1,128)S(1)}, u32[]{:S(2)}, u32[]{:S(2)}) %collective-permute-start.11) | collective-permute-done | bytes 16416 | tf_op jit(solution)/shard_map/ppermute | solution.py:15
  66.2 3.9 %collective-permute-start.12 = (f32[1,32,128]{2,0,1:T(1,128)S(1)}, f32[1,32,128]{2,0,1:T(1,128)S(1)}, u32[]{:S(2)}, u32[]{:S(2)}) collective-permute-start(f32[1,32,128]{2,0,1:T(1,128)S(1)} %get-tuple-element.174), channel_id=1, source_target_pairs={{0,1},{1,4},{4,5},{5,8},{8,9},{9,12},{12,13},{2,3},{3,6},{6,7},{7,... | collective-permute-start | bytes 49160 | tf_op jit(solution)/shard_map/ppermute | solution.py:12
  70.2 1.3 collective-permute-start.13
  71.7 1.6 %collective-permute-done.13 = f32[1,32,128]{2,0,1:T(1,128)S(1)} collective-permute-done((f32[1,32,128]{2,0,1:T(1,128)S(1)}, f32[1,32,128]{2,0,1:T(1,128)S(1)}, u32[]{:S(2)}, u32[]{:S(2)}) %collective-permute-start.13) | collective-permute-done | bytes 16416 | tf_op jit(solution)/shard_map/ppermute | solution.py:15
  74.9 58.2 %all-reduce.9.cloned.1.call-done = f32[128,2,4,128]{3,0,2,1:T(8,128)} async-done(((f32[128,2,4,128]{3,0,2,1:T(8,128)}), f32[128,2,4,128]{3,0,2,1:T(8,128)}) %all-reduce.9.cloned.1.call-update) | async-done | bytes 524304 | tf_op jit(solution)/shard_map/psum | solution.py:107
  133.1 1.4 pad_add_fusion.5
  (153 shorter events, 20.4 us)
Async XLA Ops:
  6.5 1.6 %copy-start = (f32[16,2]{0,1:T(2,128)S(1)}, f32[16,2]{0,1:T(2,128)}, u32[]{:S(2)}) copy-start(f32[16,2]{0,1:T(2,128)} %param.37) | copy-start | bytes 388
  6.5 0.8 copy-start.6
  6.5 126.6 %all-reduce.9.cloned.1.call-start = ((), (), s32[]{:S(2)}) async-start(), calls=%async_computation | async-start | bytes 1048576 | tf_op jit(solution)/shard_map/psum | solution.py:107
  7.4 0.8 copy-start.7
  8.2 0.7 copy-start.4
  9.1 5.8 %copy-start.1 = (bf16[512,4,128]{2,1,0:T(4,128)(2,1)S(1)}, bf16[512,4,128]{2,1,0:T(4,128)(2,1)}, u32[]{:S(2)}) copy-start(bf16[512,4,128]{2,1,0:T(4,128)(2,1)} %param.35) | copy-start | bytes 1572868
  11.2 4.9 %collective-permute-start = (f32[1,32,128]{2,0,1:T(1,128)S(1)}, f32[1,32,128]{2,0,1:T(1,128)S(1)}, u32[]{:S(2)}, u32[]{:S(2)}) collective-permute-start(f32[1,32,128]{2,0,1:T(1,128)S(1)} %get-tuple-element.186), channel_id=1, source_target_pairs={{0,1},{1,4},{4,5},{5,8},{8,9},{9,12},{12,13},{2,3},{3,6},{6,7},{7,... | collective-permute-start | bytes 49160 | tf_op jit(solution)/shard_map/ppermute | solution.py:12
  13.5 5.3 %collective-permute-start.1 = (f32[1,32,128]{2,0,1:T(1,128)S(1)}, f32[1,32,128]{2,0,1:T(1,128)S(1)}, u32[]{:S(2)}, u32[]{:S(2)}) collective-permute-start(f32[1,32,128]{2,0,1:T(1,128)S(1)} %get-tuple-element.185), channel_id=1, source_target_pairs={{1,0},{4,1},{5,4},{8,5},{9,8},{12,9},{13,12},{3,2},{6,3},{7,6},{10... | collective-permute-start | bytes 49160 | tf_op jit(solution)/shard_map/ppermute | solution.py:15
  15.0 0.8 copy-start.3
  19.4 1.1 copy-start.5
  21.5 5.7 %collective-permute-start.2 = (f32[1,32,128]{2,0,1:T(1,128)S(1)}, f32[1,32,128]{2,0,1:T(1,128)S(1)}, u32[]{:S(2)}, u32[]{:S(2)}) collective-permute-start(f32[1,32,128]{2,0,1:T(1,128)S(1)} %get-tuple-element.184), channel_id=1, source_target_pairs={{0,1},{1,4},{4,5},{5,8},{8,9},{9,12},{12,13},{2,3},{3,6},{6,7},{7,... | collective-permute-start | bytes 49160 | tf_op jit(solution)/shard_map/ppermute | solution.py:12
  25.9 3.1 %collective-permute-start.3 = (f32[1,32,128]{2,0,1:T(1,128)S(1)}, f32[1,32,128]{2,0,1:T(1,128)S(1)}, u32[]{:S(2)}, u32[]{:S(2)}) collective-permute-start(f32[1,32,128]{2,0,1:T(1,128)S(1)} %get-tuple-element.183), channel_id=1, source_target_pairs={{1,0},{4,1},{5,4},{8,5},{9,8},{12,9},{13,12},{3,2},{6,3},{7,6},{10... | collective-permute-start | bytes 49160 | tf_op jit(solution)/shard_map/ppermute | solution.py:15
  30.8 5.3 %collective-permute-start.4 = (f32[1,32,128]{2,0,1:T(1,128)S(1)}, f32[1,32,128]{2,0,1:T(1,128)S(1)}, u32[]{:S(2)}, u32[]{:S(2)}) collective-permute-start(f32[1,32,128]{2,0,1:T(1,128)S(1)} %get-tuple-element.182), channel_id=1, source_target_pairs={{0,1},{1,4},{4,5},{5,8},{8,9},{9,12},{12,13},{2,3},{3,6},{6,7},{7,... | collective-permute-start | bytes 49160 | tf_op jit(solution)/shard_map/ppermute | solution.py:12
  34.7 3.1 %collective-permute-start.5 = (f32[1,32,128]{2,0,1:T(1,128)S(1)}, f32[1,32,128]{2,0,1:T(1,128)S(1)}, u32[]{:S(2)}, u32[]{:S(2)}) collective-permute-start(f32[1,32,128]{2,0,1:T(1,128)S(1)} %get-tuple-element.181), channel_id=1, source_target_pairs={{1,0},{4,1},{5,4},{8,5},{9,8},{12,9},{13,12},{3,2},{6,3},{7,6},{10... | collective-permute-start | bytes 49160 | tf_op jit(solution)/shard_map/ppermute | solution.py:15
  39.7 5.3 %collective-permute-start.6 = (f32[1,32,128]{2,0,1:T(1,128)S(1)}, f32[1,32,128]{2,0,1:T(1,128)S(1)}, u32[]{:S(2)}, u32[]{:S(2)}) collective-permute-start(f32[1,32,128]{2,0,1:T(1,128)S(1)} %get-tuple-element.180), channel_id=1, source_target_pairs={{0,1},{1,4},{4,5},{5,8},{8,9},{9,12},{12,13},{2,3},{3,6},{6,7},{7,... | collective-permute-start | bytes 49160 | tf_op jit(solution)/shard_map/ppermute | solution.py:12
  43.6 3.1 %collective-permute-start.7 = (f32[1,32,128]{2,0,1:T(1,128)S(1)}, f32[1,32,128]{2,0,1:T(1,128)S(1)}, u32[]{:S(2)}, u32[]{:S(2)}) collective-permute-start(f32[1,32,128]{2,0,1:T(1,128)S(1)} %get-tuple-element.179), channel_id=1, source_target_pairs={{1,0},{4,1},{5,4},{8,5},{9,8},{12,9},{13,12},{3,2},{6,3},{7,6},{10... | collective-permute-start | bytes 49160 | tf_op jit(solution)/shard_map/ppermute | solution.py:15
  48.5 5.3 %collective-permute-start.8 = (f32[1,32,128]{2,0,1:T(1,128)S(1)}, f32[1,32,128]{2,0,1:T(1,128)S(1)}, u32[]{:S(2)}, u32[]{:S(2)}) collective-permute-start(f32[1,32,128]{2,0,1:T(1,128)S(1)} %get-tuple-element.178), channel_id=1, source_target_pairs={{0,1},{1,4},{4,5},{5,8},{8,9},{9,12},{12,13},{2,3},{3,6},{6,7},{7,... | collective-permute-start | bytes 49160 | tf_op jit(solution)/shard_map/ppermute | solution.py:12
  52.4 3.1 %collective-permute-start.9 = (f32[1,32,128]{2,0,1:T(1,128)S(1)}, f32[1,32,128]{2,0,1:T(1,128)S(1)}, u32[]{:S(2)}, u32[]{:S(2)}) collective-permute-start(f32[1,32,128]{2,0,1:T(1,128)S(1)} %get-tuple-element.177), channel_id=1, source_target_pairs={{1,0},{4,1},{5,4},{8,5},{9,8},{12,9},{13,12},{3,2},{6,3},{7,6},{10... | collective-permute-start | bytes 49160 | tf_op jit(solution)/shard_map/ppermute | solution.py:15
  57.4 5.3 %collective-permute-start.10 = (f32[1,32,128]{2,0,1:T(1,128)S(1)}, f32[1,32,128]{2,0,1:T(1,128)S(1)}, u32[]{:S(2)}, u32[]{:S(2)}) collective-permute-start(f32[1,32,128]{2,0,1:T(1,128)S(1)} %get-tuple-element.176), channel_id=1, source_target_pairs={{0,1},{1,4},{4,5},{5,8},{8,9},{9,12},{12,13},{2,3},{3,6},{6,7},{7,... | collective-permute-start | bytes 49160 | tf_op jit(solution)/shard_map/ppermute | solution.py:12
  61.3 3.1 %collective-permute-start.11 = (f32[1,32,128]{2,0,1:T(1,128)S(1)}, f32[1,32,128]{2,0,1:T(1,128)S(1)}, u32[]{:S(2)}, u32[]{:S(2)}) collective-permute-start(f32[1,32,128]{2,0,1:T(1,128)S(1)} %get-tuple-element.175), channel_id=1, source_target_pairs={{1,0},{4,1},{5,4},{8,5},{9,8},{12,9},{13,12},{3,2},{6,3},{7,6},{10... | collective-permute-start | bytes 49160 | tf_op jit(solution)/shard_map/ppermute | solution.py:15
  66.2 5.3 %collective-permute-start.12 = (f32[1,32,128]{2,0,1:T(1,128)S(1)}, f32[1,32,128]{2,0,1:T(1,128)S(1)}, u32[]{:S(2)}, u32[]{:S(2)}) collective-permute-start(f32[1,32,128]{2,0,1:T(1,128)S(1)} %get-tuple-element.174), channel_id=1, source_target_pairs={{0,1},{1,4},{4,5},{5,8},{8,9},{9,12},{12,13},{2,3},{3,6},{6,7},{7,... | collective-permute-start | bytes 49160 | tf_op jit(solution)/shard_map/ppermute | solution.py:12
  70.2 3.1 %collective-permute-start.13 = (f32[1,32,128]{2,0,1:T(1,128)S(1)}, f32[1,32,128]{2,0,1:T(1,128)S(1)}, u32[]{:S(2)}, u32[]{:S(2)}) collective-permute-start(f32[1,32,128]{2,0,1:T(1,128)S(1)} %get-tuple-element.173), channel_id=1, source_target_pairs={{1,0},{4,1},{5,4},{8,5},{9,8},{12,9},{13,12},{3,2},{6,3},{7,6},{10... | collective-permute-start | bytes 49160 | tf_op jit(solution)/shard_map/ppermute | solution.py:15
  74.1 0.8 copy-start.2
Sparse Core Ops, SparseCore 0:
  75.0 58.0 all-reduce.8
where the time goes:
time: 144 us; the launch traced here: 143 us
  waiting for transfers between devices  70.4 us (49%)
  starting transfers between devices  35.4 us (25%)
  between operations  14.3 us (10%)
  matrix products  12.2 us (8%)
  local copies, waits for them, and re-layouts  6.53 us (5%)
  other arithmetic  4.56 us (3%)
    psum x1, waiting for transfers between devices, shards(): whole = lax.psum(partial_news, ('state', 'horizon'))  58.2 us
    ppermute x7, starting transfers between devices, with_halo(): lax.ppermute(lax.slice_in_dim(block, block.shape[dim] - width, None, axis...  26.3 us
    ppermute x7, waiting for transfers between devices, with_halo(): lax.ppermute(lax.slice_in_dim(block, 0, width, axis=dim), axis, backward)  12.2 us
    ppermute x7, starting transfers between devices, with_halo(): lax.ppermute(lax.slice_in_dim(block, 0, width, axis=dim), axis, backward)  9.04 us
    dot_general x7, matrix products, pull_back(): jnp.einsum('cru,cjuv->cjrv', scaled, masked, precision=lax.Precision.HIGH...  3.92 us
    dot_general x7, matrix products, pull_back(): jnp.einsum('cjb,cjrv->brv', target, contrib, precision=lax.Precision.HIGH...  3.78 us
    unnamed x25, local copies, waits for them, and re-layouts  2.88 us
  transfers between devices with their start and end apart: 15, of which 8 were waited for; matrix products, arithmetic and copies ran while one was open for 1% of the time, Pallas kernels for 0%

commit v1 on v0

--- a/solution.py
+++ b/solution.py
@@ -102,11 +102,8 @@
             product.reshape(output_count, expect_rows, input_count, horizon).transpose(1, 0, 2, 3)
         )
     partial_news = jnp.concatenate(pieces, axis=0)
-    own_rows = horizon // lax.axis_size(("state", "horizon"))
-    first_row = lax.axis_index(("state", "horizon")) * own_rows
-    whole = lax.psum(partial_news, ("state", "horizon"))
-    jacobian = diagonal_sums(whole)
-    return lax.dynamic_slice_in_dim(jacobian, first_row, own_rows, 0)
+    jacobian = diagonal_sums(partial_news)
+    return lax.psum_scatter(jacobian, ("state", "horizon"), scatter_dimension=0, tiled=True)
 
 
 def solution(mesh):

time: 144 us -> 118 us (0.82)
  waiting for transfers between devices: 70.4 us -> 45.3 us
    psum x1 -> x0, waiting for transfers between devices: 58.2 us -> none  [shards(): whole = lax.psum(partial_news, ('state', 'horizon'))]
    reduce_scatter x0 -> x1, waiting for transfers between devices: none -> 33 us  [shards(): lax.psum_scatter(jacobian, ('state', 'horizon'), scatter_dimension=0, til...]
    reduce_scatter x0 -> x1, local copies, waits for them, and re-layouts: none -> 1.49 us  [shards(): lax.psum_scatter(jacobian, ('state', 'horizon'), scatter_dimension=0, til...]
    unnamed x25 -> x23, local copies, waits for them, and re-layouts: 2.88 us -> 2.05 us
where the time goes in v1:
time: 118 us
  waiting for transfers between devices  45.3 us (38%)
  starting transfers between devices  35.4 us (30%)
  between operations  14.2 us (12%)
  matrix products  12.2 us (10%)
  local copies, waits for them, and re-layouts  6.53 us (6%)
  other arithmetic  4.15 us (4%)
    reduce_scatter x1, waiting for transfers between devices, shards(): lax.psum_scatter(jacobian, ('state', 'horizon'), scatter_dimension=0, til...  33 us
    ppermute x7, starting transfers between devices, with_halo(): lax.ppermute(lax.slice_in_dim(block, block.shape[dim] - width, None, axis...  26.3 us
    ppermute x7, waiting for transfers between devices, with_halo(): lax.ppermute(lax.slice_in_dim(block, 0, width, axis=dim), axis, backward)  12.2 us
    ppermute x7, starting transfers between devices, with_halo(): lax.ppermute(lax.slice_in_dim(block, 0, width, axis=dim), axis, backward)  9.04 us
    dot_general x7, matrix products, pull_back(): jnp.einsum('cru,cjuv->cjrv', scaled, masked, precision=lax.Precision.HIGH...  3.93 us
    dot_general x7, matrix products, pull_back(): jnp.einsum('cjb,cjrv->brv', target, contrib, precision=lax.Precision.HIGH...  3.75 us
  transfers between devices with their start and end apart: 15, of which 8 were waited for; matrix products, arithmetic and copies ran while one was open for 1% of the time, Pallas kernels for 0%

profile of v1, /device:TPU:0, one launch (start us, length us, event | category | flops | bytes accessed | tf_op | source)
XLA Modules:
  0.0 117.7 jit_solution(11005362897370457604)
XLA Ops:
  9.1 1.5 %fusion.49 = f32[4,4,128,32]{2,3,1,0:T(8,128)S(1)} fusion(bf16[4,4,128,128]{3,2,1,0:T(8,128)(2,1)} %param.39, pred[4,4]{1,0:T(4,128)(4,1)S(1)} %iota_compare_fusion.1, f32[4,32,128,1]{2,0,1,3:T(4,128)S(1)} %multiply_bitcast_fusion.6), kind=kOutput, calls=%fused_computation.81 | convolution fusion | flops 100925440 | bytes 851984 | tf_op jit(solution)/shard_map/cru,cjuv->cjrv/dot_general | solution.py:49
  11.2 2.4 %collective-permute-start = (f32[1,32,128]{2,0,1:T(1,128)S(1)}, f32[1,32,128]{2,0,1:T(1,128)S(1)}, u32[]{:S(2)}, u32[]{:S(2)}) collective-permute-start(f32[1,32,128]{2,0,1:T(1,128)S(1)} %get-tuple-element.186), channel_id=1, source_target_pairs={{0,1},{1,4},{4,5},{5,8},{8,9},{9,12},{12,13},{2,3},{3,6},{6,7},{7,... | collective-permute-start | bytes 49160 | tf_op jit(solution)/shard_map/ppermute | solution.py:12
  13.5 1.3 %collective-permute-start.1 = (f32[1,32,128]{2,0,1:T(1,128)S(1)}, f32[1,32,128]{2,0,1:T(1,128)S(1)}, u32[]{:S(2)}, u32[]{:S(2)}) collective-permute-start(f32[1,32,128]{2,0,1:T(1,128)S(1)} %get-tuple-element.185), channel_id=1, source_target_pairs={{1,0},{4,1},{5,4},{8,5},{9,8},{12,9},{13,12},{3,2},{6,3},{7,6},{10... | collective-permute-start | bytes 49160 | tf_op jit(solution)/shard_map/ppermute | solution.py:15
  16.2 2.6 %collective-permute-done.1 = f32[1,32,128]{2,0,1:T(1,128)S(1)} collective-permute-done((f32[1,32,128]{2,0,1:T(1,128)S(1)}, f32[1,32,128]{2,0,1:T(1,128)S(1)}, u32[]{:S(2)}, u32[]{:S(2)}) %collective-permute-start.1) | collective-permute-done | bytes 16416 | tf_op jit(solution)/shard_map/ppermute | solution.py:15
  21.5 4.4 %collective-permute-start.2 = (f32[1,32,128]{2,0,1:T(1,128)S(1)}, f32[1,32,128]{2,0,1:T(1,128)S(1)}, u32[]{:S(2)}, u32[]{:S(2)}) collective-permute-start(f32[1,32,128]{2,0,1:T(1,128)S(1)} %get-tuple-element.184), channel_id=1, source_target_pairs={{0,1},{1,4},{4,5},{5,8},{8,9},{9,12},{12,13},{2,3},{3,6},{6,7},{7,... | collective-permute-start | bytes 49160 | tf_op jit(solution)/shard_map/ppermute | solution.py:12
  25.9 1.3 %collective-permute-start.3 = (f32[1,32,128]{2,0,1:T(1,128)S(1)}, f32[1,32,128]{2,0,1:T(1,128)S(1)}, u32[]{:S(2)}, u32[]{:S(2)}) collective-permute-start(f32[1,32,128]{2,0,1:T(1,128)S(1)} %get-tuple-element.183), channel_id=1, source_target_pairs={{1,0},{4,1},{5,4},{8,5},{9,8},{12,9},{13,12},{3,2},{6,3},{7,6},{10... | collective-permute-start | bytes 49160 | tf_op jit(solution)/shard_map/ppermute | solution.py:15
  27.3 1.6 %collective-permute-done.3 = f32[1,32,128]{2,0,1:T(1,128)S(1)} collective-permute-done((f32[1,32,128]{2,0,1:T(1,128)S(1)}, f32[1,32,128]{2,0,1:T(1,128)S(1)}, u32[]{:S(2)}, u32[]{:S(2)}) %collective-permute-start.3) | collective-permute-done | bytes 16416 | tf_op jit(solution)/shard_map/ppermute | solution.py:15
  30.8 3.9 %collective-permute-start.4 = (f32[1,32,128]{2,0,1:T(1,128)S(1)}, f32[1,32,128]{2,0,1:T(1,128)S(1)}, u32[]{:S(2)}, u32[]{:S(2)}) collective-permute-start(f32[1,32,128]{2,0,1:T(1,128)S(1)} %get-tuple-element.182), channel_id=1, source_target_pairs={{0,1},{1,4},{4,5},{5,8},{8,9},{9,12},{12,13},{2,3},{3,6},{6,7},{7,... | collective-permute-start | bytes 49160 | tf_op jit(solution)/shard_map/ppermute | solution.py:12
  34.7 1.3 %collective-permute-start.5 = (f32[1,32,128]{2,0,1:T(1,128)S(1)}, f32[1,32,128]{2,0,1:T(1,128)S(1)}, u32[]{:S(2)}, u32[]{:S(2)}) collective-permute-start(f32[1,32,128]{2,0,1:T(1,128)S(1)} %get-tuple-element.181), channel_id=1, source_target_pairs={{1,0},{4,1},{5,4},{8,5},{9,8},{12,9},{13,12},{3,2},{6,3},{7,6},{10... | collective-permute-start | bytes 49160 | tf_op jit(solution)/shard_map/ppermute | solution.py:15
  36.2 1.6 %collective-permute-done.5 = f32[1,32,128]{2,0,1:T(1,128)S(1)} collective-permute-done((f32[1,32,128]{2,0,1:T(1,128)S(1)}, f32[1,32,128]{2,0,1:T(1,128)S(1)}, u32[]{:S(2)}, u32[]{:S(2)}) %collective-permute-start.5) | collective-permute-done | bytes 16416 | tf_op jit(solution)/shard_map/ppermute | solution.py:15
  39.7 3.9 %collective-permute-start.6 = (f32[1,32,128]{2,0,1:T(1,128)S(1)}, f32[1,32,128]{2,0,1:T(1,128)S(1)}, u32[]{:S(2)}, u32[]{:S(2)}) collective-permute-start(f32[1,32,128]{2,0,1:T(1,128)S(1)} %get-tuple-element.180), channel_id=1, source_target_pairs={{0,1},{1,4},{4,5},{5,8},{8,9},{9,12},{12,13},{2,3},{3,6},{6,7},{7,... | collective-permute-start | bytes 49160 | tf_op jit(solution)/shard_map/ppermute | solution.py:12
  43.6 1.3 %collective-permute-start.7 = (f32[1,32,128]{2,0,1:T(1,128)S(1)}, f32[1,32,128]{2,0,1:T(1,128)S(1)}, u32[]{:S(2)}, u32[]{:S(2)}) collective-permute-start(f32[1,32,128]{2,0,1:T(1,128)S(1)} %get-tuple-element.179), channel_id=1, source_target_pairs={{1,0},{4,1},{5,4},{8,5},{9,8},{12,9},{13,12},{3,2},{6,3},{7,6},{10... | collective-permute-start | bytes 49160 | tf_op jit(solution)/shard_map/ppermute | solution.py:15
  45.1 1.6 %collective-permute-done.7 = f32[1,32,128]{2,0,1:T(1,128)S(1)} collective-permute-done((f32[1,32,128]{2,0,1:T(1,128)S(1)}, f32[1,32,128]{2,0,1:T(1,128)S(1)}, u32[]{:S(2)}, u32[]{:S(2)}) %collective-permute-start.7) | collective-permute-done | bytes 16416 | tf_op jit(solution)/shard_map/ppermute | solution.py:15
  48.5 3.9 %collective-permute-start.8 = (f32[1,32,128]{2,0,1:T(1,128)S(1)}, f32[1,32,128]{2,0,1:T(1,128)S(1)}, u32[]{:S(2)}, u32[]{:S(2)}) collective-permute-start(f32[1,32,128]{2,0,1:T(1,128)S(1)} %get-tuple-element.178), channel_id=1, source_target_pairs={{0,1},{1,4},{4,5},{5,8},{8,9},{9,12},{12,13},{2,3},{3,6},{6,7},{7,... | collective-permute-start | bytes 49160 | tf_op jit(solution)/shard_map/ppermute | solution.py:12
  52.4 1.3 %collective-permute-start.9 = (f32[1,32,128]{2,0,1:T(1,128)S(1)}, f32[1,32,128]{2,0,1:T(1,128)S(1)}, u32[]{:S(2)}, u32[]{:S(2)}) collective-permute-start(f32[1,32,128]{2,0,1:T(1,128)S(1)} %get-tuple-element.177), channel_id=1, source_target_pairs={{1,0},{4,1},{5,4},{8,5},{9,8},{12,9},{13,12},{3,2},{6,3},{7,6},{10... | collective-permute-start | bytes 49160 | tf_op jit(solution)/shard_map/ppermute | solution.py:15
  53.9 1.6 %collective-permute-done.9 = f32[1,32,128]{2,0,1:T(1,128)S(1)} collective-permute-done((f32[1,32,128]{2,0,1:T(1,128)S(1)}, f32[1,32,128]{2,0,1:T(1,128)S(1)}, u32[]{:S(2)}, u32[]{:S(2)}) %collective-permute-start.9) | collective-permute-done | bytes 16416 | tf_op jit(solution)/shard_map/ppermute | solution.py:15
  57.4 3.9 %collective-permute-start.10 = (f32[1,32,128]{2,0,1:T(1,128)S(1)}, f32[1,32,128]{2,0,1:T(1,128)S(1)}, u32[]{:S(2)}, u32[]{:S(2)}) collective-permute-start(f32[1,32,128]{2,0,1:T(1,128)S(1)} %get-tuple-element.176), channel_id=1, source_target_pairs={{0,1},{1,4},{4,5},{5,8},{8,9},{9,12},{12,13},{2,3},{3,6},{6,7},{7,... | collective-permute-start | bytes 49160 | tf_op jit(solution)/shard_map/ppermute | solution.py:12
  61.3 1.3 %collective-permute-start.11 = (f32[1,32,128]{2,0,1:T(1,128)S(1)}, f32[1,32,128]{2,0,1:T(1,128)S(1)}, u32[]{:S(2)}, u32[]{:S(2)}) collective-permute-start(f32[1,32,128]{2,0,1:T(1,128)S(1)} %get-tuple-element.175), channel_id=1, source_target_pairs={{1,0},{4,1},{5,4},{8,5},{9,8},{12,9},{13,12},{3,2},{6,3},{7,6},{10... | collective-permute-start | bytes 49160 | tf_op jit(solution)/shard_map/ppermute | solution.py:15
  62.8 1.6 %collective-permute-done.11 = f32[1,32,128]{2,0,1:T(1,128)S(1)} collective-permute-done((f32[1,32,128]{2,0,1:T(1,128)S(1)}, f32[1,32,128]{2,0,1:T(1,128)S(1)}, u32[]{:S(2)}, u32[]{:S(2)}) %collective-permute-start.11) | collective-permute-done | bytes 16416 | tf_op jit(solution)/shard_map/ppermute | solution.py:15
  66.2 3.9 %collective-permute-start.12 = (f32[1,32,128]{2,0,1:T(1,128)S(1)}, f32[1,32,128]{2,0,1:T(1,128)S(1)}, u32[]{:S(2)}, u32[]{:S(2)}) collective-permute-start(f32[1,32,128]{2,0,1:T(1,128)S(1)} %get-tuple-element.174), channel_id=1, source_target_pairs={{0,1},{1,4},{4,5},{5,8},{8,9},{9,12},{12,13},{2,3},{3,6},{6,7},{7,... | collective-permute-start | bytes 49160 | tf_op jit(solution)/shard_map/ppermute | solution.py:12
  70.2 1.3 %collective-permute-start.13 = (f32[1,32,128]{2,0,1:T(1,128)S(1)}, f32[1,32,128]{2,0,1:T(1,128)S(1)}, u32[]{:S(2)}, u32[]{:S(2)}) collective-permute-start(f32[1,32,128]{2,0,1:T(1,128)S(1)} %get-tuple-element.173), channel_id=1, source_target_pairs={{1,0},{4,1},{5,4},{8,5},{9,8},{12,9},{13,12},{3,2},{6,3},{7,6},{10... | collective-permute-start | bytes 49160 | tf_op jit(solution)/shard_map/ppermute | solution.py:15
  71.7 1.6 %collective-permute-done.13 = f32[1,32,128]{2,0,1:T(1,128)S(1)} collective-permute-done((f32[1,32,128]{2,0,1:T(1,128)S(1)}, f32[1,32,128]{2,0,1:T(1,128)S(1)}, u32[]{:S(2)}, u32[]{:S(2)}) %collective-permute-start.13) | collective-permute-done | bytes 16416 | tf_op jit(solution)/shard_map/ppermute | solution.py:15
  76.4 33.0 %reduce-scatter.2.cloned.1.call-done = f32[16,2,4,128]{3,0,2,1:T(8,128)} async-done(((f32[128,2,4,128]{3,0,2,1:T(8,128)}), f32[16,2,4,128]{3,0,2,1:T(8,128)}) %reduce-scatter.2.cloned.1.call-update) | async-done | bytes 65552 | tf_op jit(solution)/shard_map/reduce_scatter | solution.py:106
  109.4 1.5 %copy.22 = f32[16,2,4,128]{3,2,1,0:T(4,128)} copy(f32[16,2,4,128]{3,0,2,1:T(8,128)} %reduce-scatter.2.cloned.1.call-done) | data formatting | bytes 131072 | tf_op jit(solution)/shard_map/reduce_scatter | solution.py:106
  (151 shorter events, 20.0 us)
Async XLA Ops:
  6.5 1.6 %copy-start = (f32[16,2]{0,1:T(2,128)S(1)}, f32[16,2]{0,1:T(2,128)}, u32[]{:S(2)}) copy-start(f32[16,2]{0,1:T(2,128)} %param.37) | copy-start | bytes 388
  6.5 0.8 copy-start.5
  6.5 102.9 %reduce-scatter.2.cloned.1.call-start = ((), (), s32[]{:S(2)}) async-start(), calls=%async_computation.1 | async-start | bytes 589824 | tf_op jit(solution)/shard_map/reduce_scatter | solution.py:106
  7.4 0.8 copy-start.6
  8.2 0.7 copy-start.3
  9.1 5.8 %copy-start.1 = (bf16[512,4,128]{2,1,0:T(4,128)(2,1)S(1)}, bf16[512,4,128]{2,1,0:T(4,128)(2,1)}, u32[]{:S(2)}) copy-start(bf16[512,4,128]{2,1,0:T(4,128)(2,1)} %param.35) | copy-start | bytes 1572868
  11.2 4.9 %collective-permute-start = (f32[1,32,128]{2,0,1:T(1,128)S(1)}, f32[1,32,128]{2,0,1:T(1,128)S(1)}, u32[]{:S(2)}, u32[]{:S(2)}) collective-permute-start(f32[1,32,128]{2,0,1:T(1,128)S(1)} %get-tuple-element.186), channel_id=1, source_target_pairs={{0,1},{1,4},{4,5},{5,8},{8,9},{9,12},{12,13},{2,3},{3,6},{6,7},{7,... | collective-permute-start | bytes 49160 | tf_op jit(solution)/shard_map/ppermute | solution.py:12
  13.5 5.3 %collective-permute-start.1 = (f32[1,32,128]{2,0,1:T(1,128)S(1)}, f32[1,32,128]{2,0,1:T(1,128)S(1)}, u32[]{:S(2)}, u32[]{:S(2)}) collective-permute-start(f32[1,32,128]{2,0,1:T(1,128)S(1)} %get-tuple-element.185), channel_id=1, source_target_pairs={{1,0},{4,1},{5,4},{8,5},{9,8},{12,9},{13,12},{3,2},{6,3},{7,6},{10... | collective-permute-start | bytes 49160 | tf_op jit(solution)/shard_map/ppermute | solution.py:15
  15.0 0.8 copy-start.2
  19.4 1.1 copy-start.4
  21.5 5.7 %collective-permute-start.2 = (f32[1,32,128]{2,0,1:T(1,128)S(1)}, f32[1,32,128]{2,0,1:T(1,128)S(1)}, u32[]{:S(2)}, u32[]{:S(2)}) collective-permute-start(f32[1,32,128]{2,0,1:T(1,128)S(1)} %get-tuple-element.184), channel_id=1, source_target_pairs={{0,1},{1,4},{4,5},{5,8},{8,9},{9,12},{12,13},{2,3},{3,6},{6,7},{7,... | collective-permute-start | bytes 49160 | tf_op jit(solution)/shard_map/ppermute | solution.py:12
  25.9 3.1 %collective-permute-start.3 = (f32[1,32,128]{2,0,1:T(1,128)S(1)}, f32[1,32,128]{2,0,1:T(1,128)S(1)}, u32[]{:S(2)}, u32[]{:S(2)}) collective-permute-start(f32[1,32,128]{2,0,1:T(1,128)S(1)} %get-tuple-element.183), channel_id=1, source_target_pairs={{1,0},{4,1},{5,4},{8,5},{9,8},{12,9},{13,12},{3,2},{6,3},{7,6},{10... | collective-permute-start | bytes 49160 | tf_op jit(solution)/shard_map/ppermute | solution.py:15
  30.8 5.3 %collective-permute-start.4 = (f32[1,32,128]{2,0,1:T(1,128)S(1)}, f32[1,32,128]{2,0,1:T(1,128)S(1)}, u32[]{:S(2)}, u32[]{:S(2)}) collective-permute-start(f32[1,32,128]{2,0,1:T(1,128)S(1)} %get-tuple-element.182), channel_id=1, source_target_pairs={{0,1},{1,4},{4,5},{5,8},{8,9},{9,12},{12,13},{2,3},{3,6},{6,7},{7,... | collective-permute-start | bytes 49160 | tf_op jit(solution)/shard_map/ppermute | solution.py:12
  34.7 3.1 %collective-permute-start.5 = (f32[1,32,128]{2,0,1:T(1,128)S(1)}, f32[1,32,128]{2,0,1:T(1,128)S(1)}, u32[]{:S(2)}, u32[]{:S(2)}) collective-permute-start(f32[1,32,128]{2,0,1:T(1,128)S(1)} %get-tuple-element.181), channel_id=1, source_target_pairs={{1,0},{4,1},{5,4},{8,5},{9,8},{12,9},{13,12},{3,2},{6,3},{7,6},{10... | collective-permute-start | bytes 49160 | tf_op jit(solution)/shard_map/ppermute | solution.py:15
  39.7 5.3 %collective-permute-start.6 = (f32[1,32,128]{2,0,1:T(1,128)S(1)}, f32[1,32,128]{2,0,1:T(1,128)S(1)}, u32[]{:S(2)}, u32[]{:S(2)}) collective-permute-start(f32[1,32,128]{2,0,1:T(1,128)S(1)} %get-tuple-element.180), channel_id=1, source_target_pairs={{0,1},{1,4},{4,5},{5,8},{8,9},{9,12},{12,13},{2,3},{3,6},{6,7},{7,... | collective-permute-start | bytes 49160 | tf_op jit(solution)/shard_map/ppermute | solution.py:12
  43.6 3.1 %collective-permute-start.7 = (f32[1,32,128]{2,0,1:T(1,128)S(1)}, f32[1,32,128]{2,0,1:T(1,128)S(1)}, u32[]{:S(2)}, u32[]{:S(2)}) collective-permute-start(f32[1,32,128]{2,0,1:T(1,128)S(1)} %get-tuple-element.179), channel_id=1, source_target_pairs={{1,0},{4,1},{5,4},{8,5},{9,8},{12,9},{13,12},{3,2},{6,3},{7,6},{10... | collective-permute-start | bytes 49160 | tf_op jit(solution)/shard_map/ppermute | solution.py:15
  48.5 5.3 %collective-permute-start.8 = (f32[1,32,128]{2,0,1:T(1,128)S(1)}, f32[1,32,128]{2,0,1:T(1,128)S(1)}, u32[]{:S(2)}, u32[]{:S(2)}) collective-permute-start(f32[1,32,128]{2,0,1:T(1,128)S(1)} %get-tuple-element.178), channel_id=1, source_target_pairs={{0,1},{1,4},{4,5},{5,8},{8,9},{9,12},{12,13},{2,3},{3,6},{6,7},{7,... | collective-permute-start | bytes 49160 | tf_op jit(solution)/shard_map/ppermute | solution.py:12
  52.4 3.1 %collective-permute-start.9 = (f32[1,32,128]{2,0,1:T(1,128)S(1)}, f32[1,32,128]{2,0,1:T(1,128)S(1)}, u32[]{:S(2)}, u32[]{:S(2)}) collective-permute-start(f32[1,32,128]{2,0,1:T(1,128)S(1)} %get-tuple-element.177), channel_id=1, source_target_pairs={{1,0},{4,1},{5,4},{8,5},{9,8},{12,9},{13,12},{3,2},{6,3},{7,6},{10... | collective-permute-start | bytes 49160 | tf_op jit(solution)/shard_map/ppermute | solution.py:15
  57.4 5.3 %collective-permute-start.10 = (f32[1,32,128]{2,0,1:T(1,128)S(1)}, f32[1,32,128]{2,0,1:T(1,128)S(1)}, u32[]{:S(2)}, u32[]{:S(2)}) collective-permute-start(f32[1,32,128]{2,0,1:T(1,128)S(1)} %get-tuple-element.176), channel_id=1, source_target_pairs={{0,1},{1,4},{4,5},{5,8},{8,9},{9,12},{12,13},{2,3},{3,6},{6,7},{7,... | collective-permute-start | bytes 49160 | tf_op jit(solution)/shard_map/ppermute | solution.py:12
  61.3 3.1 %collective-permute-start.11 = (f32[1,32,128]{2,0,1:T(1,128)S(1)}, f32[1,32,128]{2,0,1:T(1,128)S(1)}, u32[]{:S(2)}, u32[]{:S(2)}) collective-permute-start(f32[1,32,128]{2,0,1:T(1,128)S(1)} %get-tuple-element.175), channel_id=1, source_target_pairs={{1,0},{4,1},{5,4},{8,5},{9,8},{12,9},{13,12},{3,2},{6,3},{7,6},{10... | collective-permute-start | bytes 49160 | tf_op jit(solution)/shard_map/ppermute | solution.py:15
  66.2 5.3 %collective-permute-start.12 = (f32[1,32,128]{2,0,1:T(1,128)S(1)}, f32[1,32,128]{2,0,1:T(1,128)S(1)}, u32[]{:S(2)}, u32[]{:S(2)}) collective-permute-start(f32[1,32,128]{2,0,1:T(1,128)S(1)} %get-tuple-element.174), channel_id=1, source_target_pairs={{0,1},{1,4},{4,5},{5,8},{8,9},{9,12},{12,13},{2,3},{3,6},{6,7},{7,... | collective-permute-start | bytes 49160 | tf_op jit(solution)/shard_map/ppermute | solution.py:12
  70.2 3.1 %collective-permute-start.13 = (f32[1,32,128]{2,0,1:T(1,128)S(1)}, f32[1,32,128]{2,0,1:T(1,128)S(1)}, u32[]{:S(2)}, u32[]{:S(2)}) collective-permute-start(f32[1,32,128]{2,0,1:T(1,128)S(1)} %get-tuple-element.173), channel_id=1, source_target_pairs={{1,0},{4,1},{5,4},{8,5},{9,8},{12,9},{13,12},{3,2},{6,3},{7,6},{10... | collective-permute-start | bytes 49160 | tf_op jit(solution)/shard_map/ppermute | solution.py:15
Sparse Core Ops, SparseCore 0:
  76.5 32.8 reduce-scatter.1

commit v2 on v1

--- a/solution.py
+++ b/solution.py
@@ -31,6 +31,30 @@
         total = total + moved
         shift *= 2
     return total
+
+
+def halving_scatter(full):
+    state_count = lax.axis_size("state")
+    core_count = lax.axis_size("horizon")
+    count = state_count * core_count
+    if count & (count - 1) or core_count & (core_count - 1):
+        return lax.psum_scatter(full, ("state", "horizon"), scatter_dimension=0, tiled=True)
+    index = lax.axis_index(("state", "horizon"))
+    held = full.reshape((count, full.shape[0] // count) + full.shape[1:])
+    step = 1
+    while step < count:
+        if step < core_count:
+            axis, size, flip = "horizon", core_count, step
+        else:
+            axis, size, flip = "state", state_count, step // core_count
+        pairs = [(member, member ^ flip) for member in range(size)]
+        bit = (index // step) % 2
+        halves = held.reshape((held.shape[0] // 2, 2) + held.shape[1:])
+        keep = jnp.where(bit == 1, halves[:, 1], halves[:, 0])
+        send = jnp.where(bit == 1, halves[:, 0], halves[:, 1])
+        held = keep + lax.ppermute(send, axis, pairs)
+        step *= 2
+    return held.reshape(held.shape[1:])
 
 
 def split_product(rows_full, data_half):
@@ -103,7 +127,7 @@
         )
     partial_news = jnp.concatenate(pieces, axis=0)
     jacobian = diagonal_sums(partial_news)
-    return lax.psum_scatter(jacobian, ("state", "horizon"), scatter_dimension=0, tiled=True)
+    return halving_scatter(jacobian)
 
 
 def solution(mesh):

time: 118 us -> 85.2 us (0.72)
  waiting for transfers between devices: 45.3 us -> 20.4 us
  between operations: 14.2 us -> 0.92 us
  starting transfers between devices: 35.4 us -> 41.7 us
    reduce_scatter x1 -> x0, waiting for transfers between devices: 33 us -> none  [shards(): lax.psum_scatter(jacobian, ('state', 'horizon'), scatter_dimension=0, til...]
    ppermute x0 -> x3, waiting for transfers between devices: none -> 8.22 us  [halving_scatter(): held = keep + lax.ppermute(send, axis, pairs)]
    ppermute x0 -> x3, starting transfers between devices: none -> 6.38 us  [halving_scatter(): held = keep + lax.ppermute(send, axis, pairs)]
    reduce_scatter x1 -> x0, local copies, waits for them, and re-layouts: 1.49 us -> none  [shards(): lax.psum_scatter(jacobian, ('state', 'horizon'), scatter_dimension=0, til...]
  transfers between devices with their start and end apart: 15 -> 17, of which waited for: 8 -> 10; matrix products, arithmetic and copies ran while one was open for 1% -> 2% of each run, Pallas kernels for 0% -> 0%
where the time goes in v2:
time: 85.2 us; the launch traced here: 84.5 us
  starting transfers between devices  41.7 us (49%)
  waiting for transfers between devices  20.4 us (24%)
  matrix products  12.2 us (14%)
  local copies, waits for them, and re-layouts  5.75 us (7%)
  other arithmetic  3.53 us (4%)
  between operations  0.92 us (1%)
    ppermute x7, starting transfers between devices, with_halo(): lax.ppermute(lax.slice_in_dim(block, block.shape[dim] - width, None, axis...  26.3 us
    ppermute x7, waiting for transfers between devices, with_halo(): lax.ppermute(lax.slice_in_dim(block, 0, width, axis=dim), axis, backward)  12.1 us
    ppermute x7, starting transfers between devices, with_halo(): lax.ppermute(lax.slice_in_dim(block, 0, width, axis=dim), axis, backward)  9.04 us
    ppermute x3, waiting for transfers between devices, halving_scatter(): held = keep + lax.ppermute(send, axis, pairs)  8.22 us
    ppermute x3, starting transfers between devices, halving_scatter(): held = keep + lax.ppermute(send, axis, pairs)  6.38 us
    dot_general x7, matrix products, pull_back(): jnp.einsum('cru,cjuv->cjrv', scaled, masked, precision=lax.Precision.HIGH...  3.92 us
    dot_general x7, matrix products, pull_back(): jnp.einsum('cjb,cjrv->brv', target, contrib, precision=lax.Precision.HIGH...  3.78 us
    unnamed x23, local copies, waits for them, and re-layouts  2.05 us
  transfers between devices with their start and end apart: 17, of which 10 were waited for; matrix products, arithmetic and copies ran while one was open for 2% of the time, Pallas kernels for 0%

profile of v2, /device:TPU:0, one launch (start us, length us, event | category | flops | bytes accessed | tf_op | source)
XLA Modules:
  0.0 84.5 jit_solution(3122662489814533832)
XLA Ops:
  2.5 1.5 %fusion.49 = f32[4,4,128,32]{2,3,1,0:T(8,128)S(1)} fusion(bf16[4,4,128,128]{3,2,1,0:T(8,128)(2,1)} %param.39, pred[4,4]{1,0:T(4,128)(4,1)S(1)} %iota_compare_fusion.1, f32[4,32,128,1]{2,0,1,3:T(4,128)S(1)} %multiply_bitcast_fusion.6), kind=kOutput, calls=%fused_computation.83 | convolution fusion | flops 100925440 | bytes 851984 | tf_op jit(solution)/shard_map/cru,cjuv->cjrv/dot_general | solution.py:73
  4.6 2.4 %collective-permute-start = (f32[1,32,128]{2,0,1:T(1,128)S(1)}, f32[1,32,128]{2,0,1:T(1,128)S(1)}, u32[]{:S(2)}, u32[]{:S(2)}) collective-permute-start(f32[1,32,128]{2,0,1:T(1,128)S(1)} %get-tuple-element.188), channel_id=1, source_target_pairs={{0,1},{1,4},{4,5},{5,8},{8,9},{9,12},{12,13},{2,3},{3,6},{6,7},{7,... | collective-permute-start | bytes 49160 | tf_op jit(solution)/shard_map/ppermute | solution.py:12
  7.0 1.3 %collective-permute-start.1 = (f32[1,32,128]{2,0,1:T(1,128)S(1)}, f32[1,32,128]{2,0,1:T(1,128)S(1)}, u32[]{:S(2)}, u32[]{:S(2)}) collective-permute-start(f32[1,32,128]{2,0,1:T(1,128)S(1)} %get-tuple-element.187), channel_id=1, source_target_pairs={{1,0},{4,1},{5,4},{8,5},{9,8},{12,9},{13,12},{3,2},{6,3},{7,6},{10... | collective-permute-start | bytes 49160 | tf_op jit(solution)/shard_map/ppermute | solution.py:15
  9.7 2.6 %collective-permute-done.1 = f32[1,32,128]{2,0,1:T(1,128)S(1)} collective-permute-done((f32[1,32,128]{2,0,1:T(1,128)S(1)}, f32[1,32,128]{2,0,1:T(1,128)S(1)}, u32[]{:S(2)}, u32[]{:S(2)}) %collective-permute-start.1) | collective-permute-done | bytes 16416 | tf_op jit(solution)/shard_map/ppermute | solution.py:15
  14.9 4.4 %collective-permute-start.2 = (f32[1,32,128]{2,0,1:T(1,128)S(1)}, f32[1,32,128]{2,0,1:T(1,128)S(1)}, u32[]{:S(2)}, u32[]{:S(2)}) collective-permute-start(f32[1,32,128]{2,0,1:T(1,128)S(1)} %get-tuple-element.186), channel_id=1, source_target_pairs={{0,1},{1,4},{4,5},{5,8},{8,9},{9,12},{12,13},{2,3},{3,6},{6,7},{7,... | collective-permute-start | bytes 49160 | tf_op jit(solution)/shard_map/ppermute | solution.py:12
  19.3 1.3 %collective-permute-start.3 = (f32[1,32,128]{2,0,1:T(1,128)S(1)}, f32[1,32,128]{2,0,1:T(1,128)S(1)}, u32[]{:S(2)}, u32[]{:S(2)}) collective-permute-start(f32[1,32,128]{2,0,1:T(1,128)S(1)} %get-tuple-element.185), channel_id=1, source_target_pairs={{1,0},{4,1},{5,4},{8,5},{9,8},{12,9},{13,12},{3,2},{6,3},{7,6},{10... | collective-permute-start | bytes 49160 | tf_op jit(solution)/shard_map/ppermute | solution.py:15
  20.8 1.6 %collective-permute-done.3 = f32[1,32,128]{2,0,1:T(1,128)S(1)} collective-permute-done((f32[1,32,128]{2,0,1:T(1,128)S(1)}, f32[1,32,128]{2,0,1:T(1,128)S(1)}, u32[]{:S(2)}, u32[]{:S(2)}) %collective-permute-start.3) | collective-permute-done | bytes 16416 | tf_op jit(solution)/shard_map/ppermute | solution.py:15
  24.3 3.9 %collective-permute-start.4 = (f32[1,32,128]{2,0,1:T(1,128)S(1)}, f32[1,32,128]{2,0,1:T(1,128)S(1)}, u32[]{:S(2)}, u32[]{:S(2)}) collective-permute-start(f32[1,32,128]{2,0,1:T(1,128)S(1)} %get-tuple-element.184), channel_id=1, source_target_pairs={{0,1},{1,4},{4,5},{5,8},{8,9},{9,12},{12,13},{2,3},{3,6},{6,7},{7,... | collective-permute-start | bytes 49160 | tf_op jit(solution)/shard_map/ppermute | solution.py:12
  28.2 1.3 %collective-permute-start.5 = (f32[1,32,128]{2,0,1:T(1,128)S(1)}, f32[1,32,128]{2,0,1:T(1,128)S(1)}, u32[]{:S(2)}, u32[]{:S(2)}) collective-permute-start(f32[1,32,128]{2,0,1:T(1,128)S(1)} %get-tuple-element.183), channel_id=1, source_target_pairs={{1,0},{4,1},{5,4},{8,5},{9,8},{12,9},{13,12},{3,2},{6,3},{7,6},{10... | collective-permute-start | bytes 49160 | tf_op jit(solution)/shard_map/ppermute | solution.py:15
  29.7 1.6 %collective-permute-done.5 = f32[1,32,128]{2,0,1:T(1,128)S(1)} collective-permute-done((f32[1,32,128]{2,0,1:T(1,128)S(1)}, f32[1,32,128]{2,0,1:T(1,128)S(1)}, u32[]{:S(2)}, u32[]{:S(2)}) %collective-permute-start.5) | collective-permute-done | bytes 16416 | tf_op jit(solution)/shard_map/ppermute | solution.py:15
  33.1 3.9 %collective-permute-start.6 = (f32[1,32,128]{2,0,1:T(1,128)S(1)}, f32[1,32,128]{2,0,1:T(1,128)S(1)}, u32[]{:S(2)}, u32[]{:S(2)}) collective-permute-start(f32[1,32,128]{2,0,1:T(1,128)S(1)} %get-tuple-element.182), channel_id=1, source_target_pairs={{0,1},{1,4},{4,5},{5,8},{8,9},{9,12},{12,13},{2,3},{3,6},{6,7},{7,... | collective-permute-start | bytes 49160 | tf_op jit(solution)/shard_map/ppermute | solution.py:12
  37.1 1.3 %collective-permute-start.7 = (f32[1,32,128]{2,0,1:T(1,128)S(1)}, f32[1,32,128]{2,0,1:T(1,128)S(1)}, u32[]{:S(2)}, u32[]{:S(2)}) collective-permute-start(f32[1,32,128]{2,0,1:T(1,128)S(1)} %get-tuple-element.181), channel_id=1, source_target_pairs={{1,0},{4,1},{5,4},{8,5},{9,8},{12,9},{13,12},{3,2},{6,3},{7,6},{10... | collective-permute-start | bytes 49160 | tf_op jit(solution)/shard_map/ppermute | solution.py:15
  38.5 1.6 %collective-permute-done.7 = f32[1,32,128]{2,0,1:T(1,128)S(1)} collective-permute-done((f32[1,32,128]{2,0,1:T(1,128)S(1)}, f32[1,32,128]{2,0,1:T(1,128)S(1)}, u32[]{:S(2)}, u32[]{:S(2)}) %collective-permute-start.7) | collective-permute-done | bytes 16416 | tf_op jit(solution)/shard_map/ppermute | solution.py:15
  42.0 3.9 %collective-permute-start.8 = (f32[1,32,128]{2,0,1:T(1,128)S(1)}, f32[1,32,128]{2,0,1:T(1,128)S(1)}, u32[]{:S(2)}, u32[]{:S(2)}) collective-permute-start(f32[1,32,128]{2,0,1:T(1,128)S(1)} %get-tuple-element.180), channel_id=1, source_target_pairs={{0,1},{1,4},{4,5},{5,8},{8,9},{9,12},{12,13},{2,3},{3,6},{6,7},{7,... | collective-permute-start | bytes 49160 | tf_op jit(solution)/shard_map/ppermute | solution.py:12
  47.4 1.6 %collective-permute-done.9 = f32[1,32,128]{2,0,1:T(1,128)S(1)} collective-permute-done((f32[1,32,128]{2,0,1:T(1,128)S(1)}, f32[1,32,128]{2,0,1:T(1,128)S(1)}, u32[]{:S(2)}, u32[]{:S(2)}) %collective-permute-start.9) | collective-permute-done | bytes 16416 | tf_op jit(solution)/shard_map/ppermute | solution.py:15
  50.9 3.9 %collective-permute-start.10 = (f32[1,32,128]{2,0,1:T(1,128)S(1)}, f32[1,32,128]{2,0,1:T(1,128)S(1)}, u32[]{:S(2)}, u32[]{:S(2)}) collective-permute-start(f32[1,32,128]{2,0,1:T(1,128)S(1)} %get-tuple-element.178), channel_id=1, source_target_pairs={{0,1},{1,4},{4,5},{5,8},{8,9},{9,12},{12,13},{2,3},{3,6},{6,7},{7,... | collective-permute-start | bytes 49160 | tf_op jit(solution)/shard_map/ppermute | solution.py:12
  56.3 1.6 %collective-permute-done.11 = f32[1,32,128]{2,0,1:T(1,128)S(1)} collective-permute-done((f32[1,32,128]{2,0,1:T(1,128)S(1)}, f32[1,32,128]{2,0,1:T(1,128)S(1)}, u32[]{:S(2)}, u32[]{:S(2)}) %collective-permute-start.11) | collective-permute-done | bytes 16416 | tf_op jit(solution)/shard_map/ppermute | solution.py:15
  59.7 3.9 %collective-permute-start.12 = (f32[1,32,128]{2,0,1:T(1,128)S(1)}, f32[1,32,128]{2,0,1:T(1,128)S(1)}, u32[]{:S(2)}, u32[]{:S(2)}) collective-permute-start(f32[1,32,128]{2,0,1:T(1,128)S(1)} %get-tuple-element.176), channel_id=1, source_target_pairs={{0,1},{1,4},{4,5},{5,8},{8,9},{9,12},{12,13},{2,3},{3,6},{6,7},{7,... | collective-permute-start | bytes 49160 | tf_op jit(solution)/shard_map/ppermute | solution.py:12
  65.1 1.6 %collective-permute-done.13 = f32[1,32,128]{2,0,1:T(1,128)S(1)} collective-permute-done((f32[1,32,128]{2,0,1:T(1,128)S(1)}, f32[1,32,128]{2,0,1:T(1,128)S(1)}, u32[]{:S(2)}, u32[]{:S(2)}) %collective-permute-start.13) | collective-permute-done | bytes 16416 | tf_op jit(solution)/shard_map/ppermute | solution.py:15
  69.1 2.1 %collective-permute-start.14 = (f32[4,16,2,4,128]{4,1,3,2,0:T(8,128)S(1)}, f32[4,16,2,4,128]{4,1,3,2,0:T(8,128)S(1)}, u32[]{:S(2)}, u32[]{:S(2)}) collective-permute-start(f32[4,16,2,4,128]{4,1,3,2,0:T(8,128)S(1)} %select_bitcast_fusion), channel_id=1, source_target_pairs={{0,1},{1,0},{2,3},{3,2},{4,5},{5,4},{6,7},{7,6},{8,9},{9,8},{10,11... | collective-permute-start | bytes 786440 | tf_op jit(solution)/shard_map/ppermute | solution.py:55
  72.4 1.7 %collective-permute-start.15 = (f32[2,16,2,4,128]{4,1,3,2,0:T(8,128)S(1)}, f32[2,16,2,4,128]{4,1,3,2,0:T(8,128)S(1)}, u32[]{:S(2)}, u32[]{:S(2)}) collective-permute-start(f32[2,16,2,4,128]{4,1,3,2,0:T(8,128)S(1)} %select_bitcast_fusion.1), channel_id=1, source_target_pairs={{0,4},{4,0},{8,12},{12,8},{1,5},{5,1},{9,13},{13,9},{2,6},{6,2},{1... | collective-permute-start | bytes 393224 | tf_op jit(solution)/shard_map/ppermute | solution.py:55
  74.1 4.2 %collective-permute-done.15 = f32[2,16,2,4,128]{4,1,3,2,0:T(8,128)S(1)} collective-permute-done((f32[2,16,2,4,128]{4,1,3,2,0:T(8,128)S(1)}, f32[2,16,2,4,128]{4,1,3,2,0:T(8,128)S(1)}, u32[]{:S(2)}, u32[]{:S(2)}) %collective-permute-start.15) | collective-permute-done | bytes 131104 | tf_op jit(solution)/shard_map/ppermute | solution.py:55
  78.3 2.7 %collective-permute-start.16 = (f32[1,16,2,4,128]{4,1,3,2,0:T(8,128)S(1)}, f32[1,16,2,4,128]{4,1,3,2,0:T(8,128)S(1)}, u32[]{:S(2)}, u32[]{:S(2)}) collective-permute-start(f32[1,16,2,4,128]{4,1,3,2,0:T(8,128)S(1)} %select_bitcast_fusion.2), channel_id=1, source_target_pairs={{0,8},{4,12},{8,0},{12,4},{1,9},{5,13},{9,1},{13,5},{2,10},{6,14},... | collective-permute-start | bytes 196616 | tf_op jit(solution)/shard_map/ppermute | solution.py:55
  81.0 2.9 %collective-permute-done.16 = f32[1,16,2,4,128]{4,1,3,2,0:T(8,128)S(1)} collective-permute-done((f32[1,16,2,4,128]{4,1,3,2,0:T(8,128)S(1)}, f32[1,16,2,4,128]{4,1,3,2,0:T(8,128)S(1)}, u32[]{:S(2)}, u32[]{:S(2)}) %collective-permute-start.16) | collective-permute-done | bytes 65568 | tf_op jit(solution)/shard_map/ppermute | solution.py:55
  (161 shorter events, 25.0 us)
Async XLA Ops:
  0.0 1.6 %copy-start = (f32[16,2]{0,1:T(2,128)S(1)}, f32[16,2]{0,1:T(2,128)}, u32[]{:S(2)}) copy-start(f32[16,2]{0,1:T(2,128)} %param.37) | copy-start | bytes 388
  0.0 0.8 copy-start.5
  0.8 0.8 copy-start.6
  1.6 0.7 copy-start.3
  2.5 5.8 %copy-start.1 = (bf16[512,4,128]{2,1,0:T(4,128)(2,1)S(1)}, bf16[512,4,128]{2,1,0:T(4,128)(2,1)}, u32[]{:S(2)}) copy-start(bf16[512,4,128]{2,1,0:T(4,128)(2,1)} %param.35) | copy-start | bytes 1572868
  4.6 4.9 %collective-permute-start = (f32[1,32,128]{2,0,1:T(1,128)S(1)}, f32[1,32,128]{2,0,1:T(1,128)S(1)}, u32[]{:S(2)}, u32[]{:S(2)}) collective-permute-start(f32[1,32,128]{2,0,1:T(1,128)S(1)} %get-tuple-element.188), channel_id=1, source_target_pairs={{0,1},{1,4},{4,5},{5,8},{8,9},{9,12},{12,13},{2,3},{3,6},{6,7},{7,... | collective-permute-start | bytes 49160 | tf_op jit(solution)/shard_map/ppermute | solution.py:12
  7.0 5.3 %collective-permute-start.1 = (f32[1,32,128]{2,0,1:T(1,128)S(1)}, f32[1,32,128]{2,0,1:T(1,128)S(1)}, u32[]{:S(2)}, u32[]{:S(2)}) collective-permute-start(f32[1,32,128]{2,0,1:T(1,128)S(1)} %get-tuple-element.187), channel_id=1, source_target_pairs={{1,0},{4,1},{5,4},{8,5},{9,8},{12,9},{13,12},{3,2},{6,3},{7,6},{10... | collective-permute-start | bytes 49160 | tf_op jit(solution)/shard_map/ppermute | solution.py:15
  8.5 0.8 copy-start.2
  12.9 1.1 %copy-start.4 = (bf16[4,4,128,128]{3,2,1,0:T(8,128)(2,1)S(1)}, bf16[4,4,128,128]{3,2,1,0:T(8,128)(2,1)}, u32[]{:S(2)}) copy-start(bf16[4,4,128,128]{3,2,1,0:T(8,128)(2,1)} %param.39) | copy-start | bytes 1572868
  14.9 5.7 %collective-permute-start.2 = (f32[1,32,128]{2,0,1:T(1,128)S(1)}, f32[1,32,128]{2,0,1:T(1,128)S(1)}, u32[]{:S(2)}, u32[]{:S(2)}) collective-permute-start(f32[1,32,128]{2,0,1:T(1,128)S(1)} %get-tuple-element.186), channel_id=1, source_target_pairs={{0,1},{1,4},{4,5},{5,8},{8,9},{9,12},{12,13},{2,3},{3,6},{6,7},{7,... | collective-permute-start | bytes 49160 | tf_op jit(solution)/shard_map/ppermute | solution.py:12
  19.3 3.1 %collective-permute-start.3 = (f32[1,32,128]{2,0,1:T(1,128)S(1)}, f32[1,32,128]{2,0,1:T(1,128)S(1)}, u32[]{:S(2)}, u32[]{:S(2)}) collective-permute-start(f32[1,32,128]{2,0,1:T(1,128)S(1)} %get-tuple-element.185), channel_id=1, source_target_pairs={{1,0},{4,1},{5,4},{8,5},{9,8},{12,9},{13,12},{3,2},{6,3},{7,6},{10... | collective-permute-start | bytes 49160 | tf_op jit(solution)/shard_map/ppermute | solution.py:15
  24.3 5.3 %collective-permute-start.4 = (f32[1,32,128]{2,0,1:T(1,128)S(1)}, f32[1,32,128]{2,0,1:T(1,128)S(1)}, u32[]{:S(2)}, u32[]{:S(2)}) collective-permute-start(f32[1,32,128]{2,0,1:T(1,128)S(1)} %get-tuple-element.184), channel_id=1, source_target_pairs={{0,1},{1,4},{4,5},{5,8},{8,9},{9,12},{12,13},{2,3},{3,6},{6,7},{7,... | collective-permute-start | bytes 49160 | tf_op jit(solution)/shard_map/ppermute | solution.py:12
  28.2 3.1 %collective-permute-start.5 = (f32[1,32,128]{2,0,1:T(1,128)S(1)}, f32[1,32,128]{2,0,1:T(1,128)S(1)}, u32[]{:S(2)}, u32[]{:S(2)}) collective-permute-start(f32[1,32,128]{2,0,1:T(1,128)S(1)} %get-tuple-element.183), channel_id=1, source_target_pairs={{1,0},{4,1},{5,4},{8,5},{9,8},{12,9},{13,12},{3,2},{6,3},{7,6},{10... | collective-permute-start | bytes 49160 | tf_op jit(solution)/shard_map/ppermute | solution.py:15
  33.1 5.3 %collective-permute-start.6 = (f32[1,32,128]{2,0,1:T(1,128)S(1)}, f32[1,32,128]{2,0,1:T(1,128)S(1)}, u32[]{:S(2)}, u32[]{:S(2)}) collective-permute-start(f32[1,32,128]{2,0,1:T(1,128)S(1)} %get-tuple-element.182), channel_id=1, source_target_pairs={{0,1},{1,4},{4,5},{5,8},{8,9},{9,12},{12,13},{2,3},{3,6},{6,7},{7,... | collective-permute-start | bytes 49160 | tf_op jit(solution)/shard_map/ppermute | solution.py:12
  37.1 3.1 %collective-permute-start.7 = (f32[1,32,128]{2,0,1:T(1,128)S(1)}, f32[1,32,128]{2,0,1:T(1,128)S(1)}, u32[]{:S(2)}, u32[]{:S(2)}) collective-permute-start(f32[1,32,128]{2,0,1:T(1,128)S(1)} %get-tuple-element.181), channel_id=1, source_target_pairs={{1,0},{4,1},{5,4},{8,5},{9,8},{12,9},{13,12},{3,2},{6,3},{7,6},{10... | collective-permute-start | bytes 49160 | tf_op jit(solution)/shard_map/ppermute | solution.py:15
  42.0 5.3 %collective-permute-start.8 = (f32[1,32,128]{2,0,1:T(1,128)S(1)}, f32[1,32,128]{2,0,1:T(1,128)S(1)}, u32[]{:S(2)}, u32[]{:S(2)}) collective-permute-start(f32[1,32,128]{2,0,1:T(1,128)S(1)} %get-tuple-element.180), channel_id=1, source_target_pairs={{0,1},{1,4},{4,5},{5,8},{8,9},{9,12},{12,13},{2,3},{3,6},{6,7},{7,... | collective-permute-start | bytes 49160 | tf_op jit(solution)/shard_map/ppermute | solution.py:12
  45.9 3.1 %collective-permute-start.9 = (f32[1,32,128]{2,0,1:T(1,128)S(1)}, f32[1,32,128]{2,0,1:T(1,128)S(1)}, u32[]{:S(2)}, u32[]{:S(2)}) collective-permute-start(f32[1,32,128]{2,0,1:T(1,128)S(1)} %get-tuple-element.179), channel_id=1, source_target_pairs={{1,0},{4,1},{5,4},{8,5},{9,8},{12,9},{13,12},{3,2},{6,3},{7,6},{10... | collective-permute-start | bytes 49160 | tf_op jit(solution)/shard_map/ppermute | solution.py:15
  50.9 5.3 %collective-permute-start.10 = (f32[1,32,128]{2,0,1:T(1,128)S(1)}, f32[1,32,128]{2,0,1:T(1,128)S(1)}, u32[]{:S(2)}, u32[]{:S(2)}) collective-permute-start(f32[1,32,128]{2,0,1:T(1,128)S(1)} %get-tuple-element.178), channel_id=1, source_target_pairs={{0,1},{1,4},{4,5},{5,8},{8,9},{9,12},{12,13},{2,3},{3,6},{6,7},{7,... | collective-permute-start | bytes 49160 | tf_op jit(solution)/shard_map/ppermute | solution.py:12
  54.8 3.1 %collective-permute-start.11 = (f32[1,32,128]{2,0,1:T(1,128)S(1)}, f32[1,32,128]{2,0,1:T(1,128)S(1)}, u32[]{:S(2)}, u32[]{:S(2)}) collective-permute-start(f32[1,32,128]{2,0,1:T(1,128)S(1)} %get-tuple-element.177), channel_id=1, source_target_pairs={{1,0},{4,1},{5,4},{8,5},{9,8},{12,9},{13,12},{3,2},{6,3},{7,6},{10... | collective-permute-start | bytes 49160 | tf_op jit(solution)/shard_map/ppermute | solution.py:15
  59.7 5.3 %collective-permute-start.12 = (f32[1,32,128]{2,0,1:T(1,128)S(1)}, f32[1,32,128]{2,0,1:T(1,128)S(1)}, u32[]{:S(2)}, u32[]{:S(2)}) collective-permute-start(f32[1,32,128]{2,0,1:T(1,128)S(1)} %get-tuple-element.176), channel_id=1, source_target_pairs={{0,1},{1,4},{4,5},{5,8},{8,9},{9,12},{12,13},{2,3},{3,6},{6,7},{7,... | collective-permute-start | bytes 49160 | tf_op jit(solution)/shard_map/ppermute | solution.py:12
  63.6 3.1 %collective-permute-start.13 = (f32[1,32,128]{2,0,1:T(1,128)S(1)}, f32[1,32,128]{2,0,1:T(1,128)S(1)}, u32[]{:S(2)}, u32[]{:S(2)}) collective-permute-start(f32[1,32,128]{2,0,1:T(1,128)S(1)} %get-tuple-element.175), channel_id=1, source_target_pairs={{1,0},{4,1},{5,4},{8,5},{9,8},{12,9},{13,12},{3,2},{6,3},{7,6},{10... | collective-permute-start | bytes 49160 | tf_op jit(solution)/shard_map/ppermute | solution.py:15
  69.1 3.2 %collective-permute-start.14 = (f32[4,16,2,4,128]{4,1,3,2,0:T(8,128)S(1)}, f32[4,16,2,4,128]{4,1,3,2,0:T(8,128)S(1)}, u32[]{:S(2)}, u32[]{:S(2)}) collective-permute-start(f32[4,16,2,4,128]{4,1,3,2,0:T(8,128)S(1)} %select_bitcast_fusion), channel_id=1, source_target_pairs={{0,1},{1,0},{2,3},{3,2},{4,5},{5,4},{6,7},{7,6},{8,9},{9,8},{10,11... | collective-permute-start | bytes 786440 | tf_op jit(solution)/shard_map/ppermute | solution.py:55
  72.4 5.8 %collective-permute-start.15 = (f32[2,16,2,4,128]{4,1,3,2,0:T(8,128)S(1)}, f32[2,16,2,4,128]{4,1,3,2,0:T(8,128)S(1)}, u32[]{:S(2)}, u32[]{:S(2)}) collective-permute-start(f32[2,16,2,4,128]{4,1,3,2,0:T(8,128)S(1)} %select_bitcast_fusion.1), channel_id=1, source_target_pairs={{0,4},{4,0},{8,12},{12,8},{1,5},{5,1},{9,13},{13,9},{2,6},{6,2},{1... | collective-permute-start | bytes 393224 | tf_op jit(solution)/shard_map/ppermute | solution.py:55
  78.3 5.5 %collective-permute-start.16 = (f32[1,16,2,4,128]{4,1,3,2,0:T(8,128)S(1)}, f32[1,16,2,4,128]{4,1,3,2,0:T(8,128)S(1)}, u32[]{:S(2)}, u32[]{:S(2)}) collective-permute-start(f32[1,16,2,4,128]{4,1,3,2,0:T(8,128)S(1)} %select_bitcast_fusion.2), channel_id=1, source_target_pairs={{0,8},{4,12},{8,0},{12,4},{1,9},{5,13},{9,1},{13,5},{2,10},{6,14},... | collective-permute-start | bytes 196616 | tf_op jit(solution)/shard_map/ppermute | solution.py:55

commit v3 on v2

--- a/solution.py
+++ b/solution.py
@@ -2,19 +2,6 @@
 import jax.numpy as jnp
 from jax import lax
 from jax.sharding import PartitionSpec as P
-
-
-def with_halo(block, sides, width):
-    for axis, dim in sides:
-        count = lax.axis_size(axis)
-        forward = [(i, i + 1) for i in range(count - 1)]
-        backward = [(target, source) for source, target in forward]
-        low = lax.ppermute(
-            lax.slice_in_dim(block, block.shape[dim] - width, None, axis=dim), axis, forward
-        )
-        high = lax.ppermute(lax.slice_in_dim(block, 0, width, axis=dim), axis, backward)
-        block = jnp.concatenate([low, block, high], axis=dim)
-    return block
 
 
 def diagonal_sums(news):
@@ -67,20 +54,54 @@
     return total + jnp.dot(lower, data_half, preferred_element_type=jnp.float32)
 
 
-def pull_back(rows, masked, source, scaling):
-    block_count = rows.shape[0]
-    scaled = rows * scaling[:, None, None]
-    contrib = jnp.einsum("cru,cjuv->cjrv", scaled, masked, precision=lax.Precision.HIGHEST)
-    target = (
-        source[:, :, None] == jnp.arange(block_count + 2, dtype=jnp.int32)[None, None, :]
-    ).astype(jnp.float32)
-    spread = jnp.einsum("cjb,cjrv->brv", target, contrib, precision=lax.Precision.HIGHEST)
-    edges = jnp.stack([spread[0], spread[-1]], axis=0)
-    arrived = with_halo(edges, ((("state", "horizon"), 0),), 1)
-    inner = spread[1:-1]
-    inner = inner.at[0].add(arrived[0])
-    inner = inner.at[-1].add(arrived[3])
-    return inner
+def shift_pairs(axis, step):
+    count = lax.axis_size(axis)
+    if step > 0:
+        return [(i, i + 1) for i in range(count - 1)]
+    return [(i + 1, i) for i in range(count - 1)]
+
+
+def to_right(value):
+    return lax.ppermute(value, ("state", "horizon"), shift_pairs(("state", "horizon"), 1))
+
+
+def to_left(value):
+    return lax.ppermute(value, ("state", "horizon"), shift_pairs(("state", "horizon"), -1))
+
+
+def band_step(rows, moves):
+    parts = jnp.einsum("cru,cduv->cdrv", rows, moves, precision=lax.Precision.HIGHEST)
+    down, same, up = parts[:, 0], parts[:, 1], parts[:, 2]
+    zero = jnp.zeros_like(same[:1])
+    inner = same + jnp.concatenate([down[1:], zero], 0) + jnp.concatenate([zero, up[:-1]], 0)
+    return inner, down[0], up[-1]
+
+
+def mat(rows, matrix):
+    return jnp.dot(rows, matrix, precision=lax.Precision.HIGHEST)
+
+
+def one_step(rows, moves):
+    inner, out_low, out_high = band_step(rows, moves)
+    from_low = to_right(out_high)
+    from_high = to_left(out_low)
+    inner = inner.at[0].add(from_low).at[-1].add(from_high)
+    return [inner]
+
+
+def two_steps(rows, moves, low_move, high_move):
+    inner, out_low, out_high = band_step(rows, moves)
+    from_low = to_right(jnp.stack([out_high, mat(inner[-1], moves[-1, 2])]))
+    from_high = to_left(jnp.stack([out_low, mat(inner[0], moves[0, 0])]))
+    second, _, _ = band_step(inner, moves)
+    first = inner.at[0].add(from_low[0]).at[-1].add(from_high[0])
+    second = second.at[0].add(mat(from_low[0], moves[0, 1]))
+    second = second.at[1].add(mat(from_low[0], moves[0, 2]))
+    second = second.at[-1].add(mat(from_high[0], moves[-1, 1]))
+    second = second.at[-2].add(mat(from_high[0], moves[-1, 0]))
+    second = second.at[0].add(from_low[1] + mat(out_low, low_move))
+    second = second.at[-1].add(from_high[1] + mat(out_high, high_move))
+    return [first, second]
 
 
 def shards(impulses, expectations, region_scale, regions, tiles, offsets, counts):
@@ -103,28 +124,41 @@
     )
     weighted_half = weighted.astype(jnp.bfloat16).reshape(row_count, state_count)
     in_use = jnp.arange(band_count, dtype=jnp.int32)[None, :] < counts[:, None]
-    masked = jnp.where(in_use[:, :, None, None], tiles, jnp.zeros((), jnp.bfloat16)).astype(
-        jnp.float32
-    )
     scaling = lax.rsqrt(counts.astype(jnp.float32))
-    source = jnp.arange(block_count, dtype=jnp.int32)[:, None] + 1 + offsets
+    moves = []
+    for shift in (-1, 0, 1):
+        chosen = in_use & (offsets == shift)
+        total = jnp.zeros((block_count, tile_size, tile_size), jnp.float32)
+        for slot in range(band_count):
+            total = total + jnp.where(
+                chosen[:, slot, None, None], tiles[:, slot].astype(jnp.float32), 0.0
+            )
+        moves.append(total * scaling[:, None, None])
+    moves = jnp.stack(moves, axis=1)
+    low_move = to_right(moves[-1, 2])
+    high_move = to_left(moves[0, 0])
     flat_start = impulses.reshape(state_count, width)
-    pieces = []
     rows = (
         weighted_half.astype(jnp.float32)
         .reshape(row_count, block_count, tile_size)
         .transpose(1, 0, 2)
     )
-    for section in range(sections):
-        if section > 0:
-            rows = pull_back(rows, masked, source, scaling)
-            flat_rows = rows.transpose(1, 0, 2).reshape(row_count, state_count)
-            product = split_product(flat_rows, flat_start)
-        else:
-            product = jnp.dot(weighted_half, flat_start, preferred_element_type=jnp.float32)
-        pieces.append(
-            product.reshape(output_count, expect_rows, input_count, horizon).transpose(1, 0, 2, 3)
-        )
+    levels = []
+    remaining = sections - 1
+    if remaining % 2:
+        levels += one_step(rows, moves)
+        remaining -= 1
+    while remaining:
+        levels += two_steps(levels[-1] if levels else rows, moves, low_move, high_move)
+        remaining -= 2
+    pieces = [jnp.dot(weighted_half, flat_start, preferred_element_type=jnp.float32)]
+    for level in levels:
+        flat_rows = level.transpose(1, 0, 2).reshape(row_count, state_count)
+        pieces.append(split_product(flat_rows, flat_start))
+    pieces = [
+        piece.reshape(output_count, expect_rows, input_count, horizon).transpose(1, 0, 2, 3)
+        for piece in pieces
+    ]
     partial_news = jnp.concatenate(pieces, axis=0)
     jacobian = diagonal_sums(partial_news)
     return halving_scatter(jacobian)

time: 85.2 us -> 74.4 us (0.87)
  waiting for transfers between devices: 20.4 us -> 9.78 us
  starting transfers between devices: 41.7 us -> 36.7 us
  other arithmetic: 3.53 us -> 6.15 us
  matrix products: 12.2 us -> 13.4 us
  local copies, waits for them, and re-layouts: 5.75 us -> 6.72 us
    ppermute x14 -> x10, waiting for transfers between devices: 12.2 us -> 2.19 us  [the longest x5 2.17 us: to_right(): lax.ppermute(value, ('state', 'horizon'), shift_pairs(('state', 'horizon'...]
    ppermute x14 -> x10, starting transfers between devices: 35.4 us -> 28.7 us  [the longest x5 22.1 us: to_right(): lax.ppermute(value, ('state', 'horizon'), shift_pairs(('state', 'horizon'...]
    squeeze x0 -> x3, local copies, waits for them, and re-layouts: none -> 1.88 us  [the longest x1 0.63 us: two_steps(): from_low = to_right(jnp.stack([out_high, mat(inner[-1], moves[-1, 2])]))]
    ppermute x3, starting transfers between devices: 6.38 us -> 8.02 us  [halving_scatter(): held = keep + lax.ppermute(send, axis, pairs)]
    mul x7 -> x4, other arithmetic: 0.59 us -> 2.19 us  [shards(): moves.append(total * scaling[:, None, None])]
    slice x14 -> x12, local copies, waits for them, and re-layouts: 0.35 us -> 1.81 us  [the longest x7 0.67 us: band_step(): down[1:]]
    scatter-add x14 -> x0, local copies, waits for them, and re-layouts: 1.32 us -> none  [the longest x7 0.66 us: pull_back(): inner = inner.at[0].add(arrived[0])]
    unnamed x23 -> x27, local copies, waits for them, and re-layouts: 2.05 us -> 1.52 us
  transfers between devices with their start and end apart: 17 -> 13, of which waited for: 10 -> 6; matrix products, arithmetic and copies ran while one was open for 2% -> 13% of each run, Pallas kernels for 0% -> 0%
where the time goes in v3:
time: 74.4 us; the launch traced here: 73.7 us
  starting transfers between devices  36.7 us (49%)
  matrix products  13.4 us (18%)
  waiting for transfers between devices  9.78 us (13%)
  local copies, waits for them, and re-layouts  6.72 us (9%)
  other arithmetic  6.15 us (8%)
  between operations  0.94 us (1%)
    ppermute x5, starting transfers between devices, to_right(): lax.ppermute(value, ('state', 'horizon'), shift_pairs(('state', 'horizon'...  22.1 us
    ppermute x3, starting transfers between devices, halving_scatter(): held = keep + lax.ppermute(send, axis, pairs)  8.02 us
    ppermute x3, waiting for transfers between devices, halving_scatter(): held = keep + lax.ppermute(send, axis, pairs)  7.59 us
    ppermute x5, starting transfers between devices, to_left(): lax.ppermute(value, ('state', 'horizon'), shift_pairs(('state', 'horizon'...  6.56 us
    dot_general x7, matrix products, band_step(): jnp.einsum('cru,cduv->cdrv', rows, moves, precision=lax.Precision.HIGHEST)  4.12 us
    dot_general x24, matrix products, mat(): return jnp.dot(rows, matrix, precision=lax.Precision.HIGHEST)  3.98 us
    mul x4, other arithmetic, shards(): moves.append(total * scaling[:, None, None])  2.19 us
    ppermute x5, waiting for transfers between devices, to_right(): lax.ppermute(value, ('state', 'horizon'), shift_pairs(('state', 'horizon'...  2.17 us
  transfers between devices with their start and end apart: 13, of which 6 were waited for; matrix products, arithmetic and copies ran while one was open for 13% of the time, Pallas kernels for 0%

profile of v3, /device:TPU:0, one launch (start us, length us, event | category | flops | bytes accessed | tf_op | source)
XLA Modules:
  0.0 73.7 jit_solution(5611677112826239385)
XLA Ops:
  0.0 0.7 convert_rsqrt_fusion
  0.7 0.8 %fusion.290 = (pred[4,4]{1,0:T(4,128)(4,1)S(1)}, pred[4,4]{1,0:T(4,128)(4,1)S(1)}, pred[4,4]{1,0:T(4,128)(4,1)S(1)}) fusion(s32[4,4]{1,0:T(4,128)} %param.64, s32[4]{0:T(128)S(1)} %copy-done.7), kind=kLoop, calls=%fused_computation.438 | loop fusion | flops 112 | bytes 128 | tf_op jit(solution)/shard_map/and | solution.py:130
  1.8 1.3 %fusion.76 = f32[4,128,128]{2,1,0:T(8,128)S(1)} fusion(f32[4]{0:T(128)S(1)} %convert_rsqrt_fusion, pred[4]{0:T(512)(128)(4,1)S(1)} %get-tuple-element.326, pred[4]{0:T(512)(128)(4,1)S(1)} %get-tuple-element.327, pred[4]{0:T(512)(128)(4,1)S(1)} %get-tuple-element.328, pred[4]{0:T(512)(128)(4,1)S(1)} %get-tuple-element.325, bf16[4,4,128,128]{3,2,1,0:T(8,128)(2,1)} %param.63), kind=kLoop, calls=%fused_computation.142 | loop fusion | flops 786432 | bytes 786464 | tf_op jit(solution)/shard_map/mul | solution.py:136
  3.7 2.3 %collective-permute-start.4 = (f32[128,128]{1,0:T(8,128)}, f32[128,128]{1,0:T(8,128)S(1)}, u32[]{:S(2)}, u32[]{:S(2)}) collective-permute-start(f32[128,128]{1,0:T(8,128)} %slice_bitcast_fusion.10), channel_id=1, source_target_pairs={{0,1},{1,4},{4,5},{5,8},{8,9},{9,12},{12,13},{2,3},{3,6},{6,7},{7,... | collective-permute-start | bytes 196616 | tf_op jit(solution)/shard_map/ppermute | solution.py:65
  7.3 1.3 %collective-permute-start.5 = (f32[128,128]{1,0:T(8,128)}, f32[128,128]{1,0:T(8,128)S(1)}, u32[]{:S(2)}, u32[]{:S(2)}) collective-permute-start(f32[128,128]{1,0:T(8,128)} %slice_bitcast_fusion.9), channel_id=1, source_target_pairs={{1,0},{4,1},{5,4},{8,5},{9,8},{12,9},{13,12},{3,2},{6,3},{7,6},{10... | collective-permute-start | bytes 196616 | tf_op jit(solution)/shard_map/ppermute | solution.py:69
  11.3 1.3 %collective-permute-start.1 = (f32[32,128]{1,0:T(8,128)}, f32[32,128]{1,0:T(8,128)S(1)}, u32[]{:S(2)}, u32[]{:S(2)}) collective-permute-start(f32[32,128]{1,0:T(8,128)} %get-tuple-element.353), channel_id=1, source_target_pairs={{1,0},{4,1},{5,4},{8,5},{9,8},{12,9},{13,12},{3,2},{6,3},{7,6},{10... | collective-permute-start | bytes 49160 | tf_op jit(solution)/shard_map/ppermute | solution.py:69
  12.6 6.4 %collective-permute-start = (f32[32,128]{1,0:T(8,128)}, f32[32,128]{1,0:T(8,128)}, u32[]{:S(2)}, u32[]{:S(2)}) collective-permute-start(f32[32,128]{1,0:T(8,128)} %get-tuple-element.354), channel_id=1, source_target_pairs={{0,1},{1,4},{4,5},{5,8},{8,9},{9,12},{12,13},{2,3},{3,6},{6,7},{7,... | collective-permute-start | bytes 49160 | tf_op jit(solution)/shard_map/ppermute | solution.py:65
  20.0 1.0 %fusion = f32[128,2,4,128]{3,0,2,1:T(8,128)S(1)} fusion(bf16[4,128,512,1]{2,1,0,3:T(8,128)(2,1)S(1)} %bitcast.1061, f32[2,512]{1,0:T(2,128)S(1)} %bitcast.1063, bf16[2,16,512]{2,1,0:T(8,128)(2,1)} %param.60), kind=kOutput, calls=%fused_computation.31 | convolution fusion | flops 16826368 | bytes 626688 | tf_op jit(solution)/shard_map/dot_general | solution.py:154
  21.1 0.7 fusion.226
  24.1 1.3 %collective-permute-start.3 = (f32[2,32,128]{2,1,0:T(8,128)S(1)}, f32[2,32,128]{2,1,0:T(8,128)S(1)}, u32[]{:S(2)}, u32[]{:S(2)}) collective-permute-start(f32[2,32,128]{2,1,0:T(8,128)S(1)} %pad_maximum_fusion.2), channel_id=1, source_target_pairs={{1,0},{4,1},{5,4},{8,5},{9,8},{12,9},{13,12},{3,2},{6,3},{7,6},{10... | collective-permute-start | bytes 98312 | tf_op jit(solution)/shard_map/ppermute | solution.py:69
  25.5 3.7 %collective-permute-start.2 = (f32[2,32,128]{2,1,0:T(8,128)S(1)}, f32[2,32,128]{2,1,0:T(8,128)S(1)}, u32[]{:S(2)}, u32[]{:S(2)}) collective-permute-start(f32[2,32,128]{2,1,0:T(8,128)S(1)} %pad_maximum_fusion.1), channel_id=1, source_target_pairs={{0,1},{1,4},{4,5},{5,8},{8,9},{9,12},{12,13},{2,3},{3,6},{6,7},{7,... | collective-permute-start | bytes 98312 | tf_op jit(solution)/shard_map/ppermute | solution.py:65
  29.2 0.8 %collective-permute-done.2 = f32[2,32,128]{2,1,0:T(8,128)S(1)} collective-permute-done((f32[2,32,128]{2,1,0:T(8,128)S(1)}, f32[2,32,128]{2,1,0:T(8,128)S(1)}, u32[]{:S(2)}, u32[]{:S(2)}) %collective-permute-start.2) | collective-permute-done | bytes 32800 | tf_op jit(solution)/shard_map/ppermute | solution.py:65
  34.1 1.3 %collective-permute-start.7 = (f32[2,32,128]{2,1,0:T(8,128)S(1)}, f32[2,32,128]{2,1,0:T(8,128)S(1)}, u32[]{:S(2)}, u32[]{:S(2)}) collective-permute-start(f32[2,32,128]{2,1,0:T(8,128)S(1)} %pad_maximum_fusion.4), channel_id=1, source_target_pairs={{1,0},{4,1},{5,4},{8,5},{9,8},{12,9},{13,12},{3,2},{6,3},{7,6},{10... | collective-permute-start | bytes 98312 | tf_op jit(solution)/shard_map/ppermute | solution.py:69
  35.4 4.4 %collective-permute-start.6 = (f32[2,32,128]{2,1,0:T(8,128)S(1)}, f32[2,32,128]{2,1,0:T(8,128)S(1)}, u32[]{:S(2)}, u32[]{:S(2)}) collective-permute-start(f32[2,32,128]{2,1,0:T(8,128)S(1)} %pad_maximum_fusion.3), channel_id=1, source_target_pairs={{0,1},{1,4},{4,5},{5,8},{8,9},{9,12},{12,13},{2,3},{3,6},{6,7},{7,... | collective-permute-start | bytes 98312 | tf_op jit(solution)/shard_map/ppermute | solution.py:65
  39.9 0.8 %collective-permute-done.6 = f32[2,32,128]{2,1,0:T(8,128)S(1)} collective-permute-done((f32[2,32,128]{2,1,0:T(8,128)S(1)}, f32[2,32,128]{2,1,0:T(8,128)S(1)}, u32[]{:S(2)}, u32[]{:S(2)}) %collective-permute-start.6) | collective-permute-done | bytes 32800 | tf_op jit(solution)/shard_map/ppermute | solution.py:65
  45.3 0.7 copy-done.6
  46.0 1.4 %collective-permute-start.9 = (f32[2,32,128]{2,1,0:T(8,128)S(1)}, f32[2,32,128]{2,1,0:T(8,128)S(1)}, u32[]{:S(2)}, u32[]{:S(2)}) collective-permute-start(f32[2,32,128]{2,1,0:T(8,128)S(1)} %pad_maximum_fusion.6), channel_id=1, source_target_pairs={{1,0},{4,1},{5,4},{8,5},{9,8},{12,9},{13,12},{3,2},{6,3},{7,6},{10... | collective-permute-start | bytes 98312 | tf_op jit(solution)/shard_map/ppermute | solution.py:69
  47.4 5.2 %collective-permute-start.8 = (f32[2,32,128]{2,1,0:T(8,128)S(1)}, f32[2,32,128]{2,1,0:T(8,128)S(1)}, u32[]{:S(2)}, u32[]{:S(2)}) collective-permute-start(f32[2,32,128]{2,1,0:T(8,128)S(1)} %pad_maximum_fusion.5), channel_id=1, source_target_pairs={{0,1},{1,4},{4,5},{5,8},{8,9},{9,12},{12,13},{2,3},{3,6},{6,7},{7,... | collective-permute-start | bytes 98312 | tf_op jit(solution)/shard_map/ppermute | solution.py:65
  57.3 2.6 %collective-permute-start.10 = (f32[4,16,2,4,128]{4,1,3,2,0:T(8,128)S(1)}, f32[4,16,2,4,128]{4,1,3,2,0:T(8,128)S(1)}, u32[]{:S(2)}, u32[]{:S(2)}) collective-permute-start(f32[4,16,2,4,128]{4,1,3,2,0:T(8,128)S(1)} %select_bitcast_fusion), channel_id=1, source_target_pairs={{0,1},{1,0},{2,3},{3,2},{4,5},{5,4},{6,7},{7,6},{8,9},{9,8},{10,11... | collective-permute-start | bytes 786440 | tf_op jit(solution)/shard_map/ppermute | solution.py:42
  59.9 1.2 %collective-permute-done.10 = f32[4,16,2,4,128]{4,1,3,2,0:T(8,128)S(1)} collective-permute-done((f32[4,16,2,4,128]{4,1,3,2,0:T(8,128)S(1)}, f32[4,16,2,4,128]{4,1,3,2,0:T(8,128)S(1)}, u32[]{:S(2)}, u32[]{:S(2)}) %collective-permute-start.10) | collective-permute-done | bytes 262176 | tf_op jit(solution)/shard_map/ppermute | solution.py:42
  61.1 2.6 %collective-permute-start.11 = (f32[2,16,2,4,128]{4,1,3,2,0:T(8,128)S(1)}, f32[2,16,2,4,128]{4,1,3,2,0:T(8,128)S(1)}, u32[]{:S(2)}, u32[]{:S(2)}) collective-permute-start(f32[2,16,2,4,128]{4,1,3,2,0:T(8,128)S(1)} %select_bitcast_fusion.1), channel_id=1, source_target_pairs={{0,4},{4,0},{8,12},{12,8},{1,5},{5,1},{9,13},{13,9},{2,6},{6,2},{1... | collective-permute-start | bytes 393224 | tf_op jit(solution)/shard_map/ppermute | solution.py:42
  63.8 3.8 %collective-permute-done.11 = f32[2,16,2,4,128]{4,1,3,2,0:T(8,128)S(1)} collective-permute-done((f32[2,16,2,4,128]{4,1,3,2,0:T(8,128)S(1)}, f32[2,16,2,4,128]{4,1,3,2,0:T(8,128)S(1)}, u32[]{:S(2)}, u32[]{:S(2)}) %collective-permute-start.11) | collective-permute-done | bytes 131104 | tf_op jit(solution)/shard_map/ppermute | solution.py:42
  67.6 2.8 %collective-permute-start.12 = (f32[1,16,2,4,128]{4,1,3,2,0:T(8,128)S(1)}, f32[1,16,2,4,128]{4,1,3,2,0:T(8,128)S(1)}, u32[]{:S(2)}, u32[]{:S(2)}) collective-permute-start(f32[1,16,2,4,128]{4,1,3,2,0:T(8,128)S(1)} %select_bitcast_fusion.2), channel_id=1, source_target_pairs={{0,8},{4,12},{8,0},{12,4},{1,9},{5,13},{9,1},{13,5},{2,10},{6,14},... | collective-permute-start | bytes 196616 | tf_op jit(solution)/shard_map/ppermute | solution.py:42
  70.4 2.6 %collective-permute-done.12 = f32[1,16,2,4,128]{4,1,3,2,0:T(8,128)S(1)} collective-permute-done((f32[1,16,2,4,128]{4,1,3,2,0:T(8,128)S(1)}, f32[1,16,2,4,128]{4,1,3,2,0:T(8,128)S(1)}, u32[]{:S(2)}, u32[]{:S(2)}) %collective-permute-start.12) | collective-permute-done | bytes 65568 | tf_op jit(solution)/shard_map/ppermute | solution.py:42
  (164 shorter events, 21.7 us)
Async XLA Ops:
  0.0 9.1 %copy-start = (f32[16,2]{0,1:T(2,128)S(1)}, f32[16,2]{0,1:T(2,128)}, u32[]{:S(2)}) copy-start(f32[16,2]{0,1:T(2,128)} %param.61) | copy-start | bytes 388
  0.0 0.7 copy-start.7
  0.0 6.3 %copy-start.2 = (bf16[4,4,128,128]{3,2,1,0:T(8,128)(2,1)S(1)}, bf16[4,4,128,128]{3,2,1,0:T(8,128)(2,1)}, u32[]{:S(2)}) copy-start(bf16[4,4,128,128]{3,2,1,0:T(8,128)(2,1)} %param.63) | copy-start | bytes 1572868
  3.7 27.6 %collective-permute-start.4 = (f32[128,128]{1,0:T(8,128)}, f32[128,128]{1,0:T(8,128)S(1)}, u32[]{:S(2)}, u32[]{:S(2)}) collective-permute-start(f32[128,128]{1,0:T(8,128)} %slice_bitcast_fusion.10), channel_id=1, source_target_pairs={{0,1},{1,4},{4,5},{5,8},{8,9},{9,12},{12,13},{2,3},{3,6},{6,7},{7,... | collective-permute-start | bytes 196616 | tf_op jit(solution)/shard_map/ppermute | solution.py:65
  7.3 24.3 %collective-permute-start.5 = (f32[128,128]{1,0:T(8,128)}, f32[128,128]{1,0:T(8,128)S(1)}, u32[]{:S(2)}, u32[]{:S(2)}) collective-permute-start(f32[128,128]{1,0:T(8,128)} %slice_bitcast_fusion.9), channel_id=1, source_target_pairs={{1,0},{4,1},{5,4},{8,5},{9,8},{12,9},{13,12},{3,2},{6,3},{7,6},{10... | collective-permute-start | bytes 196616 | tf_op jit(solution)/shard_map/ppermute | solution.py:69
  8.8 0.7 copy-start.8
  9.4 0.8 %copy-start.4 = (bf16[2,16,512]{2,1,0:T(8,128)(2,1)S(1)}, bf16[2,16,512]{2,1,0:T(8,128)(2,1)}, u32[]{:S(2)}) copy-start(bf16[2,16,512]{2,1,0:T(8,128)(2,1)} %param.60) | copy-start | bytes 98308
  10.2 9.5 %copy-start.1 = (bf16[512,4,128]{2,1,0:T(4,128)(2,1)S(1)}, bf16[512,4,128]{2,1,0:T(4,128)(2,1)}, u32[]{:S(2)}) copy-start(bf16[512,4,128]{2,1,0:T(4,128)(2,1)} %param.59) | copy-start | bytes 1572868
  11.3 10.6 %collective-permute-start.1 = (f32[32,128]{1,0:T(8,128)}, f32[32,128]{1,0:T(8,128)S(1)}, u32[]{:S(2)}, u32[]{:S(2)}) collective-permute-start(f32[32,128]{1,0:T(8,128)} %get-tuple-element.353), channel_id=1, source_target_pairs={{1,0},{4,1},{5,4},{8,5},{9,8},{12,9},{13,12},{3,2},{6,3},{7,6},{10... | collective-permute-start | bytes 49160 | tf_op jit(solution)/shard_map/ppermute | solution.py:69
  12.6 8.5 %collective-permute-start = (f32[32,128]{1,0:T(8,128)}, f32[32,128]{1,0:T(8,128)}, u32[]{:S(2)}, u32[]{:S(2)}) collective-permute-start(f32[32,128]{1,0:T(8,128)} %get-tuple-element.354), channel_id=1, source_target_pairs={{0,1},{1,4},{4,5},{5,8},{8,9},{9,12},{12,13},{2,3},{3,6},{6,7},{7,... | collective-permute-start | bytes 49160 | tf_op jit(solution)/shard_map/ppermute | solution.py:65
  20.0 1.0 %copy-start.3 = (f32[3,32,128]{2,1,0:T(8,128)S(1)}, f32[3,32,128]{2,1,0:T(8,128)}, u32[]{:S(2)}) copy-start(f32[3,32,128]{2,1,0:T(8,128)} %get-tuple-element.356) | copy-start | bytes 147460
  24.1 5.9 %collective-permute-start.3 = (f32[2,32,128]{2,1,0:T(8,128)S(1)}, f32[2,32,128]{2,1,0:T(8,128)S(1)}, u32[]{:S(2)}, u32[]{:S(2)}) collective-permute-start(f32[2,32,128]{2,1,0:T(8,128)S(1)} %pad_maximum_fusion.2), channel_id=1, source_target_pairs={{1,0},{4,1},{5,4},{8,5},{9,8},{12,9},{13,12},{3,2},{6,3},{7,6},{10... | collective-permute-start | bytes 98312 | tf_op jit(solution)/shard_map/ppermute | solution.py:69
  25.5 4.5 %collective-permute-start.2 = (f32[2,32,128]{2,1,0:T(8,128)S(1)}, f32[2,32,128]{2,1,0:T(8,128)S(1)}, u32[]{:S(2)}, u32[]{:S(2)}) collective-permute-start(f32[2,32,128]{2,1,0:T(8,128)S(1)} %pad_maximum_fusion.1), channel_id=1, source_target_pairs={{0,1},{1,4},{4,5},{5,8},{8,9},{9,12},{12,13},{2,3},{3,6},{6,7},{7,... | collective-permute-start | bytes 98312 | tf_op jit(solution)/shard_map/ppermute | solution.py:65
  34.1 6.6 %collective-permute-start.7 = (f32[2,32,128]{2,1,0:T(8,128)S(1)}, f32[2,32,128]{2,1,0:T(8,128)S(1)}, u32[]{:S(2)}, u32[]{:S(2)}) collective-permute-start(f32[2,32,128]{2,1,0:T(8,128)S(1)} %pad_maximum_fusion.4), channel_id=1, source_target_pairs={{1,0},{4,1},{5,4},{8,5},{9,8},{12,9},{13,12},{3,2},{6,3},{7,6},{10... | collective-permute-start | bytes 98312 | tf_op jit(solution)/shard_map/ppermute | solution.py:69
  35.4 5.3 %collective-permute-start.6 = (f32[2,32,128]{2,1,0:T(8,128)S(1)}, f32[2,32,128]{2,1,0:T(8,128)S(1)}, u32[]{:S(2)}, u32[]{:S(2)}) collective-permute-start(f32[2,32,128]{2,1,0:T(8,128)S(1)} %pad_maximum_fusion.3), channel_id=1, source_target_pairs={{0,1},{1,4},{4,5},{5,8},{8,9},{9,12},{12,13},{2,3},{3,6},{6,7},{7,... | collective-permute-start | bytes 98312 | tf_op jit(solution)/shard_map/ppermute | solution.py:65
  45.3 0.7 copy-start.6
  46.0 1.4 %copy-start.5 = (f32[1,32,128]{2,1,0:T(8,128)S(1)}, f32[1,32,128]{2,1,0:T(8,128)}, u32[]{:S(2)}) copy-start(f32[1,32,128]{2,1,0:T(8,128)} %get-tuple-element.338) | copy-start | bytes 49156
  46.0 7.3 %collective-permute-start.9 = (f32[2,32,128]{2,1,0:T(8,128)S(1)}, f32[2,32,128]{2,1,0:T(8,128)S(1)}, u32[]{:S(2)}, u32[]{:S(2)}) collective-permute-start(f32[2,32,128]{2,1,0:T(8,128)S(1)} %pad_maximum_fusion.6), channel_id=1, source_target_pairs={{1,0},{4,1},{5,4},{8,5},{9,8},{12,9},{13,12},{3,2},{6,3},{7,6},{10... | collective-permute-start | bytes 98312 | tf_op jit(solution)/shard_map/ppermute | solution.py:69
  47.4 5.9 %collective-permute-start.8 = (f32[2,32,128]{2,1,0:T(8,128)S(1)}, f32[2,32,128]{2,1,0:T(8,128)S(1)}, u32[]{:S(2)}, u32[]{:S(2)}) collective-permute-start(f32[2,32,128]{2,1,0:T(8,128)S(1)} %pad_maximum_fusion.5), channel_id=1, source_target_pairs={{0,1},{1,4},{4,5},{5,8},{8,9},{9,12},{12,13},{2,3},{3,6},{6,7},{7,... | collective-permute-start | bytes 98312 | tf_op jit(solution)/shard_map/ppermute | solution.py:65
  57.3 3.7 %collective-permute-start.10 = (f32[4,16,2,4,128]{4,1,3,2,0:T(8,128)S(1)}, f32[4,16,2,4,128]{4,1,3,2,0:T(8,128)S(1)}, u32[]{:S(2)}, u32[]{:S(2)}) collective-permute-start(f32[4,16,2,4,128]{4,1,3,2,0:T(8,128)S(1)} %select_bitcast_fusion), channel_id=1, source_target_pairs={{0,1},{1,0},{2,3},{3,2},{4,5},{5,4},{6,7},{7,6},{8,9},{9,8},{10,11... | collective-permute-start | bytes 786440 | tf_op jit(solution)/shard_map/ppermute | solution.py:42
  61.1 6.4 %collective-permute-start.11 = (f32[2,16,2,4,128]{4,1,3,2,0:T(8,128)S(1)}, f32[2,16,2,4,128]{4,1,3,2,0:T(8,128)S(1)}, u32[]{:S(2)}, u32[]{:S(2)}) collective-permute-start(f32[2,16,2,4,128]{4,1,3,2,0:T(8,128)S(1)} %select_bitcast_fusion.1), channel_id=1, source_target_pairs={{0,4},{4,0},{8,12},{12,8},{1,5},{5,1},{9,13},{13,9},{2,6},{6,2},{1... | collective-permute-start | bytes 393224 | tf_op jit(solution)/shard_map/ppermute | solution.py:42
  67.6 5.4 %collective-permute-start.12 = (f32[1,16,2,4,128]{4,1,3,2,0:T(8,128)S(1)}, f32[1,16,2,4,128]{4,1,3,2,0:T(8,128)S(1)}, u32[]{:S(2)}, u32[]{:S(2)}) collective-permute-start(f32[1,16,2,4,128]{4,1,3,2,0:T(8,128)S(1)} %select_bitcast_fusion.2), channel_id=1, source_target_pairs={{0,8},{4,12},{8,0},{12,4},{1,9},{5,13},{9,1},{13,5},{2,10},{6,14},... | collective-permute-start | bytes 196616 | tf_op jit(solution)/shard_map/ppermute | solution.py:42

commit v4 on v3

--- a/solution.py
+++ b/solution.py
@@ -81,27 +81,35 @@
     return jnp.dot(rows, matrix, precision=lax.Precision.HIGHEST)
 
 
-def one_step(rows, moves):
-    inner, out_low, out_high = band_step(rows, moves)
-    from_low = to_right(out_high)
-    from_high = to_left(out_low)
-    inner = inner.at[0].add(from_low).at[-1].add(from_high)
-    return [inner]
-
-
-def two_steps(rows, moves, low_move, high_move):
-    inner, out_low, out_high = band_step(rows, moves)
-    from_low = to_right(jnp.stack([out_high, mat(inner[-1], moves[-1, 2])]))
-    from_high = to_left(jnp.stack([out_low, mat(inner[0], moves[0, 0])]))
-    second, _, _ = band_step(inner, moves)
-    first = inner.at[0].add(from_low[0]).at[-1].add(from_high[0])
-    second = second.at[0].add(mat(from_low[0], moves[0, 1]))
-    second = second.at[1].add(mat(from_low[0], moves[0, 2]))
-    second = second.at[-1].add(mat(from_high[0], moves[-1, 1]))
-    second = second.at[-2].add(mat(from_high[0], moves[-1, 0]))
-    second = second.at[0].add(from_low[1] + mat(out_low, low_move))
-    second = second.at[-1].add(from_high[1] + mat(out_high, high_move))
-    return [first, second]
+def ext_step(rows, moves):
+    parts = jnp.einsum("cru,cduv->cdrv", rows, moves, precision=lax.Precision.HIGHEST)
+    down, same, up = parts[:, 0], parts[:, 1], parts[:, 2]
+    zero = jnp.zeros_like(same[:1])
+    inner = same + jnp.concatenate([down[1:], zero], 0) + jnp.concatenate([zero, up[:-1]], 0)
+    return inner, parts[1, 0], parts[-2, 2]
+
+
+def exchange_round(rows, moves, wide, steps):
+    zero = jnp.zeros_like(rows[:1])
+    held = jnp.concatenate([zero, rows, zero], 0)
+    to_low, to_high, mine = [], [], []
+    for _ in range(steps):
+        held, out_low, out_high = ext_step(held, wide)
+        to_low.append(out_low)
+        to_high.append(out_high)
+        mine.append(held[1:-1])
+    from_low = to_right(jnp.stack(to_high))
+    from_high = to_left(jnp.stack(to_low))
+    levels = []
+    carried = None
+    for step in range(steps):
+        if carried is None:
+            carried = jnp.zeros_like(rows)
+        else:
+            carried, _, _ = band_step(carried, moves)
+        carried = carried.at[0].add(from_low[step]).at[-1].add(from_high[step])
+        levels.append(mine[step] + carried)
+    return levels
 
 
 def shards(impulses, expectations, region_scale, regions, tiles, offsets, counts):
@@ -135,29 +143,43 @@
             )
         moves.append(total * scaling[:, None, None])
     moves = jnp.stack(moves, axis=1)
-    low_move = to_right(moves[-1, 2])
-    high_move = to_left(moves[0, 0])
     flat_start = impulses.reshape(state_count, width)
     rows = (
         weighted_half.astype(jnp.float32)
         .reshape(row_count, block_count, tile_size)
         .transpose(1, 0, 2)
     )
-    levels = []
-    remaining = sections - 1
-    if remaining % 2:
-        levels += one_step(rows, moves)
-        remaining -= 1
-    while remaining:
-        levels += two_steps(levels[-1] if levels else rows, moves, low_move, high_move)
-        remaining -= 2
-    pieces = [jnp.dot(weighted_half, flat_start, preferred_element_type=jnp.float32)]
-    for level in levels:
-        flat_rows = level.transpose(1, 0, 2).reshape(row_count, state_count)
-        pieces.append(split_product(flat_rows, flat_start))
+    inner, out_low, out_high = band_step(rows, moves)
+    edge_low = jnp.concatenate([out_high, moves[-1, 1], moves[-1, 2]], 0)
+    edge_high = jnp.concatenate([out_low, moves[0, 0], moves[0, 1]], 0)
+    from_low = to_right(edge_low)
+    from_high = to_left(edge_high)
+    levels = [rows, inner.at[0].add(from_low[:row_count]).at[-1].add(from_high[:row_count])]
+    left_self = from_low[row_count : row_count + tile_size]
+    left_up = from_low[row_count + tile_size :]
+    right_down = from_high[row_count : row_count + tile_size]
+    right_self = from_high[row_count + tile_size :]
+    blank = jnp.zeros_like(left_self)
+    wide = jnp.concatenate(
+        [
+            jnp.stack([blank, left_self, left_up])[None],
+            moves,
+            jnp.stack([right_down, right_self, blank])[None],
+        ],
+        0,
+    )
+    remaining = sections - 2
+    while remaining > 0:
+        steps = min(3, remaining)
+        levels += exchange_round(levels[-1], moves, wide, steps)
+        remaining -= steps
+    stacked = jnp.concatenate(
+        [level.transpose(1, 0, 2).reshape(row_count, state_count) for level in levels], 0
+    )
+    product = split_product(stacked, flat_start)
     pieces = [
         piece.reshape(output_count, expect_rows, input_count, horizon).transpose(1, 0, 2, 3)
-        for piece in pieces
+        for piece in jnp.split(product, sections, 0)
     ]
     partial_news = jnp.concatenate(pieces, axis=0)
     jacobian = diagonal_sums(partial_news)

time: 74.4 us -> 63 us (0.85)
  starting transfers between devices: 36.7 us -> 26.9 us
  matrix products: 13.4 us -> 9.13 us
  other arithmetic: 6.15 us -> 9.15 us
    ppermute x5 -> x3, starting transfers between devices: 22.1 us -> 14.8 us  [to_right(): lax.ppermute(value, ('state', 'horizon'), shift_pairs(('state', 'horizon'...]
    squeeze x0 -> x1, other arithmetic: none -> 3.88 us  [shards(): edge_high = jnp.concatenate([out_low, moves[0, 0], moves[0, 1]], 0)]
    ppermute x5 -> x3, starting transfers between devices: 6.56 us -> 3.88 us  [to_left(): lax.ppermute(value, ('state', 'horizon'), shift_pairs(('state', 'horizon'...]
    slice x4 -> x13, local copies, waits for them, and re-layouts: 0.68 us -> 3.24 us  [the longest x4 2.5 us: shards(): edge_low = jnp.concatenate([out_high, moves[-1, 1], moves[-1, 2]], 0)]
    dot_general x7 -> x5, matrix products: 4.12 us -> 2.87 us  [band_step(): jnp.einsum('cru,cduv->cdrv', rows, moves, precision=lax.Precision.HIGHEST)]
    squeeze x2 -> x3, local copies, waits for them, and re-layouts: 1.27 us -> 0.03 us  [the longest x2 0.02 us: ext_step(): down, same, up = (parts[:, 0], parts[:, 1], parts[:, 2])]
    dot_general x7 -> x1, matrix products: 1.42 us -> 0.31 us  [split_product(): return total + jnp.dot(lower, data_half, preferred_element_type=jnp.float32)]
    dot_general x7 -> x1, matrix products: 1.38 us -> 0.31 us  [split_product(): jnp.dot(middle, data_half, preferred_element_type=jnp.float32)]
  transfers between devices with their start and end apart: 13 -> 9, of which waited for: 6 -> 6; matrix products, arithmetic and copies ran while one was open for 13% -> 0% of each run, Pallas kernels for 0% -> 0%
where the time goes in v4:
time: 63 us; the launch traced here: 62.6 us
  starting transfers between devices  26.9 us (43%)
  waiting for transfers between devices  9.87 us (16%)
  other arithmetic  9.15 us (15%)
  matrix products  9.13 us (14%)
  local copies, waits for them, and re-layouts  6.61 us (10%)
  between operations  0.97 us (2%)
    ppermute x3, starting transfers between devices, to_right(): lax.ppermute(value, ('state', 'horizon'), shift_pairs(('state', 'horizon'...  14.8 us
    ppermute x3, starting transfers between devices, halving_scatter(): held = keep + lax.ppermute(send, axis, pairs)  8.19 us
    ppermute x3, waiting for transfers between devices, halving_scatter(): held = keep + lax.ppermute(send, axis, pairs)  7.59 us
    dot_general x6, matrix products, ext_step(): jnp.einsum('cru,cduv->cdrv', rows, moves, precision=lax.Precision.HIGHEST)  5.16 us
    squeeze x1, other arithmetic, shards(): edge_high = jnp.concatenate([out_low, moves[0, 0], moves[0, 1]], 0)  3.88 us
    ppermute x3, starting transfers between devices, to_left(): lax.ppermute(value, ('state', 'horizon'), shift_pairs(('state', 'horizon'...  3.88 us
    dot_general x5, matrix products, band_step(): jnp.einsum('cru,cduv->cdrv', rows, moves, precision=lax.Precision.HIGHEST)  2.87 us
    slice x4, local copies, waits for them, and re-layouts, shards(): edge_low = jnp.concatenate([out_high, moves[-1, 1], moves[-1, 2]], 0)  2.5 us
  transfers between devices with their start and end apart: 9, of which 6 were waited for; matrix products, arithmetic and copies ran while one was open for 0% of the time, Pallas kernels for 0%

profile of v4, /device:TPU:0, one launch (start us, length us, event | category | flops | bytes accessed | tf_op | source)
XLA Modules:
  0.0 62.6 jit_solution(8161639932540023240)
XLA Ops:
  0.7 0.8 %fusion.106 = (pred[4,4]{1,0:T(4,128)(4,1)S(1)}, pred[4,4]{1,0:T(4,128)(4,1)S(1)}, pred[4,4]{1,0:T(4,128)(4,1)S(1)}) fusion(s32[4,4]{1,0:T(4,128)} %param.40, s32[4]{0:T(128)} %param.41), kind=kLoop, calls=%fused_computation.263 | loop fusion | flops 112 | bytes 128 | tf_op jit(solution)/shard_map/and | solution.py:138
  4.9 1.3 %fusion.32 = f32[4,1,128,128]{3,2,1,0:T(8,128)S(1)} fusion(f32[4]{0:T(128)S(1)} %convert_rsqrt_fusion, pred[4]{0:T(512)(128)(4,1)S(1)} %get-tuple-element.182, pred[4]{0:T(512)(128)(4,1)S(1)} %get-tuple-element.183, pred[4]{0:T(512)(128)(4,1)S(1)} %get-tuple-element.184, pred[4]{0:T(512)(128)(4,1)S(1)} %get-tuple-element.181, bf16[4,4,128,128]{3,2,1,0:T(8,128)(2,1)} %param.39), kind=kLoop, calls=%fused_computation.72 | loop fusion | flops 786432 | bytes 786464 | tf_op jit(solution)/shard_map/mul | solution.py:144
  8.4 3.9 %fusion.73 = (f32[128,128]{1,0:T(8,128)S(1)}, f32[128,128]{1,0:T(8,128)S(1)}) fusion(f32[4,128,128]{2,1,0:T(8,128)S(1)} %get-tuple-element.198, f32[4,128,128]{2,1,0:T(8,128)S(1)} %get-tuple-element.199, f32[4,128,128]{2,1,0:T(8,128)S(1)} %get-tuple-element.200, f32[4,128,128]{2,1,0:T(8,128)S(1)} %get-tuple-element.197, f32[1]{0:T(128)} %get-tuple-element.248, ...), kind=kLoop, calls=%fused_computation.169 | loop fusion | flops 262144 | bytes 655376 | tf_op jit(solution)/shard_map/squeeze | solution.py:154
  12.3 1.3 %collective-permute-start.1 = (f32[288,128]{1,0:T(8,128)S(1)}, f32[288,128]{1,0:T(8,128)S(1)}, u32[]{:S(2)}, u32[]{:S(2)}) collective-permute-start(f32[288,128]{1,0:T(8,128)S(1)} %pad_maximum_fusion.3), channel_id=1, source_target_pairs={{1,0},{4,1},{5,4},{8,5},{9,8},{12,9},{13,12},{3,2},{6,3},{7,6},{10... | collective-permute-start | bytes 442376 | tf_op jit(solution)/shard_map/ppermute | solution.py:69
  13.6 3.0 %collective-permute-start = (f32[288,128]{1,0:T(8,128)S(1)}, f32[288,128]{1,0:T(8,128)S(1)}, u32[]{:S(2)}, u32[]{:S(2)}) collective-permute-start(f32[288,128]{1,0:T(8,128)S(1)} %pad_maximum_fusion.2), channel_id=1, source_target_pairs={{0,1},{1,4},{4,5},{5,8},{8,9},{9,12},{12,13},{2,3},{3,6},{6,7},{7,... | collective-permute-start | bytes 442376 | tf_op jit(solution)/shard_map/ppermute | solution.py:65
  16.8 0.8 %collective-permute-done = f32[288,128]{1,0:T(8,128)S(1)} collective-permute-done((f32[288,128]{1,0:T(8,128)S(1)}, f32[288,128]{1,0:T(8,128)S(1)}, u32[]{:S(2)}, u32[]{:S(2)}) %collective-permute-start) | collective-permute-done | bytes 147488 | tf_op jit(solution)/shard_map/ppermute | solution.py:65
  17.7 0.9 %convolution_bitcast_fusion.5 = f32[6,3,32,128]{3,2,1,0:T(8,128)S(1)} fusion(f32[1,32,128]{2,1,0:T(8,128)S(1)} %broadcast.326, f32[4,32,128]{2,1,0:T(8,128)S(1)} %fusion.101, f32[1,3,128,128]{3,2,1,0:T(8,128)S(1)} %get-tuple-element.244, f32[4,1,128,128]{3,2,1,0:T(8,128)S(1)} %fusion.32, f32[4,1,128,128]{3,2,1,0:T(8,128)S(1)} %get-tuple-element.188, ...), kind=kOutput, calls=%fused_computation.8 | convolution fusion | flops 114475008 | bytes 1556480 | tf_op jit(solution)/shard_map/cru,cduv->cdrv/dot_general | solution.py:85
  18.7 0.9 %convolution_bitcast_fusion.4 = f32[6,3,32,128]{3,2,0,1:T(8,128)S(1)} fusion(f32[6,32,128]{2,1,0:T(8,128)S(1)} %fusion.48, f32[1,3,128,128]{3,2,1,0:T(8,128)S(1)} %get-tuple-element.244, f32[4,1,128,128]{3,2,1,0:T(8,128)S(1)} %fusion.32, f32[4,1,128,128]{3,2,1,0:T(8,128)S(1)} %get-tuple-element.188, f32[4,1,128,128]{3,2,1,0:T(8,128)S(1)} %get-tuple-element.187, ...), kind=kOutput, calls=%fused_computation.7 | convolution fusion | flops 114425856 | bytes 1572864 | tf_op jit(solution)/shard_map/cru,cduv->cdrv/dot_general | solution.py:85
  19.6 0.9 %convolution_bitcast_fusion.3 = f32[6,3,32,128]{3,2,0,1:T(8,128)S(1)} fusion(f32[6,32,128]{2,1,0:T(8,128)S(1)} %fusion.46, f32[1,3,128,128]{3,2,1,0:T(8,128)S(1)} %get-tuple-element.244, f32[4,1,128,128]{3,2,1,0:T(8,128)S(1)} %fusion.32, f32[4,1,128,128]{3,2,1,0:T(8,128)S(1)} %get-tuple-element.188, f32[4,1,128,128]{3,2,1,0:T(8,128)S(1)} %get-tuple-element.187, ...), kind=kOutput, calls=%fused_computation.6 | convolution fusion | flops 114425856 | bytes 1572864 | tf_op jit(solution)/shard_map/cru,cduv->cdrv/dot_general | solution.py:85
  20.5 1.3 %collective-permute-start.3 = (f32[3,32,128]{2,1,0:T(8,128)S(1)}, f32[3,32,128]{2,1,0:T(8,128)S(1)}, u32[]{:S(2)}, u32[]{:S(2)}) collective-permute-start(f32[3,32,128]{2,1,0:T(8,128)S(1)} %pad_maximum_fusion.9), channel_id=1, source_target_pairs={{1,0},{4,1},{5,4},{8,5},{9,8},{12,9},{13,12},{3,2},{6,3},{7,6},{10... | collective-permute-start | bytes 147464 | tf_op jit(solution)/shard_map/ppermute | solution.py:69
  21.8 6.3 %collective-permute-start.2 = (f32[3,32,128]{2,1,0:T(8,128)S(1)}, f32[3,32,128]{2,1,0:T(8,128)S(1)}, u32[]{:S(2)}, u32[]{:S(2)}) collective-permute-start(f32[3,32,128]{2,1,0:T(8,128)S(1)} %pad_maximum_fusion.8), channel_id=1, source_target_pairs={{0,1},{1,4},{4,5},{5,8},{8,9},{9,12},{12,13},{2,3},{3,6},{6,7},{7,... | collective-permute-start | bytes 147464 | tf_op jit(solution)/shard_map/ppermute | solution.py:65
  28.1 0.8 %collective-permute-done.2 = f32[3,32,128]{2,1,0:T(8,128)S(1)} collective-permute-done((f32[3,32,128]{2,1,0:T(8,128)S(1)}, f32[3,32,128]{2,1,0:T(8,128)S(1)}, u32[]{:S(2)}, u32[]{:S(2)}) %collective-permute-start.2) | collective-permute-done | bytes 49184 | tf_op jit(solution)/shard_map/ppermute | solution.py:65
  30.4 0.9 %convolution_bitcast_fusion.2 = f32[6,3,32,128]{3,2,1,0:T(8,128)S(1)} fusion(f32[1,32,128]{2,1,0:T(8,128)S(1)} %broadcast.326, f32[4,32,128]{2,1,0:T(8,128)S(1)} %fusion.66, f32[1,3,128,128]{3,2,1,0:T(8,128)S(1)} %get-tuple-element.244, f32[4,1,128,128]{3,2,1,0:T(8,128)S(1)} %fusion.32, f32[4,1,128,128]{3,2,1,0:T(8,128)S(1)} %get-tuple-element.188, ...), kind=kOutput, calls=%fused_computation.5 | convolution fusion | flops 114475008 | bytes 1556480 | tf_op jit(solution)/shard_map/cru,cduv->cdrv/dot_general | solution.py:85
  31.3 0.9 %convolution_bitcast_fusion.1 = f32[6,3,32,128]{3,2,0,1:T(8,128)S(1)} fusion(f32[6,32,128]{2,1,0:T(8,128)S(1)} %fusion.44, f32[1,3,128,128]{3,2,1,0:T(8,128)S(1)} %get-tuple-element.244, f32[4,1,128,128]{3,2,1,0:T(8,128)S(1)} %fusion.32, f32[4,1,128,128]{3,2,1,0:T(8,128)S(1)} %get-tuple-element.188, f32[4,1,128,128]{3,2,1,0:T(8,128)S(1)} %get-tuple-element.187, ...), kind=kOutput, calls=%fused_computation.4 | convolution fusion | flops 114425856 | bytes 1572864 | tf_op jit(solution)/shard_map/cru,cduv->cdrv/dot_general | solution.py:85
  32.3 0.9 %convolution_bitcast_fusion = f32[6,3,32,128]{3,2,0,1:T(8,128)S(1)} fusion(f32[6,32,128]{2,1,0:T(8,128)S(1)} %fusion.42, f32[1,3,128,128]{3,2,1,0:T(8,128)S(1)} %get-tuple-element.244, f32[4,1,128,128]{3,2,1,0:T(8,128)S(1)} %fusion.32, f32[4,1,128,128]{3,2,1,0:T(8,128)S(1)} %get-tuple-element.188, f32[4,1,128,128]{3,2,1,0:T(8,128)S(1)} %get-tuple-element.187, ...), kind=kOutput, calls=%fused_computation.3 | convolution fusion | flops 114425856 | bytes 1572864 | tf_op jit(solution)/shard_map/cru,cduv->cdrv/dot_general | solution.py:85
  33.2 1.3 %collective-permute-start.5 = (f32[3,32,128]{2,1,0:T(8,128)S(1)}, f32[3,32,128]{2,1,0:T(8,128)S(1)}, u32[]{:S(2)}, u32[]{:S(2)}) collective-permute-start(f32[3,32,128]{2,1,0:T(8,128)S(1)} %pad_maximum_fusion.11), channel_id=1, source_target_pairs={{1,0},{4,1},{5,4},{8,5},{9,8},{12,9},{13,12},{3,2},{6,3},{7,6},{10... | collective-permute-start | bytes 147464 | tf_op jit(solution)/shard_map/ppermute | solution.py:69
  34.5 5.5 %collective-permute-start.4 = (f32[3,32,128]{2,1,0:T(8,128)S(1)}, f32[3,32,128]{2,1,0:T(8,128)S(1)}, u32[]{:S(2)}, u32[]{:S(2)}) collective-permute-start(f32[3,32,128]{2,1,0:T(8,128)S(1)} %pad_maximum_fusion.10), channel_id=1, source_target_pairs={{0,1},{1,4},{4,5},{5,8},{8,9},{9,12},{12,13},{2,3},{3,6},{6,7},{7,... | collective-permute-start | bytes 147464 | tf_op jit(solution)/shard_map/ppermute | solution.py:65
  42.2 0.9 %copy-done.2 = bf16[512,4,128]{2,1,0:T(4,128)(2,1)S(1)} copy-done((bf16[512,4,128]{2,1,0:T(4,128)(2,1)S(1)}, bf16[512,4,128]{2,1,0:T(4,128)(2,1)}, u32[]{:S(2)}) %copy-start.2) | copy-done | bytes 524312
  46.0 2.7 %collective-permute-start.6 = (f32[4,16,2,4,128]{4,1,0,3,2:T(8,128)S(1)}, f32[4,16,2,4,128]{4,1,0,3,2:T(8,128)S(1)}, u32[]{:S(2)}, u32[]{:S(2)}) collective-permute-start(f32[4,16,2,4,128]{4,1,0,3,2:T(8,128)S(1)} %select_bitcast_fusion), channel_id=1, source_target_pairs={{0,1},{1,0},{2,3},{3,2},{4,5},{5,4},{6,7},{7,6},{8,9},{9,8},{10,11... | collective-permute-start | bytes 786440 | tf_op jit(solution)/shard_map/ppermute | solution.py:42
  48.7 1.2 %collective-permute-done.6 = f32[4,16,2,4,128]{4,1,0,3,2:T(8,128)S(1)} collective-permute-done((f32[4,16,2,4,128]{4,1,0,3,2:T(8,128)S(1)}, f32[4,16,2,4,128]{4,1,0,3,2:T(8,128)S(1)}, u32[]{:S(2)}, u32[]{:S(2)}) %collective-permute-start.6) | collective-permute-done | bytes 262176 | tf_op jit(solution)/shard_map/ppermute | solution.py:42
  50.0 2.7 %collective-permute-start.7 = (f32[2,16,2,4,128]{4,1,3,2,0:T(8,128)S(1)}, f32[2,16,2,4,128]{4,1,3,2,0:T(8,128)S(1)}, u32[]{:S(2)}, u32[]{:S(2)}) collective-permute-start(f32[2,16,2,4,128]{4,1,3,2,0:T(8,128)S(1)} %fusion.35), channel_id=1, source_target_pairs={{0,4},{4,0},{8,12},{12,8},{1,5},{5,1},{9,13},{13,9},{2,6},{6,2},{1... | collective-permute-start | bytes 393224 | tf_op jit(solution)/shard_map/ppermute | solution.py:42
  52.6 3.8 %collective-permute-done.7 = f32[2,16,2,4,128]{4,1,3,2,0:T(8,128)S(1)} collective-permute-done((f32[2,16,2,4,128]{4,1,3,2,0:T(8,128)S(1)}, f32[2,16,2,4,128]{4,1,3,2,0:T(8,128)S(1)}, u32[]{:S(2)}, u32[]{:S(2)}) %collective-permute-start.7) | collective-permute-done | bytes 131104 | tf_op jit(solution)/shard_map/ppermute | solution.py:42
  56.5 2.8 %collective-permute-start.8 = (f32[1,16,2,4,128]{4,1,3,2,0:T(8,128)S(1)}, f32[1,16,2,4,128]{4,1,3,2,0:T(8,128)S(1)}, u32[]{:S(2)}, u32[]{:S(2)}) collective-permute-start(f32[1,16,2,4,128]{4,1,3,2,0:T(8,128)S(1)} %select_bitcast_fusion.1), channel_id=1, source_target_pairs={{0,8},{4,12},{8,0},{12,4},{1,9},{5,13},{9,1},{13,5},{2,10},{6,14},... | collective-permute-start | bytes 196616 | tf_op jit(solution)/shard_map/ppermute | solution.py:42
  59.3 2.6 %collective-permute-done.8 = f32[1,16,2,4,128]{4,1,3,2,0:T(8,128)S(1)} collective-permute-done((f32[1,16,2,4,128]{4,1,3,2,0:T(8,128)S(1)}, f32[1,16,2,4,128]{4,1,3,2,0:T(8,128)S(1)}, u32[]{:S(2)}, u32[]{:S(2)}) %collective-permute-start.8) | collective-permute-done | bytes 65568 | tf_op jit(solution)/shard_map/ppermute | solution.py:42
  (140 shorter events, 13.5 us)
Async XLA Ops:
  0.0 6.6 %copy-start = (f32[16,2]{0,1:T(2,128)S(1)}, f32[16,2]{0,1:T(2,128)}, u32[]{:S(2)}) copy-start(f32[16,2]{0,1:T(2,128)} %param.37) | copy-start | bytes 388
  0.0 6.2 %copy-start.1 = (bf16[4,4,128,128]{3,2,1,0:T(8,128)(2,1)S(1)}, bf16[4,4,128,128]{3,2,1,0:T(8,128)(2,1)}, u32[]{:S(2)}) copy-start(bf16[4,4,128,128]{3,2,1,0:T(8,128)(2,1)} %param.39) | copy-start | bytes 1572868
  6.2 0.7 %copy-start.4 = (s32[4]{0:T(128)S(1)}, s32[4]{0:T(128)}, u32[]{:S(2)}) copy-start(s32[4]{0:T(128)} %param.38) | copy-start | bytes 52
  6.3 1.1 %copy-start.3 = (bf16[2,16,512]{2,1,0:T(8,128)(2,1)S(1)}, bf16[2,16,512]{2,1,0:T(8,128)(2,1)}, u32[]{:S(2)}) copy-start(bf16[2,16,512]{2,1,0:T(8,128)(2,1)} %param.36) | copy-start | bytes 98308
  12.3 4.5 %collective-permute-start.1 = (f32[288,128]{1,0:T(8,128)S(1)}, f32[288,128]{1,0:T(8,128)S(1)}, u32[]{:S(2)}, u32[]{:S(2)}) collective-permute-start(f32[288,128]{1,0:T(8,128)S(1)} %pad_maximum_fusion.3), channel_id=1, source_target_pairs={{1,0},{4,1},{5,4},{8,5},{9,8},{12,9},{13,12},{3,2},{6,3},{7,6},{10... | collective-permute-start | bytes 442376 | tf_op jit(solution)/shard_map/ppermute | solution.py:69
  13.6 4.0 %collective-permute-start = (f32[288,128]{1,0:T(8,128)S(1)}, f32[288,128]{1,0:T(8,128)S(1)}, u32[]{:S(2)}, u32[]{:S(2)}) collective-permute-start(f32[288,128]{1,0:T(8,128)S(1)} %pad_maximum_fusion.2), channel_id=1, source_target_pairs={{0,1},{1,4},{4,5},{5,8},{8,9},{9,12},{12,13},{2,3},{3,6},{6,7},{7,... | collective-permute-start | bytes 442376 | tf_op jit(solution)/shard_map/ppermute | solution.py:65
  20.5 8.5 %collective-permute-start.3 = (f32[3,32,128]{2,1,0:T(8,128)S(1)}, f32[3,32,128]{2,1,0:T(8,128)S(1)}, u32[]{:S(2)}, u32[]{:S(2)}) collective-permute-start(f32[3,32,128]{2,1,0:T(8,128)S(1)} %pad_maximum_fusion.9), channel_id=1, source_target_pairs={{1,0},{4,1},{5,4},{8,5},{9,8},{12,9},{13,12},{3,2},{6,3},{7,6},{10... | collective-permute-start | bytes 147464 | tf_op jit(solution)/shard_map/ppermute | solution.py:69
  21.8 7.1 %collective-permute-start.2 = (f32[3,32,128]{2,1,0:T(8,128)S(1)}, f32[3,32,128]{2,1,0:T(8,128)S(1)}, u32[]{:S(2)}, u32[]{:S(2)}) collective-permute-start(f32[3,32,128]{2,1,0:T(8,128)S(1)} %pad_maximum_fusion.8), channel_id=1, source_target_pairs={{0,1},{1,4},{4,5},{5,8},{8,9},{9,12},{12,13},{2,3},{3,6},{6,7},{7,... | collective-permute-start | bytes 147464 | tf_op jit(solution)/shard_map/ppermute | solution.py:65
  33.2 7.5 %collective-permute-start.5 = (f32[3,32,128]{2,1,0:T(8,128)S(1)}, f32[3,32,128]{2,1,0:T(8,128)S(1)}, u32[]{:S(2)}, u32[]{:S(2)}) collective-permute-start(f32[3,32,128]{2,1,0:T(8,128)S(1)} %pad_maximum_fusion.11), channel_id=1, source_target_pairs={{1,0},{4,1},{5,4},{8,5},{9,8},{12,9},{13,12},{3,2},{6,3},{7,6},{10... | collective-permute-start | bytes 147464 | tf_op jit(solution)/shard_map/ppermute | solution.py:69
  34.5 6.2 %collective-permute-start.4 = (f32[3,32,128]{2,1,0:T(8,128)S(1)}, f32[3,32,128]{2,1,0:T(8,128)S(1)}, u32[]{:S(2)}, u32[]{:S(2)}) collective-permute-start(f32[3,32,128]{2,1,0:T(8,128)S(1)} %pad_maximum_fusion.10), channel_id=1, source_target_pairs={{0,1},{1,4},{4,5},{5,8},{8,9},{9,12},{12,13},{2,3},{3,6},{6,7},{7,... | collective-permute-start | bytes 147464 | tf_op jit(solution)/shard_map/ppermute | solution.py:65
  42.0 1.0 %copy-start.2 = (bf16[512,4,128]{2,1,0:T(4,128)(2,1)S(1)}, bf16[512,4,128]{2,1,0:T(4,128)(2,1)}, u32[]{:S(2)}) copy-start(bf16[512,4,128]{2,1,0:T(4,128)(2,1)} %param.35) | copy-start | bytes 1572868
  46.0 3.9 %collective-permute-start.6 = (f32[4,16,2,4,128]{4,1,0,3,2:T(8,128)S(1)}, f32[4,16,2,4,128]{4,1,0,3,2:T(8,128)S(1)}, u32[]{:S(2)}, u32[]{:S(2)}) collective-permute-start(f32[4,16,2,4,128]{4,1,0,3,2:T(8,128)S(1)} %select_bitcast_fusion), channel_id=1, source_target_pairs={{0,1},{1,0},{2,3},{3,2},{4,5},{5,4},{6,7},{7,6},{8,9},{9,8},{10,11... | collective-permute-start | bytes 786440 | tf_op jit(solution)/shard_map/ppermute | solution.py:42
  50.0 6.5 %collective-permute-start.7 = (f32[2,16,2,4,128]{4,1,3,2,0:T(8,128)S(1)}, f32[2,16,2,4,128]{4,1,3,2,0:T(8,128)S(1)}, u32[]{:S(2)}, u32[]{:S(2)}) collective-permute-start(f32[2,16,2,4,128]{4,1,3,2,0:T(8,128)S(1)} %fusion.35), channel_id=1, source_target_pairs={{0,4},{4,0},{8,12},{12,8},{1,5},{5,1},{9,13},{13,9},{2,6},{6,2},{1... | collective-permute-start | bytes 393224 | tf_op jit(solution)/shard_map/ppermute | solution.py:42
  56.5 5.4 %collective-permute-start.8 = (f32[1,16,2,4,128]{4,1,3,2,0:T(8,128)S(1)}, f32[1,16,2,4,128]{4,1,3,2,0:T(8,128)S(1)}, u32[]{:S(2)}, u32[]{:S(2)}) collective-permute-start(f32[1,16,2,4,128]{4,1,3,2,0:T(8,128)S(1)} %select_bitcast_fusion.1), channel_id=1, source_target_pairs={{0,8},{4,12},{8,0},{12,4},{1,9},{5,13},{9,1},{13,5},{2,10},{6,14},... | collective-permute-start | bytes 196616 | tf_op jit(solution)/shard_map/ppermute | solution.py:42

commit v5 on v4

--- a/solution.py
+++ b/solution.py
@@ -133,16 +133,12 @@
     weighted_half = weighted.astype(jnp.bfloat16).reshape(row_count, state_count)
     in_use = jnp.arange(band_count, dtype=jnp.int32)[None, :] < counts[:, None]
     scaling = lax.rsqrt(counts.astype(jnp.float32))
-    moves = []
-    for shift in (-1, 0, 1):
-        chosen = in_use & (offsets == shift)
-        total = jnp.zeros((block_count, tile_size, tile_size), jnp.float32)
-        for slot in range(band_count):
-            total = total + jnp.where(
-                chosen[:, slot, None, None], tiles[:, slot].astype(jnp.float32), 0.0
-            )
-        moves.append(total * scaling[:, None, None])
-    moves = jnp.stack(moves, axis=1)
+    shifts = jnp.arange(-1, 2, dtype=jnp.int32)
+    chosen = in_use[:, :, None] & (offsets[:, :, None] == shifts[None, None, :])
+    weight = chosen.astype(jnp.float32) * scaling[:, None, None]
+    moves = jnp.sum(
+        weight[:, :, :, None, None] * tiles.astype(jnp.float32)[:, :, None, :, :], axis=1
+    )
     flat_start = impulses.reshape(state_count, width)
     rows = (
         weighted_half.astype(jnp.float32)

time: 63 us -> 54.1 us (0.86)
  local copies, waits for them, and re-layouts: 6.61 us -> 2.01 us
  other arithmetic: 9.15 us -> 4.89 us
    squeeze x1 -> x0, other arithmetic: 3.88 us -> none  [shards(): edge_high = jnp.concatenate([out_low, moves[0, 0], moves[0, 1]], 0)]
    slice x7 -> x0, local copies, waits for them, and re-layouts: 3.66 us -> none  [the longest x4 2.5 us: shards(): edge_low = jnp.concatenate([out_high, moves[-1, 1], moves[-1, 2]], 0)]
    mul x3 -> x1, other arithmetic: 1.84 us -> 0.08 us  [shards(): weight = chosen.astype(jnp.float32) * scaling[:, None, None]]
    convert_element_type x1, other arithmetic: 0.1 us -> 1.14 us  [shards(): tiles.astype(jnp.float32)[:, :, None, :, :]]
    unnamed x19, local copies, waits for them, and re-layouts: 1.31 us -> 0.37 us
    and x1 -> x0, other arithmetic: 0.76 us -> none  [shards(): chosen = in_use & (offsets == shift)]
    lt x0 -> x1, other arithmetic: none -> 0.73 us  [shards(): in_use = jnp.arange(band_count, dtype=jnp.int32)[None, :] < counts[:, None]]
where the time goes in v5:
time: 54.1 us; the launch traced here: 53.7 us
  starting transfers between devices  26.9 us (50%)
  waiting for transfers between devices  9.88 us (18%)
  matrix products  9.13 us (17%)
  other arithmetic  4.89 us (9%)
  local copies, waits for them, and re-layouts  2.01 us (4%)
  between operations  0.95 us (2%)
    ppermute x3, starting transfers between devices, to_right(): lax.ppermute(value, ('state', 'horizon'), shift_pairs(('state', 'horizon'...  14.8 us
    ppermute x3, starting transfers between devices, halving_scatter(): held = keep + lax.ppermute(send, axis, pairs)  8.19 us
    ppermute x3, waiting for transfers between devices, halving_scatter(): held = keep + lax.ppermute(send, axis, pairs)  7.59 us
    dot_general x6, matrix products, ext_step(): jnp.einsum('cru,cduv->cdrv', rows, moves, precision=lax.Precision.HIGHEST)  5.16 us
    ppermute x3, starting transfers between devices, to_left(): lax.ppermute(value, ('state', 'horizon'), shift_pairs(('state', 'horizon'...  3.88 us
    dot_general x5, matrix products, band_step(): jnp.einsum('cru,cduv->cdrv', rows, moves, precision=lax.Precision.HIGHEST)  2.86 us
    ppermute x3, waiting for transfers between devices, to_right(): lax.ppermute(value, ('state', 'horizon'), shift_pairs(('state', 'horizon'...  2.28 us
    add x7, other arithmetic, diagonal_sums(): total = total + moved  1.31 us
  transfers between devices with their start and end apart: 9, of which 6 were waited for; matrix products, arithmetic and copies ran while one was open for 0% of the time, Pallas kernels for 0%

profile of v5, /device:TPU:0, one launch (start us, length us, event | category | flops | bytes accessed | tf_op | source)
XLA Modules:
  0.0 53.7 jit_solution(3161285579148504105)
XLA Ops:
  0.0 0.7 %convert_rsqrt_fusion = f32[4]{0:T(128)S(1)} fusion(s32[4]{0:T(128)} %param.41), kind=kLoop, calls=%fused_computation.216 | loop fusion | flops 4 | bytes 32 | tf_op jit(solution)/shard_map/rsqrt | solution.py:135
  0.7 0.7 %iota_compare_fusion = pred[4,4]{1,0:T(4,128)(4,1)S(1)} fusion(s32[4]{0:T(128)} %param.41), kind=kLoop, calls=%fused_computation.213 | loop fusion | flops 16 | bytes 32 | tf_op jit(solution)/shard_map/lt | solution.py:134
  1.5 1.1 %convert_element_type.40 = f32[4,4,128,128]{3,2,1,0:T(8,128)S(1)} convert(bf16[4,4,128,128]{3,2,1,0:T(8,128)(2,1)} %param.39) | non-fusion elementwise | flops 262144 | bytes 1572864 | tf_op jit(solution)/shard_map/convert_element_type | solution.py:140
  4.1 1.3 %collective-permute-start.1 = (f32[288,128]{1,0:T(8,128)S(1)}, f32[288,128]{1,0:T(8,128)S(1)}, u32[]{:S(2)}, u32[]{:S(2)}) collective-permute-start(f32[288,128]{1,0:T(8,128)S(1)} %pad_maximum_fusion.2), channel_id=1, source_target_pairs={{1,0},{4,1},{5,4},{8,5},{9,8},{12,9},{13,12},{3,2},{6,3},{7,6},{10... | collective-permute-start | bytes 442376 | tf_op jit(solution)/shard_map/ppermute | solution.py:69
  5.4 3.0 %collective-permute-start = (f32[288,128]{1,0:T(8,128)S(1)}, f32[288,128]{1,0:T(8,128)S(1)}, u32[]{:S(2)}, u32[]{:S(2)}) collective-permute-start(f32[288,128]{1,0:T(8,128)S(1)} %pad_maximum_fusion.1), channel_id=1, source_target_pairs={{0,1},{1,4},{4,5},{5,8},{8,9},{9,12},{12,13},{2,3},{3,6},{6,7},{7,... | collective-permute-start | bytes 442376 | tf_op jit(solution)/shard_map/ppermute | solution.py:65
  8.6 0.8 %collective-permute-done = f32[288,128]{1,0:T(8,128)S(1)} collective-permute-done((f32[288,128]{1,0:T(8,128)S(1)}, f32[288,128]{1,0:T(8,128)S(1)}, u32[]{:S(2)}, u32[]{:S(2)}) %collective-permute-start) | collective-permute-done | bytes 147488 | tf_op jit(solution)/shard_map/ppermute | solution.py:65
  9.5 0.9 %convolution_bitcast_fusion.5 = f32[6,3,32,128]{3,2,1,0:T(8,128)S(1)} fusion(f32[1,32,128]{2,1,0:T(8,128)S(1)} %broadcast.334, f32[4,32,128]{2,1,0:T(8,128)S(1)} %fusion.76, f32[1,3,128,128]{3,2,1,0:T(8,128)S(1)} %get-tuple-element.226, f32[4,3,128,128]{3,2,1,0:T(8,128)S(1)} %multiply_reduce_fusion, f32[1,3,128,128]{3,2,1,0:T(8,128)S(1)} %get-tuple-element.225), kind=kOutput, calls=%fused_computation.9 | convolution fusion | flops 113885184 | bytes 1556480 | tf_op jit(solution)/shard_map/cru,cduv->cdrv/dot_general | solution.py:85
  10.4 0.9 %convolution_bitcast_fusion.4 = f32[6,3,32,128]{3,2,0,1:T(8,128)S(1)} fusion(f32[6,32,128]{2,1,0:T(8,128)S(1)} %fusion.33, f32[1,3,128,128]{3,2,1,0:T(8,128)S(1)} %get-tuple-element.226, f32[4,3,128,128]{3,2,1,0:T(8,128)S(1)} %multiply_reduce_fusion, f32[1,3,128,128]{3,2,1,0:T(8,128)S(1)} %get-tuple-element.225), kind=kOutput, calls=%fused_computation.8 | convolution fusion | flops 113836032 | bytes 1572864 | tf_op jit(solution)/shard_map/cru,cduv->cdrv/dot_general | solution.py:85
  11.4 0.9 %convolution_bitcast_fusion.3 = f32[6,3,32,128]{3,2,0,1:T(8,128)S(1)} fusion(f32[6,32,128]{2,1,0:T(8,128)S(1)} %fusion.31, f32[1,3,128,128]{3,2,1,0:T(8,128)S(1)} %get-tuple-element.226, f32[4,3,128,128]{3,2,1,0:T(8,128)S(1)} %multiply_reduce_fusion, f32[1,3,128,128]{3,2,1,0:T(8,128)S(1)} %get-tuple-element.225), kind=kOutput, calls=%fused_computation.7 | convolution fusion | flops 113836032 | bytes 1572864 | tf_op jit(solution)/shard_map/cru,cduv->cdrv/dot_general | solution.py:85
  12.3 1.3 %collective-permute-start.3 = (f32[3,32,128]{2,1,0:T(8,128)S(1)}, f32[3,32,128]{2,1,0:T(8,128)S(1)}, u32[]{:S(2)}, u32[]{:S(2)}) collective-permute-start(f32[3,32,128]{2,1,0:T(8,128)S(1)} %pad_maximum_fusion.8), channel_id=1, source_target_pairs={{1,0},{4,1},{5,4},{8,5},{9,8},{12,9},{13,12},{3,2},{6,3},{7,6},{10... | collective-permute-start | bytes 147464 | tf_op jit(solution)/shard_map/ppermute | solution.py:69
  13.6 6.3 %collective-permute-start.2 = (f32[3,32,128]{2,1,0:T(8,128)S(1)}, f32[3,32,128]{2,1,0:T(8,128)S(1)}, u32[]{:S(2)}, u32[]{:S(2)}) collective-permute-start(f32[3,32,128]{2,1,0:T(8,128)S(1)} %pad_maximum_fusion.7), channel_id=1, source_target_pairs={{0,1},{1,4},{4,5},{5,8},{8,9},{9,12},{12,13},{2,3},{3,6},{6,7},{7,... | collective-permute-start | bytes 147464 | tf_op jit(solution)/shard_map/ppermute | solution.py:65
  19.9 0.8 %collective-permute-done.2 = f32[3,32,128]{2,1,0:T(8,128)S(1)} collective-permute-done((f32[3,32,128]{2,1,0:T(8,128)S(1)}, f32[3,32,128]{2,1,0:T(8,128)S(1)}, u32[]{:S(2)}, u32[]{:S(2)}) %collective-permute-start.2) | collective-permute-done | bytes 49184 | tf_op jit(solution)/shard_map/ppermute | solution.py:65
  22.2 0.9 %convolution_bitcast_fusion.2 = f32[6,3,32,128]{3,2,1,0:T(8,128)S(1)} fusion(f32[1,32,128]{2,1,0:T(8,128)S(1)} %broadcast.334, f32[4,32,128]{2,1,0:T(8,128)S(1)} %fusion.51, f32[1,3,128,128]{3,2,1,0:T(8,128)S(1)} %get-tuple-element.226, f32[4,3,128,128]{3,2,1,0:T(8,128)S(1)} %multiply_reduce_fusion, f32[1,3,128,128]{3,2,1,0:T(8,128)S(1)} %get-tuple-element.225), kind=kOutput, calls=%fused_computation.6 | convolution fusion | flops 113885184 | bytes 1556480 | tf_op jit(solution)/shard_map/cru,cduv->cdrv/dot_general | solution.py:85
  23.1 0.9 %convolution_bitcast_fusion.1 = f32[6,3,32,128]{3,2,0,1:T(8,128)S(1)} fusion(f32[6,32,128]{2,1,0:T(8,128)S(1)} %fusion.29, f32[1,3,128,128]{3,2,1,0:T(8,128)S(1)} %get-tuple-element.226, f32[4,3,128,128]{3,2,1,0:T(8,128)S(1)} %multiply_reduce_fusion, f32[1,3,128,128]{3,2,1,0:T(8,128)S(1)} %get-tuple-element.225), kind=kOutput, calls=%fused_computation.5 | convolution fusion | flops 113836032 | bytes 1572864 | tf_op jit(solution)/shard_map/cru,cduv->cdrv/dot_general | solution.py:85
  24.0 0.9 %convolution_bitcast_fusion = f32[6,3,32,128]{3,2,0,1:T(8,128)S(1)} fusion(f32[6,32,128]{2,1,0:T(8,128)S(1)} %fusion.27, f32[1,3,128,128]{3,2,1,0:T(8,128)S(1)} %get-tuple-element.226, f32[4,3,128,128]{3,2,1,0:T(8,128)S(1)} %multiply_reduce_fusion, f32[1,3,128,128]{3,2,1,0:T(8,128)S(1)} %get-tuple-element.225), kind=kOutput, calls=%fused_computation.4 | convolution fusion | flops 113836032 | bytes 1572864 | tf_op jit(solution)/shard_map/cru,cduv->cdrv/dot_general | solution.py:85
  25.0 1.3 %collective-permute-start.5 = (f32[3,32,128]{2,1,0:T(8,128)S(1)}, f32[3,32,128]{2,1,0:T(8,128)S(1)}, u32[]{:S(2)}, u32[]{:S(2)}) collective-permute-start(f32[3,32,128]{2,1,0:T(8,128)S(1)} %pad_maximum_fusion.10), channel_id=1, source_target_pairs={{1,0},{4,1},{5,4},{8,5},{9,8},{12,9},{13,12},{3,2},{6,3},{7,6},{10... | collective-permute-start | bytes 147464 | tf_op jit(solution)/shard_map/ppermute | solution.py:69
  26.3 5.5 %collective-permute-start.4 = (f32[3,32,128]{2,1,0:T(8,128)S(1)}, f32[3,32,128]{2,1,0:T(8,128)S(1)}, u32[]{:S(2)}, u32[]{:S(2)}) collective-permute-start(f32[3,32,128]{2,1,0:T(8,128)S(1)} %pad_maximum_fusion.9), channel_id=1, source_target_pairs={{0,1},{1,4},{4,5},{5,8},{8,9},{9,12},{12,13},{2,3},{3,6},{6,7},{7,... | collective-permute-start | bytes 147464 | tf_op jit(solution)/shard_map/ppermute | solution.py:65
  37.1 2.7 %collective-permute-start.6 = (f32[4,16,2,4,128]{4,1,0,3,2:T(8,128)S(1)}, f32[4,16,2,4,128]{4,1,0,3,2:T(8,128)S(1)}, u32[]{:S(2)}, u32[]{:S(2)}) collective-permute-start(f32[4,16,2,4,128]{4,1,0,3,2:T(8,128)S(1)} %select_bitcast_fusion), channel_id=1, source_target_pairs={{0,1},{1,0},{2,3},{3,2},{4,5},{5,4},{6,7},{7,6},{8,9},{9,8},{10,11... | collective-permute-start | bytes 786440 | tf_op jit(solution)/shard_map/ppermute | solution.py:42
  39.8 1.2 %collective-permute-done.6 = f32[4,16,2,4,128]{4,1,0,3,2:T(8,128)S(1)} collective-permute-done((f32[4,16,2,4,128]{4,1,0,3,2:T(8,128)S(1)}, f32[4,16,2,4,128]{4,1,0,3,2:T(8,128)S(1)}, u32[]{:S(2)}, u32[]{:S(2)}) %collective-permute-start.6) | collective-permute-done | bytes 262176 | tf_op jit(solution)/shard_map/ppermute | solution.py:42
  41.1 2.7 %collective-permute-start.7 = (f32[2,16,2,4,128]{4,1,3,2,0:T(8,128)S(1)}, f32[2,16,2,4,128]{4,1,3,2,0:T(8,128)S(1)}, u32[]{:S(2)}, u32[]{:S(2)}) collective-permute-start(f32[2,16,2,4,128]{4,1,3,2,0:T(8,128)S(1)} %fusion.20), channel_id=1, source_target_pairs={{0,4},{4,0},{8,12},{12,8},{1,5},{5,1},{9,13},{13,9},{2,6},{6,2},{1... | collective-permute-start | bytes 393224 | tf_op jit(solution)/shard_map/ppermute | solution.py:42
  43.7 3.8 %collective-permute-done.7 = f32[2,16,2,4,128]{4,1,3,2,0:T(8,128)S(1)} collective-permute-done((f32[2,16,2,4,128]{4,1,3,2,0:T(8,128)S(1)}, f32[2,16,2,4,128]{4,1,3,2,0:T(8,128)S(1)}, u32[]{:S(2)}, u32[]{:S(2)}) %collective-permute-start.7) | collective-permute-done | bytes 131104 | tf_op jit(solution)/shard_map/ppermute | solution.py:42
  47.6 2.8 %collective-permute-start.8 = (f32[1,16,2,4,128]{4,1,3,2,0:T(8,128)S(1)}, f32[1,16,2,4,128]{4,1,3,2,0:T(8,128)S(1)}, u32[]{:S(2)}, u32[]{:S(2)}) collective-permute-start(f32[1,16,2,4,128]{4,1,3,2,0:T(8,128)S(1)} %select_bitcast_fusion.1), channel_id=1, source_target_pairs={{0,8},{4,12},{8,0},{12,4},{1,9},{5,13},{9,1},{13,5},{2,10},{6,14},... | collective-permute-start | bytes 196616 | tf_op jit(solution)/shard_map/ppermute | solution.py:42
  50.4 2.6 %collective-permute-done.8 = f32[1,16,2,4,128]{4,1,3,2,0:T(8,128)S(1)} collective-permute-done((f32[1,16,2,4,128]{4,1,3,2,0:T(8,128)S(1)}, f32[1,16,2,4,128]{4,1,3,2,0:T(8,128)S(1)}, u32[]{:S(2)}, u32[]{:S(2)}) %collective-permute-start.8) | collective-permute-done | bytes 65568 | tf_op jit(solution)/shard_map/ppermute | solution.py:42
  53.1 0.7 %copy.145 = f32[16,2,4,128]{3,2,1,0:T(4,128)} copy(f32[16,2,4,128]{3,0,2,1:T(8,128)S(1)} %fusion.58) | data formatting | bytes 131072 | tf_op jit(solution)/shard_map/reshape | solution.py:44
  (131 shorter events, 8.3 us)
Async XLA Ops:
  0.0 2.6 %copy-start = (f32[16,2]{0,1:T(2,128)S(1)}, f32[16,2]{0,1:T(2,128)}, u32[]{:S(2)}) copy-start(f32[16,2]{0,1:T(2,128)} %param.37) | copy-start | bytes 388
  0.0 2.6 %copy-start.4 = (s32[4]{0:T(128)S(1)}, s32[4]{0:T(128)}, u32[]{:S(2)}) copy-start(s32[4]{0:T(128)} %param.38) | copy-start | bytes 52
  0.0 3.1 %copy-start.2 = (bf16[2,16,512]{2,1,0:T(8,128)(2,1)S(1)}, bf16[2,16,512]{2,1,0:T(8,128)(2,1)}, u32[]{:S(2)}) copy-start(bf16[2,16,512]{2,1,0:T(8,128)(2,1)} %param.36) | copy-start | bytes 98308
  0.0 3.1 %copy-start.3 = (s32[4,4]{1,0:T(4,128)S(1)}, s32[4,4]{1,0:T(4,128)}, u32[]{:S(2)}) copy-start(s32[4,4]{1,0:T(4,128)} %param.40) | copy-start | bytes 196
  4.1 4.5 %collective-permute-start.1 = (f32[288,128]{1,0:T(8,128)S(1)}, f32[288,128]{1,0:T(8,128)S(1)}, u32[]{:S(2)}, u32[]{:S(2)}) collective-permute-start(f32[288,128]{1,0:T(8,128)S(1)} %pad_maximum_fusion.2), channel_id=1, source_target_pairs={{1,0},{4,1},{5,4},{8,5},{9,8},{12,9},{13,12},{3,2},{6,3},{7,6},{10... | collective-permute-start | bytes 442376 | tf_op jit(solution)/shard_map/ppermute | solution.py:69
  5.4 4.0 %collective-permute-start = (f32[288,128]{1,0:T(8,128)S(1)}, f32[288,128]{1,0:T(8,128)S(1)}, u32[]{:S(2)}, u32[]{:S(2)}) collective-permute-start(f32[288,128]{1,0:T(8,128)S(1)} %pad_maximum_fusion.1), channel_id=1, source_target_pairs={{0,1},{1,4},{4,5},{5,8},{8,9},{9,12},{12,13},{2,3},{3,6},{6,7},{7,... | collective-permute-start | bytes 442376 | tf_op jit(solution)/shard_map/ppermute | solution.py:65
  12.3 8.5 %collective-permute-start.3 = (f32[3,32,128]{2,1,0:T(8,128)S(1)}, f32[3,32,128]{2,1,0:T(8,128)S(1)}, u32[]{:S(2)}, u32[]{:S(2)}) collective-permute-start(f32[3,32,128]{2,1,0:T(8,128)S(1)} %pad_maximum_fusion.8), channel_id=1, source_target_pairs={{1,0},{4,1},{5,4},{8,5},{9,8},{12,9},{13,12},{3,2},{6,3},{7,6},{10... | collective-permute-start | bytes 147464 | tf_op jit(solution)/shard_map/ppermute | solution.py:69
  13.6 7.1 %collective-permute-start.2 = (f32[3,32,128]{2,1,0:T(8,128)S(1)}, f32[3,32,128]{2,1,0:T(8,128)S(1)}, u32[]{:S(2)}, u32[]{:S(2)}) collective-permute-start(f32[3,32,128]{2,1,0:T(8,128)S(1)} %pad_maximum_fusion.7), channel_id=1, source_target_pairs={{0,1},{1,4},{4,5},{5,8},{8,9},{9,12},{12,13},{2,3},{3,6},{6,7},{7,... | collective-permute-start | bytes 147464 | tf_op jit(solution)/shard_map/ppermute | solution.py:65
  25.0 7.5 %collective-permute-start.5 = (f32[3,32,128]{2,1,0:T(8,128)S(1)}, f32[3,32,128]{2,1,0:T(8,128)S(1)}, u32[]{:S(2)}, u32[]{:S(2)}) collective-permute-start(f32[3,32,128]{2,1,0:T(8,128)S(1)} %pad_maximum_fusion.10), channel_id=1, source_target_pairs={{1,0},{4,1},{5,4},{8,5},{9,8},{12,9},{13,12},{3,2},{6,3},{7,6},{10... | collective-permute-start | bytes 147464 | tf_op jit(solution)/shard_map/ppermute | solution.py:69
  26.3 6.2 %collective-permute-start.4 = (f32[3,32,128]{2,1,0:T(8,128)S(1)}, f32[3,32,128]{2,1,0:T(8,128)S(1)}, u32[]{:S(2)}, u32[]{:S(2)}) collective-permute-start(f32[3,32,128]{2,1,0:T(8,128)S(1)} %pad_maximum_fusion.9), channel_id=1, source_target_pairs={{0,1},{1,4},{4,5},{5,8},{8,9},{9,12},{12,13},{2,3},{3,6},{6,7},{7,... | collective-permute-start | bytes 147464 | tf_op jit(solution)/shard_map/ppermute | solution.py:65
  33.2 1.0 %copy-start.1 = (bf16[512,4,128]{2,1,0:T(4,128)(2,1)S(1)}, bf16[512,4,128]{2,1,0:T(4,128)(2,1)}, u32[]{:S(2)}) copy-start(bf16[512,4,128]{2,1,0:T(4,128)(2,1)} %param.35) | copy-start | bytes 1572868
  37.1 3.9 %collective-permute-start.6 = (f32[4,16,2,4,128]{4,1,0,3,2:T(8,128)S(1)}, f32[4,16,2,4,128]{4,1,0,3,2:T(8,128)S(1)}, u32[]{:S(2)}, u32[]{:S(2)}) collective-permute-start(f32[4,16,2,4,128]{4,1,0,3,2:T(8,128)S(1)} %select_bitcast_fusion), channel_id=1, source_target_pairs={{0,1},{1,0},{2,3},{3,2},{4,5},{5,4},{6,7},{7,6},{8,9},{9,8},{10,11... | collective-permute-start | bytes 786440 | tf_op jit(solution)/shard_map/ppermute | solution.py:42
  41.1 6.5 %collective-permute-start.7 = (f32[2,16,2,4,128]{4,1,3,2,0:T(8,128)S(1)}, f32[2,16,2,4,128]{4,1,3,2,0:T(8,128)S(1)}, u32[]{:S(2)}, u32[]{:S(2)}) collective-permute-start(f32[2,16,2,4,128]{4,1,3,2,0:T(8,128)S(1)} %fusion.20), channel_id=1, source_target_pairs={{0,4},{4,0},{8,12},{12,8},{1,5},{5,1},{9,13},{13,9},{2,6},{6,2},{1... | collective-permute-start | bytes 393224 | tf_op jit(solution)/shard_map/ppermute | solution.py:42
  47.6 5.4 %collective-permute-start.8 = (f32[1,16,2,4,128]{4,1,3,2,0:T(8,128)S(1)}, f32[1,16,2,4,128]{4,1,3,2,0:T(8,128)S(1)}, u32[]{:S(2)}, u32[]{:S(2)}) collective-permute-start(f32[1,16,2,4,128]{4,1,3,2,0:T(8,128)S(1)} %select_bitcast_fusion.1), channel_id=1, source_target_pairs={{0,8},{4,12},{8,0},{12,4},{1,9},{5,13},{9,1},{13,5},{2,10},{6,14},... | collective-permute-start | bytes 196616 | tf_op jit(solution)/shard_map/ppermute | solution.py:42

commit v6 on v5

--- a/solution.py
+++ b/solution.py
@@ -70,19 +70,15 @@
 
 
 def band_step(rows, moves):
-    parts = jnp.einsum("cru,cduv->cdrv", rows, moves, precision=lax.Precision.HIGHEST)
+    parts = jnp.einsum("cru,cduv->cdrv", rows, moves, precision=lax.Precision.HIGH)
     down, same, up = parts[:, 0], parts[:, 1], parts[:, 2]
     zero = jnp.zeros_like(same[:1])
     inner = same + jnp.concatenate([down[1:], zero], 0) + jnp.concatenate([zero, up[:-1]], 0)
     return inner, down[0], up[-1]
 
 
-def mat(rows, matrix):
-    return jnp.dot(rows, matrix, precision=lax.Precision.HIGHEST)
-
-
 def ext_step(rows, moves):
-    parts = jnp.einsum("cru,cduv->cdrv", rows, moves, precision=lax.Precision.HIGHEST)
+    parts = jnp.einsum("cru,cduv->cdrv", rows, moves, precision=lax.Precision.HIGH)
     down, same, up = parts[:, 0], parts[:, 1], parts[:, 2]
     zero = jnp.zeros_like(same[:1])
     inner = same + jnp.concatenate([down[1:], zero], 0) + jnp.concatenate([zero, up[:-1]], 0)
@@ -135,10 +131,12 @@
     scaling = lax.rsqrt(counts.astype(jnp.float32))
     shifts = jnp.arange(-1, 2, dtype=jnp.int32)
     chosen = in_use[:, :, None] & (offsets[:, :, None] == shifts[None, None, :])
-    weight = chosen.astype(jnp.float32) * scaling[:, None, None]
-    moves = jnp.sum(
-        weight[:, :, :, None, None] * tiles.astype(jnp.float32)[:, :, None, :, :], axis=1
-    )
+    moves = jnp.einsum(
+        "cjd,cjuv->cduv",
+        chosen.astype(jnp.bfloat16),
+        tiles,
+        preferred_element_type=jnp.float32,
+    ) * scaling[:, None, None, None]
     flat_start = impulses.reshape(state_count, width)
     rows = (
         weighted_half.astype(jnp.float32)

time: 54.1 us -> 51.9 us (0.959)
  matrix products: 9.13 us -> 7.33 us
  other arithmetic: 4.89 us -> 3.44 us
  local copies, waits for them, and re-layouts: 2.01 us -> 3.04 us
    dot_general x11 -> x12, matrix products: 8.02 us -> 5.52 us  [the longest x6 2.65 us: ext_step(): jnp.einsum('cru,cduv->cdrv', rows, moves, precision=lax.Precision.HIGH)]
    convert_element_type x1 -> x0, other arithmetic: 1.14 us -> none  [shards(): tiles.astype(jnp.float32)[:, :, None, :, :]]
    reshape x1, local copies, waits for them, and re-layouts: 0.03 us -> 0.79 us  [shards(): expectations.astype(jnp.float32)]
    dot_general x1, matrix products: 0.18 us -> 0.88 us  [shards(): jnp.dot(onehot, region_scale, precision=lax.Precision.HIGHEST, preferred_...]
where the time goes in v6:
time: 51.9 us; the launch traced here: 51.5 us
  starting transfers between devices  26.7 us (51%)
  waiting for transfers between devices  10 us (19%)
  matrix products  7.33 us (14%)
  other arithmetic  3.44 us (7%)
  local copies, waits for them, and re-layouts  3.04 us (6%)
  between operations  0.93 us (2%)
    ppermute x3, starting transfers between devices, to_right(): lax.ppermute(value, ('state', 'horizon'), shift_pairs(('state', 'horizon'...  14.6 us
    ppermute x3, starting transfers between devices, halving_scatter(): held = keep + lax.ppermute(send, axis, pairs)  8.19 us
    ppermute x3, waiting for transfers between devices, halving_scatter(): held = keep + lax.ppermute(send, axis, pairs)  7.59 us
    ppermute x3, starting transfers between devices, to_left(): lax.ppermute(value, ('state', 'horizon'), shift_pairs(('state', 'horizon'...  3.88 us
    dot_general x6, matrix products, ext_step(): jnp.einsum('cru,cduv->cdrv', rows, moves, precision=lax.Precision.HIGH)  2.65 us
    ppermute x3, waiting for transfers between devices, to_right(): lax.ppermute(value, ('state', 'horizon'), shift_pairs(('state', 'horizon'...  2.45 us
    dot_general x5, matrix products, band_step(): jnp.einsum('cru,cduv->cdrv', rows, moves, precision=lax.Precision.HIGH)  1.65 us
    add x7, other arithmetic, diagonal_sums(): total = total + moved  1.31 us
  transfers between devices with their start and end apart: 9, of which 6 were waited for; matrix products, arithmetic and copies ran while one was open for 0% of the time, Pallas kernels for 0%

profile of v6, /device:TPU:0, one launch (start us, length us, event | category | flops | bytes accessed | tf_op | source)
XLA Modules:
  0.0 51.5 jit_solution(11731343781425311567)
XLA Ops:
  0.0 0.8 %iota_compare_fusion = pred[4,4]{1,0:T(4,128)(4,1)S(1)} fusion(s32[4]{0:T(128)} %param.41), kind=kLoop, calls=%fused_computation.220 | loop fusion | flops 16 | bytes 32 | tf_op jit(solution)/shard_map/lt | solution.py:130
  0.8 0.7 %convert_rsqrt_fusion = f32[4]{0:T(128)S(1)} fusion(s32[4]{0:T(128)} %param.41), kind=kLoop, calls=%fused_computation.223 | loop fusion | flops 4 | bytes 32 | tf_op jit(solution)/shard_map/rsqrt | solution.py:131
  1.4 0.9 %convolution_bitcast_fusion.11 = f32[2,4]{1,0:T(2,128)S(1)} fusion(f32[16,2]{0,1:T(2,128)} %param.37, s32[4]{0:T(128)} %param.38), kind=kOutput, calls=%fused_computation.14 | convolution fusion | flops 1600 | bytes 176 | tf_op jit(solution)/shard_map/dot_general | solution.py:122
  2.6 0.8 %reshape.567 = f32[32,4,128]{2,1,0:T(4,128)S(1)} reshape(bf16[2,16,512]{2,1,0:T(8,128)(2,1)} %param.36) | data formatting | bytes 98304 | tf_op jit(solution)/shard_map/reshape | solution.py:126
  3.4 1.2 %fusion.12 = f32[4,3,128,128]{3,1,2,0:T(4,128)S(1)} fusion(bf16[4,4,128,128]{3,2,1,0:T(8,128)(2,1)S(1)} %copy-done, s32[4,4]{1,0:T(4,128)} %param.40, s32[3]{0:T(128)S(1)} %iota_add_fusion, pred[4,4]{1,0:T(4,128)(4,1)S(1)} %iota_compare_fusion), kind=kOutput, calls=%fused_computation.28 | convolution fusion | flops 1572960 | bytes 1310812 | tf_op jit(solution)/shard_map/cjd,cjuv->cduv/dot_general | solution.py:134
  5.2 1.3 %collective-permute-start.1 = (f32[288,128]{1,0:T(8,128)S(1)}, f32[288,128]{1,0:T(8,128)S(1)}, u32[]{:S(2)}, u32[]{:S(2)}) collective-permute-start(f32[288,128]{1,0:T(8,128)S(1)} %pad_maximum_fusion.2), channel_id=1, source_target_pairs={{1,0},{4,1},{5,4},{8,5},{9,8},{12,9},{13,12},{3,2},{6,3},{7,6},{10... | collective-permute-start | bytes 442376 | tf_op jit(solution)/shard_map/ppermute | solution.py:69
  6.5 3.0 %collective-permute-start = (f32[288,128]{1,0:T(8,128)S(1)}, f32[288,128]{1,0:T(8,128)S(1)}, u32[]{:S(2)}, u32[]{:S(2)}) collective-permute-start(f32[288,128]{1,0:T(8,128)S(1)} %pad_maximum_fusion.1), channel_id=1, source_target_pairs={{0,1},{1,4},{4,5},{5,8},{8,9},{9,12},{12,13},{2,3},{3,6},{6,7},{7,... | collective-permute-start | bytes 442376 | tf_op jit(solution)/shard_map/ppermute | solution.py:65
  9.7 0.8 %collective-permute-done = f32[288,128]{1,0:T(8,128)S(1)} collective-permute-done((f32[288,128]{1,0:T(8,128)S(1)}, f32[288,128]{1,0:T(8,128)S(1)}, u32[]{:S(2)}, u32[]{:S(2)}) %collective-permute-start) | collective-permute-done | bytes 147488 | tf_op jit(solution)/shard_map/ppermute | solution.py:65
  10.6 0.4 convolution_bitcast_fusion.5
  11.1 0.4 convolution_bitcast_fusion.4
  12.1 1.3 %collective-permute-start.3 = (f32[3,32,128]{2,1,0:T(8,128)S(1)}, f32[3,32,128]{2,1,0:T(8,128)S(1)}, u32[]{:S(2)}, u32[]{:S(2)}) collective-permute-start(f32[3,32,128]{2,1,0:T(8,128)S(1)} %pad_maximum_fusion.8), channel_id=1, source_target_pairs={{1,0},{4,1},{5,4},{8,5},{9,8},{12,9},{13,12},{3,2},{6,3},{7,6},{10... | collective-permute-start | bytes 147464 | tf_op jit(solution)/shard_map/ppermute | solution.py:69
  13.4 6.3 %collective-permute-start.2 = (f32[3,32,128]{2,1,0:T(8,128)S(1)}, f32[3,32,128]{2,1,0:T(8,128)S(1)}, u32[]{:S(2)}, u32[]{:S(2)}) collective-permute-start(f32[3,32,128]{2,1,0:T(8,128)S(1)} %pad_maximum_fusion.7), channel_id=1, source_target_pairs={{0,1},{1,4},{4,5},{5,8},{8,9},{9,12},{12,13},{2,3},{3,6},{6,7},{7,... | collective-permute-start | bytes 147464 | tf_op jit(solution)/shard_map/ppermute | solution.py:65
  19.7 0.8 %collective-permute-done.2 = f32[3,32,128]{2,1,0:T(8,128)S(1)} collective-permute-done((f32[3,32,128]{2,1,0:T(8,128)S(1)}, f32[3,32,128]{2,1,0:T(8,128)S(1)}, u32[]{:S(2)}, u32[]{:S(2)}) %collective-permute-start.2) | collective-permute-done | bytes 49184 | tf_op jit(solution)/shard_map/ppermute | solution.py:65
  23.0 1.3 %collective-permute-start.5 = (f32[3,32,128]{2,1,0:T(8,128)S(1)}, f32[3,32,128]{2,1,0:T(8,128)S(1)}, u32[]{:S(2)}, u32[]{:S(2)}) collective-permute-start(f32[3,32,128]{2,1,0:T(8,128)S(1)} %pad_maximum_fusion.10), channel_id=1, source_target_pairs={{1,0},{4,1},{5,4},{8,5},{9,8},{12,9},{13,12},{3,2},{6,3},{7,6},{10... | collective-permute-start | bytes 147464 | tf_op jit(solution)/shard_map/ppermute | solution.py:69
  24.3 5.3 %collective-permute-start.4 = (f32[3,32,128]{2,1,0:T(8,128)S(1)}, f32[3,32,128]{2,1,0:T(8,128)S(1)}, u32[]{:S(2)}, u32[]{:S(2)}) collective-permute-start(f32[3,32,128]{2,1,0:T(8,128)S(1)} %pad_maximum_fusion.9), channel_id=1, source_target_pairs={{0,1},{1,4},{4,5},{5,8},{8,9},{9,12},{12,13},{2,3},{3,6},{6,7},{7,... | collective-permute-start | bytes 147464 | tf_op jit(solution)/shard_map/ppermute | solution.py:65
  29.7 0.8 %collective-permute-done.4 = f32[3,32,128]{2,1,0:T(8,128)S(1)} collective-permute-done((f32[3,32,128]{2,1,0:T(8,128)S(1)}, f32[3,32,128]{2,1,0:T(8,128)S(1)}, u32[]{:S(2)}, u32[]{:S(2)}) %collective-permute-start.4) | collective-permute-done | bytes 49184 | tf_op jit(solution)/shard_map/ppermute | solution.py:65
  31.4 0.6 %copy-done.1 = bf16[512,4,128]{2,1,0:T(4,128)(2,1)S(1)} copy-done((bf16[512,4,128]{2,1,0:T(4,128)(2,1)S(1)}, bf16[512,4,128]{2,1,0:T(4,128)(2,1)}, u32[]{:S(2)}) %copy-start.1) | copy-done | bytes 524312
  34.8 2.7 %collective-permute-start.6 = (f32[4,16,2,4,128]{4,1,0,3,2:T(8,128)S(1)}, f32[4,16,2,4,128]{4,1,0,3,2:T(8,128)S(1)}, u32[]{:S(2)}, u32[]{:S(2)}) collective-permute-start(f32[4,16,2,4,128]{4,1,0,3,2:T(8,128)S(1)} %select_bitcast_fusion), channel_id=1, source_target_pairs={{0,1},{1,0},{2,3},{3,2},{4,5},{5,4},{6,7},{7,6},{8,9},{9,8},{10,11... | collective-permute-start | bytes 786440 | tf_op jit(solution)/shard_map/ppermute | solution.py:42
  37.6 1.2 %collective-permute-done.6 = f32[4,16,2,4,128]{4,1,0,3,2:T(8,128)S(1)} collective-permute-done((f32[4,16,2,4,128]{4,1,0,3,2:T(8,128)S(1)}, f32[4,16,2,4,128]{4,1,0,3,2:T(8,128)S(1)}, u32[]{:S(2)}, u32[]{:S(2)}) %collective-permute-start.6) | collective-permute-done | bytes 262176 | tf_op jit(solution)/shard_map/ppermute | solution.py:42
  38.8 2.7 %collective-permute-start.7 = (f32[2,16,2,4,128]{4,1,3,2,0:T(8,128)S(1)}, f32[2,16,2,4,128]{4,1,3,2,0:T(8,128)S(1)}, u32[]{:S(2)}, u32[]{:S(2)}) collective-permute-start(f32[2,16,2,4,128]{4,1,3,2,0:T(8,128)S(1)} %fusion.22), channel_id=1, source_target_pairs={{0,4},{4,0},{8,12},{12,8},{1,5},{5,1},{9,13},{13,9},{2,6},{6,2},{1... | collective-permute-start | bytes 393224 | tf_op jit(solution)/shard_map/ppermute | solution.py:42
  41.5 3.8 %collective-permute-done.7 = f32[2,16,2,4,128]{4,1,3,2,0:T(8,128)S(1)} collective-permute-done((f32[2,16,2,4,128]{4,1,3,2,0:T(8,128)S(1)}, f32[2,16,2,4,128]{4,1,3,2,0:T(8,128)S(1)}, u32[]{:S(2)}, u32[]{:S(2)}) %collective-permute-start.7) | collective-permute-done | bytes 131104 | tf_op jit(solution)/shard_map/ppermute | solution.py:42
  45.3 2.8 %collective-permute-start.8 = (f32[1,16,2,4,128]{4,1,3,2,0:T(8,128)S(1)}, f32[1,16,2,4,128]{4,1,3,2,0:T(8,128)S(1)}, u32[]{:S(2)}, u32[]{:S(2)}) collective-permute-start(f32[1,16,2,4,128]{4,1,3,2,0:T(8,128)S(1)} %select_bitcast_fusion.1), channel_id=1, source_target_pairs={{0,8},{4,12},{8,0},{12,4},{1,9},{5,13},{9,1},{13,5},{2,10},{6,14},... | collective-permute-start | bytes 196616 | tf_op jit(solution)/shard_map/ppermute | solution.py:42
  48.2 2.6 %collective-permute-done.8 = f32[1,16,2,4,128]{4,1,3,2,0:T(8,128)S(1)} collective-permute-done((f32[1,16,2,4,128]{4,1,3,2,0:T(8,128)S(1)}, f32[1,16,2,4,128]{4,1,3,2,0:T(8,128)S(1)}, u32[]{:S(2)}, u32[]{:S(2)}) %collective-permute-start.8) | collective-permute-done | bytes 65568 | tf_op jit(solution)/shard_map/ppermute | solution.py:42
  50.8 0.7 %copy.200 = f32[16,2,4,128]{3,2,1,0:T(4,128)} copy(f32[16,2,4,128]{3,0,2,1:T(8,128)S(1)} %fusion.60) | data formatting | bytes 131072 | tf_op jit(solution)/shard_map/reshape | solution.py:44
  (126 shorter events, 7.4 us)
Async XLA Ops:
  0.0 3.4 %copy-start = (bf16[4,4,128,128]{3,2,1,0:T(8,128)(2,1)S(1)}, bf16[4,4,128,128]{3,2,1,0:T(8,128)(2,1)}, u32[]{:S(2)}) copy-start(bf16[4,4,128,128]{3,2,1,0:T(8,128)(2,1)} %param.39) | copy-start | bytes 1572868
  4.8 4.8 %copy-start.2 = (bf16[2,16,512]{2,1,0:T(8,128)(2,1)S(1)}, bf16[2,16,512]{2,1,0:T(8,128)(2,1)}, u32[]{:S(2)}) copy-start(bf16[2,16,512]{2,1,0:T(8,128)(2,1)} %param.36) | copy-start | bytes 98308
  5.2 4.5 %collective-permute-start.1 = (f32[288,128]{1,0:T(8,128)S(1)}, f32[288,128]{1,0:T(8,128)S(1)}, u32[]{:S(2)}, u32[]{:S(2)}) collective-permute-start(f32[288,128]{1,0:T(8,128)S(1)} %pad_maximum_fusion.2), channel_id=1, source_target_pairs={{1,0},{4,1},{5,4},{8,5},{9,8},{12,9},{13,12},{3,2},{6,3},{7,6},{10... | collective-permute-start | bytes 442376 | tf_op jit(solution)/shard_map/ppermute | solution.py:69
  6.5 4.0 %collective-permute-start = (f32[288,128]{1,0:T(8,128)S(1)}, f32[288,128]{1,0:T(8,128)S(1)}, u32[]{:S(2)}, u32[]{:S(2)}) collective-permute-start(f32[288,128]{1,0:T(8,128)S(1)} %pad_maximum_fusion.1), channel_id=1, source_target_pairs={{0,1},{1,4},{4,5},{5,8},{8,9},{9,12},{12,13},{2,3},{3,6},{6,7},{7,... | collective-permute-start | bytes 442376 | tf_op jit(solution)/shard_map/ppermute | solution.py:65
  12.1 8.5 %collective-permute-start.3 = (f32[3,32,128]{2,1,0:T(8,128)S(1)}, f32[3,32,128]{2,1,0:T(8,128)S(1)}, u32[]{:S(2)}, u32[]{:S(2)}) collective-permute-start(f32[3,32,128]{2,1,0:T(8,128)S(1)} %pad_maximum_fusion.8), channel_id=1, source_target_pairs={{1,0},{4,1},{5,4},{8,5},{9,8},{12,9},{13,12},{3,2},{6,3},{7,6},{10... | collective-permute-start | bytes 147464 | tf_op jit(solution)/shard_map/ppermute | solution.py:69
  13.4 7.1 %collective-permute-start.2 = (f32[3,32,128]{2,1,0:T(8,128)S(1)}, f32[3,32,128]{2,1,0:T(8,128)S(1)}, u32[]{:S(2)}, u32[]{:S(2)}) collective-permute-start(f32[3,32,128]{2,1,0:T(8,128)S(1)} %pad_maximum_fusion.7), channel_id=1, source_target_pairs={{0,1},{1,4},{4,5},{5,8},{8,9},{9,12},{12,13},{2,3},{3,6},{6,7},{7,... | collective-permute-start | bytes 147464 | tf_op jit(solution)/shard_map/ppermute | solution.py:65
  23.0 7.5 %collective-permute-start.5 = (f32[3,32,128]{2,1,0:T(8,128)S(1)}, f32[3,32,128]{2,1,0:T(8,128)S(1)}, u32[]{:S(2)}, u32[]{:S(2)}) collective-permute-start(f32[3,32,128]{2,1,0:T(8,128)S(1)} %pad_maximum_fusion.10), channel_id=1, source_target_pairs={{1,0},{4,1},{5,4},{8,5},{9,8},{12,9},{13,12},{3,2},{6,3},{7,6},{10... | collective-permute-start | bytes 147464 | tf_op jit(solution)/shard_map/ppermute | solution.py:69
  24.3 6.2 %collective-permute-start.4 = (f32[3,32,128]{2,1,0:T(8,128)S(1)}, f32[3,32,128]{2,1,0:T(8,128)S(1)}, u32[]{:S(2)}, u32[]{:S(2)}) collective-permute-start(f32[3,32,128]{2,1,0:T(8,128)S(1)} %pad_maximum_fusion.9), channel_id=1, source_target_pairs={{0,1},{1,4},{4,5},{5,8},{8,9},{9,12},{12,13},{2,3},{3,6},{6,7},{7,... | collective-permute-start | bytes 147464 | tf_op jit(solution)/shard_map/ppermute | solution.py:65
  30.9 1.0 %copy-start.1 = (bf16[512,4,128]{2,1,0:T(4,128)(2,1)S(1)}, bf16[512,4,128]{2,1,0:T(4,128)(2,1)}, u32[]{:S(2)}) copy-start(bf16[512,4,128]{2,1,0:T(4,128)(2,1)} %param.35) | copy-start | bytes 1572868
  34.8 3.9 %collective-permute-start.6 = (f32[4,16,2,4,128]{4,1,0,3,2:T(8,128)S(1)}, f32[4,16,2,4,128]{4,1,0,3,2:T(8,128)S(1)}, u32[]{:S(2)}, u32[]{:S(2)}) collective-permute-start(f32[4,16,2,4,128]{4,1,0,3,2:T(8,128)S(1)} %select_bitcast_fusion), channel_id=1, source_target_pairs={{0,1},{1,0},{2,3},{3,2},{4,5},{5,4},{6,7},{7,6},{8,9},{9,8},{10,11... | collective-permute-start | bytes 786440 | tf_op jit(solution)/shard_map/ppermute | solution.py:42
  38.8 6.5 %collective-permute-start.7 = (f32[2,16,2,4,128]{4,1,3,2,0:T(8,128)S(1)}, f32[2,16,2,4,128]{4,1,3,2,0:T(8,128)S(1)}, u32[]{:S(2)}, u32[]{:S(2)}) collective-permute-start(f32[2,16,2,4,128]{4,1,3,2,0:T(8,128)S(1)} %fusion.22), channel_id=1, source_target_pairs={{0,4},{4,0},{8,12},{12,8},{1,5},{5,1},{9,13},{13,9},{2,6},{6,2},{1... | collective-permute-start | bytes 393224 | tf_op jit(solution)/shard_map/ppermute | solution.py:42
  45.3 5.4 %collective-permute-start.8 = (f32[1,16,2,4,128]{4,1,3,2,0:T(8,128)S(1)}, f32[1,16,2,4,128]{4,1,3,2,0:T(8,128)S(1)}, u32[]{:S(2)}, u32[]{:S(2)}) collective-permute-start(f32[1,16,2,4,128]{4,1,3,2,0:T(8,128)S(1)} %select_bitcast_fusion.1), channel_id=1, source_target_pairs={{0,8},{4,12},{8,0},{12,4},{1,9},{5,13},{9,1},{13,5},{2,10},{6,14},... | collective-permute-start | bytes 196616 | tf_op jit(solution)/shard_map/ppermute | solution.py:42

commit v7 on v6

--- a/solution.py
+++ b/solution.py
@@ -69,6 +69,20 @@
     return lax.ppermute(value, ("state", "horizon"), shift_pairs(("state", "horizon"), -1))
 
 
+def swap_edges(to_low, to_high):
+    cores = lax.axis_size("horizon")
+    if cores != 2:
+        return to_right(to_high), to_left(to_low)
+    count = lax.axis_size(("state", "horizon"))
+    first = lax.axis_index("horizon") == 0
+    on_chip = lax.ppermute(jnp.where(first, to_high, to_low), "horizon", [(0, 1), (1, 0)])
+    pairs = []
+    for chip in range(count // 2 - 1):
+        pairs += [(2 * chip + 1, 2 * chip + 2), (2 * chip + 2, 2 * chip + 1)]
+    across = lax.ppermute(jnp.where(first, to_low, to_high), ("state", "horizon"), pairs)
+    return jnp.where(first, across, on_chip), jnp.where(first, on_chip, across)
+
+
 def band_step(rows, moves):
     parts = jnp.einsum("cru,cduv->cdrv", rows, moves, precision=lax.Precision.HIGH)
     down, same, up = parts[:, 0], parts[:, 1], parts[:, 2]
@@ -94,8 +108,7 @@
         to_low.append(out_low)
         to_high.append(out_high)
         mine.append(held[1:-1])
-    from_low = to_right(jnp.stack(to_high))
-    from_high = to_left(jnp.stack(to_low))
+    from_low, from_high = swap_edges(jnp.stack(to_low), jnp.stack(to_high))
     levels = []
     carried = None
     for step in range(steps):
@@ -119,9 +132,7 @@
     onehot = (regions[:, None] == jnp.arange(region_total, dtype=jnp.int32)[None, :]).astype(
         jnp.float32
     )
-    block_scale = jnp.dot(
-        onehot, region_scale, precision=lax.Precision.HIGHEST, preferred_element_type=jnp.float32
-    )
+    block_scale = jnp.sum(jnp.where(onehot[:, :, None] > 0, region_scale[None], 0.0), axis=1)
     weighted = (
         expectations.astype(jnp.float32).reshape(output_count, expect_rows, block_count, tile_size)
         * block_scale.T[:, None, :, None]
@@ -146,8 +157,7 @@
     inner, out_low, out_high = band_step(rows, moves)
     edge_low = jnp.concatenate([out_high, moves[-1, 1], moves[-1, 2]], 0)
     edge_high = jnp.concatenate([out_low, moves[0, 0], moves[0, 1]], 0)
-    from_low = to_right(edge_low)
-    from_high = to_left(edge_high)
+    from_low, from_high = swap_edges(edge_high, edge_low)
     levels = [rows, inner.at[0].add(from_low[:row_count]).at[-1].add(from_high[:row_count])]
     left_self = from_low[row_count : row_count + tile_size]
     left_up = from_low[row_count + tile_size :]

time: 51.9 us -> 46.7 us (0.90)
  starting transfers between devices: 26.7 us -> 20.8 us
  other arithmetic: 3.44 us -> 4.98 us
  matrix products: 7.33 us -> 6.45 us
    ppermute x6, starting transfers between devices: 18.5 us -> 15.1 us  [the longest x3 13.1 us: swap_edges(): lax.ppermute(jnp.where(first, to_high, to_low), 'horizon', [(0, 1), (1, 0)])]
    ppermute x3, starting transfers between devices: 8.19 us -> 5.76 us  [halving_scatter(): held = keep + lax.ppermute(send, axis, pairs)]
    dot_general x1 -> x0, matrix products: 0.88 us -> none  [shards(): jnp.dot(onehot, region_scale, precision=lax.Precision.HIGHEST, preferred_...]
    reduce_sum x0 -> x1, other arithmetic: none -> 0.77 us  [shards(): jnp.sum(jnp.where(onehot[:, :, None] > 0, region_scale[None], 0.0), axis=1)]
    gt x0 -> x1, other arithmetic: none -> 0.73 us  [shards(): onehot[:, :, None] > 0]
where the time goes in v7:
time: 46.7 us; the launch traced here: 46.4 us
  starting transfers between devices  20.8 us (45%)
  waiting for transfers between devices  10.1 us (22%)
  matrix products  6.45 us (14%)
  other arithmetic  4.98 us (11%)
  local copies, waits for them, and re-layouts  3.03 us (6%)
  between operations  0.92 us (2%)
    ppermute x3, starting transfers between devices, swap_edges(): lax.ppermute(jnp.where(first, to_high, to_low), 'horizon', [(0, 1), (1, 0)])  13.1 us
    ppermute x3, waiting for transfers between devices, halving_scatter(): held = keep + lax.ppermute(send, axis, pairs)  7.58 us
    ppermute x3, starting transfers between devices, halving_scatter(): held = keep + lax.ppermute(send, axis, pairs)  5.76 us
    dot_general x6, matrix products, ext_step(): jnp.einsum('cru,cduv->cdrv', rows, moves, precision=lax.Precision.HIGH)  2.65 us
    ppermute x3, waiting for transfers between devices, swap_edges(): lax.ppermute(jnp.where(first, to_high, to_low), 'horizon', [(0, 1), (1, 0)])  2.55 us
    ppermute x3, starting transfers between devices, swap_edges(): lax.ppermute(jnp.where(first, to_low, to_high), ('state', 'horizon'), pairs)  2 us
    dot_general x5, matrix products, band_step(): jnp.einsum('cru,cduv->cdrv', rows, moves, precision=lax.Precision.HIGH)  1.65 us
    add x7, other arithmetic, diagonal_sums(): total = total + moved  1.31 us
  transfers between devices with their start and end apart: 9, of which 6 were waited for; matrix products, arithmetic and copies ran while one was open for 0% of the time, Pallas kernels for 0%

profile of v7, /device:TPU:0, one launch (start us, length us, event | category | flops | bytes accessed | tf_op | source)
XLA Modules:
  0.0 46.4 jit_solution(8873882523656007623)
XLA Ops:
  0.0 0.8 %iota_compare_fusion = pred[4,4]{1,0:T(4,128)(4,1)S(1)} fusion(s32[4]{0:T(128)} %param.41), kind=kLoop, calls=%fused_computation.232 | loop fusion | flops 16 | bytes 32 | tf_op jit(solution)/shard_map/lt | solution.py:141
  0.8 0.7 %convert_rsqrt_fusion = f32[4]{0:T(128)S(1)} fusion(s32[4]{0:T(128)} %param.41), kind=kLoop, calls=%fused_computation.235 | loop fusion | flops 4 | bytes 32 | tf_op jit(solution)/shard_map/rsqrt | solution.py:142
  1.4 0.7 %convert_compare_fusion = pred[4,16]{1,0:T(4,128)(4,1)S(1)} fusion(s32[4]{0:T(128)} %param.38), kind=kLoop, calls=%fused_computation.233 | loop fusion | flops 192 | bytes 80 | tf_op jit(solution)/shard_map/gt | solution.py:135
  2.2 0.8 %select_reduce_fusion = f32[4,2]{0,1:T(2,128)S(1)} fusion(f32[16,2]{0,1:T(2,128)} %param.37, pred[4,16]{1,0:T(4,128)(4,1)S(1)} %convert_compare_fusion), kind=kLoop, calls=%fused_computation.229 | loop fusion | flops 248 | bytes 224 | tf_op jit(solution)/shard_map/reduce_sum | solution.py:135
  3.2 0.8 %reshape.591 = f32[32,4,128]{2,1,0:T(4,128)S(1)} reshape(bf16[2,16,512]{2,1,0:T(8,128)(2,1)} %param.36) | data formatting | bytes 98304 | tf_op jit(solution)/shard_map/reshape | solution.py:137
  4.0 1.2 %fusion.12 = f32[4,3,128,128]{3,1,2,0:T(4,128)S(1)} fusion(bf16[4,4,128,128]{3,2,1,0:T(8,128)(2,1)S(1)} %copy-done, s32[4,4]{1,0:T(4,128)} %param.40, s32[3]{0:T(128)S(1)} %iota_add_fusion, pred[4,4]{1,0:T(4,128)(4,1)S(1)} %iota_compare_fusion), kind=kOutput, calls=%fused_computation.27 | convolution fusion | flops 1572960 | bytes 1310812 | tf_op jit(solution)/shard_map/cjd,cjuv->cduv/dot_general | solution.py:145
  5.8 0.7 %collective-permute-start = (f32[288,128]{1,0:T(8,128)S(1)}, f32[288,128]{1,0:T(8,128)S(1)}, u32[]{:S(2)}, u32[]{:S(2)}) collective-permute-start(f32[288,128]{1,0:T(8,128)S(1)} %get-tuple-element.212), channel_id=1, source_target_pairs={{1,4},{4,1},{5,8},{8,5},{9,12},{12,9},{3,6},{6,3},{7,10},{10,7},{1... | collective-permute-start | bytes 442376 | tf_op jit(solution)/shard_map/ppermute | solution.py:82
  6.5 4.4 %collective-permute-start.1 = (f32[288,128]{1,0:T(8,128)S(1)}, f32[288,128]{1,0:T(8,128)S(1)}, u32[]{:S(2)}, u32[]{:S(2)}) collective-permute-start(f32[288,128]{1,0:T(8,128)S(1)} %get-tuple-element.211), channel_id=1, source_target_pairs={{0,1},{1,0},{2,3},{3,2},{4,5},{5,4},{6,7},{7,6},{8,9},{9,8},{10,11... | collective-permute-start | bytes 442376 | tf_op jit(solution)/shard_map/ppermute | solution.py:78
  11.1 0.9 %collective-permute-done.1 = f32[288,128]{1,0:T(8,128)S(1)} collective-permute-done((f32[288,128]{1,0:T(8,128)S(1)}, f32[288,128]{1,0:T(8,128)S(1)}, u32[]{:S(2)}, u32[]{:S(2)}) %collective-permute-start.1) | collective-permute-done | bytes 147488 | tf_op jit(solution)/shard_map/ppermute | solution.py:78
  12.1 0.4 convolution_bitcast_fusion.5
  13.6 0.7 %collective-permute-start.2 = (f32[3,32,128]{2,1,0:T(8,128)S(1)}, f32[3,32,128]{2,1,0:T(8,128)S(1)}, u32[]{:S(2)}, u32[]{:S(2)}) collective-permute-start(f32[3,32,128]{2,1,0:T(8,128)S(1)} %get-tuple-element.236), channel_id=1, source_target_pairs={{1,4},{4,1},{5,8},{8,5},{9,12},{12,9},{3,6},{6,3},{7,10},{10,7},{1... | collective-permute-start | bytes 147464 | tf_op jit(solution)/shard_map/ppermute | solution.py:82
  14.3 4.8 %collective-permute-start.3 = (f32[3,32,128]{2,1,0:T(8,128)S(1)}, f32[3,32,128]{2,1,0:T(8,128)S(1)}, u32[]{:S(2)}, u32[]{:S(2)}) collective-permute-start(f32[3,32,128]{2,1,0:T(8,128)S(1)} %get-tuple-element.235), channel_id=1, source_target_pairs={{0,1},{1,0},{2,3},{3,2},{4,5},{5,4},{6,7},{7,6},{8,9},{9,8},{10,11... | collective-permute-start | bytes 147464 | tf_op jit(solution)/shard_map/ppermute | solution.py:78
  19.1 0.9 %collective-permute-done.3 = f32[3,32,128]{2,1,0:T(8,128)S(1)} collective-permute-done((f32[3,32,128]{2,1,0:T(8,128)S(1)}, f32[3,32,128]{2,1,0:T(8,128)S(1)}, u32[]{:S(2)}, u32[]{:S(2)}) %collective-permute-start.3) | collective-permute-done | bytes 49184 | tf_op jit(solution)/shard_map/ppermute | solution.py:78
  22.4 0.7 %collective-permute-start.4 = (f32[3,32,128]{2,1,0:T(8,128)S(1)}, f32[3,32,128]{2,1,0:T(8,128)S(1)}, u32[]{:S(2)}, u32[]{:S(2)}) collective-permute-start(f32[3,32,128]{2,1,0:T(8,128)S(1)} %get-tuple-element.232), channel_id=1, source_target_pairs={{1,4},{4,1},{5,8},{8,5},{9,12},{12,9},{3,6},{6,3},{7,10},{10,7},{1... | collective-permute-start | bytes 147464 | tf_op jit(solution)/shard_map/ppermute | solution.py:82
  23.0 3.9 %collective-permute-start.5 = (f32[3,32,128]{2,1,0:T(8,128)S(1)}, f32[3,32,128]{2,1,0:T(8,128)S(1)}, u32[]{:S(2)}, u32[]{:S(2)}) collective-permute-start(f32[3,32,128]{2,1,0:T(8,128)S(1)} %get-tuple-element.231), channel_id=1, source_target_pairs={{0,1},{1,0},{2,3},{3,2},{4,5},{5,4},{6,7},{7,6},{8,9},{9,8},{10,11... | collective-permute-start | bytes 147464 | tf_op jit(solution)/shard_map/ppermute | solution.py:78
  27.0 0.8 %collective-permute-done.5 = f32[3,32,128]{2,1,0:T(8,128)S(1)} collective-permute-done((f32[3,32,128]{2,1,0:T(8,128)S(1)}, f32[3,32,128]{2,1,0:T(8,128)S(1)}, u32[]{:S(2)}, u32[]{:S(2)}) %collective-permute-start.5) | collective-permute-done | bytes 49184 | tf_op jit(solution)/shard_map/ppermute | solution.py:78
  28.7 0.6 %copy-done.1 = bf16[512,4,128]{2,1,0:T(4,128)(2,1)S(1)} copy-done((bf16[512,4,128]{2,1,0:T(4,128)(2,1)S(1)}, bf16[512,4,128]{2,1,0:T(4,128)(2,1)}, u32[]{:S(2)}) %copy-start.1) | copy-done | bytes 524312
  32.2 0.9 %collective-permute-start.6 = (f32[4,16,2,4,128]{4,1,0,3,2:T(8,128)S(1)}, f32[4,16,2,4,128]{4,1,0,3,2:T(8,128)S(1)}, u32[]{:S(2)}, u32[]{:S(2)}) collective-permute-start(f32[4,16,2,4,128]{4,1,0,3,2:T(8,128)S(1)} %select_bitcast_fusion), channel_id=1, source_target_pairs={{0,1},{1,0},{2,3},{3,2},{4,5},{5,4},{6,7},{7,6},{8,9},{9,8},{10,11... | collective-permute-start | bytes 786440 | tf_op jit(solution)/shard_map/ppermute | solution.py:42
  33.1 1.2 %collective-permute-done.6 = f32[4,16,2,4,128]{4,1,0,3,2:T(8,128)S(1)} collective-permute-done((f32[4,16,2,4,128]{4,1,0,3,2:T(8,128)S(1)}, f32[4,16,2,4,128]{4,1,0,3,2:T(8,128)S(1)}, u32[]{:S(2)}, u32[]{:S(2)}) %collective-permute-start.6) | collective-permute-done | bytes 262176 | tf_op jit(solution)/shard_map/ppermute | solution.py:42
  34.3 2.1 %collective-permute-start.7 = (f32[2,16,2,4,128]{4,1,3,2,0:T(8,128)S(1)}, f32[2,16,2,4,128]{4,1,3,2,0:T(8,128)S(1)}, u32[]{:S(2)}, u32[]{:S(2)}) collective-permute-start(f32[2,16,2,4,128]{4,1,3,2,0:T(8,128)S(1)} %fusion.22), channel_id=1, source_target_pairs={{0,4},{4,0},{8,12},{12,8},{1,5},{5,1},{9,13},{13,9},{2,6},{6,2},{1... | collective-permute-start | bytes 393224 | tf_op jit(solution)/shard_map/ppermute | solution.py:42
  36.4 3.8 %collective-permute-done.7 = f32[2,16,2,4,128]{4,1,3,2,0:T(8,128)S(1)} collective-permute-done((f32[2,16,2,4,128]{4,1,3,2,0:T(8,128)S(1)}, f32[2,16,2,4,128]{4,1,3,2,0:T(8,128)S(1)}, u32[]{:S(2)}, u32[]{:S(2)}) %collective-permute-start.7) | collective-permute-done | bytes 131104 | tf_op jit(solution)/shard_map/ppermute | solution.py:42
  40.2 2.8 %collective-permute-start.8 = (f32[1,16,2,4,128]{4,1,3,2,0:T(8,128)S(1)}, f32[1,16,2,4,128]{4,1,3,2,0:T(8,128)S(1)}, u32[]{:S(2)}, u32[]{:S(2)}) collective-permute-start(f32[1,16,2,4,128]{4,1,3,2,0:T(8,128)S(1)} %select_bitcast_fusion.1), channel_id=1, source_target_pairs={{0,8},{4,12},{8,0},{12,4},{1,9},{5,13},{9,1},{13,5},{2,10},{6,14},... | collective-permute-start | bytes 196616 | tf_op jit(solution)/shard_map/ppermute | solution.py:42
  43.1 2.6 %collective-permute-done.8 = f32[1,16,2,4,128]{4,1,3,2,0:T(8,128)S(1)} collective-permute-done((f32[1,16,2,4,128]{4,1,3,2,0:T(8,128)S(1)}, f32[1,16,2,4,128]{4,1,3,2,0:T(8,128)S(1)}, u32[]{:S(2)}, u32[]{:S(2)}) %collective-permute-start.8) | collective-permute-done | bytes 65568 | tf_op jit(solution)/shard_map/ppermute | solution.py:42
  45.7 0.7 %copy.264 = f32[16,2,4,128]{3,2,1,0:T(4,128)} copy(f32[16,2,4,128]{3,0,2,1:T(8,128)S(1)} %fusion.62) | data formatting | bytes 131072 | tf_op jit(solution)/shard_map/reshape | solution.py:44
  (127 shorter events, 7.8 us)
Async XLA Ops:
  0.0 4.0 %copy-start = (bf16[4,4,128,128]{3,2,1,0:T(8,128)(2,1)S(1)}, bf16[4,4,128,128]{3,2,1,0:T(8,128)(2,1)}, u32[]{:S(2)}) copy-start(bf16[4,4,128,128]{3,2,1,0:T(8,128)(2,1)} %param.39) | copy-start | bytes 1572868
  5.4 5.6 %copy-start.2 = (bf16[2,16,512]{2,1,0:T(8,128)(2,1)S(1)}, bf16[2,16,512]{2,1,0:T(8,128)(2,1)}, u32[]{:S(2)}) copy-start(bf16[2,16,512]{2,1,0:T(8,128)(2,1)} %param.36) | copy-start | bytes 98308
  5.8 5.3 %collective-permute-start = (f32[288,128]{1,0:T(8,128)S(1)}, f32[288,128]{1,0:T(8,128)S(1)}, u32[]{:S(2)}, u32[]{:S(2)}) collective-permute-start(f32[288,128]{1,0:T(8,128)S(1)} %get-tuple-element.212), channel_id=1, source_target_pairs={{1,4},{4,1},{5,8},{8,5},{9,12},{12,9},{3,6},{6,3},{7,10},{10,7},{1... | collective-permute-start | bytes 442376 | tf_op jit(solution)/shard_map/ppermute | solution.py:82
  6.5 5.4 %collective-permute-start.1 = (f32[288,128]{1,0:T(8,128)S(1)}, f32[288,128]{1,0:T(8,128)S(1)}, u32[]{:S(2)}, u32[]{:S(2)}) collective-permute-start(f32[288,128]{1,0:T(8,128)S(1)} %get-tuple-element.211), channel_id=1, source_target_pairs={{0,1},{1,0},{2,3},{3,2},{4,5},{5,4},{6,7},{7,6},{8,9},{9,8},{10,11... | collective-permute-start | bytes 442376 | tf_op jit(solution)/shard_map/ppermute | solution.py:78
  13.6 5.5 %collective-permute-start.2 = (f32[3,32,128]{2,1,0:T(8,128)S(1)}, f32[3,32,128]{2,1,0:T(8,128)S(1)}, u32[]{:S(2)}, u32[]{:S(2)}) collective-permute-start(f32[3,32,128]{2,1,0:T(8,128)S(1)} %get-tuple-element.236), channel_id=1, source_target_pairs={{1,4},{4,1},{5,8},{8,5},{9,12},{12,9},{3,6},{6,3},{7,10},{10,7},{1... | collective-permute-start | bytes 147464 | tf_op jit(solution)/shard_map/ppermute | solution.py:82
  14.3 5.7 %collective-permute-start.3 = (f32[3,32,128]{2,1,0:T(8,128)S(1)}, f32[3,32,128]{2,1,0:T(8,128)S(1)}, u32[]{:S(2)}, u32[]{:S(2)}) collective-permute-start(f32[3,32,128]{2,1,0:T(8,128)S(1)} %get-tuple-element.235), channel_id=1, source_target_pairs={{0,1},{1,0},{2,3},{3,2},{4,5},{5,4},{6,7},{7,6},{8,9},{9,8},{10,11... | collective-permute-start | bytes 147464 | tf_op jit(solution)/shard_map/ppermute | solution.py:78
  22.4 4.6 %collective-permute-start.4 = (f32[3,32,128]{2,1,0:T(8,128)S(1)}, f32[3,32,128]{2,1,0:T(8,128)S(1)}, u32[]{:S(2)}, u32[]{:S(2)}) collective-permute-start(f32[3,32,128]{2,1,0:T(8,128)S(1)} %get-tuple-element.232), channel_id=1, source_target_pairs={{1,4},{4,1},{5,8},{8,5},{9,12},{12,9},{3,6},{6,3},{7,10},{10,7},{1... | collective-permute-start | bytes 147464 | tf_op jit(solution)/shard_map/ppermute | solution.py:82
  23.0 4.7 %collective-permute-start.5 = (f32[3,32,128]{2,1,0:T(8,128)S(1)}, f32[3,32,128]{2,1,0:T(8,128)S(1)}, u32[]{:S(2)}, u32[]{:S(2)}) collective-permute-start(f32[3,32,128]{2,1,0:T(8,128)S(1)} %get-tuple-element.231), channel_id=1, source_target_pairs={{0,1},{1,0},{2,3},{3,2},{4,5},{5,4},{6,7},{7,6},{8,9},{9,8},{10,11... | collective-permute-start | bytes 147464 | tf_op jit(solution)/shard_map/ppermute | solution.py:78
  28.2 1.0 %copy-start.1 = (bf16[512,4,128]{2,1,0:T(4,128)(2,1)S(1)}, bf16[512,4,128]{2,1,0:T(4,128)(2,1)}, u32[]{:S(2)}) copy-start(bf16[512,4,128]{2,1,0:T(4,128)(2,1)} %param.35) | copy-start | bytes 1572868
  32.2 2.0 %collective-permute-start.6 = (f32[4,16,2,4,128]{4,1,0,3,2:T(8,128)S(1)}, f32[4,16,2,4,128]{4,1,0,3,2:T(8,128)S(1)}, u32[]{:S(2)}, u32[]{:S(2)}) collective-permute-start(f32[4,16,2,4,128]{4,1,0,3,2:T(8,128)S(1)} %select_bitcast_fusion), channel_id=1, source_target_pairs={{0,1},{1,0},{2,3},{3,2},{4,5},{5,4},{6,7},{7,6},{8,9},{9,8},{10,11... | collective-permute-start | bytes 786440 | tf_op jit(solution)/shard_map/ppermute | solution.py:42
  34.3 5.9 %collective-permute-start.7 = (f32[2,16,2,4,128]{4,1,3,2,0:T(8,128)S(1)}, f32[2,16,2,4,128]{4,1,3,2,0:T(8,128)S(1)}, u32[]{:S(2)}, u32[]{:S(2)}) collective-permute-start(f32[2,16,2,4,128]{4,1,3,2,0:T(8,128)S(1)} %fusion.22), channel_id=1, source_target_pairs={{0,4},{4,0},{8,12},{12,8},{1,5},{5,1},{9,13},{13,9},{2,6},{6,2},{1... | collective-permute-start | bytes 393224 | tf_op jit(solution)/shard_map/ppermute | solution.py:42
  40.2 5.4 %collective-permute-start.8 = (f32[1,16,2,4,128]{4,1,3,2,0:T(8,128)S(1)}, f32[1,16,2,4,128]{4,1,3,2,0:T(8,128)S(1)}, u32[]{:S(2)}, u32[]{:S(2)}) collective-permute-start(f32[1,16,2,4,128]{4,1,3,2,0:T(8,128)S(1)} %select_bitcast_fusion.1), channel_id=1, source_target_pairs={{0,8},{4,12},{8,0},{12,4},{1,9},{5,13},{9,1},{13,5},{2,10},{6,14},... | collective-permute-start | bytes 196616 | tf_op jit(solution)/shard_map/ppermute | solution.py:42

commit v8 on v7

--- a/solution.py
+++ b/solution.py
@@ -2,6 +2,8 @@
 import jax.numpy as jnp
 from jax import lax
 from jax.sharding import PartitionSpec as P
+from jax.experimental import pallas as pl
+from jax.experimental.pallas import tpu as pltpu
 
 
 def diagonal_sums(news):
@@ -44,6 +46,44 @@
     return held.reshape(held.shape[1:])
 
 
+def prepare_kernel(counts, offsets, regions, scales, tiles, expect, moves, rows):
+    block_count, band_count, tile_size, _ = tiles.shape
+    output_count, expect_rows, _ = expect.shape
+    for block in range(block_count):
+        count = counts[block]
+        scale = lax.rsqrt(jnp.full((1, tile_size), count.astype(jnp.float32), jnp.float32))
+        for shift in range(3):
+            total = jnp.zeros((tile_size, tile_size), jnp.float32)
+            for slot in range(band_count):
+                use = jnp.logical_and(slot < count, offsets[block, slot] == shift - 1)
+                weight = jnp.where(use, 1.0, 0.0).astype(jnp.float32)
+                total = total + weight * tiles[block, slot].astype(jnp.float32)
+            moves[block, shift] = total * scale
+        region = regions[block]
+        for out in range(output_count):
+            part = expect[out, :, block * tile_size : (block + 1) * tile_size]
+            weighted = part.astype(jnp.float32) * scales[region, out]
+            rows[block, out * expect_rows : (out + 1) * expect_rows, :] = weighted.astype(
+                jnp.bfloat16
+            ).astype(jnp.float32)
+
+
+def prepare(counts, offsets, regions, region_scale, tiles, expectations):
+    block_count, band_count, tile_size, _ = tiles.shape
+    output_count, expect_rows, _ = expectations.shape
+    smem = pl.BlockSpec(memory_space=pltpu.SMEM)
+    vmem = pl.BlockSpec(memory_space=pltpu.VMEM)
+    return pl.pallas_call(
+        prepare_kernel,
+        out_shape=(
+            jax.ShapeDtypeStruct((block_count, 3, tile_size, tile_size), jnp.float32),
+            jax.ShapeDtypeStruct((block_count, output_count * expect_rows, tile_size), jnp.float32),
+        ),
+        in_specs=[smem, smem, smem, smem, vmem, vmem],
+        out_specs=(vmem, vmem),
+    )(counts, offsets, regions, region_scale, tiles, expectations)
+
+
 def split_product(rows_full, data_half):
     upper = rows_full.astype(jnp.bfloat16)
     remain = rows_full - upper.astype(jnp.float32)
@@ -129,31 +169,8 @@
     width = input_count * horizon
     sections = horizon // expect_rows
     row_count = output_count * expect_rows
-    onehot = (regions[:, None] == jnp.arange(region_total, dtype=jnp.int32)[None, :]).astype(
-        jnp.float32
-    )
-    block_scale = jnp.sum(jnp.where(onehot[:, :, None] > 0, region_scale[None], 0.0), axis=1)
-    weighted = (
-        expectations.astype(jnp.float32).reshape(output_count, expect_rows, block_count, tile_size)
-        * block_scale.T[:, None, :, None]
-    )
-    weighted_half = weighted.astype(jnp.bfloat16).reshape(row_count, state_count)
-    in_use = jnp.arange(band_count, dtype=jnp.int32)[None, :] < counts[:, None]
-    scaling = lax.rsqrt(counts.astype(jnp.float32))
-    shifts = jnp.arange(-1, 2, dtype=jnp.int32)
-    chosen = in_use[:, :, None] & (offsets[:, :, None] == shifts[None, None, :])
-    moves = jnp.einsum(
-        "cjd,cjuv->cduv",
-        chosen.astype(jnp.bfloat16),
-        tiles,
-        preferred_element_type=jnp.float32,
-    ) * scaling[:, None, None, None]
+    moves, rows = prepare(counts, offsets, regions, region_scale, tiles, expectations)
     flat_start = impulses.reshape(state_count, width)
-    rows = (
-        weighted_half.astype(jnp.float32)
-        .reshape(row_count, block_count, tile_size)
-        .transpose(1, 0, 2)
-    )
     inner, out_low, out_high = band_step(rows, moves)
     edge_low = jnp.concatenate([out_high, moves[-1, 1], moves[-1, 2]], 0)
     edge_high = jnp.concatenate([out_low, moves[0, 0], moves[0, 1]], 0)

time: 46.7 us -> 49.7 us (1.064)
  other arithmetic: 4.98 us -> 1.88 us
  starting transfers between devices: 20.8 us -> 23.6 us
  local copies, waits for them, and re-layouts: 3.03 us -> 5.56 us
  Pallas kernels: 0 us -> 2.26 us
  waiting for transfers between devices: 10.1 us -> 8.7 us
    ppermute x3, starting transfers between devices: 5.76 us -> 9.6 us  [halving_scatter(): held = keep + lax.ppermute(send, axis, pairs)]
    unnamed x15 -> x17, local copies, waits for them, and re-layouts: 0.64 us -> 3.35 us
    pallas_call x0 -> x1, Pallas kernels: none -> 2.26 us  [prepare(): pl.pallas_call(prepare_kernel, out_shape=(jax.ShapeDtypeStruct((block_cou...]
    ppermute x3, waiting for transfers between devices: 2.55 us -> 0.64 us  [swap_edges(): lax.ppermute(jnp.where(first, to_high, to_low), 'horizon', [(0, 1), (1, 0)])]
    dot_general x1 -> x0, matrix products: 1.23 us -> none  [shards(): jnp.einsum('cjd,cjuv->cduv', chosen.astype(jnp.bfloat16), tiles, preferre...]
    dot_general x5, matrix products: 1.65 us -> 2.85 us  [band_step(): jnp.einsum('cru,cduv->cdrv', rows, moves, precision=lax.Precision.HIGH)]
    ppermute x3, starting transfers between devices: 13.1 us -> 12.1 us  [swap_edges(): lax.ppermute(jnp.where(first, to_high, to_low), 'horizon', [(0, 1), (1, 0)])]
    squeeze x1, local copies, waits for them, and re-layouts: 0.02 us -> 0.95 us  [shards(): edge_high = jnp.concatenate([out_low, moves[0, 0], moves[0, 1]], 0)]
where the time goes in v8:
time: 49.7 us; the launch traced here: 49.4 us
  starting transfers between devices  23.6 us (47%)
  waiting for transfers between devices  8.7 us (18%)
  matrix products  6.41 us (13%)
  local copies, waits for them, and re-layouts  5.56 us (11%)
  Pallas kernels  2.26 us (5%)
  other arithmetic  1.88 us (4%)
  between operations  0.92 us (2%)
    ppermute x3, starting transfers between devices, swap_edges(): lax.ppermute(jnp.where(first, to_high, to_low), 'horizon', [(0, 1), (1, 0)])  12.1 us
    ppermute x3, starting transfers between devices, halving_scatter(): held = keep + lax.ppermute(send, axis, pairs)  9.6 us
    ppermute x3, waiting for transfers between devices, halving_scatter(): held = keep + lax.ppermute(send, axis, pairs)  8.06 us
    unnamed x17, local copies, waits for them, and re-layouts  3.35 us
    dot_general x5, matrix products, band_step(): jnp.einsum('cru,cduv->cdrv', rows, moves, precision=lax.Precision.HIGH)  2.85 us
    dot_general x6, matrix products, ext_step(): jnp.einsum('cru,cduv->cdrv', rows, moves, precision=lax.Precision.HIGH)  2.65 us
    pallas_call x1, Pallas kernels, prepare(): pl.pallas_call(prepare_kernel, out_shape=(jax.ShapeDtypeStruct((block_cou...  2.26 us
    ppermute x3, starting transfers between devices, swap_edges(): lax.ppermute(jnp.where(first, to_low, to_high), ('state', 'horizon'), pairs)  1.96 us
  transfers between devices with their start and end apart: 9, of which 6 were waited for; matrix products, arithmetic and copies ran while one was open for 0% of the time, Pallas kernels for 0%

profile of v8, /device:TPU:0, one launch (start us, length us, event | category | flops | bytes accessed | tf_op | source)
XLA Modules:
  0.0 49.4 jit_solution(10412914197716383122)
XLA Ops:
  0.0 1.3 %copy.57.scales = f32[16,2]{1,0:T(8,128)} copy(f32[16,2]{0,1:T(2,128)} %param.37) | data formatting | bytes 256 | tf_op args[2]
  1.3 2.3 %shard_map.73 = (f32[4,3,128,128]{3,2,1,0:T(8,128)}, f32[4,32,128]{2,1,0:T(8,128)}) custom-call(s32[4]{0:T(128)} %counts.1, s32[4,4]{1,0:T(4,128)} %offsets.1, s32[4]{0:T(128)} %regions.1, f32[16,2]{1,0:T(8,128)} %copy.57.scales, bf16[4,4,128,128]{3,2,1,0:T(8,128)(2,1)} %tiles.1, bf16[2,16,512]{2,1,0:T(8,128)(2,1)} %expect.1), custom_call_target="tpu_custom_call" | custom-call | tf_op jit(solution)/shard_map/pallas_call | solution.py:76
  3.6 1.0 %slice_bitcast_fusion.30 = (f32[128,128]{1,0:T(8,128)S(1)}, f32[128,128]{1,0:T(8,128)S(1)}, f32[128,128]{1,0:T(8,128)S(1)}, f32[128,128]{1,0:T(8,128)S(1)}) fusion(f32[4,3,128,128]{3,2,1,0:T(8,128)} %get-tuple-element.176), kind=kLoop, calls=%fused_computation.156 | loop fusion | bytes 524288 | tf_op jit(solution)/shard_map/squeeze | solution.py:176
  4.6 1.5 %convolution_bitcast_fusion.10 = f32[4,3,32,128]{3,2,1,0:T(8,128)S(1)} fusion(f32[4,3,128,128]{3,2,1,0:T(8,128)} %get-tuple-element.176, f32[4,32,128]{2,1,0:T(8,128)} %get-tuple-element.175), kind=kOutput, calls=%fused_computation.13 | convolution fusion | flops 37748736 | bytes 1048576 | tf_op jit(solution)/shard_map/cru,cduv->cdrv/dot_general | solution.py:127
  6.1 0.5 %collective-permute-start.1 = (f32[288,128]{1,0:T(8,128)S(1)}, f32[288,128]{1,0:T(8,128)S(1)}, u32[]{:S(2)}, u32[]{:S(2)}) collective-permute-start(f32[288,128]{1,0:T(8,128)S(1)} %get-tuple-element.215), channel_id=1, source_target_pairs={{0,1},{1,0},{2,3},{3,2},{4,5},{5,4},{6,7},{7,6},{8,9},{9,8},{10,11... | collective-permute-start | bytes 442376 | tf_op jit(solution)/shard_map/ppermute | solution.py:118
  6.7 0.7 %collective-permute-start = (f32[288,128]{1,0:T(8,128)S(1)}, f32[288,128]{1,0:T(8,128)S(1)}, u32[]{:S(2)}, u32[]{:S(2)}) collective-permute-start(f32[288,128]{1,0:T(8,128)S(1)} %get-tuple-element.216), channel_id=1, source_target_pairs={{1,4},{4,1},{5,8},{8,5},{9,12},{12,9},{3,6},{6,3},{7,10},{10,7},{1... | collective-permute-start | bytes 442376 | tf_op jit(solution)/shard_map/ppermute | solution.py:122
  7.8 1.0 %copy-done = f32[4,3,128,128]{3,2,1,0:T(8,128)S(1)} copy-done((f32[4,3,128,128]{3,2,1,0:T(8,128)S(1)}, f32[4,3,128,128]{3,2,1,0:T(8,128)}, u32[]{:S(2)}) %copy-start) | copy-done | bytes 786456
  9.3 0.4 convolution_bitcast_fusion.4
  9.9 0.4 convolution_bitcast_fusion.3
  10.4 6.5 %collective-permute-start.3 = (f32[3,32,128]{2,1,0:T(8,128)S(1)}, f32[3,32,128]{2,1,0:T(8,128)S(1)}, u32[]{:S(2)}, u32[]{:S(2)}) collective-permute-start(f32[3,32,128]{2,1,0:T(8,128)S(1)} %get-tuple-element.239), channel_id=1, source_target_pairs={{0,1},{1,0},{2,3},{3,2},{4,5},{5,4},{6,7},{7,6},{8,9},{9,8},{10,11... | collective-permute-start | bytes 147464 | tf_op jit(solution)/shard_map/ppermute | solution.py:118
  16.9 0.7 %collective-permute-start.2 = (f32[3,32,128]{2,1,0:T(8,128)S(1)}, f32[3,32,128]{2,1,0:T(8,128)S(1)}, u32[]{:S(2)}, u32[]{:S(2)}) collective-permute-start(f32[3,32,128]{2,1,0:T(8,128)S(1)} %get-tuple-element.240), channel_id=1, source_target_pairs={{1,4},{4,1},{5,8},{8,5},{9,12},{12,9},{3,6},{6,3},{7,10},{10,7},{1... | collective-permute-start | bytes 147464 | tf_op jit(solution)/shard_map/ppermute | solution.py:122
  18.6 0.4 convolution_bitcast_fusion.2
  19.1 0.4 convolution_bitcast_fusion.1
  19.7 0.4 convolution_bitcast_fusion
  20.2 5.1 %collective-permute-start.5 = (f32[3,32,128]{2,1,0:T(8,128)S(1)}, f32[3,32,128]{2,1,0:T(8,128)S(1)}, u32[]{:S(2)}, u32[]{:S(2)}) collective-permute-start(f32[3,32,128]{2,1,0:T(8,128)S(1)} %get-tuple-element.235), channel_id=1, source_target_pairs={{0,1},{1,0},{2,3},{3,2},{4,5},{5,4},{6,7},{7,6},{8,9},{9,8},{10,11... | collective-permute-start | bytes 147464 | tf_op jit(solution)/shard_map/ppermute | solution.py:118
  25.2 0.7 %collective-permute-start.4 = (f32[3,32,128]{2,1,0:T(8,128)S(1)}, f32[3,32,128]{2,1,0:T(8,128)S(1)}, u32[]{:S(2)}, u32[]{:S(2)}) collective-permute-start(f32[3,32,128]{2,1,0:T(8,128)S(1)} %get-tuple-element.236), channel_id=1, source_target_pairs={{1,4},{4,1},{5,8},{8,5},{9,12},{12,9},{3,6},{6,3},{7,10},{10,7},{1... | collective-permute-start | bytes 147464 | tf_op jit(solution)/shard_map/ppermute | solution.py:122
  27.1 0.9 %copy-done.1 = bf16[512,4,128]{2,1,0:T(4,128)(2,1)S(1)} copy-done((bf16[512,4,128]{2,1,0:T(4,128)(2,1)S(1)}, bf16[512,4,128]{2,1,0:T(4,128)(2,1)}, u32[]{:S(2)}) %copy-start.1) | copy-done | bytes 524312
  30.9 4.7 %collective-permute-start.6 = (f32[4,16,2,4,128]{4,1,0,3,2:T(8,128)S(1)}, f32[4,16,2,4,128]{4,1,0,3,2:T(8,128)S(1)}, u32[]{:S(2)}, u32[]{:S(2)}) collective-permute-start(f32[4,16,2,4,128]{4,1,0,3,2:T(8,128)S(1)} %select_bitcast_fusion), channel_id=1, source_target_pairs={{0,1},{1,0},{2,3},{3,2},{4,5},{5,4},{6,7},{7,6},{8,9},{9,8},{10,11... | collective-permute-start | bytes 786440 | tf_op jit(solution)/shard_map/ppermute | solution.py:44
  35.6 1.2 %collective-permute-done.6 = f32[4,16,2,4,128]{4,1,0,3,2:T(8,128)S(1)} collective-permute-done((f32[4,16,2,4,128]{4,1,0,3,2:T(8,128)S(1)}, f32[4,16,2,4,128]{4,1,0,3,2:T(8,128)S(1)}, u32[]{:S(2)}, u32[]{:S(2)}) %collective-permute-start.6) | collective-permute-done | bytes 262176 | tf_op jit(solution)/shard_map/ppermute | solution.py:44
  36.8 2.1 %collective-permute-start.7 = (f32[2,16,2,4,128]{4,1,3,2,0:T(8,128)S(1)}, f32[2,16,2,4,128]{4,1,3,2,0:T(8,128)S(1)}, u32[]{:S(2)}, u32[]{:S(2)}) collective-permute-start(f32[2,16,2,4,128]{4,1,3,2,0:T(8,128)S(1)} %fusion.20), channel_id=1, source_target_pairs={{0,4},{4,0},{8,12},{12,8},{1,5},{5,1},{9,13},{13,9},{2,6},{6,2},{1... | collective-permute-start | bytes 393224 | tf_op jit(solution)/shard_map/ppermute | solution.py:44
  38.9 4.0 %collective-permute-done.7 = f32[2,16,2,4,128]{4,1,3,2,0:T(8,128)S(1)} collective-permute-done((f32[2,16,2,4,128]{4,1,3,2,0:T(8,128)S(1)}, f32[2,16,2,4,128]{4,1,3,2,0:T(8,128)S(1)}, u32[]{:S(2)}, u32[]{:S(2)}) %collective-permute-start.7) | collective-permute-done | bytes 131104 | tf_op jit(solution)/shard_map/ppermute | solution.py:44
  43.0 2.8 %collective-permute-start.8 = (f32[1,16,2,4,128]{4,1,3,2,0:T(8,128)S(1)}, f32[1,16,2,4,128]{4,1,3,2,0:T(8,128)S(1)}, u32[]{:S(2)}, u32[]{:S(2)}) collective-permute-start(f32[1,16,2,4,128]{4,1,3,2,0:T(8,128)S(1)} %select_bitcast_fusion.1), channel_id=1, source_target_pairs={{0,8},{4,12},{8,0},{12,4},{1,9},{5,13},{9,1},{13,5},{2,10},{6,14},... | collective-permute-start | bytes 196616 | tf_op jit(solution)/shard_map/ppermute | solution.py:44
  45.8 2.9 %collective-permute-done.8 = f32[1,16,2,4,128]{4,1,3,2,0:T(8,128)S(1)} collective-permute-done((f32[1,16,2,4,128]{4,1,3,2,0:T(8,128)S(1)}, f32[1,16,2,4,128]{4,1,3,2,0:T(8,128)S(1)}, u32[]{:S(2)}, u32[]{:S(2)}) %collective-permute-start.8) | collective-permute-done | bytes 65568 | tf_op jit(solution)/shard_map/ppermute | solution.py:44
  48.7 0.7 %copy.98 = f32[16,2,4,128]{3,2,1,0:T(4,128)} copy(f32[16,2,4,128]{3,0,2,1:T(8,128)S(1)} %fusion.60) | data formatting | bytes 131072 | tf_op jit(solution)/shard_map/reshape | solution.py:46
  (117 shorter events, 5.9 us)
Async XLA Ops:
  4.6 2.8 %copy-start.2 = (f32[4,32,128]{2,1,0:T(8,128)S(1)}, f32[4,32,128]{2,1,0:T(8,128)}, u32[]{:S(2)}) copy-start(f32[4,32,128]{2,1,0:T(8,128)} %get-tuple-element.175) | copy-start | bytes 196612
  6.1 1.5 %collective-permute-start.1 = (f32[288,128]{1,0:T(8,128)S(1)}, f32[288,128]{1,0:T(8,128)S(1)}, u32[]{:S(2)}, u32[]{:S(2)}) collective-permute-start(f32[288,128]{1,0:T(8,128)S(1)} %get-tuple-element.215), channel_id=1, source_target_pairs={{0,1},{1,0},{2,3},{3,2},{4,5},{5,4},{6,7},{7,6},{8,9},{9,8},{10,11... | collective-permute-start | bytes 442376 | tf_op jit(solution)/shard_map/ppermute | solution.py:118
  6.7 1.0 %collective-permute-start = (f32[288,128]{1,0:T(8,128)S(1)}, f32[288,128]{1,0:T(8,128)S(1)}, u32[]{:S(2)}, u32[]{:S(2)}) collective-permute-start(f32[288,128]{1,0:T(8,128)S(1)} %get-tuple-element.216), channel_id=1, source_target_pairs={{1,4},{4,1},{5,8},{8,5},{9,12},{12,9},{3,6},{6,3},{7,10},{10,7},{1... | collective-permute-start | bytes 442376 | tf_op jit(solution)/shard_map/ppermute | solution.py:122
  7.7 1.1 %copy-start = (f32[4,3,128,128]{3,2,1,0:T(8,128)S(1)}, f32[4,3,128,128]{3,2,1,0:T(8,128)}, u32[]{:S(2)}) copy-start(f32[4,3,128,128]{3,2,1,0:T(8,128)} %get-tuple-element.176) | copy-start | bytes 2359300
  10.4 7.4 %collective-permute-start.3 = (f32[3,32,128]{2,1,0:T(8,128)S(1)}, f32[3,32,128]{2,1,0:T(8,128)S(1)}, u32[]{:S(2)}, u32[]{:S(2)}) collective-permute-start(f32[3,32,128]{2,1,0:T(8,128)S(1)} %get-tuple-element.239), channel_id=1, source_target_pairs={{0,1},{1,0},{2,3},{3,2},{4,5},{5,4},{6,7},{7,6},{8,9},{9,8},{10,11... | collective-permute-start | bytes 147464 | tf_op jit(solution)/shard_map/ppermute | solution.py:118
  16.9 0.9 %collective-permute-start.2 = (f32[3,32,128]{2,1,0:T(8,128)S(1)}, f32[3,32,128]{2,1,0:T(8,128)S(1)}, u32[]{:S(2)}, u32[]{:S(2)}) collective-permute-start(f32[3,32,128]{2,1,0:T(8,128)S(1)} %get-tuple-element.240), channel_id=1, source_target_pairs={{1,4},{4,1},{5,8},{8,5},{9,12},{12,9},{3,6},{6,3},{7,10},{10,7},{1... | collective-permute-start | bytes 147464 | tf_op jit(solution)/shard_map/ppermute | solution.py:122
  20.2 5.9 %collective-permute-start.5 = (f32[3,32,128]{2,1,0:T(8,128)S(1)}, f32[3,32,128]{2,1,0:T(8,128)S(1)}, u32[]{:S(2)}, u32[]{:S(2)}) collective-permute-start(f32[3,32,128]{2,1,0:T(8,128)S(1)} %get-tuple-element.235), channel_id=1, source_target_pairs={{0,1},{1,0},{2,3},{3,2},{4,5},{5,4},{6,7},{7,6},{8,9},{9,8},{10,11... | collective-permute-start | bytes 147464 | tf_op jit(solution)/shard_map/ppermute | solution.py:118
  25.2 0.9 %collective-permute-start.4 = (f32[3,32,128]{2,1,0:T(8,128)S(1)}, f32[3,32,128]{2,1,0:T(8,128)S(1)}, u32[]{:S(2)}, u32[]{:S(2)}) collective-permute-start(f32[3,32,128]{2,1,0:T(8,128)S(1)} %get-tuple-element.236), channel_id=1, source_target_pairs={{1,4},{4,1},{5,8},{8,5},{9,12},{12,9},{3,6},{6,3},{7,10},{10,7},{1... | collective-permute-start | bytes 147464 | tf_op jit(solution)/shard_map/ppermute | solution.py:122
  26.9 1.0 %copy-start.1 = (bf16[512,4,128]{2,1,0:T(4,128)(2,1)S(1)}, bf16[512,4,128]{2,1,0:T(4,128)(2,1)}, u32[]{:S(2)}) copy-start(bf16[512,4,128]{2,1,0:T(4,128)(2,1)} %param.35) | copy-start | bytes 1572868
  30.9 5.9 %collective-permute-start.6 = (f32[4,16,2,4,128]{4,1,0,3,2:T(8,128)S(1)}, f32[4,16,2,4,128]{4,1,0,3,2:T(8,128)S(1)}, u32[]{:S(2)}, u32[]{:S(2)}) collective-permute-start(f32[4,16,2,4,128]{4,1,0,3,2:T(8,128)S(1)} %select_bitcast_fusion), channel_id=1, source_target_pairs={{0,1},{1,0},{2,3},{3,2},{4,5},{5,4},{6,7},{7,6},{8,9},{9,8},{10,11... | collective-permute-start | bytes 786440 | tf_op jit(solution)/shard_map/ppermute | solution.py:44
  36.8 6.1 %collective-permute-start.7 = (f32[2,16,2,4,128]{4,1,3,2,0:T(8,128)S(1)}, f32[2,16,2,4,128]{4,1,3,2,0:T(8,128)S(1)}, u32[]{:S(2)}, u32[]{:S(2)}) collective-permute-start(f32[2,16,2,4,128]{4,1,3,2,0:T(8,128)S(1)} %fusion.20), channel_id=1, source_target_pairs={{0,4},{4,0},{8,12},{12,8},{1,5},{5,1},{9,13},{13,9},{2,6},{6,2},{1... | collective-permute-start | bytes 393224 | tf_op jit(solution)/shard_map/ppermute | solution.py:44
  43.0 5.7 %collective-permute-start.8 = (f32[1,16,2,4,128]{4,1,3,2,0:T(8,128)S(1)}, f32[1,16,2,4,128]{4,1,3,2,0:T(8,128)S(1)}, u32[]{:S(2)}, u32[]{:S(2)}) collective-permute-start(f32[1,16,2,4,128]{4,1,3,2,0:T(8,128)S(1)} %select_bitcast_fusion.1), channel_id=1, source_target_pairs={{0,8},{4,12},{8,0},{12,4},{1,9},{5,13},{9,1},{13,5},{2,10},{6,14},... | collective-permute-start | bytes 196616 | tf_op jit(solution)/shard_map/ppermute | solution.py:44

commit v9 on v8

--- a/solution.py
+++ b/solution.py
@@ -46,23 +46,28 @@
     return held.reshape(held.shape[1:])
 
 
-def prepare_kernel(counts, offsets, regions, scales, tiles, expect, moves, rows):
+def prepare_kernel(counts, offsets, regions, scales, tiles, expect, moves, rows, edges):
     block_count, band_count, tile_size, _ = tiles.shape
     output_count, expect_rows, _ = expect.shape
     for block in range(block_count):
         count = counts[block]
         scale = lax.rsqrt(jnp.full((1, tile_size), count.astype(jnp.float32), jnp.float32))
+        wide = [tiles[block, slot].astype(jnp.float32) for slot in range(band_count)]
         for shift in range(3):
             total = jnp.zeros((tile_size, tile_size), jnp.float32)
             for slot in range(band_count):
                 use = jnp.logical_and(slot < count, offsets[block, slot] == shift - 1)
-                weight = jnp.where(use, 1.0, 0.0).astype(jnp.float32)
-                total = total + weight * tiles[block, slot].astype(jnp.float32)
-            moves[block, shift] = total * scale
+                total = total + jnp.where(use, 1.0, 0.0).astype(jnp.float32) * wide[slot]
+            total = total * scale
+            moves[block, :, shift * tile_size : (shift + 1) * tile_size] = total
+            if block == block_count - 1 and shift > 0:
+                edges[0, (shift - 1) * tile_size : shift * tile_size, :] = total
+            if block == 0 and shift < 2:
+                edges[1, shift * tile_size : (shift + 1) * tile_size, :] = total
         region = regions[block]
         for out in range(output_count):
             part = expect[out, :, block * tile_size : (block + 1) * tile_size]
-            weighted = part.astype(jnp.float32) * scales[region, out]
+            weighted = part.astype(jnp.float32) * scales[out, region]
             rows[block, out * expect_rows : (out + 1) * expect_rows, :] = weighted.astype(
                 jnp.bfloat16
             ).astype(jnp.float32)
@@ -76,12 +81,13 @@
     return pl.pallas_call(
         prepare_kernel,
         out_shape=(
-            jax.ShapeDtypeStruct((block_count, 3, tile_size, tile_size), jnp.float32),
+            jax.ShapeDtypeStruct((block_count, tile_size, 3 * tile_size), jnp.float32),
             jax.ShapeDtypeStruct((block_count, output_count * expect_rows, tile_size), jnp.float32),
+            jax.ShapeDtypeStruct((2, 2 * tile_size, tile_size), jnp.float32),
         ),
         in_specs=[smem, smem, smem, smem, vmem, vmem],
-        out_specs=(vmem, vmem),
-    )(counts, offsets, regions, region_scale, tiles, expectations)
+        out_specs=(vmem, vmem, vmem),
+    )(counts, offsets, regions, region_scale.T, tiles, expectations)
 
 
 def split_product(rows_full, data_half):
@@ -123,20 +129,23 @@
     return jnp.where(first, across, on_chip), jnp.where(first, on_chip, across)
 
 
-def band_step(rows, moves):
-    parts = jnp.einsum("cru,cduv->cdrv", rows, moves, precision=lax.Precision.HIGH)
-    down, same, up = parts[:, 0], parts[:, 1], parts[:, 2]
+def band_parts(rows, moves):
+    parts = jnp.einsum("cru,cun->crn", rows, moves, precision=lax.Precision.HIGH)
+    size = rows.shape[-1]
+    down, same, up = parts[..., :size], parts[..., size : 2 * size], parts[..., 2 * size :]
     zero = jnp.zeros_like(same[:1])
     inner = same + jnp.concatenate([down[1:], zero], 0) + jnp.concatenate([zero, up[:-1]], 0)
+    return inner, down, up
+
+
+def band_step(rows, moves):
+    inner, down, up = band_parts(rows, moves)
     return inner, down[0], up[-1]
 
 
 def ext_step(rows, moves):
-    parts = jnp.einsum("cru,cduv->cdrv", rows, moves, precision=lax.Precision.HIGH)
-    down, same, up = parts[:, 0], parts[:, 1], parts[:, 2]
-    zero = jnp.zeros_like(same[:1])
-    inner = same + jnp.concatenate([down[1:], zero], 0) + jnp.concatenate([zero, up[:-1]], 0)
-    return inner, parts[1, 0], parts[-2, 2]
+    inner, down, up = band_parts(rows, moves)
+    return inner, down[1], up[-2]
 
 
 def exchange_round(rows, moves, wide, steps):
@@ -169,11 +178,11 @@
     width = input_count * horizon
     sections = horizon // expect_rows
     row_count = output_count * expect_rows
-    moves, rows = prepare(counts, offsets, regions, region_scale, tiles, expectations)
+    moves, rows, edges = prepare(counts, offsets, regions, region_scale, tiles, expectations)
     flat_start = impulses.reshape(state_count, width)
     inner, out_low, out_high = band_step(rows, moves)
-    edge_low = jnp.concatenate([out_high, moves[-1, 1], moves[-1, 2]], 0)
-    edge_high = jnp.concatenate([out_low, moves[0, 0], moves[0, 1]], 0)
+    edge_low = jnp.concatenate([out_high, edges[0]], 0)
+    edge_high = jnp.concatenate([out_low, edges[1]], 0)
     from_low, from_high = swap_edges(edge_high, edge_low)
     levels = [rows, inner.at[0].add(from_low[:row_count]).at[-1].add(from_high[:row_count])]
     left_self = from_low[row_count : row_count + tile_size]
@@ -183,9 +192,9 @@
     blank = jnp.zeros_like(left_self)
     wide = jnp.concatenate(
         [
-            jnp.stack([blank, left_self, left_up])[None],
+            jnp.concatenate([blank, left_self, left_up], 1)[None],
             moves,
-            jnp.stack([right_down, right_self, blank])[None],
+            jnp.concatenate([right_down, right_self, blank], 1)[None],
         ],
         0,
     )

time: 49.7 us -> 48.8 us (0.982)
  local copies, waits for them, and re-layouts: 5.56 us -> 4.74 us
    unnamed x17 -> x20, local copies, waits for them, and re-layouts: 3.35 us -> 1.58 us
    slice x11 -> x22, local copies, waits for them, and re-layouts: 0.12 us -> 1.11 us  [the longest x4 0.93 us: band_parts(): parts[..., size:2 * size]]
where the time goes in v9:
time: 48.8 us; the launch traced here: 48.5 us
  starting transfers between devices  23.6 us (48%)
  waiting for transfers between devices  8.7 us (18%)
  matrix products  6.36 us (13%)
  local copies, waits for them, and re-layouts  4.74 us (10%)
  Pallas kernels  2.29 us (5%)
  other arithmetic  1.89 us (4%)
  between operations  0.9 us (2%)
    ppermute x3, starting transfers between devices, swap_edges(): lax.ppermute(jnp.where(first, to_high, to_low), 'horizon', [(0, 1), (1, 0)])  12.1 us
    ppermute x3, starting transfers between devices, halving_scatter(): held = keep + lax.ppermute(send, axis, pairs)  9.61 us
    ppermute x3, waiting for transfers between devices, halving_scatter(): held = keep + lax.ppermute(send, axis, pairs)  8.06 us
    dot_general x11, matrix products, band_parts(): jnp.einsum('cru,cun->crn', rows, moves, precision=lax.Precision.HIGH)  5.45 us
    pallas_call x1, Pallas kernels, prepare(): pl.pallas_call(prepare_kernel, out_shape=(jax.ShapeDtypeStruct((block_cou...  2.29 us
    ppermute x3, starting transfers between devices, swap_edges(): lax.ppermute(jnp.where(first, to_low, to_high), ('state', 'horizon'), pairs)  1.96 us
    unnamed x20, local copies, waits for them, and re-layouts  1.58 us
    add x7, other arithmetic, diagonal_sums(): total = total + moved  1.31 us
  transfers between devices with their start and end apart: 9, of which 6 were waited for; matrix products, arithmetic and copies ran while one was open for 0% of the time, Pallas kernels for 0%

profile of v9, /device:TPU:0, one launch (start us, length us, event | category | flops | bytes accessed | tf_op | source)
XLA Modules:
  0.0 48.5 jit_solution(2021447331900015255)
XLA Ops:
  0.0 2.3 %shard_map.73 = (f32[4,128,384]{2,1,0:T(8,128)}, f32[4,32,128]{2,1,0:T(8,128)}, f32[2,256,128]{2,1,0:T(8,128)}) custom-call(s32[4]{0:T(128)} %counts.1, s32[4,4]{1,0:T(4,128)} %offsets.1, s32[4]{0:T(128)} %regions.1, f32[2,16]{1,0:T(2,128)} %bitcast.173, bf16[4,4,128,128]{3,2,1,0:T(8,128)(2,1)} %tiles.1, bf16[2,16,512]{2,1,0:T(8,128)(2,1)} %expect.1), custom_call_target="tpu_custom_call" | custom-call | tf_op jit(solution)/shard_map/pallas_call | solution.py:81
  2.3 1.0 %slice_bitcast_fusion.1 = (f32[256,128]{1,0:T(8,128)S(1)}, f32[256,128]{1,0:T(8,128)S(1)}) fusion(f32[2,256,128]{2,1,0:T(8,128)} %get-tuple-element.178), kind=kLoop, calls=%fused_computation.39 | loop fusion | bytes 524288 | tf_op jit(solution)/shard_map/squeeze | solution.py:185
  3.3 1.5 %fusion.79 = f32[4,32,384]{2,1,0:T(8,128)S(1)} fusion(f32[4,32,128]{2,1,0:T(8,128)} %get-tuple-element.176, f32[4,128,384]{2,1,0:T(8,128)} %get-tuple-element.177), kind=kOutput, calls=%fused_computation.164 | convolution fusion | flops 37748736 | bytes 1048576 | tf_op jit(solution)/shard_map/cru,cun->crn/dot_general | solution.py:133
  4.9 0.5 %collective-permute-start.1 = (f32[288,128]{1,0:T(8,128)S(1)}, f32[288,128]{1,0:T(8,128)S(1)}, u32[]{:S(2)}, u32[]{:S(2)}) collective-permute-start(f32[288,128]{1,0:T(8,128)S(1)} %get-tuple-element.213), channel_id=1, source_target_pairs={{0,1},{1,0},{2,3},{3,2},{4,5},{5,4},{6,7},{7,6},{8,9},{9,8},{10,11... | collective-permute-start | bytes 442376 | tf_op jit(solution)/shard_map/ppermute | solution.py:124
  5.4 0.7 %collective-permute-start = (f32[288,128]{1,0:T(8,128)S(1)}, f32[288,128]{1,0:T(8,128)S(1)}, u32[]{:S(2)}, u32[]{:S(2)}) collective-permute-start(f32[288,128]{1,0:T(8,128)S(1)} %get-tuple-element.214), channel_id=1, source_target_pairs={{1,4},{4,1},{5,8},{8,5},{9,12},{12,9},{3,6},{6,3},{7,10},{10,7},{1... | collective-permute-start | bytes 442376 | tf_op jit(solution)/shard_map/ppermute | solution.py:128
  6.6 1.0 %copy-done = f32[4,128,384]{2,1,0:T(8,128)S(1)} copy-done((f32[4,128,384]{2,1,0:T(8,128)S(1)}, f32[4,128,384]{2,1,0:T(8,128)}, u32[]{:S(2)}) %copy-start) | copy-done | bytes 786456
  8.1 0.4 fusion.58
  8.6 0.4 fusion.57
  9.1 6.5 %collective-permute-start.3 = (f32[3,32,128]{2,1,0:T(8,128)S(1)}, f32[3,32,128]{2,1,0:T(8,128)S(1)}, u32[]{:S(2)}, u32[]{:S(2)}) collective-permute-start(f32[3,32,128]{2,1,0:T(8,128)S(1)} %get-tuple-element.239), channel_id=1, source_target_pairs={{0,1},{1,0},{2,3},{3,2},{4,5},{5,4},{6,7},{7,6},{8,9},{9,8},{10,11... | collective-permute-start | bytes 147464 | tf_op jit(solution)/shard_map/ppermute | solution.py:124
  15.6 0.7 %collective-permute-start.2 = (f32[3,32,128]{2,1,0:T(8,128)S(1)}, f32[3,32,128]{2,1,0:T(8,128)S(1)}, u32[]{:S(2)}, u32[]{:S(2)}) collective-permute-start(f32[3,32,128]{2,1,0:T(8,128)S(1)} %get-tuple-element.240), channel_id=1, source_target_pairs={{1,4},{4,1},{5,8},{8,5},{9,12},{12,9},{3,6},{6,3},{7,10},{10,7},{1... | collective-permute-start | bytes 147464 | tf_op jit(solution)/shard_map/ppermute | solution.py:128
  17.3 0.5 %slice-done.1 = f32[6,32,128]{2,1,0:T(8,128)S(1)} async-done(((f32[6,32,384]{2,1,0:T(8,128)}), f32[6,32,128]{2,1,0:T(8,128)S(1)}, s32[]{:S(2)}) %slice-start.1) | async-done | bytes 98328 | tf_op jit(solution)/shard_map/slice | solution.py:135
  17.8 0.4 fusion.17
  18.3 0.4 fusion.56
  19.3 5.1 %collective-permute-start.5 = (f32[3,32,128]{2,1,0:T(8,128)S(1)}, f32[3,32,128]{2,1,0:T(8,128)S(1)}, u32[]{:S(2)}, u32[]{:S(2)}) collective-permute-start(f32[3,32,128]{2,1,0:T(8,128)S(1)} %get-tuple-element.235), channel_id=1, source_target_pairs={{0,1},{1,0},{2,3},{3,2},{4,5},{5,4},{6,7},{7,6},{8,9},{9,8},{10,11... | collective-permute-start | bytes 147464 | tf_op jit(solution)/shard_map/ppermute | solution.py:124
  24.4 0.7 %collective-permute-start.4 = (f32[3,32,128]{2,1,0:T(8,128)S(1)}, f32[3,32,128]{2,1,0:T(8,128)S(1)}, u32[]{:S(2)}, u32[]{:S(2)}) collective-permute-start(f32[3,32,128]{2,1,0:T(8,128)S(1)} %get-tuple-element.236), channel_id=1, source_target_pairs={{1,4},{4,1},{5,8},{8,5},{9,12},{12,9},{3,6},{6,3},{7,10},{10,7},{1... | collective-permute-start | bytes 147464 | tf_op jit(solution)/shard_map/ppermute | solution.py:128
  26.2 0.4 slice-done
  26.7 0.5 %copy-done.1 = bf16[512,4,128]{2,1,0:T(4,128)(2,1)S(1)} copy-done((bf16[512,4,128]{2,1,0:T(4,128)(2,1)S(1)}, bf16[512,4,128]{2,1,0:T(4,128)(2,1)}, u32[]{:S(2)}) %copy-start.1) | copy-done | bytes 524312
  30.0 4.7 %collective-permute-start.6 = (f32[4,16,2,4,128]{4,1,0,3,2:T(8,128)S(1)}, f32[4,16,2,4,128]{4,1,0,3,2:T(8,128)S(1)}, u32[]{:S(2)}, u32[]{:S(2)}) collective-permute-start(f32[4,16,2,4,128]{4,1,0,3,2:T(8,128)S(1)} %select_bitcast_fusion), channel_id=1, source_target_pairs={{0,1},{1,0},{2,3},{3,2},{4,5},{5,4},{6,7},{7,6},{8,9},{9,8},{10,11... | collective-permute-start | bytes 786440 | tf_op jit(solution)/shard_map/ppermute | solution.py:44
  34.7 1.2 %collective-permute-done.6 = f32[4,16,2,4,128]{4,1,0,3,2:T(8,128)S(1)} collective-permute-done((f32[4,16,2,4,128]{4,1,0,3,2:T(8,128)S(1)}, f32[4,16,2,4,128]{4,1,0,3,2:T(8,128)S(1)}, u32[]{:S(2)}, u32[]{:S(2)}) %collective-permute-start.6) | collective-permute-done | bytes 262176 | tf_op jit(solution)/shard_map/ppermute | solution.py:44
  36.0 2.1 %collective-permute-start.7 = (f32[2,16,2,4,128]{4,1,3,2,0:T(8,128)S(1)}, f32[2,16,2,4,128]{4,1,3,2,0:T(8,128)S(1)}, u32[]{:S(2)}, u32[]{:S(2)}) collective-permute-start(f32[2,16,2,4,128]{4,1,3,2,0:T(8,128)S(1)} %fusion.12), channel_id=1, source_target_pairs={{0,4},{4,0},{8,12},{12,8},{1,5},{5,1},{9,13},{13,9},{2,6},{6,2},{1... | collective-permute-start | bytes 393224 | tf_op jit(solution)/shard_map/ppermute | solution.py:44
  38.1 4.0 %collective-permute-done.7 = f32[2,16,2,4,128]{4,1,3,2,0:T(8,128)S(1)} collective-permute-done((f32[2,16,2,4,128]{4,1,3,2,0:T(8,128)S(1)}, f32[2,16,2,4,128]{4,1,3,2,0:T(8,128)S(1)}, u32[]{:S(2)}, u32[]{:S(2)}) %collective-permute-start.7) | collective-permute-done | bytes 131104 | tf_op jit(solution)/shard_map/ppermute | solution.py:44
  42.2 2.8 %collective-permute-start.8 = (f32[1,16,2,4,128]{4,1,3,2,0:T(8,128)S(1)}, f32[1,16,2,4,128]{4,1,3,2,0:T(8,128)S(1)}, u32[]{:S(2)}, u32[]{:S(2)}) collective-permute-start(f32[1,16,2,4,128]{4,1,3,2,0:T(8,128)S(1)} %select_bitcast_fusion.1), channel_id=1, source_target_pairs={{0,8},{4,12},{8,0},{12,4},{1,9},{5,13},{9,1},{13,5},{2,10},{6,14},... | collective-permute-start | bytes 196616 | tf_op jit(solution)/shard_map/ppermute | solution.py:44
  45.0 2.9 %collective-permute-done.8 = f32[1,16,2,4,128]{4,1,3,2,0:T(8,128)S(1)} collective-permute-done((f32[1,16,2,4,128]{4,1,3,2,0:T(8,128)S(1)}, f32[1,16,2,4,128]{4,1,3,2,0:T(8,128)S(1)}, u32[]{:S(2)}, u32[]{:S(2)}) %collective-permute-start.8) | collective-permute-done | bytes 65568 | tf_op jit(solution)/shard_map/ppermute | solution.py:44
  47.9 0.7 %copy.50 = f32[16,2,4,128]{3,2,1,0:T(4,128)} copy(f32[16,2,4,128]{3,0,2,1:T(8,128)S(1)} %fusion.36) | data formatting | bytes 131072 | tf_op jit(solution)/shard_map/reshape | solution.py:46
  (122 shorter events, 6.3 us)
Async XLA Ops:
  3.3 2.8 %copy-start.4 = (f32[4,32,128]{2,1,0:T(8,128)S(1)}, f32[4,32,128]{2,1,0:T(8,128)}, u32[]{:S(2)}) copy-start(f32[4,32,128]{2,1,0:T(8,128)} %get-tuple-element.176) | copy-start | bytes 196612
  4.9 1.5 %collective-permute-start.1 = (f32[288,128]{1,0:T(8,128)S(1)}, f32[288,128]{1,0:T(8,128)S(1)}, u32[]{:S(2)}, u32[]{:S(2)}) collective-permute-start(f32[288,128]{1,0:T(8,128)S(1)} %get-tuple-element.213), channel_id=1, source_target_pairs={{0,1},{1,0},{2,3},{3,2},{4,5},{5,4},{6,7},{7,6},{8,9},{9,8},{10,11... | collective-permute-start | bytes 442376 | tf_op jit(solution)/shard_map/ppermute | solution.py:124
  5.4 1.0 %collective-permute-start = (f32[288,128]{1,0:T(8,128)S(1)}, f32[288,128]{1,0:T(8,128)S(1)}, u32[]{:S(2)}, u32[]{:S(2)}) collective-permute-start(f32[288,128]{1,0:T(8,128)S(1)} %get-tuple-element.214), channel_id=1, source_target_pairs={{1,4},{4,1},{5,8},{8,5},{9,12},{12,9},{3,6},{6,3},{7,10},{10,7},{1... | collective-permute-start | bytes 442376 | tf_op jit(solution)/shard_map/ppermute | solution.py:128
  6.4 1.1 %copy-start = (f32[4,128,384]{2,1,0:T(8,128)S(1)}, f32[4,128,384]{2,1,0:T(8,128)}, u32[]{:S(2)}) copy-start(f32[4,128,384]{2,1,0:T(8,128)} %get-tuple-element.177) | copy-start | bytes 2359300
  9.0 7.8 %copy-start.3 = (f32[6,32,384]{2,1,0:T(8,128)}, f32[6,32,384]{2,1,0:T(8,128)S(1)}, u32[]{:S(2)}) copy-start(f32[6,32,384]{2,1,0:T(8,128)S(1)} %fusion.57) | copy-start | bytes 884740
  9.1 7.4 %collective-permute-start.3 = (f32[3,32,128]{2,1,0:T(8,128)S(1)}, f32[3,32,128]{2,1,0:T(8,128)S(1)}, u32[]{:S(2)}, u32[]{:S(2)}) collective-permute-start(f32[3,32,128]{2,1,0:T(8,128)S(1)} %get-tuple-element.239), channel_id=1, source_target_pairs={{0,1},{1,0},{2,3},{3,2},{4,5},{5,4},{6,7},{7,6},{8,9},{9,8},{10,11... | collective-permute-start | bytes 147464 | tf_op jit(solution)/shard_map/ppermute | solution.py:124
  15.6 0.9 %collective-permute-start.2 = (f32[3,32,128]{2,1,0:T(8,128)S(1)}, f32[3,32,128]{2,1,0:T(8,128)S(1)}, u32[]{:S(2)}, u32[]{:S(2)}) collective-permute-start(f32[3,32,128]{2,1,0:T(8,128)S(1)} %get-tuple-element.240), channel_id=1, source_target_pairs={{1,4},{4,1},{5,8},{8,5},{9,12},{12,9},{3,6},{6,3},{7,10},{10,7},{1... | collective-permute-start | bytes 147464 | tf_op jit(solution)/shard_map/ppermute | solution.py:128
  16.9 0.9 %slice-start.1 = ((f32[6,32,384]{2,1,0:T(8,128)}), f32[6,32,128]{2,1,0:T(8,128)S(1)}, s32[]{:S(2)}) async-start(f32[6,32,384]{2,1,0:T(8,128)} %copy-done.3), calls=%async_computation.1 | async-start | bytes 196608 | tf_op jit(solution)/shard_map/slice | solution.py:135
  19.3 6.1 %copy-start.2 = (f32[6,32,384]{2,1,0:T(8,128)}, f32[6,32,384]{2,1,0:T(8,128)S(1)}, u32[]{:S(2)}) copy-start(f32[6,32,384]{2,1,0:T(8,128)S(1)} %fusion.55) | copy-start | bytes 884740
  19.3 5.9 %collective-permute-start.5 = (f32[3,32,128]{2,1,0:T(8,128)S(1)}, f32[3,32,128]{2,1,0:T(8,128)S(1)}, u32[]{:S(2)}, u32[]{:S(2)}) collective-permute-start(f32[3,32,128]{2,1,0:T(8,128)S(1)} %get-tuple-element.235), channel_id=1, source_target_pairs={{0,1},{1,0},{2,3},{3,2},{4,5},{5,4},{6,7},{7,6},{8,9},{9,8},{10,11... | collective-permute-start | bytes 147464 | tf_op jit(solution)/shard_map/ppermute | solution.py:124
  24.4 0.9 %collective-permute-start.4 = (f32[3,32,128]{2,1,0:T(8,128)S(1)}, f32[3,32,128]{2,1,0:T(8,128)S(1)}, u32[]{:S(2)}, u32[]{:S(2)}) collective-permute-start(f32[3,32,128]{2,1,0:T(8,128)S(1)} %get-tuple-element.236), channel_id=1, source_target_pairs={{1,4},{4,1},{5,8},{8,5},{9,12},{12,9},{3,6},{6,3},{7,10},{10,7},{1... | collective-permute-start | bytes 147464 | tf_op jit(solution)/shard_map/ppermute | solution.py:128
  25.7 0.9 %slice-start = ((f32[6,32,384]{2,1,0:T(8,128)}), f32[6,32,128]{2,1,0:T(8,128)S(1)}, s32[]{:S(2)}) async-start(f32[6,32,384]{2,1,0:T(8,128)} %copy-done.2), calls=%async_computation | async-start | bytes 196608 | tf_op jit(solution)/shard_map/slice | solution.py:135
  26.1 1.1 %copy-start.1 = (bf16[512,4,128]{2,1,0:T(4,128)(2,1)S(1)}, bf16[512,4,128]{2,1,0:T(4,128)(2,1)}, u32[]{:S(2)}) copy-start(bf16[512,4,128]{2,1,0:T(4,128)(2,1)} %param.35) | copy-start | bytes 1572868
  30.0 5.9 %collective-permute-start.6 = (f32[4,16,2,4,128]{4,1,0,3,2:T(8,128)S(1)}, f32[4,16,2,4,128]{4,1,0,3,2:T(8,128)S(1)}, u32[]{:S(2)}, u32[]{:S(2)}) collective-permute-start(f32[4,16,2,4,128]{4,1,0,3,2:T(8,128)S(1)} %select_bitcast_fusion), channel_id=1, source_target_pairs={{0,1},{1,0},{2,3},{3,2},{4,5},{5,4},{6,7},{7,6},{8,9},{9,8},{10,11... | collective-permute-start | bytes 786440 | tf_op jit(solution)/shard_map/ppermute | solution.py:44
  36.0 6.1 %collective-permute-start.7 = (f32[2,16,2,4,128]{4,1,3,2,0:T(8,128)S(1)}, f32[2,16,2,4,128]{4,1,3,2,0:T(8,128)S(1)}, u32[]{:S(2)}, u32[]{:S(2)}) collective-permute-start(f32[2,16,2,4,128]{4,1,3,2,0:T(8,128)S(1)} %fusion.12), channel_id=1, source_target_pairs={{0,4},{4,0},{8,12},{12,8},{1,5},{5,1},{9,13},{13,9},{2,6},{6,2},{1... | collective-permute-start | bytes 393224 | tf_op jit(solution)/shard_map/ppermute | solution.py:44
  42.2 5.7 %collective-permute-start.8 = (f32[1,16,2,4,128]{4,1,3,2,0:T(8,128)S(1)}, f32[1,16,2,4,128]{4,1,3,2,0:T(8,128)S(1)}, u32[]{:S(2)}, u32[]{:S(2)}) collective-permute-start(f32[1,16,2,4,128]{4,1,3,2,0:T(8,128)S(1)} %select_bitcast_fusion.1), channel_id=1, source_target_pairs={{0,8},{4,12},{8,0},{12,4},{1,9},{5,13},{9,1},{13,5},{2,10},{6,14},... | collective-permute-start | bytes 196616 | tf_op jit(solution)/shard_map/ppermute | solution.py:44

commit v10 on v9

--- a/solution.py
+++ b/solution.py
@@ -10,15 +10,20 @@
     rows = news.shape[0]
     width = news.shape[-1]
     total = news
-    shift = 1
-    while shift < rows:
-        moved = lax.pad(
-            total[: rows - shift, ..., : width - shift],
-            jnp.zeros((), total.dtype),
-            [(shift, 0, 0)] + [(0, 0, 0)] * (total.ndim - 2) + [(shift, 0, 0)],
-        )
-        total = total + moved
-        shift *= 2
+    stride = 1
+    while stride < rows:
+        summed = total
+        for step in range(1, 8):
+            shift = step * stride
+            if shift >= rows:
+                break
+            summed = summed + lax.pad(
+                total[: rows - shift, ..., : max(width - shift, 0)],
+                jnp.zeros((), total.dtype),
+                [(shift, 0, 0)] + [(0, 0, 0)] * (total.ndim - 2) + [(min(shift, width), 0, 0)],
+            )
+        total = summed
+        stride *= 8
     return total
 
 
@@ -46,47 +51,72 @@
     return held.reshape(held.shape[1:])
 
 
-def prepare_kernel(counts, offsets, regions, scales, tiles, expect, moves, rows, edges):
+def prepare_kernel(counts, offsets, regions, scales, tiles, expect, moves, rows, inner, up, down):
     block_count, band_count, tile_size, _ = tiles.shape
     output_count, expect_rows, _ = expect.shape
+    row_count = output_count * expect_rows
+    parts = []
     for block in range(block_count):
         count = counts[block]
         scale = lax.rsqrt(jnp.full((1, tile_size), count.astype(jnp.float32), jnp.float32))
+        region = regions[block]
+        pieces = []
+        for out in range(output_count):
+            part = expect[out, :, block * tile_size : (block + 1) * tile_size]
+            pieces.append((part.astype(jnp.float32) * scales[out, region]).astype(jnp.bfloat16))
+        half = jnp.concatenate(pieces, 0)
+        rows[block] = half.astype(jnp.float32)
+        carried = [
+            jnp.dot(half, tiles[block, slot], preferred_element_type=jnp.float32)
+            for slot in range(band_count)
+        ]
         wide = [tiles[block, slot].astype(jnp.float32) for slot in range(band_count)]
+        block_parts = []
         for shift in range(3):
             total = jnp.zeros((tile_size, tile_size), jnp.float32)
+            flow = jnp.zeros((row_count, tile_size), jnp.float32)
             for slot in range(band_count):
                 use = jnp.logical_and(slot < count, offsets[block, slot] == shift - 1)
-                total = total + jnp.where(use, 1.0, 0.0).astype(jnp.float32) * wide[slot]
+                weight = jnp.where(use, 1.0, 0.0).astype(jnp.float32)
+                total = total + weight * wide[slot]
+                flow = flow + weight * carried[slot]
             total = total * scale
             moves[block, :, shift * tile_size : (shift + 1) * tile_size] = total
+            block_parts.append(flow * scale)
             if block == block_count - 1 and shift > 0:
-                edges[0, (shift - 1) * tile_size : shift * tile_size, :] = total
+                up[row_count + (shift - 1) * tile_size : row_count + shift * tile_size, :] = total
             if block == 0 and shift < 2:
-                edges[1, shift * tile_size : (shift + 1) * tile_size, :] = total
-        region = regions[block]
-        for out in range(output_count):
-            part = expect[out, :, block * tile_size : (block + 1) * tile_size]
-            weighted = part.astype(jnp.float32) * scales[out, region]
-            rows[block, out * expect_rows : (out + 1) * expect_rows, :] = weighted.astype(
-                jnp.bfloat16
-            ).astype(jnp.float32)
+                down[row_count + shift * tile_size : row_count + (shift + 1) * tile_size, :] = total
+        parts.append(block_parts)
+    for block in range(block_count):
+        total = parts[block][1]
+        if block + 1 < block_count:
+            total = total + parts[block + 1][0]
+        if block > 0:
+            total = total + parts[block - 1][2]
+        inner[block] = total
+    up[:row_count, :] = parts[-1][2]
+    down[:row_count, :] = parts[0][0]
 
 
 def prepare(counts, offsets, regions, region_scale, tiles, expectations):
     block_count, band_count, tile_size, _ = tiles.shape
     output_count, expect_rows, _ = expectations.shape
+    row_count = output_count * expect_rows
     smem = pl.BlockSpec(memory_space=pltpu.SMEM)
     vmem = pl.BlockSpec(memory_space=pltpu.VMEM)
+    edge = jax.ShapeDtypeStruct((row_count + 2 * tile_size, tile_size), jnp.float32)
     return pl.pallas_call(
         prepare_kernel,
         out_shape=(
             jax.ShapeDtypeStruct((block_count, tile_size, 3 * tile_size), jnp.float32),
-            jax.ShapeDtypeStruct((block_count, output_count * expect_rows, tile_size), jnp.float32),
-            jax.ShapeDtypeStruct((2, 2 * tile_size, tile_size), jnp.float32),
+            jax.ShapeDtypeStruct((block_count, row_count, tile_size), jnp.float32),
+            jax.ShapeDtypeStruct((block_count, row_count, tile_size), jnp.float32),
+            edge,
+            edge,
         ),
         in_specs=[smem, smem, smem, smem, vmem, vmem],
-        out_specs=(vmem, vmem, vmem),
+        out_specs=(vmem, vmem, vmem, vmem, vmem),
     )(counts, offsets, regions, region_scale.T, tiles, expectations)
 
 
@@ -178,11 +208,10 @@
     width = input_count * horizon
     sections = horizon // expect_rows
     row_count = output_count * expect_rows
-    moves, rows, edges = prepare(counts, offsets, regions, region_scale, tiles, expectations)
+    moves, rows, inner, edge_low, edge_high = prepare(
+        counts, offsets, regions, region_scale, tiles, expectations
+    )
     flat_start = impulses.reshape(state_count, width)
-    inner, out_low, out_high = band_step(rows, moves)
-    edge_low = jnp.concatenate([out_high, edges[0]], 0)
-    edge_high = jnp.concatenate([out_low, edges[1]], 0)
     from_low, from_high = swap_edges(edge_high, edge_low)
     levels = [rows, inner.at[0].add(from_low[:row_count]).at[-1].add(from_high[:row_count])]
     left_self = from_low[row_count : row_count + tile_size]

time: 48.8 us -> 46.9 us (0.961)
  starting transfers between devices: 23.6 us -> 21 us
  other arithmetic: 1.89 us -> 3.45 us
  matrix products: 6.36 us -> 4.84 us
  waiting for transfers between devices: 8.7 us -> 9.44 us
    ppermute x3, starting transfers between devices: 9.61 us -> 5.77 us  [halving_scatter(): held = keep + lax.ppermute(send, axis, pairs)]
    dot_general x11 -> x10, matrix products: 5.45 us -> 3.92 us  [band_parts(): jnp.einsum('cru,cun->crn', rows, moves, precision=lax.Precision.HIGH)]
    ppermute x3, waiting for transfers between devices: 0.64 us -> 1.85 us  [swap_edges(): lax.ppermute(jnp.where(first, to_high, to_low), 'horizon', [(0, 1), (1, 0)])]
    ppermute x3, starting transfers between devices: 12.1 us -> 13.1 us  [swap_edges(): lax.ppermute(jnp.where(first, to_high, to_low), 'horizon', [(0, 1), (1, 0)])]
    squeeze x2 -> x0, local copies, waits for them, and re-layouts: 0.99 us -> none  [the longest x1 0.99 us: shards(): edge_high = jnp.concatenate([out_low, edges[1]], 0)]
    select_n x3, other arithmetic: 0.05 us -> 1.03 us  [swap_edges(): jnp.where(first, to_high, to_low)]
    unnamed x20, local copies, waits for them, and re-layouts: 1.58 us -> 2.41 us
    add x7 -> x3, other arithmetic: 1.31 us -> 1.93 us  [diagonal_sums(): summed + lax.pad(total[:rows - shift, ..., :max(width - shift, 0)], jnp.z...]
  transfers between devices with their start and end apart: 9 -> 9, of which waited for: 6 -> 6; matrix products, arithmetic and copies ran while one was open for 0% -> 2% of each run, Pallas kernels for 0% -> 0%
where the time goes in v10:
time: 46.9 us; the launch traced here: 46.6 us
  starting transfers between devices  21 us (45%)
  waiting for transfers between devices  9.44 us (20%)
  matrix products  4.84 us (10%)
  local copies, waits for them, and re-layouts  4.67 us (10%)
  other arithmetic  3.45 us (7%)
  Pallas kernels  2.3 us (5%)
  between operations  0.86 us (2%)
    ppermute x3, starting transfers between devices, swap_edges(): lax.ppermute(jnp.where(first, to_high, to_low), 'horizon', [(0, 1), (1, 0)])  13.1 us
    ppermute x3, waiting for transfers between devices, halving_scatter(): held = keep + lax.ppermute(send, axis, pairs)  7.58 us
    ppermute x3, starting transfers between devices, halving_scatter(): held = keep + lax.ppermute(send, axis, pairs)  5.77 us
    dot_general x10, matrix products, band_parts(): jnp.einsum('cru,cun->crn', rows, moves, precision=lax.Precision.HIGH)  3.92 us
    unnamed x20, local copies, waits for them, and re-layouts  2.41 us
    pallas_call x1, Pallas kernels, prepare(): pl.pallas_call(prepare_kernel, out_shape=(jax.ShapeDtypeStruct((block_cou...  2.3 us
    ppermute x3, starting transfers between devices, swap_edges(): lax.ppermute(jnp.where(first, to_low, to_high), ('state', 'horizon'), pairs)  2.13 us
    add x3, other arithmetic, diagonal_sums(): summed + lax.pad(total[:rows - shift, ..., :max(width - shift, 0)], jnp.z...  1.93 us
  transfers between devices with their start and end apart: 9, of which 6 were waited for; matrix products, arithmetic and copies ran while one was open for 2% of the time, Pallas kernels for 0%

profile of v10, /device:TPU:0, one launch (start us, length us, event | category | flops | bytes accessed | tf_op | source)
XLA Modules:
  0.0 46.6 jit_solution(6480267904497364444)
XLA Ops:
  0.0 2.3 %shard_map.73 = (f32[4,128,384]{2,1,0:T(8,128)}, f32[4,32,128]{2,1,0:T(8,128)}, f32[4,32,128]{2,1,0:T(8,128)}, f32[288,128]{1,0:T(8,128)}, f32[288,128]{1,0:T(8,128)}) custom-call(s32[4]{0:T(128)} %counts.1, s32[4,4]{1,0:T(4,128)} %offsets.1, s32[4]{0:T(128)} %regions.1, f32[2,16]{1,0:T(2,128)} %bitcast.171, bf16[4,4,128,128]{3,2,1,0:T(8,128)(2,1)} %tiles.1, ...), custom_call_target="tpu_custom_call" | custom-call | tf_op jit(solution)/shard_map/pallas_call | solution.py:109
  2.3 1.0 %broadcast_select_fusion.2 = (f32[288,128]{1,0:T(8,128)S(1)}, f32[288,128]{1,0:T(8,128)S(1)}) fusion(f32[288,128]{1,0:T(8,128)} %get-tuple-element.181, f32[288,128]{1,0:T(8,128)} %get-tuple-element.180, pred[]{:T(512)S(6)} %eq.24), kind=kLoop, calls=%fused_computation.46 | loop fusion | flops 73728 | bytes 589825 | tf_op jit(solution)/shard_map/jit(_where)/select_n | solution.py:154
  3.3 0.8 %collective-permute-start = (f32[288,128]{1,0:T(8,128)S(1)}, f32[288,128]{1,0:T(8,128)S(1)}, u32[]{:S(2)}, u32[]{:S(2)}) collective-permute-start(f32[288,128]{1,0:T(8,128)S(1)} %get-tuple-element.218), channel_id=1, source_target_pairs={{1,4},{4,1},{5,8},{8,5},{9,12},{12,9},{3,6},{6,3},{7,10},{10,7},{1... | collective-permute-start | bytes 442376 | tf_op jit(solution)/shard_map/ppermute | solution.py:158
  4.1 4.4 %collective-permute-start.1 = (f32[288,128]{1,0:T(8,128)S(1)}, f32[288,128]{1,0:T(8,128)S(1)}, u32[]{:S(2)}, u32[]{:S(2)}) collective-permute-start(f32[288,128]{1,0:T(8,128)S(1)} %get-tuple-element.217), channel_id=1, source_target_pairs={{0,1},{1,0},{2,3},{3,2},{4,5},{5,4},{6,7},{7,6},{8,9},{9,8},{10,11... | collective-permute-start | bytes 442376 | tf_op jit(solution)/shard_map/ppermute | solution.py:154
  8.6 0.8 %bitcast_dynamic-update-slice_fusion.7 = f32[256,512]{1,0:T(8,128)S(1)} fusion(f32[4,32,128]{2,1,0:T(8,128)} %get-tuple-element.178), kind=kLoop, calls=%fused_computation.55 | loop fusion | bytes 131072
  9.7 1.0 %copy-done = f32[4,128,384]{2,1,0:T(8,128)S(1)} copy-done((f32[4,128,384]{2,1,0:T(8,128)S(1)}, f32[4,128,384]{2,1,0:T(8,128)}, u32[]{:S(2)}) %copy-start) | copy-done | bytes 786456
  12.3 0.7 %collective-permute-start.2 = (f32[3,32,128]{2,1,0:T(8,128)S(1)}, f32[3,32,128]{2,1,0:T(8,128)S(1)}, u32[]{:S(2)}, u32[]{:S(2)}) collective-permute-start(f32[3,32,128]{2,1,0:T(8,128)S(1)} %get-tuple-element.238), channel_id=1, source_target_pairs={{1,4},{4,1},{5,8},{8,5},{9,12},{12,9},{3,6},{6,3},{7,10},{10,7},{1... | collective-permute-start | bytes 147464 | tf_op jit(solution)/shard_map/ppermute | solution.py:158
  12.9 4.8 %collective-permute-start.3 = (f32[3,32,128]{2,1,0:T(8,128)S(1)}, f32[3,32,128]{2,1,0:T(8,128)S(1)}, u32[]{:S(2)}, u32[]{:S(2)}) collective-permute-start(f32[3,32,128]{2,1,0:T(8,128)S(1)} %get-tuple-element.237), channel_id=1, source_target_pairs={{0,1},{1,0},{2,3},{3,2},{4,5},{5,4},{6,7},{7,6},{8,9},{9,8},{10,11... | collective-permute-start | bytes 147464 | tf_op jit(solution)/shard_map/ppermute | solution.py:154
  17.7 0.9 %collective-permute-done.3 = f32[3,32,128]{2,1,0:T(8,128)S(1)} collective-permute-done((f32[3,32,128]{2,1,0:T(8,128)S(1)}, f32[3,32,128]{2,1,0:T(8,128)S(1)}, u32[]{:S(2)}, u32[]{:S(2)}) %collective-permute-start.3) | collective-permute-done | bytes 49184 | tf_op jit(solution)/shard_map/ppermute | solution.py:154
  19.5 0.5 %slice-done.1 = f32[6,32,128]{2,1,0:T(8,128)S(1)} async-done(((f32[6,32,384]{2,1,0:T(8,128)}), f32[6,32,128]{2,1,0:T(8,128)S(1)}, s32[]{:S(2)}) %slice-start.1) | async-done | bytes 98328 | tf_op jit(solution)/shard_map/slice | solution.py:165
  20.5 0.4 fusion.53
  21.5 0.7 %collective-permute-start.4 = (f32[3,32,128]{2,1,0:T(8,128)S(1)}, f32[3,32,128]{2,1,0:T(8,128)S(1)}, u32[]{:S(2)}, u32[]{:S(2)}) collective-permute-start(f32[3,32,128]{2,1,0:T(8,128)S(1)} %get-tuple-element.234), channel_id=1, source_target_pairs={{1,4},{4,1},{5,8},{8,5},{9,12},{12,9},{3,6},{6,3},{7,10},{10,7},{1... | collective-permute-start | bytes 147464 | tf_op jit(solution)/shard_map/ppermute | solution.py:158
  22.1 3.9 %collective-permute-start.5 = (f32[3,32,128]{2,1,0:T(8,128)S(1)}, f32[3,32,128]{2,1,0:T(8,128)S(1)}, u32[]{:S(2)}, u32[]{:S(2)}) collective-permute-start(f32[3,32,128]{2,1,0:T(8,128)S(1)} %get-tuple-element.233), channel_id=1, source_target_pairs={{0,1},{1,0},{2,3},{3,2},{4,5},{5,4},{6,7},{7,6},{8,9},{9,8},{10,11... | collective-permute-start | bytes 147464 | tf_op jit(solution)/shard_map/ppermute | solution.py:154
  26.1 0.8 %collective-permute-done.5 = f32[3,32,128]{2,1,0:T(8,128)S(1)} collective-permute-done((f32[3,32,128]{2,1,0:T(8,128)S(1)}, f32[3,32,128]{2,1,0:T(8,128)S(1)}, u32[]{:S(2)}, u32[]{:S(2)}) %collective-permute-start.5) | collective-permute-done | bytes 49184 | tf_op jit(solution)/shard_map/ppermute | solution.py:154
  28.3 0.5 %copy-done.1 = bf16[512,4,128]{2,1,0:T(4,128)(2,1)S(1)} copy-done((bf16[512,4,128]{2,1,0:T(4,128)(2,1)S(1)}, bf16[512,4,128]{2,1,0:T(4,128)(2,1)}, u32[]{:S(2)}) %copy-start.1) | copy-done | bytes 524312
  30.1 1.0 %pad_add_fusion.2 = f32[128,2,4,128]{3,0,2,1:T(8,128)S(1)} fusion(f32[121,2,4,121]{3,0,2,1:T(8,128)S(1)} %bitcast.155, f32[122,2,4,122]{3,0,2,1:T(8,128)S(1)} %bitcast.156, f32[123,2,4,123]{3,0,2,1:T(8,128)S(1)} %bitcast.157, f32[124,2,4,124]{3,0,2,1:T(8,128)S(1)} %bitcast.158, f32[125,2,4,125]{3,0,2,1:T(8,128)S(1)} %bitcast.159, ...), kind=kLoop, calls=%fused_computation.9 | loop fusion | flops 917504 | bytes 4493696 | tf_op jit(solution)/shard_map/add | solution.py:20
  31.4 0.8 %pad_add_fusion.1 = f32[128,2,4,128]{3,0,2,1:T(8,128)S(1)} fusion(f32[72,2,4,72]{3,0,2,1:T(8,128)S(1)} %slice.802, f32[80,2,4,80]{3,0,2,1:T(8,128)S(1)} %slice.801, f32[88,2,4,88]{3,0,2,1:T(8,128)S(1)} %slice.800, f32[96,2,4,96]{3,0,2,1:T(8,128)S(1)} %slice.799, f32[104,2,4,104]{3,0,2,1:T(8,128)S(1)} %slice.798, f32[112,2,4,112]{3,0,2,1:T(8,128)S(1)} %slice.797, ...), kind=kLoop, calls=%fused_computation.8 | loop fusion | flops 917504 | bytes 3170304 | tf_op jit(solution)/shard_map/add | solution.py:20
  32.4 0.9 %collective-permute-start.6 = (f32[4,16,2,4,128]{4,1,0,3,2:T(8,128)S(1)}, f32[4,16,2,4,128]{4,1,0,3,2:T(8,128)S(1)}, u32[]{:S(2)}, u32[]{:S(2)}) collective-permute-start(f32[4,16,2,4,128]{4,1,0,3,2:T(8,128)S(1)} %select_bitcast_fusion), channel_id=1, source_target_pairs={{0,1},{1,0},{2,3},{3,2},{4,5},{5,4},{6,7},{7,6},{8,9},{9,8},{10,11... | collective-permute-start | bytes 786440 | tf_op jit(solution)/shard_map/ppermute | solution.py:49
  33.3 1.2 %collective-permute-done.6 = f32[4,16,2,4,128]{4,1,0,3,2:T(8,128)S(1)} collective-permute-done((f32[4,16,2,4,128]{4,1,0,3,2:T(8,128)S(1)}, f32[4,16,2,4,128]{4,1,0,3,2:T(8,128)S(1)}, u32[]{:S(2)}, u32[]{:S(2)}) %collective-permute-start.6) | collective-permute-done | bytes 262176 | tf_op jit(solution)/shard_map/ppermute | solution.py:49
  34.5 2.1 %collective-permute-start.7 = (f32[2,16,2,4,128]{4,1,3,2,0:T(8,128)S(1)}, f32[2,16,2,4,128]{4,1,3,2,0:T(8,128)S(1)}, u32[]{:S(2)}, u32[]{:S(2)}) collective-permute-start(f32[2,16,2,4,128]{4,1,3,2,0:T(8,128)S(1)} %fusion.12), channel_id=1, source_target_pairs={{0,4},{4,0},{8,12},{12,8},{1,5},{5,1},{9,13},{13,9},{2,6},{6,2},{1... | collective-permute-start | bytes 393224 | tf_op jit(solution)/shard_map/ppermute | solution.py:49
  36.6 3.8 %collective-permute-done.7 = f32[2,16,2,4,128]{4,1,3,2,0:T(8,128)S(1)} collective-permute-done((f32[2,16,2,4,128]{4,1,3,2,0:T(8,128)S(1)}, f32[2,16,2,4,128]{4,1,3,2,0:T(8,128)S(1)}, u32[]{:S(2)}, u32[]{:S(2)}) %collective-permute-start.7) | collective-permute-done | bytes 131104 | tf_op jit(solution)/shard_map/ppermute | solution.py:49
  40.4 2.8 %collective-permute-start.8 = (f32[1,16,2,4,128]{4,1,3,2,0:T(8,128)S(1)}, f32[1,16,2,4,128]{4,1,3,2,0:T(8,128)S(1)}, u32[]{:S(2)}, u32[]{:S(2)}) collective-permute-start(f32[1,16,2,4,128]{4,1,3,2,0:T(8,128)S(1)} %select_bitcast_fusion.1), channel_id=1, source_target_pairs={{0,8},{4,12},{8,0},{12,4},{1,9},{5,13},{9,1},{13,5},{2,10},{6,14},... | collective-permute-start | bytes 196616 | tf_op jit(solution)/shard_map/ppermute | solution.py:49
  43.3 2.6 %collective-permute-done.8 = f32[1,16,2,4,128]{4,1,3,2,0:T(8,128)S(1)} collective-permute-done((f32[1,16,2,4,128]{4,1,3,2,0:T(8,128)S(1)}, f32[1,16,2,4,128]{4,1,3,2,0:T(8,128)S(1)}, u32[]{:S(2)}, u32[]{:S(2)}) %collective-permute-start.8) | collective-permute-done | bytes 65568 | tf_op jit(solution)/shard_map/ppermute | solution.py:49
  45.9 0.7 %copy.50 = f32[16,2,4,128]{3,2,1,0:T(4,128)} copy(f32[16,2,4,128]{3,0,2,1:T(8,128)S(1)} %fusion.33) | data formatting | bytes 131072 | tf_op jit(solution)/shard_map/reshape | solution.py:51
  (117 shorter events, 6.4 us)
Async XLA Ops:
  3.3 6.3 %copy-start.4 = (f32[4,32,128]{2,1,0:T(8,128)S(1)}, f32[4,32,128]{2,1,0:T(8,128)}, u32[]{:S(2)}) copy-start(f32[4,32,128]{2,1,0:T(8,128)} %get-tuple-element.179) | copy-start | bytes 196612
  3.3 6.1 %collective-permute-start = (f32[288,128]{1,0:T(8,128)S(1)}, f32[288,128]{1,0:T(8,128)S(1)}, u32[]{:S(2)}, u32[]{:S(2)}) collective-permute-start(f32[288,128]{1,0:T(8,128)S(1)} %get-tuple-element.218), channel_id=1, source_target_pairs={{1,4},{4,1},{5,8},{8,5},{9,12},{12,9},{3,6},{6,3},{7,10},{10,7},{1... | collective-permute-start | bytes 442376 | tf_op jit(solution)/shard_map/ppermute | solution.py:158
  4.1 5.5 %collective-permute-start.1 = (f32[288,128]{1,0:T(8,128)S(1)}, f32[288,128]{1,0:T(8,128)S(1)}, u32[]{:S(2)}, u32[]{:S(2)}) collective-permute-start(f32[288,128]{1,0:T(8,128)S(1)} %get-tuple-element.217), channel_id=1, source_target_pairs={{0,1},{1,0},{2,3},{3,2},{4,5},{5,4},{6,7},{7,6},{8,9},{9,8},{10,11... | collective-permute-start | bytes 442376 | tf_op jit(solution)/shard_map/ppermute | solution.py:154
  9.6 1.1 %copy-start = (f32[4,128,384]{2,1,0:T(8,128)S(1)}, f32[4,128,384]{2,1,0:T(8,128)}, u32[]{:S(2)}) copy-start(f32[4,128,384]{2,1,0:T(8,128)} %get-tuple-element.182) | copy-start | bytes 2359300
  12.2 6.8 %copy-start.3 = (f32[6,32,384]{2,1,0:T(8,128)}, f32[6,32,384]{2,1,0:T(8,128)S(1)}, u32[]{:S(2)}) copy-start(f32[6,32,384]{2,1,0:T(8,128)S(1)} %fusion.54) | copy-start | bytes 884740
  12.3 5.5 %collective-permute-start.2 = (f32[3,32,128]{2,1,0:T(8,128)S(1)}, f32[3,32,128]{2,1,0:T(8,128)S(1)}, u32[]{:S(2)}, u32[]{:S(2)}) collective-permute-start(f32[3,32,128]{2,1,0:T(8,128)S(1)} %get-tuple-element.238), channel_id=1, source_target_pairs={{1,4},{4,1},{5,8},{8,5},{9,12},{12,9},{3,6},{6,3},{7,10},{10,7},{1... | collective-permute-start | bytes 147464 | tf_op jit(solution)/shard_map/ppermute | solution.py:158
  12.9 5.7 %collective-permute-start.3 = (f32[3,32,128]{2,1,0:T(8,128)S(1)}, f32[3,32,128]{2,1,0:T(8,128)S(1)}, u32[]{:S(2)}, u32[]{:S(2)}) collective-permute-start(f32[3,32,128]{2,1,0:T(8,128)S(1)} %get-tuple-element.237), channel_id=1, source_target_pairs={{0,1},{1,0},{2,3},{3,2},{4,5},{5,4},{6,7},{7,6},{8,9},{9,8},{10,11... | collective-permute-start | bytes 147464 | tf_op jit(solution)/shard_map/ppermute | solution.py:154
  19.0 0.9 %slice-start.1 = ((f32[6,32,384]{2,1,0:T(8,128)}), f32[6,32,128]{2,1,0:T(8,128)S(1)}, s32[]{:S(2)}) async-start(f32[6,32,384]{2,1,0:T(8,128)} %copy-done.3), calls=%async_computation.1 | async-start | bytes 196608 | tf_op jit(solution)/shard_map/slice | solution.py:165
  21.4 5.5 %copy-start.2 = (f32[6,32,384]{2,1,0:T(8,128)}, f32[6,32,384]{2,1,0:T(8,128)S(1)}, u32[]{:S(2)}) copy-start(f32[6,32,384]{2,1,0:T(8,128)S(1)} %fusion.52) | copy-start | bytes 884740
  21.5 4.6 %collective-permute-start.4 = (f32[3,32,128]{2,1,0:T(8,128)S(1)}, f32[3,32,128]{2,1,0:T(8,128)S(1)}, u32[]{:S(2)}, u32[]{:S(2)}) collective-permute-start(f32[3,32,128]{2,1,0:T(8,128)S(1)} %get-tuple-element.234), channel_id=1, source_target_pairs={{1,4},{4,1},{5,8},{8,5},{9,12},{12,9},{3,6},{6,3},{7,10},{10,7},{1... | collective-permute-start | bytes 147464 | tf_op jit(solution)/shard_map/ppermute | solution.py:158
  22.1 4.7 %collective-permute-start.5 = (f32[3,32,128]{2,1,0:T(8,128)S(1)}, f32[3,32,128]{2,1,0:T(8,128)S(1)}, u32[]{:S(2)}, u32[]{:S(2)}) collective-permute-start(f32[3,32,128]{2,1,0:T(8,128)S(1)} %get-tuple-element.233), channel_id=1, source_target_pairs={{0,1},{1,0},{2,3},{3,2},{4,5},{5,4},{6,7},{7,6},{8,9},{9,8},{10,11... | collective-permute-start | bytes 147464 | tf_op jit(solution)/shard_map/ppermute | solution.py:154
  27.3 0.9 %slice-start = ((f32[6,32,384]{2,1,0:T(8,128)}), f32[6,32,128]{2,1,0:T(8,128)S(1)}, s32[]{:S(2)}) async-start(f32[6,32,384]{2,1,0:T(8,128)} %copy-done.2), calls=%async_computation | async-start | bytes 196608 | tf_op jit(solution)/shard_map/slice | solution.py:165
  27.7 1.1 %copy-start.1 = (bf16[512,4,128]{2,1,0:T(4,128)(2,1)S(1)}, bf16[512,4,128]{2,1,0:T(4,128)(2,1)}, u32[]{:S(2)}) copy-start(bf16[512,4,128]{2,1,0:T(4,128)(2,1)} %param.35) | copy-start | bytes 1572868
  32.4 2.0 %collective-permute-start.6 = (f32[4,16,2,4,128]{4,1,0,3,2:T(8,128)S(1)}, f32[4,16,2,4,128]{4,1,0,3,2:T(8,128)S(1)}, u32[]{:S(2)}, u32[]{:S(2)}) collective-permute-start(f32[4,16,2,4,128]{4,1,0,3,2:T(8,128)S(1)} %select_bitcast_fusion), channel_id=1, source_target_pairs={{0,1},{1,0},{2,3},{3,2},{4,5},{5,4},{6,7},{7,6},{8,9},{9,8},{10,11... | collective-permute-start | bytes 786440 | tf_op jit(solution)/shard_map/ppermute | solution.py:49
  34.5 5.9 %collective-permute-start.7 = (f32[2,16,2,4,128]{4,1,3,2,0:T(8,128)S(1)}, f32[2,16,2,4,128]{4,1,3,2,0:T(8,128)S(1)}, u32[]{:S(2)}, u32[]{:S(2)}) collective-permute-start(f32[2,16,2,4,128]{4,1,3,2,0:T(8,128)S(1)} %fusion.12), channel_id=1, source_target_pairs={{0,4},{4,0},{8,12},{12,8},{1,5},{5,1},{9,13},{13,9},{2,6},{6,2},{1... | collective-permute-start | bytes 393224 | tf_op jit(solution)/shard_map/ppermute | solution.py:49
  40.4 5.4 %collective-permute-start.8 = (f32[1,16,2,4,128]{4,1,3,2,0:T(8,128)S(1)}, f32[1,16,2,4,128]{4,1,3,2,0:T(8,128)S(1)}, u32[]{:S(2)}, u32[]{:S(2)}) collective-permute-start(f32[1,16,2,4,128]{4,1,3,2,0:T(8,128)S(1)} %select_bitcast_fusion.1), channel_id=1, source_target_pairs={{0,8},{4,12},{8,0},{12,4},{1,9},{5,13},{9,1},{13,5},{2,10},{6,14},... | collective-permute-start | bytes 196616 | tf_op jit(solution)/shard_map/ppermute | solution.py:49

commit v11 on v10

--- a/solution.py
+++ b/solution.py
@@ -10,20 +10,15 @@
     rows = news.shape[0]
     width = news.shape[-1]
     total = news
-    stride = 1
-    while stride < rows:
-        summed = total
-        for step in range(1, 8):
-            shift = step * stride
-            if shift >= rows:
-                break
-            summed = summed + lax.pad(
-                total[: rows - shift, ..., : max(width - shift, 0)],
-                jnp.zeros((), total.dtype),
-                [(shift, 0, 0)] + [(0, 0, 0)] * (total.ndim - 2) + [(min(shift, width), 0, 0)],
-            )
-        total = summed
-        stride *= 8
+    shift = 1
+    while shift < rows:
+        moved = lax.pad(
+            total[: rows - shift, ..., : width - shift],
+            jnp.zeros((), total.dtype),
+            [(shift, 0, 0)] + [(0, 0, 0)] * (total.ndim - 2) + [(shift, 0, 0)],
+        )
+        total = total + moved
+        shift *= 2
     return total
 
 
@@ -213,7 +208,12 @@
     )
     flat_start = impulses.reshape(state_count, width)
     from_low, from_high = swap_edges(edge_high, edge_low)
-    levels = [rows, inner.at[0].add(from_low[:row_count]).at[-1].add(from_high[:row_count])]
+    edge_in = jnp.zeros_like(inner[1:-1])
+    levels = [
+        rows,
+        inner
+        + jnp.concatenate([from_low[None, :row_count], edge_in, from_high[None, :row_count]], 0),
+    ]
     left_self = from_low[row_count : row_count + tile_size]
     left_up = from_low[row_count + tile_size :]
     right_down = from_high[row_count : row_count + tile_size]

time: 46.9 us -> 46.8 us (level)
  starting transfers between devices: 21 us -> 22.9 us
  waiting for transfers between devices: 9.44 us -> 8 us
    ppermute x3, starting transfers between devices: 5.77 us -> 9.84 us  [halving_scatter(): held = keep + lax.ppermute(send, axis, pairs)]
    ppermute x3, starting transfers between devices: 13.1 us -> 10.9 us  [swap_edges(): lax.ppermute(jnp.where(first, to_high, to_low), 'horizon', [(0, 1), (1, 0)])]
    ppermute x3, waiting for transfers between devices: 1.85 us -> 0.4 us  [swap_edges(): lax.ppermute(jnp.where(first, to_high, to_low), 'horizon', [(0, 1), (1, 0)])]
    select_n x0 -> x2, other arithmetic: none -> 1.03 us  [the longest x1 1 us: swap_edges(): jnp.where(first, to_low, to_high)]
    select_n x3 -> x2, other arithmetic: 1.03 us -> 0.03 us  [swap_edges(): jnp.where(first, to_high, to_low)]
    add x3 -> x8, other arithmetic: 1.93 us -> 1.39 us  [the longest x7 1.31 us: diagonal_sums(): total = total + moved]
    unnamed x20 -> x19, local copies, waits for them, and re-layouts: 2.41 us -> 2.34 us
where the time goes in v11:
time: 46.8 us; the launch traced here: 46.4 us
  starting transfers between devices  22.9 us (49%)
  waiting for transfers between devices  8 us (17%)
  matrix products  4.84 us (10%)
  local copies, waits for them, and re-layouts  4.59 us (10%)
  other arithmetic  2.99 us (6%)
  Pallas kernels  2.31 us (5%)
  between operations  0.82 us (2%)
    ppermute x3, starting transfers between devices, swap_edges(): lax.ppermute(jnp.where(first, to_high, to_low), 'horizon', [(0, 1), (1, 0)])  10.9 us
    ppermute x3, starting transfers between devices, halving_scatter(): held = keep + lax.ppermute(send, axis, pairs)  9.84 us
    ppermute x3, waiting for transfers between devices, halving_scatter(): held = keep + lax.ppermute(send, axis, pairs)  7.6 us
    dot_general x10, matrix products, band_parts(): jnp.einsum('cru,cun->crn', rows, moves, precision=lax.Precision.HIGH)  3.92 us
    unnamed x19, local copies, waits for them, and re-layouts  2.34 us
    pallas_call x1, Pallas kernels, prepare(): pl.pallas_call(prepare_kernel, out_shape=(jax.ShapeDtypeStruct((block_cou...  2.31 us
    ppermute x3, starting transfers between devices, swap_edges(): lax.ppermute(jnp.where(first, to_low, to_high), ('state', 'horizon'), pairs)  2.1 us
    add x7, other arithmetic, diagonal_sums(): total = total + moved  1.31 us
  transfers between devices with their start and end apart: 9, of which 6 were waited for; matrix products, arithmetic and copies ran while one was open for 2% of the time, Pallas kernels for 0%

profile of v11, /device:TPU:0, one launch (start us, length us, event | category | flops | bytes accessed | tf_op | source)
XLA Modules:
  0.0 46.4 jit_solution(15223138969449729721)
XLA Ops:
  0.0 2.3 %shard_map.73 = (f32[4,128,384]{2,1,0:T(8,128)}, f32[4,32,128]{2,1,0:T(8,128)}, f32[4,32,128]{2,1,0:T(8,128)}, f32[288,128]{1,0:T(8,128)}, f32[288,128]{1,0:T(8,128)}) custom-call(s32[4]{0:T(128)} %counts.1, s32[4,4]{1,0:T(4,128)} %offsets.1, s32[4]{0:T(128)} %regions.1, f32[2,16]{1,0:T(2,128)} %bitcast.155, bf16[4,4,128,128]{3,2,1,0:T(8,128)(2,1)} %tiles.1, ...), custom_call_target="tpu_custom_call" | custom-call | tf_op jit(solution)/shard_map/pallas_call | solution.py:104
  2.3 1.0 %broadcast_select_fusion.3 = (f32[288,128]{1,0:T(8,128)S(1)}, f32[288,128]{1,0:T(8,128)S(1)}) fusion(f32[288,128]{1,0:T(8,128)} %get-tuple-element.156, f32[288,128]{1,0:T(8,128)} %get-tuple-element.157, pred[]{:T(512)S(6)} %eq.24), kind=kLoop, calls=%fused_computation.51 | loop fusion | flops 73728 | bytes 589825 | tf_op jit(solution)/shard_map/jit(_where)/select_n | solution.py:153
  3.3 0.8 %collective-permute-start = (f32[288,128]{1,0:T(8,128)S(1)}, f32[288,128]{1,0:T(8,128)S(1)}, u32[]{:S(2)}, u32[]{:S(2)}) collective-permute-start(f32[288,128]{1,0:T(8,128)S(1)} %get-tuple-element.193), channel_id=1, source_target_pairs={{1,4},{4,1},{5,8},{8,5},{9,12},{12,9},{3,6},{6,3},{7,10},{10,7},{1... | collective-permute-start | bytes 442376 | tf_op jit(solution)/shard_map/ppermute | solution.py:153
  4.1 4.4 %collective-permute-start.1 = (f32[288,128]{1,0:T(8,128)S(1)}, f32[288,128]{1,0:T(8,128)S(1)}, u32[]{:S(2)}, u32[]{:S(2)}) collective-permute-start(f32[288,128]{1,0:T(8,128)S(1)} %get-tuple-element.194), channel_id=1, source_target_pairs={{0,1},{1,0},{2,3},{3,2},{4,5},{5,4},{6,7},{7,6},{8,9},{9,8},{10,11... | collective-permute-start | bytes 442376 | tf_op jit(solution)/shard_map/ppermute | solution.py:149
  8.7 0.8 %bitcast_dynamic-update-slice_fusion.7 = f32[256,512]{1,0:T(8,128)S(1)} fusion(f32[4,32,128]{2,1,0:T(8,128)} %get-tuple-element.154), kind=kLoop, calls=%fused_computation.59 | loop fusion | bytes 131072
  9.8 0.9 %copy-done = f32[4,128,384]{2,1,0:T(8,128)S(1)} copy-done((f32[4,128,384]{2,1,0:T(8,128)S(1)}, f32[4,128,384]{2,1,0:T(8,128)}, u32[]{:S(2)}) %copy-start) | copy-done | bytes 786456
  11.3 0.4 fusion.51
  11.8 0.4 fusion.50
  12.3 1.8 %collective-permute-start.3 = (f32[3,32,128]{2,1,0:T(8,128)S(1)}, f32[3,32,128]{2,1,0:T(8,128)S(1)}, u32[]{:S(2)}, u32[]{:S(2)}) collective-permute-start(f32[3,32,128]{2,1,0:T(8,128)S(1)} %get-tuple-element.213), channel_id=1, source_target_pairs={{0,1},{1,0},{2,3},{3,2},{4,5},{5,4},{6,7},{7,6},{8,9},{9,8},{10,11... | collective-permute-start | bytes 147464 | tf_op jit(solution)/shard_map/ppermute | solution.py:149
  14.1 0.7 %collective-permute-start.2 = (f32[3,32,128]{2,1,0:T(8,128)S(1)}, f32[3,32,128]{2,1,0:T(8,128)S(1)}, u32[]{:S(2)}, u32[]{:S(2)}) collective-permute-start(f32[3,32,128]{2,1,0:T(8,128)S(1)} %get-tuple-element.214), channel_id=1, source_target_pairs={{1,4},{4,1},{5,8},{8,5},{9,12},{12,9},{3,6},{6,3},{7,10},{10,7},{1... | collective-permute-start | bytes 147464 | tf_op jit(solution)/shard_map/ppermute | solution.py:153
  15.8 0.5 %slice-done.1 = f32[6,32,128]{2,1,0:T(8,128)S(1)} async-done(((f32[6,32,384]{2,1,0:T(8,128)}), f32[6,32,128]{2,1,0:T(8,128)S(1)}, s32[]{:S(2)}) %slice-start.1) | async-done | bytes 98328 | tf_op jit(solution)/shard_map/slice | solution.py:160
  16.3 0.4 fusion.15
  16.8 0.4 fusion.49
  17.8 4.7 %collective-permute-start.5 = (f32[3,32,128]{2,1,0:T(8,128)S(1)}, f32[3,32,128]{2,1,0:T(8,128)S(1)}, u32[]{:S(2)}, u32[]{:S(2)}) collective-permute-start(f32[3,32,128]{2,1,0:T(8,128)S(1)} %get-tuple-element.209), channel_id=1, source_target_pairs={{0,1},{1,0},{2,3},{3,2},{4,5},{5,4},{6,7},{7,6},{8,9},{9,8},{10,11... | collective-permute-start | bytes 147464 | tf_op jit(solution)/shard_map/ppermute | solution.py:149
  22.5 0.7 %collective-permute-start.4 = (f32[3,32,128]{2,1,0:T(8,128)S(1)}, f32[3,32,128]{2,1,0:T(8,128)S(1)}, u32[]{:S(2)}, u32[]{:S(2)}) collective-permute-start(f32[3,32,128]{2,1,0:T(8,128)S(1)} %get-tuple-element.210), channel_id=1, source_target_pairs={{1,4},{4,1},{5,8},{8,5},{9,12},{12,9},{3,6},{6,3},{7,10},{10,7},{1... | collective-permute-start | bytes 147464 | tf_op jit(solution)/shard_map/ppermute | solution.py:153
  24.3 0.4 slice-done
  24.8 0.5 %copy-done.1 = bf16[512,4,128]{2,1,0:T(4,128)(2,1)S(1)} copy-done((bf16[512,4,128]{2,1,0:T(4,128)(2,1)S(1)}, bf16[512,4,128]{2,1,0:T(4,128)(2,1)}, u32[]{:S(2)}) %copy-start.1) | copy-done | bytes 524312
  28.2 5.0 %collective-permute-start.6 = (f32[4,16,2,4,128]{4,1,0,3,2:T(8,128)S(1)}, f32[4,16,2,4,128]{4,1,0,3,2:T(8,128)S(1)}, u32[]{:S(2)}, u32[]{:S(2)}) collective-permute-start(f32[4,16,2,4,128]{4,1,0,3,2:T(8,128)S(1)} %select_bitcast_fusion), channel_id=1, source_target_pairs={{0,1},{1,0},{2,3},{3,2},{4,5},{5,4},{6,7},{7,6},{8,9},{9,8},{10,11... | collective-permute-start | bytes 786440 | tf_op jit(solution)/shard_map/ppermute | solution.py:44
  33.1 1.2 %collective-permute-done.6 = f32[4,16,2,4,128]{4,1,0,3,2:T(8,128)S(1)} collective-permute-done((f32[4,16,2,4,128]{4,1,0,3,2:T(8,128)S(1)}, f32[4,16,2,4,128]{4,1,0,3,2:T(8,128)S(1)}, u32[]{:S(2)}, u32[]{:S(2)}) %collective-permute-start.6) | collective-permute-done | bytes 262176 | tf_op jit(solution)/shard_map/ppermute | solution.py:44
  34.4 2.1 %collective-permute-start.7 = (f32[2,16,2,4,128]{4,1,3,2,0:T(8,128)S(1)}, f32[2,16,2,4,128]{4,1,3,2,0:T(8,128)S(1)}, u32[]{:S(2)}, u32[]{:S(2)}) collective-permute-start(f32[2,16,2,4,128]{4,1,3,2,0:T(8,128)S(1)} %fusion.12), channel_id=1, source_target_pairs={{0,4},{4,0},{8,12},{12,8},{1,5},{5,1},{9,13},{13,9},{2,6},{6,2},{1... | collective-permute-start | bytes 393224 | tf_op jit(solution)/shard_map/ppermute | solution.py:44
  36.5 3.8 %collective-permute-done.7 = f32[2,16,2,4,128]{4,1,3,2,0:T(8,128)S(1)} collective-permute-done((f32[2,16,2,4,128]{4,1,3,2,0:T(8,128)S(1)}, f32[2,16,2,4,128]{4,1,3,2,0:T(8,128)S(1)}, u32[]{:S(2)}, u32[]{:S(2)}) %collective-permute-start.7) | collective-permute-done | bytes 131104 | tf_op jit(solution)/shard_map/ppermute | solution.py:44
  40.3 2.8 %collective-permute-start.8 = (f32[1,16,2,4,128]{4,1,3,2,0:T(8,128)S(1)}, f32[1,16,2,4,128]{4,1,3,2,0:T(8,128)S(1)}, u32[]{:S(2)}, u32[]{:S(2)}) collective-permute-start(f32[1,16,2,4,128]{4,1,3,2,0:T(8,128)S(1)} %select_bitcast_fusion.1), channel_id=1, source_target_pairs={{0,8},{4,12},{8,0},{12,4},{1,9},{5,13},{9,1},{13,5},{2,10},{6,14},... | collective-permute-start | bytes 196616 | tf_op jit(solution)/shard_map/ppermute | solution.py:44
  43.1 2.6 %collective-permute-done.8 = f32[1,16,2,4,128]{4,1,3,2,0:T(8,128)S(1)} collective-permute-done((f32[1,16,2,4,128]{4,1,3,2,0:T(8,128)S(1)}, f32[1,16,2,4,128]{4,1,3,2,0:T(8,128)S(1)}, u32[]{:S(2)}, u32[]{:S(2)}) %collective-permute-start.8) | collective-permute-done | bytes 65568 | tf_op jit(solution)/shard_map/ppermute | solution.py:44
  45.8 0.7 %copy.50 = f32[16,2,4,128]{3,2,1,0:T(4,128)} copy(f32[16,2,4,128]{3,0,2,1:T(8,128)S(1)} %fusion.33) | data formatting | bytes 131072 | tf_op jit(solution)/shard_map/reshape | solution.py:46
  (119 shorter events, 6.2 us)
Async XLA Ops:
  3.3 6.3 %copy-start.4 = (f32[4,32,128]{2,1,0:T(8,128)S(1)}, f32[4,32,128]{2,1,0:T(8,128)}, u32[]{:S(2)}) copy-start(f32[4,32,128]{2,1,0:T(8,128)} %get-tuple-element.155) | copy-start | bytes 196612
  3.3 6.2 %collective-permute-start = (f32[288,128]{1,0:T(8,128)S(1)}, f32[288,128]{1,0:T(8,128)S(1)}, u32[]{:S(2)}, u32[]{:S(2)}) collective-permute-start(f32[288,128]{1,0:T(8,128)S(1)} %get-tuple-element.193), channel_id=1, source_target_pairs={{1,4},{4,1},{5,8},{8,5},{9,12},{12,9},{3,6},{6,3},{7,10},{10,7},{1... | collective-permute-start | bytes 442376 | tf_op jit(solution)/shard_map/ppermute | solution.py:153
  4.1 5.5 %collective-permute-start.1 = (f32[288,128]{1,0:T(8,128)S(1)}, f32[288,128]{1,0:T(8,128)S(1)}, u32[]{:S(2)}, u32[]{:S(2)}) collective-permute-start(f32[288,128]{1,0:T(8,128)S(1)} %get-tuple-element.194), channel_id=1, source_target_pairs={{0,1},{1,0},{2,3},{3,2},{4,5},{5,4},{6,7},{7,6},{8,9},{9,8},{10,11... | collective-permute-start | bytes 442376 | tf_op jit(solution)/shard_map/ppermute | solution.py:149
  9.6 1.1 %copy-start = (f32[4,128,384]{2,1,0:T(8,128)S(1)}, f32[4,128,384]{2,1,0:T(8,128)}, u32[]{:S(2)}) copy-start(f32[4,128,384]{2,1,0:T(8,128)} %get-tuple-element.158) | copy-start | bytes 2359300
  12.2 3.1 %copy-start.3 = (f32[6,32,384]{2,1,0:T(8,128)}, f32[6,32,384]{2,1,0:T(8,128)S(1)}, u32[]{:S(2)}) copy-start(f32[6,32,384]{2,1,0:T(8,128)S(1)} %fusion.50) | copy-start | bytes 884740
  12.3 2.7 %collective-permute-start.3 = (f32[3,32,128]{2,1,0:T(8,128)S(1)}, f32[3,32,128]{2,1,0:T(8,128)S(1)}, u32[]{:S(2)}, u32[]{:S(2)}) collective-permute-start(f32[3,32,128]{2,1,0:T(8,128)S(1)} %get-tuple-element.213), channel_id=1, source_target_pairs={{0,1},{1,0},{2,3},{3,2},{4,5},{5,4},{6,7},{7,6},{8,9},{9,8},{10,11... | collective-permute-start | bytes 147464 | tf_op jit(solution)/shard_map/ppermute | solution.py:149
  14.1 0.9 %collective-permute-start.2 = (f32[3,32,128]{2,1,0:T(8,128)S(1)}, f32[3,32,128]{2,1,0:T(8,128)S(1)}, u32[]{:S(2)}, u32[]{:S(2)}) collective-permute-start(f32[3,32,128]{2,1,0:T(8,128)S(1)} %get-tuple-element.214), channel_id=1, source_target_pairs={{1,4},{4,1},{5,8},{8,5},{9,12},{12,9},{3,6},{6,3},{7,10},{10,7},{1... | collective-permute-start | bytes 147464 | tf_op jit(solution)/shard_map/ppermute | solution.py:153
  15.4 0.9 %slice-start.1 = ((f32[6,32,384]{2,1,0:T(8,128)}), f32[6,32,128]{2,1,0:T(8,128)S(1)}, s32[]{:S(2)}) async-start(f32[6,32,384]{2,1,0:T(8,128)} %copy-done.3), calls=%async_computation.1 | async-start | bytes 196608 | tf_op jit(solution)/shard_map/slice | solution.py:160
  17.8 5.7 %copy-start.2 = (f32[6,32,384]{2,1,0:T(8,128)}, f32[6,32,384]{2,1,0:T(8,128)S(1)}, u32[]{:S(2)}) copy-start(f32[6,32,384]{2,1,0:T(8,128)S(1)} %fusion.48) | copy-start | bytes 884740
  17.8 5.6 %collective-permute-start.5 = (f32[3,32,128]{2,1,0:T(8,128)S(1)}, f32[3,32,128]{2,1,0:T(8,128)S(1)}, u32[]{:S(2)}, u32[]{:S(2)}) collective-permute-start(f32[3,32,128]{2,1,0:T(8,128)S(1)} %get-tuple-element.209), channel_id=1, source_target_pairs={{0,1},{1,0},{2,3},{3,2},{4,5},{5,4},{6,7},{7,6},{8,9},{9,8},{10,11... | collective-permute-start | bytes 147464 | tf_op jit(solution)/shard_map/ppermute | solution.py:149
  22.5 0.9 %collective-permute-start.4 = (f32[3,32,128]{2,1,0:T(8,128)S(1)}, f32[3,32,128]{2,1,0:T(8,128)S(1)}, u32[]{:S(2)}, u32[]{:S(2)}) collective-permute-start(f32[3,32,128]{2,1,0:T(8,128)S(1)} %get-tuple-element.210), channel_id=1, source_target_pairs={{1,4},{4,1},{5,8},{8,5},{9,12},{12,9},{3,6},{6,3},{7,10},{10,7},{1... | collective-permute-start | bytes 147464 | tf_op jit(solution)/shard_map/ppermute | solution.py:153
  23.9 0.9 %slice-start = ((f32[6,32,384]{2,1,0:T(8,128)}), f32[6,32,128]{2,1,0:T(8,128)S(1)}, s32[]{:S(2)}) async-start(f32[6,32,384]{2,1,0:T(8,128)} %copy-done.2), calls=%async_computation | async-start | bytes 196608 | tf_op jit(solution)/shard_map/slice | solution.py:160
  24.2 1.1 %copy-start.1 = (bf16[512,4,128]{2,1,0:T(4,128)(2,1)S(1)}, bf16[512,4,128]{2,1,0:T(4,128)(2,1)}, u32[]{:S(2)}) copy-start(bf16[512,4,128]{2,1,0:T(4,128)(2,1)} %param.31) | copy-start | bytes 1572868
  28.2 6.1 %collective-permute-start.6 = (f32[4,16,2,4,128]{4,1,0,3,2:T(8,128)S(1)}, f32[4,16,2,4,128]{4,1,0,3,2:T(8,128)S(1)}, u32[]{:S(2)}, u32[]{:S(2)}) collective-permute-start(f32[4,16,2,4,128]{4,1,0,3,2:T(8,128)S(1)} %select_bitcast_fusion), channel_id=1, source_target_pairs={{0,1},{1,0},{2,3},{3,2},{4,5},{5,4},{6,7},{7,6},{8,9},{9,8},{10,11... | collective-permute-start | bytes 786440 | tf_op jit(solution)/shard_map/ppermute | solution.py:44
  34.4 5.9 %collective-permute-start.7 = (f32[2,16,2,4,128]{4,1,3,2,0:T(8,128)S(1)}, f32[2,16,2,4,128]{4,1,3,2,0:T(8,128)S(1)}, u32[]{:S(2)}, u32[]{:S(2)}) collective-permute-start(f32[2,16,2,4,128]{4,1,3,2,0:T(8,128)S(1)} %fusion.12), channel_id=1, source_target_pairs={{0,4},{4,0},{8,12},{12,8},{1,5},{5,1},{9,13},{13,9},{2,6},{6,2},{1... | collective-permute-start | bytes 393224 | tf_op jit(solution)/shard_map/ppermute | solution.py:44
  40.3 5.4 %collective-permute-start.8 = (f32[1,16,2,4,128]{4,1,3,2,0:T(8,128)S(1)}, f32[1,16,2,4,128]{4,1,3,2,0:T(8,128)S(1)}, u32[]{:S(2)}, u32[]{:S(2)}) collective-permute-start(f32[1,16,2,4,128]{4,1,3,2,0:T(8,128)S(1)} %select_bitcast_fusion.1), channel_id=1, source_target_pairs={{0,8},{4,12},{8,0},{12,4},{1,9},{5,13},{9,1},{13,5},{2,10},{6,14},... | collective-permute-start | bytes 196616 | tf_op jit(solution)/shard_map/ppermute | solution.py:44

commit v12 on v11

--- a/solution.py
+++ b/solution.py
@@ -46,7 +46,7 @@
     return held.reshape(held.shape[1:])
 
 
-def prepare_kernel(counts, offsets, regions, scales, tiles, expect, moves, rows, inner, up, down):
+def prepare_kernel(flip, counts, offsets, regions, scales, tiles, expect, moves, rows, inner, up, down):
     block_count, band_count, tile_size, _ = tiles.shape
     output_count, expect_rows, _ = expect.shape
     row_count = output_count * expect_rows
@@ -92,9 +92,14 @@
         inner[block] = total
     up[:row_count, :] = parts[-1][2]
     down[:row_count, :] = parts[0][0]
-
-
-def prepare(counts, offsets, regions, region_scale, tiles, expectations):
+    keep_up = up[...]
+    keep_down = down[...]
+    swap = flip[0] == 1
+    up[...] = jnp.where(swap, keep_up, keep_down)
+    down[...] = jnp.where(swap, keep_down, keep_up)
+
+
+def prepare(flip, counts, offsets, regions, region_scale, tiles, expectations):
     block_count, band_count, tile_size, _ = tiles.shape
     output_count, expect_rows, _ = expectations.shape
     row_count = output_count * expect_rows
@@ -110,9 +115,9 @@
             edge,
             edge,
         ),
-        in_specs=[smem, smem, smem, smem, vmem, vmem],
+        in_specs=[smem, smem, smem, smem, smem, vmem, vmem],
         out_specs=(vmem, vmem, vmem, vmem, vmem),
-    )(counts, offsets, regions, region_scale.T, tiles, expectations)
+    )(flip, counts, offsets, regions, region_scale.T, tiles, expectations)
 
 
 def split_product(rows_full, data_half):
@@ -141,16 +146,20 @@
 
 
 def swap_edges(to_low, to_high):
-    cores = lax.axis_size("horizon")
-    if cores != 2:
+    if lax.axis_size("horizon") != 2:
         return to_right(to_high), to_left(to_low)
+    first = lax.axis_index("horizon") == 0
+    return swap_links(jnp.where(first, to_high, to_low), jnp.where(first, to_low, to_high))
+
+
+def swap_links(chip_part, cross_part):
     count = lax.axis_size(("state", "horizon"))
     first = lax.axis_index("horizon") == 0
-    on_chip = lax.ppermute(jnp.where(first, to_high, to_low), "horizon", [(0, 1), (1, 0)])
+    on_chip = lax.ppermute(chip_part, "horizon", [(0, 1), (1, 0)])
     pairs = []
     for chip in range(count // 2 - 1):
         pairs += [(2 * chip + 1, 2 * chip + 2), (2 * chip + 2, 2 * chip + 1)]
-    across = lax.ppermute(jnp.where(first, to_low, to_high), ("state", "horizon"), pairs)
+    across = lax.ppermute(cross_part, ("state", "horizon"), pairs)
     return jnp.where(first, across, on_chip), jnp.where(first, on_chip, across)
 
 
@@ -203,11 +212,17 @@
     width = input_count * horizon
     sections = horizon // expect_rows
     row_count = output_count * expect_rows
-    moves, rows, inner, edge_low, edge_high = prepare(
-        counts, offsets, regions, region_scale, tiles, expectations
+    paired = lax.axis_size("horizon") == 2
+    flip = jnp.where(lax.axis_index("horizon") == 0, 1, 0) if paired else 0
+    flip = jnp.full((1,), flip, jnp.int32)
+    moves, rows, inner, first_part, second_part = prepare(
+        flip, counts, offsets, regions, region_scale, tiles, expectations
     )
     flat_start = impulses.reshape(state_count, width)
-    from_low, from_high = swap_edges(edge_high, edge_low)
+    if paired:
+        from_low, from_high = swap_links(first_part, second_part)
+    else:
+        from_low, from_high = swap_edges(second_part, first_part)
     edge_in = jnp.zeros_like(inner[1:-1])
     levels = [
         rows,

time: 46.8 us -> 46 us (0.983)
  other arithmetic: 2.99 us -> 1.99 us
    select_n x4 -> x3, other arithmetic: 1.04 us -> 0.04 us  [the longest x1 0.02 us: swap_links(): jnp.where(first, across, on_chip)]
where the time goes in v12:
time: 46 us; the launch traced here: 45.6 us
  starting transfers between devices  22.9 us (50%)
  waiting for transfers between devices  8.2 us (18%)
  matrix products  4.83 us (10%)
  local copies, waits for them, and re-layouts  4.59 us (10%)
  Pallas kernels  2.31 us (5%)
  other arithmetic  1.99 us (4%)
  between operations  0.81 us (2%)
    ppermute x3, starting transfers between devices, swap_links(): on_chip = lax.ppermute(chip_part, 'horizon', [(0, 1), (1, 0)])  10.9 us
    ppermute x3, starting transfers between devices, halving_scatter(): held = keep + lax.ppermute(send, axis, pairs)  9.85 us
    ppermute x3, waiting for transfers between devices, halving_scatter(): held = keep + lax.ppermute(send, axis, pairs)  7.59 us
    dot_general x10, matrix products, band_parts(): jnp.einsum('cru,cun->crn', rows, moves, precision=lax.Precision.HIGH)  3.92 us
    unnamed x19, local copies, waits for them, and re-layouts  2.34 us
    pallas_call x1, Pallas kernels, prepare(): pl.pallas_call(prepare_kernel, out_shape=(jax.ShapeDtypeStruct((block_cou...  2.31 us
    ppermute x3, starting transfers between devices, swap_links(): across = lax.ppermute(cross_part, ('state', 'horizon'), pairs)  2.09 us
    add x7, other arithmetic, diagonal_sums(): total = total + moved  1.31 us
  transfers between devices with their start and end apart: 9, of which 6 were waited for; matrix products, arithmetic and copies ran while one was open for 2% of the time, Pallas kernels for 0%

profile of v12, /device:TPU:0, one launch (start us, length us, event | category | flops | bytes accessed | tf_op | source)
XLA Modules:
  0.0 45.6 jit_solution(3491188725756667169)
XLA Ops:
  0.0 2.3 %shard_map.73 = (f32[4,128,384]{2,1,0:T(8,128)}, f32[4,32,128]{2,1,0:T(8,128)}, f32[4,32,128]{2,1,0:T(8,128)}, f32[288,128]{1,0:T(8,128)}, f32[288,128]{1,0:T(8,128)}) custom-call(s32[1]{0:T(128)} %bitcast.flip, s32[4]{0:T(128)} %counts.1, s32[4,4]{1,0:T(4,128)} %offsets.1, s32[4]{0:T(128)} %regions.1, f32[2,16]{1,0:T(2,128)} %bitcast.156, ...), custom_call_target="tpu_custom_call" | custom-call | tf_op jit(solution)/shard_map/pallas_call | solution.py:109
  2.3 0.8 %collective-permute-start = (f32[288,128]{1,0:T(8,128)}, f32[288,128]{1,0:T(8,128)S(1)}, u32[]{:S(2)}, u32[]{:S(2)}) collective-permute-start(f32[288,128]{1,0:T(8,128)} %get-tuple-element.156), channel_id=1, source_target_pairs={{1,4},{4,1},{5,8},{8,5},{9,12},{12,9},{3,6},{6,3},{7,10},{10,7},{1... | collective-permute-start | bytes 442376 | tf_op jit(solution)/shard_map/ppermute | solution.py:162
  3.1 4.4 %collective-permute-start.1 = (f32[288,128]{1,0:T(8,128)}, f32[288,128]{1,0:T(8,128)S(1)}, u32[]{:S(2)}, u32[]{:S(2)}) collective-permute-start(f32[288,128]{1,0:T(8,128)} %get-tuple-element.157), channel_id=1, source_target_pairs={{0,1},{1,0},{2,3},{3,2},{4,5},{5,4},{6,7},{7,6},{8,9},{9,8},{10,11... | collective-permute-start | bytes 442376 | tf_op jit(solution)/shard_map/ppermute | solution.py:158
  7.6 0.8 %bitcast_dynamic-update-slice_fusion.7 = f32[256,512]{1,0:T(8,128)S(1)} fusion(f32[4,32,128]{2,1,0:T(8,128)} %get-tuple-element.154), kind=kLoop, calls=%fused_computation.57 | loop fusion | bytes 131072
  9.0 0.9 %copy-done = f32[4,128,384]{2,1,0:T(8,128)S(1)} copy-done((f32[4,128,384]{2,1,0:T(8,128)S(1)}, f32[4,128,384]{2,1,0:T(8,128)}, u32[]{:S(2)}) %copy-start) | copy-done | bytes 786456
  10.4 0.4 fusion.51
  10.9 0.4 fusion.50
  11.4 1.8 %collective-permute-start.3 = (f32[3,32,128]{2,1,0:T(8,128)S(1)}, f32[3,32,128]{2,1,0:T(8,128)S(1)}, u32[]{:S(2)}, u32[]{:S(2)}) collective-permute-start(f32[3,32,128]{2,1,0:T(8,128)S(1)} %get-tuple-element.211), channel_id=1, source_target_pairs={{0,1},{1,0},{2,3},{3,2},{4,5},{5,4},{6,7},{7,6},{8,9},{9,8},{10,11... | collective-permute-start | bytes 147464 | tf_op jit(solution)/shard_map/ppermute | solution.py:158
  13.3 0.7 %collective-permute-start.2 = (f32[3,32,128]{2,1,0:T(8,128)S(1)}, f32[3,32,128]{2,1,0:T(8,128)S(1)}, u32[]{:S(2)}, u32[]{:S(2)}) collective-permute-start(f32[3,32,128]{2,1,0:T(8,128)S(1)} %get-tuple-element.212), channel_id=1, source_target_pairs={{1,4},{4,1},{5,8},{8,5},{9,12},{12,9},{3,6},{6,3},{7,10},{10,7},{1... | collective-permute-start | bytes 147464 | tf_op jit(solution)/shard_map/ppermute | solution.py:162
  15.0 0.5 %slice-done.1 = f32[6,32,128]{2,1,0:T(8,128)S(1)} async-done(((f32[6,32,384]{2,1,0:T(8,128)}), f32[6,32,128]{2,1,0:T(8,128)S(1)}, s32[]{:S(2)}) %slice-start.1) | async-done | bytes 98328 | tf_op jit(solution)/shard_map/slice | solution.py:169
  15.5 0.4 fusion.15
  16.0 0.4 fusion.49
  16.5 0.4 fusion.48
  17.0 4.7 %collective-permute-start.5 = (f32[3,32,128]{2,1,0:T(8,128)S(1)}, f32[3,32,128]{2,1,0:T(8,128)S(1)}, u32[]{:S(2)}, u32[]{:S(2)}) collective-permute-start(f32[3,32,128]{2,1,0:T(8,128)S(1)} %get-tuple-element.207), channel_id=1, source_target_pairs={{0,1},{1,0},{2,3},{3,2},{4,5},{5,4},{6,7},{7,6},{8,9},{9,8},{10,11... | collective-permute-start | bytes 147464 | tf_op jit(solution)/shard_map/ppermute | solution.py:158
  21.7 0.7 %collective-permute-start.4 = (f32[3,32,128]{2,1,0:T(8,128)S(1)}, f32[3,32,128]{2,1,0:T(8,128)S(1)}, u32[]{:S(2)}, u32[]{:S(2)}) collective-permute-start(f32[3,32,128]{2,1,0:T(8,128)S(1)} %get-tuple-element.208), channel_id=1, source_target_pairs={{1,4},{4,1},{5,8},{8,5},{9,12},{12,9},{3,6},{6,3},{7,10},{10,7},{1... | collective-permute-start | bytes 147464 | tf_op jit(solution)/shard_map/ppermute | solution.py:162
  23.5 0.4 slice-done
  24.0 0.5 %copy-done.1 = bf16[512,4,128]{2,1,0:T(4,128)(2,1)S(1)} copy-done((bf16[512,4,128]{2,1,0:T(4,128)(2,1)S(1)}, bf16[512,4,128]{2,1,0:T(4,128)(2,1)}, u32[]{:S(2)}) %copy-start.1) | copy-done | bytes 524312
  27.4 5.0 %collective-permute-start.6 = (f32[4,16,2,4,128]{4,1,0,3,2:T(8,128)S(1)}, f32[4,16,2,4,128]{4,1,0,3,2:T(8,128)S(1)}, u32[]{:S(2)}, u32[]{:S(2)}) collective-permute-start(f32[4,16,2,4,128]{4,1,0,3,2:T(8,128)S(1)} %select_bitcast_fusion), channel_id=1, source_target_pairs={{0,1},{1,0},{2,3},{3,2},{4,5},{5,4},{6,7},{7,6},{8,9},{9,8},{10,11... | collective-permute-start | bytes 786440 | tf_op jit(solution)/shard_map/ppermute | solution.py:44
  32.3 1.2 %collective-permute-done.6 = f32[4,16,2,4,128]{4,1,0,3,2:T(8,128)S(1)} collective-permute-done((f32[4,16,2,4,128]{4,1,0,3,2:T(8,128)S(1)}, f32[4,16,2,4,128]{4,1,0,3,2:T(8,128)S(1)}, u32[]{:S(2)}, u32[]{:S(2)}) %collective-permute-start.6) | collective-permute-done | bytes 262176 | tf_op jit(solution)/shard_map/ppermute | solution.py:44
  33.6 2.1 %collective-permute-start.7 = (f32[2,16,2,4,128]{4,1,3,2,0:T(8,128)S(1)}, f32[2,16,2,4,128]{4,1,3,2,0:T(8,128)S(1)}, u32[]{:S(2)}, u32[]{:S(2)}) collective-permute-start(f32[2,16,2,4,128]{4,1,3,2,0:T(8,128)S(1)} %fusion.12), channel_id=1, source_target_pairs={{0,4},{4,0},{8,12},{12,8},{1,5},{5,1},{9,13},{13,9},{2,6},{6,2},{1... | collective-permute-start | bytes 393224 | tf_op jit(solution)/shard_map/ppermute | solution.py:44
  35.7 3.8 %collective-permute-done.7 = f32[2,16,2,4,128]{4,1,3,2,0:T(8,128)S(1)} collective-permute-done((f32[2,16,2,4,128]{4,1,3,2,0:T(8,128)S(1)}, f32[2,16,2,4,128]{4,1,3,2,0:T(8,128)S(1)}, u32[]{:S(2)}, u32[]{:S(2)}) %collective-permute-start.7) | collective-permute-done | bytes 131104 | tf_op jit(solution)/shard_map/ppermute | solution.py:44
  39.5 2.8 %collective-permute-start.8 = (f32[1,16,2,4,128]{4,1,3,2,0:T(8,128)S(1)}, f32[1,16,2,4,128]{4,1,3,2,0:T(8,128)S(1)}, u32[]{:S(2)}, u32[]{:S(2)}) collective-permute-start(f32[1,16,2,4,128]{4,1,3,2,0:T(8,128)S(1)} %select_bitcast_fusion.1), channel_id=1, source_target_pairs={{0,8},{4,12},{8,0},{12,4},{1,9},{5,13},{9,1},{13,5},{2,10},{6,14},... | collective-permute-start | bytes 196616 | tf_op jit(solution)/shard_map/ppermute | solution.py:44
  42.3 2.6 %collective-permute-done.8 = f32[1,16,2,4,128]{4,1,3,2,0:T(8,128)S(1)} collective-permute-done((f32[1,16,2,4,128]{4,1,3,2,0:T(8,128)S(1)}, f32[1,16,2,4,128]{4,1,3,2,0:T(8,128)S(1)}, u32[]{:S(2)}, u32[]{:S(2)}) %collective-permute-start.8) | collective-permute-done | bytes 65568 | tf_op jit(solution)/shard_map/ppermute | solution.py:44
  45.0 0.7 %copy.50 = f32[16,2,4,128]{3,2,1,0:T(4,128)} copy(f32[16,2,4,128]{3,0,2,1:T(8,128)S(1)} %fusion.33) | data formatting | bytes 131072 | tf_op jit(solution)/shard_map/reshape | solution.py:46
  (118 shorter events, 6.0 us)
Async XLA Ops:
  2.3 6.5 %copy-start.4 = (f32[4,32,128]{2,1,0:T(8,128)S(1)}, f32[4,32,128]{2,1,0:T(8,128)}, u32[]{:S(2)}) copy-start(f32[4,32,128]{2,1,0:T(8,128)} %get-tuple-element.155) | copy-start | bytes 196612
  2.3 6.2 %collective-permute-start = (f32[288,128]{1,0:T(8,128)}, f32[288,128]{1,0:T(8,128)S(1)}, u32[]{:S(2)}, u32[]{:S(2)}) collective-permute-start(f32[288,128]{1,0:T(8,128)} %get-tuple-element.156), channel_id=1, source_target_pairs={{1,4},{4,1},{5,8},{8,5},{9,12},{12,9},{3,6},{6,3},{7,10},{10,7},{1... | collective-permute-start | bytes 442376 | tf_op jit(solution)/shard_map/ppermute | solution.py:162
  3.1 5.7 %collective-permute-start.1 = (f32[288,128]{1,0:T(8,128)}, f32[288,128]{1,0:T(8,128)S(1)}, u32[]{:S(2)}, u32[]{:S(2)}) collective-permute-start(f32[288,128]{1,0:T(8,128)} %get-tuple-element.157), channel_id=1, source_target_pairs={{0,1},{1,0},{2,3},{3,2},{4,5},{5,4},{6,7},{7,6},{8,9},{9,8},{10,11... | collective-permute-start | bytes 442376 | tf_op jit(solution)/shard_map/ppermute | solution.py:158
  8.8 1.1 %copy-start = (f32[4,128,384]{2,1,0:T(8,128)S(1)}, f32[4,128,384]{2,1,0:T(8,128)}, u32[]{:S(2)}) copy-start(f32[4,128,384]{2,1,0:T(8,128)} %get-tuple-element.158) | copy-start | bytes 2359300
  11.4 3.1 %copy-start.3 = (f32[6,32,384]{2,1,0:T(8,128)}, f32[6,32,384]{2,1,0:T(8,128)S(1)}, u32[]{:S(2)}) copy-start(f32[6,32,384]{2,1,0:T(8,128)S(1)} %fusion.50) | copy-start | bytes 884740
  11.4 2.7 %collective-permute-start.3 = (f32[3,32,128]{2,1,0:T(8,128)S(1)}, f32[3,32,128]{2,1,0:T(8,128)S(1)}, u32[]{:S(2)}, u32[]{:S(2)}) collective-permute-start(f32[3,32,128]{2,1,0:T(8,128)S(1)} %get-tuple-element.211), channel_id=1, source_target_pairs={{0,1},{1,0},{2,3},{3,2},{4,5},{5,4},{6,7},{7,6},{8,9},{9,8},{10,11... | collective-permute-start | bytes 147464 | tf_op jit(solution)/shard_map/ppermute | solution.py:158
  13.3 0.9 %collective-permute-start.2 = (f32[3,32,128]{2,1,0:T(8,128)S(1)}, f32[3,32,128]{2,1,0:T(8,128)S(1)}, u32[]{:S(2)}, u32[]{:S(2)}) collective-permute-start(f32[3,32,128]{2,1,0:T(8,128)S(1)} %get-tuple-element.212), channel_id=1, source_target_pairs={{1,4},{4,1},{5,8},{8,5},{9,12},{12,9},{3,6},{6,3},{7,10},{10,7},{1... | collective-permute-start | bytes 147464 | tf_op jit(solution)/shard_map/ppermute | solution.py:162
  14.6 0.9 %slice-start.1 = ((f32[6,32,384]{2,1,0:T(8,128)}), f32[6,32,128]{2,1,0:T(8,128)S(1)}, s32[]{:S(2)}) async-start(f32[6,32,384]{2,1,0:T(8,128)} %copy-done.3), calls=%async_computation.1 | async-start | bytes 196608 | tf_op jit(solution)/shard_map/slice | solution.py:169
  17.0 5.7 %copy-start.2 = (f32[6,32,384]{2,1,0:T(8,128)}, f32[6,32,384]{2,1,0:T(8,128)S(1)}, u32[]{:S(2)}) copy-start(f32[6,32,384]{2,1,0:T(8,128)S(1)} %fusion.48) | copy-start | bytes 884740
  17.0 5.6 %collective-permute-start.5 = (f32[3,32,128]{2,1,0:T(8,128)S(1)}, f32[3,32,128]{2,1,0:T(8,128)S(1)}, u32[]{:S(2)}, u32[]{:S(2)}) collective-permute-start(f32[3,32,128]{2,1,0:T(8,128)S(1)} %get-tuple-element.207), channel_id=1, source_target_pairs={{0,1},{1,0},{2,3},{3,2},{4,5},{5,4},{6,7},{7,6},{8,9},{9,8},{10,11... | collective-permute-start | bytes 147464 | tf_op jit(solution)/shard_map/ppermute | solution.py:158
  21.7 0.9 %collective-permute-start.4 = (f32[3,32,128]{2,1,0:T(8,128)S(1)}, f32[3,32,128]{2,1,0:T(8,128)S(1)}, u32[]{:S(2)}, u32[]{:S(2)}) collective-permute-start(f32[3,32,128]{2,1,0:T(8,128)S(1)} %get-tuple-element.208), channel_id=1, source_target_pairs={{1,4},{4,1},{5,8},{8,5},{9,12},{12,9},{3,6},{6,3},{7,10},{10,7},{1... | collective-permute-start | bytes 147464 | tf_op jit(solution)/shard_map/ppermute | solution.py:162
  23.1 0.9 %slice-start = ((f32[6,32,384]{2,1,0:T(8,128)}), f32[6,32,128]{2,1,0:T(8,128)S(1)}, s32[]{:S(2)}) async-start(f32[6,32,384]{2,1,0:T(8,128)} %copy-done.2), calls=%async_computation | async-start | bytes 196608 | tf_op jit(solution)/shard_map/slice | solution.py:169
  23.4 1.1 %copy-start.1 = (bf16[512,4,128]{2,1,0:T(4,128)(2,1)S(1)}, bf16[512,4,128]{2,1,0:T(4,128)(2,1)}, u32[]{:S(2)}) copy-start(bf16[512,4,128]{2,1,0:T(4,128)(2,1)} %param.31) | copy-start | bytes 1572868
  27.4 6.1 %collective-permute-start.6 = (f32[4,16,2,4,128]{4,1,0,3,2:T(8,128)S(1)}, f32[4,16,2,4,128]{4,1,0,3,2:T(8,128)S(1)}, u32[]{:S(2)}, u32[]{:S(2)}) collective-permute-start(f32[4,16,2,4,128]{4,1,0,3,2:T(8,128)S(1)} %select_bitcast_fusion), channel_id=1, source_target_pairs={{0,1},{1,0},{2,3},{3,2},{4,5},{5,4},{6,7},{7,6},{8,9},{9,8},{10,11... | collective-permute-start | bytes 786440 | tf_op jit(solution)/shard_map/ppermute | solution.py:44
  33.6 5.9 %collective-permute-start.7 = (f32[2,16,2,4,128]{4,1,3,2,0:T(8,128)S(1)}, f32[2,16,2,4,128]{4,1,3,2,0:T(8,128)S(1)}, u32[]{:S(2)}, u32[]{:S(2)}) collective-permute-start(f32[2,16,2,4,128]{4,1,3,2,0:T(8,128)S(1)} %fusion.12), channel_id=1, source_target_pairs={{0,4},{4,0},{8,12},{12,8},{1,5},{5,1},{9,13},{13,9},{2,6},{6,2},{1... | collective-permute-start | bytes 393224 | tf_op jit(solution)/shard_map/ppermute | solution.py:44
  39.5 5.4 %collective-permute-start.8 = (f32[1,16,2,4,128]{4,1,3,2,0:T(8,128)S(1)}, f32[1,16,2,4,128]{4,1,3,2,0:T(8,128)S(1)}, u32[]{:S(2)}, u32[]{:S(2)}) collective-permute-start(f32[1,16,2,4,128]{4,1,3,2,0:T(8,128)S(1)} %select_bitcast_fusion.1), channel_id=1, source_target_pairs={{0,8},{4,12},{8,0},{12,4},{1,9},{5,13},{9,1},{13,5},{2,10},{6,14},... | collective-permute-start | bytes 196616 | tf_op jit(solution)/shard_map/ppermute | solution.py:44

commit v13 on v12

--- a/solution.py
+++ b/solution.py
@@ -60,7 +60,7 @@
             part = expect[out, :, block * tile_size : (block + 1) * tile_size]
             pieces.append((part.astype(jnp.float32) * scales[out, region]).astype(jnp.bfloat16))
         half = jnp.concatenate(pieces, 0)
-        rows[block] = half.astype(jnp.float32)
+        rows[:, block * tile_size : (block + 1) * tile_size] = half
         carried = [
             jnp.dot(half, tiles[block, slot], preferred_element_type=jnp.float32)
             for slot in range(band_count)
@@ -110,7 +110,7 @@
         prepare_kernel,
         out_shape=(
             jax.ShapeDtypeStruct((block_count, tile_size, 3 * tile_size), jnp.float32),
-            jax.ShapeDtypeStruct((block_count, row_count, tile_size), jnp.float32),
+            jax.ShapeDtypeStruct((row_count, block_count * tile_size), jnp.bfloat16),
             jax.ShapeDtypeStruct((block_count, row_count, tile_size), jnp.float32),
             edge,
             edge,
@@ -225,7 +225,6 @@
         from_low, from_high = swap_edges(second_part, first_part)
     edge_in = jnp.zeros_like(inner[1:-1])
     levels = [
-        rows,
         inner
         + jnp.concatenate([from_low[None, :row_count], edge_in, from_high[None, :row_count]], 0),
     ]
@@ -251,9 +250,10 @@
         [level.transpose(1, 0, 2).reshape(row_count, state_count) for level in levels], 0
     )
     product = split_product(stacked, flat_start)
+    first = jnp.dot(rows, flat_start, preferred_element_type=jnp.float32)
     pieces = [
         piece.reshape(output_count, expect_rows, input_count, horizon).transpose(1, 0, 2, 3)
-        for piece in jnp.split(product, sections, 0)
+        for piece in [first] + jnp.split(product, sections - 1, 0)
     ]
     partial_news = jnp.concatenate(pieces, axis=0)
     jacobian = diagonal_sums(partial_news)

time: 46 us -> 44.8 us (0.974)
  starting transfers between devices: 22.9 us -> 20.8 us
  waiting for transfers between devices: 8.2 us -> 9.34 us
  local copies, waits for them, and re-layouts: 4.59 us -> 4.01 us
    ppermute x3, starting transfers between devices: 9.85 us -> 5.75 us  [halving_scatter(): held = keep + lax.ppermute(send, axis, pairs)]
    ppermute x3, starting transfers between devices: 10.9 us -> 13.1 us  [swap_links(): on_chip = lax.ppermute(chip_part, 'horizon', [(0, 1), (1, 0)])]
    ppermute x3, waiting for transfers between devices: 0.61 us -> 1.74 us  [swap_links(): on_chip = lax.ppermute(chip_part, 'horizon', [(0, 1), (1, 0)])]
    unnamed x19 -> x20, local copies, waits for them, and re-layouts: 2.34 us -> 1.55 us
where the time goes in v13:
time: 44.8 us; the launch traced here: 44.4 us
  starting transfers between devices  20.8 us (46%)
  waiting for transfers between devices  9.34 us (21%)
  matrix products  5.04 us (11%)
  local copies, waits for them, and re-layouts  4.01 us (9%)
  Pallas kernels  2.41 us (5%)
  other arithmetic  1.97 us (4%)
  between operations  0.84 us (2%)
    ppermute x3, starting transfers between devices, swap_links(): on_chip = lax.ppermute(chip_part, 'horizon', [(0, 1), (1, 0)])  13.1 us
    ppermute x3, waiting for transfers between devices, halving_scatter(): held = keep + lax.ppermute(send, axis, pairs)  7.59 us
    ppermute x3, starting transfers between devices, halving_scatter(): held = keep + lax.ppermute(send, axis, pairs)  5.75 us
    dot_general x10, matrix products, band_parts(): jnp.einsum('cru,cun->crn', rows, moves, precision=lax.Precision.HIGH)  3.92 us
    pallas_call x1, Pallas kernels, prepare(): pl.pallas_call(prepare_kernel, out_shape=(jax.ShapeDtypeStruct((block_cou...  2.41 us
    ppermute x3, starting transfers between devices, swap_links(): across = lax.ppermute(cross_part, ('state', 'horizon'), pairs)  1.99 us
    ppermute x3, waiting for transfers between devices, swap_links(): on_chip = lax.ppermute(chip_part, 'horizon', [(0, 1), (1, 0)])  1.74 us
    unnamed x20, local copies, waits for them, and re-layouts  1.55 us
  transfers between devices with their start and end apart: 9, of which 6 were waited for; matrix products, arithmetic and copies ran while one was open for 2% of the time, Pallas kernels for 0%

profile of v13, /device:TPU:0, one launch (start us, length us, event | category | flops | bytes accessed | tf_op | source)
XLA Modules:
  0.0 44.4 jit_solution(16618743005311460820)
XLA Ops:
  0.0 2.4 %shard_map.73 = (f32[4,128,384]{2,1,0:T(8,128)}, bf16[32,512]{1,0:T(8,128)(2,1)}, f32[4,32,128]{2,1,0:T(8,128)}, f32[288,128]{1,0:T(8,128)}, f32[288,128]{1,0:T(8,128)}) custom-call(s32[1]{0:T(128)} %bitcast.flip, s32[4]{0:T(128)} %counts.1, s32[4,4]{1,0:T(4,128)} %offsets.1, s32[4]{0:T(128)} %regions.1, f32[2,16]{1,0:T(2,128)} %bitcast.159, ...), custom_call_target="tpu_custom_call" | custom-call | tf_op jit(solution)/shard_map/pallas_call | solution.py:109
  2.4 0.7 %collective-permute-start = (f32[288,128]{1,0:T(8,128)}, f32[288,128]{1,0:T(8,128)S(1)}, u32[]{:S(2)}, u32[]{:S(2)}) collective-permute-start(f32[288,128]{1,0:T(8,128)} %get-tuple-element.156), channel_id=1, source_target_pairs={{1,4},{4,1},{5,8},{8,5},{9,12},{12,9},{3,6},{6,3},{7,10},{10,7},{1... | collective-permute-start | bytes 442376 | tf_op jit(solution)/shard_map/ppermute | solution.py:162
  3.1 4.4 %collective-permute-start.1 = (f32[288,128]{1,0:T(8,128)}, f32[288,128]{1,0:T(8,128)S(1)}, u32[]{:S(2)}, u32[]{:S(2)}) collective-permute-start(f32[288,128]{1,0:T(8,128)} %get-tuple-element.157), channel_id=1, source_target_pairs={{0,1},{1,0},{2,3},{3,2},{4,5},{5,4},{6,7},{7,6},{8,9},{9,8},{10,11... | collective-permute-start | bytes 442376 | tf_op jit(solution)/shard_map/ppermute | solution.py:158
  9.3 0.6 %copy-done = f32[4,128,384]{2,1,0:T(8,128)S(1)} copy-done((f32[4,128,384]{2,1,0:T(8,128)S(1)}, f32[4,128,384]{2,1,0:T(8,128)}, u32[]{:S(2)}) %copy-start) | copy-done | bytes 786456
  10.4 0.4 fusion.51
  10.9 0.4 fusion.50
  11.4 0.7 %collective-permute-start.2 = (f32[3,32,128]{2,1,0:T(8,128)S(1)}, f32[3,32,128]{2,1,0:T(8,128)S(1)}, u32[]{:S(2)}, u32[]{:S(2)}) collective-permute-start(f32[3,32,128]{2,1,0:T(8,128)S(1)} %get-tuple-element.213), channel_id=1, source_target_pairs={{1,4},{4,1},{5,8},{8,5},{9,12},{12,9},{3,6},{6,3},{7,10},{10,7},{1... | collective-permute-start | bytes 147464 | tf_op jit(solution)/shard_map/ppermute | solution.py:162
  12.1 4.8 %collective-permute-start.3 = (f32[3,32,128]{2,1,0:T(8,128)S(1)}, f32[3,32,128]{2,1,0:T(8,128)S(1)}, u32[]{:S(2)}, u32[]{:S(2)}) collective-permute-start(f32[3,32,128]{2,1,0:T(8,128)S(1)} %get-tuple-element.212), channel_id=1, source_target_pairs={{0,1},{1,0},{2,3},{3,2},{4,5},{5,4},{6,7},{7,6},{8,9},{9,8},{10,11... | collective-permute-start | bytes 147464 | tf_op jit(solution)/shard_map/ppermute | solution.py:158
  16.9 0.8 %collective-permute-done.3 = f32[3,32,128]{2,1,0:T(8,128)S(1)} collective-permute-done((f32[3,32,128]{2,1,0:T(8,128)S(1)}, f32[3,32,128]{2,1,0:T(8,128)S(1)}, u32[]{:S(2)}, u32[]{:S(2)}) %collective-permute-start.3) | collective-permute-done | bytes 49184 | tf_op jit(solution)/shard_map/ppermute | solution.py:158
  18.6 0.5 %slice-done.1 = f32[6,32,128]{2,1,0:T(8,128)S(1)} async-done(((f32[6,32,384]{2,1,0:T(8,128)}), f32[6,32,128]{2,1,0:T(8,128)S(1)}, s32[]{:S(2)}) %slice-start.1) | async-done | bytes 98328 | tf_op jit(solution)/shard_map/slice | solution.py:169
  19.1 0.4 fusion.15
  19.6 0.4 fusion.49
  20.1 0.4 fusion.48
  20.6 0.7 %collective-permute-start.4 = (f32[3,32,128]{2,1,0:T(8,128)S(1)}, f32[3,32,128]{2,1,0:T(8,128)S(1)}, u32[]{:S(2)}, u32[]{:S(2)}) collective-permute-start(f32[3,32,128]{2,1,0:T(8,128)S(1)} %get-tuple-element.209), channel_id=1, source_target_pairs={{1,4},{4,1},{5,8},{8,5},{9,12},{12,9},{3,6},{6,3},{7,10},{10,7},{1... | collective-permute-start | bytes 147464 | tf_op jit(solution)/shard_map/ppermute | solution.py:162
  21.3 3.9 %collective-permute-start.5 = (f32[3,32,128]{2,1,0:T(8,128)S(1)}, f32[3,32,128]{2,1,0:T(8,128)S(1)}, u32[]{:S(2)}, u32[]{:S(2)}) collective-permute-start(f32[3,32,128]{2,1,0:T(8,128)S(1)} %get-tuple-element.208), channel_id=1, source_target_pairs={{0,1},{1,0},{2,3},{3,2},{4,5},{5,4},{6,7},{7,6},{8,9},{9,8},{10,11... | collective-permute-start | bytes 147464 | tf_op jit(solution)/shard_map/ppermute | solution.py:158
  25.2 0.8 %collective-permute-done.5 = f32[3,32,128]{2,1,0:T(8,128)S(1)} collective-permute-done((f32[3,32,128]{2,1,0:T(8,128)S(1)}, f32[3,32,128]{2,1,0:T(8,128)S(1)}, u32[]{:S(2)}, u32[]{:S(2)}) %collective-permute-start.5) | collective-permute-done | bytes 49184 | tf_op jit(solution)/shard_map/ppermute | solution.py:158
  26.9 0.5 %slice-done = f32[6,32,128]{2,1,0:T(8,128)S(1)} async-done(((f32[6,32,384]{2,1,0:T(8,128)}), f32[6,32,128]{2,1,0:T(8,128)S(1)}, s32[]{:S(2)}) %slice-start) | async-done | bytes 98328 | tf_op jit(solution)/shard_map/slice | solution.py:169
  30.3 0.9 %collective-permute-start.6 = (f32[4,16,2,4,128]{4,1,3,2,0:T(8,128)S(1)}, f32[4,16,2,4,128]{4,1,3,2,0:T(8,128)S(1)}, u32[]{:S(2)}, u32[]{:S(2)}) collective-permute-start(f32[4,16,2,4,128]{4,1,3,2,0:T(8,128)S(1)} %select_bitcast_fusion), channel_id=1, source_target_pairs={{0,1},{1,0},{2,3},{3,2},{4,5},{5,4},{6,7},{7,6},{8,9},{9,8},{10,11... | collective-permute-start | bytes 786440 | tf_op jit(solution)/shard_map/ppermute | solution.py:44
  31.2 1.2 %collective-permute-done.6 = f32[4,16,2,4,128]{4,1,3,2,0:T(8,128)S(1)} collective-permute-done((f32[4,16,2,4,128]{4,1,3,2,0:T(8,128)S(1)}, f32[4,16,2,4,128]{4,1,3,2,0:T(8,128)S(1)}, u32[]{:S(2)}, u32[]{:S(2)}) %collective-permute-start.6) | collective-permute-done | bytes 262176 | tf_op jit(solution)/shard_map/ppermute | solution.py:44
  32.4 2.1 %collective-permute-start.7 = (f32[2,16,2,4,128]{4,1,3,2,0:T(8,128)S(1)}, f32[2,16,2,4,128]{4,1,3,2,0:T(8,128)S(1)}, u32[]{:S(2)}, u32[]{:S(2)}) collective-permute-start(f32[2,16,2,4,128]{4,1,3,2,0:T(8,128)S(1)} %select_bitcast_fusion.1), channel_id=1, source_target_pairs={{0,4},{4,0},{8,12},{12,8},{1,5},{5,1},{9,13},{13,9},{2,6},{6,2},{1... | collective-permute-start | bytes 393224 | tf_op jit(solution)/shard_map/ppermute | solution.py:44
  34.5 3.8 %collective-permute-done.7 = f32[2,16,2,4,128]{4,1,3,2,0:T(8,128)S(1)} collective-permute-done((f32[2,16,2,4,128]{4,1,3,2,0:T(8,128)S(1)}, f32[2,16,2,4,128]{4,1,3,2,0:T(8,128)S(1)}, u32[]{:S(2)}, u32[]{:S(2)}) %collective-permute-start.7) | collective-permute-done | bytes 131104 | tf_op jit(solution)/shard_map/ppermute | solution.py:44
  38.3 2.8 %collective-permute-start.8 = (f32[1,16,2,4,128]{4,1,3,2,0:T(8,128)S(1)}, f32[1,16,2,4,128]{4,1,3,2,0:T(8,128)S(1)}, u32[]{:S(2)}, u32[]{:S(2)}) collective-permute-start(f32[1,16,2,4,128]{4,1,3,2,0:T(8,128)S(1)} %select_bitcast_fusion.2), channel_id=1, source_target_pairs={{0,8},{4,12},{8,0},{12,4},{1,9},{5,13},{9,1},{13,5},{2,10},{6,14},... | collective-permute-start | bytes 196616 | tf_op jit(solution)/shard_map/ppermute | solution.py:44
  41.1 2.6 %collective-permute-done.8 = f32[1,16,2,4,128]{4,1,3,2,0:T(8,128)S(1)} collective-permute-done((f32[1,16,2,4,128]{4,1,3,2,0:T(8,128)S(1)}, f32[1,16,2,4,128]{4,1,3,2,0:T(8,128)S(1)}, u32[]{:S(2)}, u32[]{:S(2)}) %collective-permute-start.8) | collective-permute-done | bytes 65568 | tf_op jit(solution)/shard_map/ppermute | solution.py:44
  43.8 0.7 %copy.34 = f32[16,2,4,128]{3,2,1,0:T(4,128)} copy(f32[16,2,4,128]{3,0,2,1:T(8,128)S(1)} %fusion.33) | data formatting | bytes 131072 | tf_op jit(solution)/shard_map/reshape | solution.py:46
  (120 shorter events, 6.8 us)
Async XLA Ops:
  0.0 7.5 %copy-start.1 = (bf16[512,4,128]{2,1,0:T(4,128)(2,1)S(1)}, bf16[512,4,128]{2,1,0:T(4,128)(2,1)}, u32[]{:S(2)}) copy-start(bf16[512,4,128]{2,1,0:T(4,128)(2,1)} %param.31) | copy-start | bytes 1572868
  2.4 6.2 %collective-permute-start = (f32[288,128]{1,0:T(8,128)}, f32[288,128]{1,0:T(8,128)S(1)}, u32[]{:S(2)}, u32[]{:S(2)}) collective-permute-start(f32[288,128]{1,0:T(8,128)} %get-tuple-element.156), channel_id=1, source_target_pairs={{1,4},{4,1},{5,8},{8,5},{9,12},{12,9},{3,6},{6,3},{7,10},{10,7},{1... | collective-permute-start | bytes 442376 | tf_op jit(solution)/shard_map/ppermute | solution.py:162
  3.1 5.7 %collective-permute-start.1 = (f32[288,128]{1,0:T(8,128)}, f32[288,128]{1,0:T(8,128)S(1)}, u32[]{:S(2)}, u32[]{:S(2)}) collective-permute-start(f32[288,128]{1,0:T(8,128)} %get-tuple-element.157), channel_id=1, source_target_pairs={{0,1},{1,0},{2,3},{3,2},{4,5},{5,4},{6,7},{7,6},{8,9},{9,8},{10,11... | collective-permute-start | bytes 442376 | tf_op jit(solution)/shard_map/ppermute | solution.py:158
  7.6 0.8 %copy-start.5 = (bf16[32,512]{1,0:T(8,128)(2,1)S(1)}, bf16[32,512]{1,0:T(8,128)(2,1)}, u32[]{:S(2)}) copy-start(bf16[32,512]{1,0:T(8,128)(2,1)} %get-tuple-element.154) | copy-start | bytes 98308
  8.4 0.8 %copy-start.4 = (f32[4,32,128]{2,1,0:T(8,128)S(1)}, f32[4,32,128]{2,1,0:T(8,128)}, u32[]{:S(2)}) copy-start(f32[4,32,128]{2,1,0:T(8,128)} %get-tuple-element.155) | copy-start | bytes 196612
  8.8 1.1 %copy-start = (f32[4,128,384]{2,1,0:T(8,128)S(1)}, f32[4,128,384]{2,1,0:T(8,128)}, u32[]{:S(2)}) copy-start(f32[4,128,384]{2,1,0:T(8,128)} %get-tuple-element.158) | copy-start | bytes 2359300
  11.4 6.8 %copy-start.3 = (f32[6,32,384]{2,1,0:T(8,128)}, f32[6,32,384]{2,1,0:T(8,128)S(1)}, u32[]{:S(2)}) copy-start(f32[6,32,384]{2,1,0:T(8,128)S(1)} %fusion.50) | copy-start | bytes 884740
  11.4 5.5 %collective-permute-start.2 = (f32[3,32,128]{2,1,0:T(8,128)S(1)}, f32[3,32,128]{2,1,0:T(8,128)S(1)}, u32[]{:S(2)}, u32[]{:S(2)}) collective-permute-start(f32[3,32,128]{2,1,0:T(8,128)S(1)} %get-tuple-element.213), channel_id=1, source_target_pairs={{1,4},{4,1},{5,8},{8,5},{9,12},{12,9},{3,6},{6,3},{7,10},{10,7},{1... | collective-permute-start | bytes 147464 | tf_op jit(solution)/shard_map/ppermute | solution.py:162
  12.1 5.7 %collective-permute-start.3 = (f32[3,32,128]{2,1,0:T(8,128)S(1)}, f32[3,32,128]{2,1,0:T(8,128)S(1)}, u32[]{:S(2)}, u32[]{:S(2)}) collective-permute-start(f32[3,32,128]{2,1,0:T(8,128)S(1)} %get-tuple-element.212), channel_id=1, source_target_pairs={{0,1},{1,0},{2,3},{3,2},{4,5},{5,4},{6,7},{7,6},{8,9},{9,8},{10,11... | collective-permute-start | bytes 147464 | tf_op jit(solution)/shard_map/ppermute | solution.py:158
  18.2 0.9 %slice-start.1 = ((f32[6,32,384]{2,1,0:T(8,128)}), f32[6,32,128]{2,1,0:T(8,128)S(1)}, s32[]{:S(2)}) async-start(f32[6,32,384]{2,1,0:T(8,128)} %copy-done.3), calls=%async_computation.1 | async-start | bytes 196608 | tf_op jit(solution)/shard_map/slice | solution.py:169
  20.6 5.5 %copy-start.2 = (f32[6,32,384]{2,1,0:T(8,128)}, f32[6,32,384]{2,1,0:T(8,128)S(1)}, u32[]{:S(2)}) copy-start(f32[6,32,384]{2,1,0:T(8,128)S(1)} %fusion.48) | copy-start | bytes 884740
  20.6 4.6 %collective-permute-start.4 = (f32[3,32,128]{2,1,0:T(8,128)S(1)}, f32[3,32,128]{2,1,0:T(8,128)S(1)}, u32[]{:S(2)}, u32[]{:S(2)}) collective-permute-start(f32[3,32,128]{2,1,0:T(8,128)S(1)} %get-tuple-element.209), channel_id=1, source_target_pairs={{1,4},{4,1},{5,8},{8,5},{9,12},{12,9},{3,6},{6,3},{7,10},{10,7},{1... | collective-permute-start | bytes 147464 | tf_op jit(solution)/shard_map/ppermute | solution.py:162
  21.3 4.7 %collective-permute-start.5 = (f32[3,32,128]{2,1,0:T(8,128)S(1)}, f32[3,32,128]{2,1,0:T(8,128)S(1)}, u32[]{:S(2)}, u32[]{:S(2)}) collective-permute-start(f32[3,32,128]{2,1,0:T(8,128)S(1)} %get-tuple-element.208), channel_id=1, source_target_pairs={{0,1},{1,0},{2,3},{3,2},{4,5},{5,4},{6,7},{7,6},{8,9},{9,8},{10,11... | collective-permute-start | bytes 147464 | tf_op jit(solution)/shard_map/ppermute | solution.py:158
  26.5 0.9 %slice-start = ((f32[6,32,384]{2,1,0:T(8,128)}), f32[6,32,128]{2,1,0:T(8,128)S(1)}, s32[]{:S(2)}) async-start(f32[6,32,384]{2,1,0:T(8,128)} %copy-done.2), calls=%async_computation | async-start | bytes 196608 | tf_op jit(solution)/shard_map/slice | solution.py:169
  30.3 2.0 %collective-permute-start.6 = (f32[4,16,2,4,128]{4,1,3,2,0:T(8,128)S(1)}, f32[4,16,2,4,128]{4,1,3,2,0:T(8,128)S(1)}, u32[]{:S(2)}, u32[]{:S(2)}) collective-permute-start(f32[4,16,2,4,128]{4,1,3,2,0:T(8,128)S(1)} %select_bitcast_fusion), channel_id=1, source_target_pairs={{0,1},{1,0},{2,3},{3,2},{4,5},{5,4},{6,7},{7,6},{8,9},{9,8},{10,11... | collective-permute-start | bytes 786440 | tf_op jit(solution)/shard_map/ppermute | solution.py:44
  32.4 5.9 %collective-permute-start.7 = (f32[2,16,2,4,128]{4,1,3,2,0:T(8,128)S(1)}, f32[2,16,2,4,128]{4,1,3,2,0:T(8,128)S(1)}, u32[]{:S(2)}, u32[]{:S(2)}) collective-permute-start(f32[2,16,2,4,128]{4,1,3,2,0:T(8,128)S(1)} %select_bitcast_fusion.1), channel_id=1, source_target_pairs={{0,4},{4,0},{8,12},{12,8},{1,5},{5,1},{9,13},{13,9},{2,6},{6,2},{1... | collective-permute-start | bytes 393224 | tf_op jit(solution)/shard_map/ppermute | solution.py:44
  38.3 5.4 %collective-permute-start.8 = (f32[1,16,2,4,128]{4,1,3,2,0:T(8,128)S(1)}, f32[1,16,2,4,128]{4,1,3,2,0:T(8,128)S(1)}, u32[]{:S(2)}, u32[]{:S(2)}) collective-permute-start(f32[1,16,2,4,128]{4,1,3,2,0:T(8,128)S(1)} %select_bitcast_fusion.2), channel_id=1, source_target_pairs={{0,8},{4,12},{8,0},{12,4},{1,9},{5,13},{9,1},{13,5},{2,10},{6,14},... | collective-permute-start | bytes 196616 | tf_op jit(solution)/shard_map/ppermute | solution.py:44

commit v14 on v13

--- a/solution.py
+++ b/solution.py
@@ -164,9 +164,10 @@
 
 
 def band_parts(rows, moves):
-    parts = jnp.einsum("cru,cun->crn", rows, moves, precision=lax.Precision.HIGH)
     size = rows.shape[-1]
-    down, same, up = parts[..., :size], parts[..., size : 2 * size], parts[..., 2 * size :]
+    split = moves.reshape(moves.shape[:2] + (3, size))
+    parts = jnp.einsum("cru,cudv->dcrv", rows, split, precision=lax.Precision.HIGH)
+    down, same, up = parts[0], parts[1], parts[2]
     zero = jnp.zeros_like(same[:1])
     inner = same + jnp.concatenate([down[1:], zero], 0) + jnp.concatenate([zero, up[:-1]], 0)
     return inner, down, up

time: 44.8 us -> 45 us (level)
  starting transfers between devices: 20.8 us -> 19 us
  local copies, waits for them, and re-layouts: 4.01 us -> 5.35 us
  matrix products: 5.04 us -> 5.85 us
    ppermute x3, starting transfers between devices: 13.1 us -> 11.3 us  [swap_links(): on_chip = lax.ppermute(chip_part, 'horizon', [(0, 1), (1, 0)])]
    pallas_call x0 -> x1, local copies, waits for them, and re-layouts: none -> 1.39 us  [prepare(): pl.pallas_call(prepare_kernel, out_shape=(jax.ShapeDtypeStruct((block_cou...]
    slice x4 -> x0, local copies, waits for them, and re-layouts: 0.95 us -> none  [band_parts(): parts[..., size:2 * size]]
    dot_general x10, matrix products: 3.92 us -> 4.74 us  [band_parts(): jnp.einsum('cru,cudv->dcrv', rows, split, precision=lax.Precision.HIGH)]
    concatenate x0 -> x5, local copies, waits for them, and re-layouts: none -> 0.78 us  [the longest x3 0.53 us: shards(): jnp.concatenate([jnp.concatenate([blank, left_self, left_up], 1)[None], m...]
    unnamed x20 -> x14, local copies, waits for them, and re-layouts: 1.55 us -> 1.64 us
  transfers between devices with their start and end apart: 9 -> 9, of which waited for: 6 -> 5; matrix products, arithmetic and copies ran while one was open for 2% -> 5% of each run, Pallas kernels for 0% -> 0%
where the time goes in v14:
time: 45 us; the launch traced here: 44.6 us
  starting transfers between devices  19 us (42%)
  waiting for transfers between devices  9.29 us (21%)
  matrix products  5.85 us (13%)
  local copies, waits for them, and re-layouts  5.35 us (12%)
  Pallas kernels  2.32 us (5%)
  other arithmetic  1.99 us (4%)
  between operations  0.85 us (2%)
    ppermute x3, starting transfers between devices, swap_links(): on_chip = lax.ppermute(chip_part, 'horizon', [(0, 1), (1, 0)])  11.3 us
    ppermute x3, waiting for transfers between devices, halving_scatter(): held = keep + lax.ppermute(send, axis, pairs)  7.65 us
    ppermute x3, starting transfers between devices, halving_scatter(): held = keep + lax.ppermute(send, axis, pairs)  5.69 us
    dot_general x10, matrix products, band_parts(): jnp.einsum('cru,cudv->dcrv', rows, split, precision=lax.Precision.HIGH)  4.74 us
    pallas_call x1, Pallas kernels, prepare(): pl.pallas_call(prepare_kernel, out_shape=(jax.ShapeDtypeStruct((block_cou...  2.32 us
    ppermute x3, starting transfers between devices, swap_links(): across = lax.ppermute(cross_part, ('state', 'horizon'), pairs)  1.99 us
    unnamed x14, local copies, waits for them, and re-layouts  1.64 us
    ppermute x3, waiting for transfers between devices, swap_links(): on_chip = lax.ppermute(chip_part, 'horizon', [(0, 1), (1, 0)])  1.64 us
  transfers between devices with their start and end apart: 9, of which 5 were waited for; matrix products, arithmetic and copies ran while one was open for 5% of the time, Pallas kernels for 0%

profile of v14, /device:TPU:0, one launch (start us, length us, event | category | flops | bytes accessed | tf_op | source)
XLA Modules:
  0.0 44.6 jit_solution(2875837122948880330)
XLA Ops:
  0.0 2.3 %shard_map.73 = (f32[4,128,384]{2,1,0:T(8,128)}, bf16[32,512]{1,0:T(8,128)(2,1)}, f32[4,32,128]{2,1,0:T(8,128)}, f32[288,128]{1,0:T(8,128)}, f32[288,128]{1,0:T(8,128)}) custom-call(s32[1]{0:T(128)} %bitcast.flip, s32[4]{0:T(128)} %counts.1, s32[4,4]{1,0:T(4,128)} %offsets.1, s32[4]{0:T(128)} %regions.1, f32[2,16]{1,0:T(2,128)} %bitcast.329, ...), custom_call_target="tpu_custom_call" | custom-call | tf_op jit(solution)/shard_map/pallas_call | solution.py:109
  2.3 0.7 %collective-permute-start = (f32[288,128]{1,0:T(8,128)}, f32[288,128]{1,0:T(8,128)S(1)}, u32[]{:S(2)}, u32[]{:S(2)}) collective-permute-start(f32[288,128]{1,0:T(8,128)} %get-tuple-element.156), channel_id=1, source_target_pairs={{1,4},{4,1},{5,8},{8,5},{9,12},{12,9},{3,6},{6,3},{7,10},{10,7},{1... | collective-permute-start | bytes 442376 | tf_op jit(solution)/shard_map/ppermute | solution.py:162
  3.0 4.4 %collective-permute-start.1 = (f32[288,128]{1,0:T(8,128)}, f32[288,128]{1,0:T(8,128)S(1)}, u32[]{:S(2)}, u32[]{:S(2)}) collective-permute-start(f32[288,128]{1,0:T(8,128)} %get-tuple-element.157), channel_id=1, source_target_pairs={{0,1},{1,0},{2,3},{3,2},{4,5},{5,4},{6,7},{7,6},{8,9},{9,8},{10,11... | collective-permute-start | bytes 442376 | tf_op jit(solution)/shard_map/ppermute | solution.py:158
  7.4 1.4 %copy.36 = f32[4,128,384]{1,2,0:T(8,128)S(1)} copy(f32[4,128,384]{2,1,0:T(8,128)} %get-tuple-element.158) | data formatting | bytes 1572864 | tf_op jit(solution)/shard_map/pallas_call | solution.py:109
  9.1 0.8 %copy-done = bf16[512,4,128]{2,1,0:T(4,128)(2,1)S(1)} copy-done((bf16[512,4,128]{2,1,0:T(4,128)(2,1)S(1)}, bf16[512,4,128]{2,1,0:T(4,128)(2,1)}, u32[]{:S(2)}) %copy-start) | copy-done | bytes 524312
  12.5 0.4 convolution_bitcast_fusion.4
  13.6 0.7 %collective-permute-start.2 = (f32[3,32,128]{2,1,0:T(8,128)S(1)}, f32[3,32,128]{2,1,0:T(8,128)S(1)}, u32[]{:S(2)}, u32[]{:S(2)}) collective-permute-start(f32[3,32,128]{2,1,0:T(8,128)S(1)} %get-tuple-element.213), channel_id=1, source_target_pairs={{1,4},{4,1},{5,8},{8,5},{9,12},{12,9},{3,6},{6,3},{7,10},{10,7},{1... | collective-permute-start | bytes 147464 | tf_op jit(solution)/shard_map/ppermute | solution.py:162
  14.2 3.0 %collective-permute-start.3 = (f32[3,32,128]{2,1,0:T(8,128)S(1)}, f32[3,32,128]{2,1,0:T(8,128)S(1)}, u32[]{:S(2)}, u32[]{:S(2)}) collective-permute-start(f32[3,32,128]{2,1,0:T(8,128)S(1)} %get-tuple-element.212), channel_id=1, source_target_pairs={{0,1},{1,0},{2,3},{3,2},{4,5},{5,4},{6,7},{7,6},{8,9},{9,8},{10,11... | collective-permute-start | bytes 147464 | tf_op jit(solution)/shard_map/ppermute | solution.py:158
  17.3 0.8 %collective-permute-done.3 = f32[3,32,128]{2,1,0:T(8,128)S(1)} collective-permute-done((f32[3,32,128]{2,1,0:T(8,128)S(1)}, f32[3,32,128]{2,1,0:T(8,128)S(1)}, u32[]{:S(2)}, u32[]{:S(2)}) %collective-permute-start.3) | collective-permute-done | bytes 49184 | tf_op jit(solution)/shard_map/ppermute | solution.py:158
  18.2 0.5 %convolution_bitcast_fusion.9 = f32[3,4,32,128]{3,2,1,0:T(8,128)S(1)} fusion(f32[4,128,3,128]{1,3,2,0:T(8,128)S(1)} %bitcast.310, f32[4,32,128]{2,1,0:T(8,128)S(1)} %slice_dynamic-update-slice_fusion.1), kind=kOutput, calls=%fused_computation.12 | convolution fusion | flops 37748736 | bytes 1048576 | tf_op jit(solution)/shard_map/cru,cudv->dcrv/dot_general | solution.py:169
  18.8 0.5 %convolution_bitcast_fusion.8 = f32[3,4,32,128]{3,2,1,0:T(8,128)S(1)} fusion(f32[4,128,3,128]{1,3,2,0:T(8,128)S(1)} %bitcast.311, f32[4,32,128]{2,1,0:T(8,128)S(1)} %fusion.71), kind=kOutput, calls=%fused_computation.11 | convolution fusion | flops 37748736 | bytes 1048576 | tf_op jit(solution)/shard_map/cru,cudv->dcrv/dot_general | solution.py:169
  19.4 0.4 convolution_bitcast_fusion.2
  20.9 0.7 %collective-permute-start.4 = (f32[3,32,128]{2,1,0:T(8,128)S(1)}, f32[3,32,128]{2,1,0:T(8,128)S(1)}, u32[]{:S(2)}, u32[]{:S(2)}) collective-permute-start(f32[3,32,128]{2,1,0:T(8,128)S(1)} %get-tuple-element.209), channel_id=1, source_target_pairs={{1,4},{4,1},{5,8},{8,5},{9,12},{12,9},{3,6},{6,3},{7,10},{10,7},{1... | collective-permute-start | bytes 147464 | tf_op jit(solution)/shard_map/ppermute | solution.py:162
  21.6 3.9 %collective-permute-start.5 = (f32[3,32,128]{2,1,0:T(8,128)S(1)}, f32[3,32,128]{2,1,0:T(8,128)S(1)}, u32[]{:S(2)}, u32[]{:S(2)}) collective-permute-start(f32[3,32,128]{2,1,0:T(8,128)S(1)} %get-tuple-element.208), channel_id=1, source_target_pairs={{0,1},{1,0},{2,3},{3,2},{4,5},{5,4},{6,7},{7,6},{8,9},{9,8},{10,11... | collective-permute-start | bytes 147464 | tf_op jit(solution)/shard_map/ppermute | solution.py:158
  25.5 0.8 %collective-permute-done.5 = f32[3,32,128]{2,1,0:T(8,128)S(1)} collective-permute-done((f32[3,32,128]{2,1,0:T(8,128)S(1)}, f32[3,32,128]{2,1,0:T(8,128)S(1)}, u32[]{:S(2)}, u32[]{:S(2)}) %collective-permute-start.5) | collective-permute-done | bytes 49184 | tf_op jit(solution)/shard_map/ppermute | solution.py:158
  26.4 0.5 %convolution_bitcast_fusion.7 = f32[3,4,32,128]{3,2,1,0:T(8,128)S(1)} fusion(f32[4,128,3,128]{1,3,2,0:T(8,128)S(1)} %bitcast.312, f32[4,32,128]{2,1,0:T(8,128)S(1)} %slice_dynamic-update-slice_fusion), kind=kOutput, calls=%fused_computation.10 | convolution fusion | flops 37748736 | bytes 1048576 | tf_op jit(solution)/shard_map/cru,cudv->dcrv/dot_general | solution.py:169
  27.0 0.5 %convolution_bitcast_fusion.6 = f32[3,4,32,128]{3,2,1,0:T(8,128)S(1)} fusion(f32[4,128,3,128]{1,3,2,0:T(8,128)S(1)} %bitcast.313, f32[4,32,128]{2,1,0:T(8,128)S(1)} %fusion.67), kind=kOutput, calls=%fused_computation.9 | convolution fusion | flops 37748736 | bytes 1048576 | tf_op jit(solution)/shard_map/cru,cudv->dcrv/dot_general | solution.py:169
  30.5 0.9 %collective-permute-start.6 = (f32[4,16,2,4,128]{4,1,3,2,0:T(8,128)S(1)}, f32[4,16,2,4,128]{4,1,3,2,0:T(8,128)S(1)}, u32[]{:S(2)}, u32[]{:S(2)}) collective-permute-start(f32[4,16,2,4,128]{4,1,3,2,0:T(8,128)S(1)} %select_bitcast_fusion), channel_id=1, source_target_pairs={{0,1},{1,0},{2,3},{3,2},{4,5},{5,4},{6,7},{7,6},{8,9},{9,8},{10,11... | collective-permute-start | bytes 786440 | tf_op jit(solution)/shard_map/ppermute | solution.py:44
  31.4 1.2 %collective-permute-done.6 = f32[4,16,2,4,128]{4,1,3,2,0:T(8,128)S(1)} collective-permute-done((f32[4,16,2,4,128]{4,1,3,2,0:T(8,128)S(1)}, f32[4,16,2,4,128]{4,1,3,2,0:T(8,128)S(1)}, u32[]{:S(2)}, u32[]{:S(2)}) %collective-permute-start.6) | collective-permute-done | bytes 262176 | tf_op jit(solution)/shard_map/ppermute | solution.py:44
  32.7 2.0 %collective-permute-start.7 = (f32[2,16,2,4,128]{4,1,3,2,0:T(8,128)S(1)}, f32[2,16,2,4,128]{4,1,3,2,0:T(8,128)S(1)}, u32[]{:S(2)}, u32[]{:S(2)}) collective-permute-start(f32[2,16,2,4,128]{4,1,3,2,0:T(8,128)S(1)} %select_bitcast_fusion.1), channel_id=1, source_target_pairs={{0,4},{4,0},{8,12},{12,8},{1,5},{5,1},{9,13},{13,9},{2,6},{6,2},{1... | collective-permute-start | bytes 393224 | tf_op jit(solution)/shard_map/ppermute | solution.py:44
  34.7 3.9 %collective-permute-done.7 = f32[2,16,2,4,128]{4,1,3,2,0:T(8,128)S(1)} collective-permute-done((f32[2,16,2,4,128]{4,1,3,2,0:T(8,128)S(1)}, f32[2,16,2,4,128]{4,1,3,2,0:T(8,128)S(1)}, u32[]{:S(2)}, u32[]{:S(2)}) %collective-permute-start.7) | collective-permute-done | bytes 131104 | tf_op jit(solution)/shard_map/ppermute | solution.py:44
  38.6 2.8 %collective-permute-start.8 = (f32[1,16,2,4,128]{4,1,3,2,0:T(8,128)S(1)}, f32[1,16,2,4,128]{4,1,3,2,0:T(8,128)S(1)}, u32[]{:S(2)}, u32[]{:S(2)}) collective-permute-start(f32[1,16,2,4,128]{4,1,3,2,0:T(8,128)S(1)} %select_bitcast_fusion.2), channel_id=1, source_target_pairs={{0,8},{4,12},{8,0},{12,4},{1,9},{5,13},{9,1},{13,5},{2,10},{6,14},... | collective-permute-start | bytes 196616 | tf_op jit(solution)/shard_map/ppermute | solution.py:44
  41.3 2.6 %collective-permute-done.8 = f32[1,16,2,4,128]{4,1,3,2,0:T(8,128)S(1)} collective-permute-done((f32[1,16,2,4,128]{4,1,3,2,0:T(8,128)S(1)}, f32[1,16,2,4,128]{4,1,3,2,0:T(8,128)S(1)}, u32[]{:S(2)}, u32[]{:S(2)}) %collective-permute-start.8) | collective-permute-done | bytes 65568 | tf_op jit(solution)/shard_map/ppermute | solution.py:44
  44.0 0.7 %copy.77 = f32[16,2,4,128]{3,2,1,0:T(4,128)} copy(f32[16,2,4,128]{3,0,2,1:T(8,128)S(1)} %fusion.56) | data formatting | bytes 131072 | tf_op jit(solution)/shard_map/reshape | solution.py:46
  (118 shorter events, 7.4 us)
Async XLA Ops:
  2.3 8.6 %collective-permute-start = (f32[288,128]{1,0:T(8,128)}, f32[288,128]{1,0:T(8,128)S(1)}, u32[]{:S(2)}, u32[]{:S(2)}) collective-permute-start(f32[288,128]{1,0:T(8,128)} %get-tuple-element.156), channel_id=1, source_target_pairs={{1,4},{4,1},{5,8},{8,5},{9,12},{12,9},{3,6},{6,3},{7,10},{10,7},{1... | collective-permute-start | bytes 442376 | tf_op jit(solution)/shard_map/ppermute | solution.py:162
  3.0 8.0 %collective-permute-start.1 = (f32[288,128]{1,0:T(8,128)}, f32[288,128]{1,0:T(8,128)S(1)}, u32[]{:S(2)}, u32[]{:S(2)}) collective-permute-start(f32[288,128]{1,0:T(8,128)} %get-tuple-element.157), channel_id=1, source_target_pairs={{0,1},{1,0},{2,3},{3,2},{4,5},{5,4},{6,7},{7,6},{8,9},{9,8},{10,11... | collective-permute-start | bytes 442376 | tf_op jit(solution)/shard_map/ppermute | solution.py:158
  8.8 1.0 %copy-start = (bf16[512,4,128]{2,1,0:T(4,128)(2,1)S(1)}, bf16[512,4,128]{2,1,0:T(4,128)(2,1)}, u32[]{:S(2)}) copy-start(bf16[512,4,128]{2,1,0:T(4,128)(2,1)} %param.31) | copy-start | bytes 1572868
  10.0 0.8 %copy-start.2 = (bf16[32,512]{1,0:T(8,128)(2,1)S(1)}, bf16[32,512]{1,0:T(8,128)(2,1)}, u32[]{:S(2)}) copy-start(bf16[32,512]{1,0:T(8,128)(2,1)} %get-tuple-element.154) | copy-start | bytes 98308
  11.1 0.8 %copy-start.1 = (f32[4,32,128]{2,1,0:T(8,128)S(1)}, f32[4,32,128]{2,1,0:T(8,128)}, u32[]{:S(2)}) copy-start(f32[4,32,128]{2,1,0:T(8,128)} %get-tuple-element.155) | copy-start | bytes 196612
  13.6 3.8 %collective-permute-start.2 = (f32[3,32,128]{2,1,0:T(8,128)S(1)}, f32[3,32,128]{2,1,0:T(8,128)S(1)}, u32[]{:S(2)}, u32[]{:S(2)}) collective-permute-start(f32[3,32,128]{2,1,0:T(8,128)S(1)} %get-tuple-element.213), channel_id=1, source_target_pairs={{1,4},{4,1},{5,8},{8,5},{9,12},{12,9},{3,6},{6,3},{7,10},{10,7},{1... | collective-permute-start | bytes 147464 | tf_op jit(solution)/shard_map/ppermute | solution.py:162
  14.2 3.9 %collective-permute-start.3 = (f32[3,32,128]{2,1,0:T(8,128)S(1)}, f32[3,32,128]{2,1,0:T(8,128)S(1)}, u32[]{:S(2)}, u32[]{:S(2)}) collective-permute-start(f32[3,32,128]{2,1,0:T(8,128)S(1)} %get-tuple-element.212), channel_id=1, source_target_pairs={{0,1},{1,0},{2,3},{3,2},{4,5},{5,4},{6,7},{7,6},{8,9},{9,8},{10,11... | collective-permute-start | bytes 147464 | tf_op jit(solution)/shard_map/ppermute | solution.py:158
  20.9 4.6 %collective-permute-start.4 = (f32[3,32,128]{2,1,0:T(8,128)S(1)}, f32[3,32,128]{2,1,0:T(8,128)S(1)}, u32[]{:S(2)}, u32[]{:S(2)}) collective-permute-start(f32[3,32,128]{2,1,0:T(8,128)S(1)} %get-tuple-element.209), channel_id=1, source_target_pairs={{1,4},{4,1},{5,8},{8,5},{9,12},{12,9},{3,6},{6,3},{7,10},{10,7},{1... | collective-permute-start | bytes 147464 | tf_op jit(solution)/shard_map/ppermute | solution.py:162
  21.6 4.7 %collective-permute-start.5 = (f32[3,32,128]{2,1,0:T(8,128)S(1)}, f32[3,32,128]{2,1,0:T(8,128)S(1)}, u32[]{:S(2)}, u32[]{:S(2)}) collective-permute-start(f32[3,32,128]{2,1,0:T(8,128)S(1)} %get-tuple-element.208), channel_id=1, source_target_pairs={{0,1},{1,0},{2,3},{3,2},{4,5},{5,4},{6,7},{7,6},{8,9},{9,8},{10,11... | collective-permute-start | bytes 147464 | tf_op jit(solution)/shard_map/ppermute | solution.py:158
  30.5 2.1 %collective-permute-start.6 = (f32[4,16,2,4,128]{4,1,3,2,0:T(8,128)S(1)}, f32[4,16,2,4,128]{4,1,3,2,0:T(8,128)S(1)}, u32[]{:S(2)}, u32[]{:S(2)}) collective-permute-start(f32[4,16,2,4,128]{4,1,3,2,0:T(8,128)S(1)} %select_bitcast_fusion), channel_id=1, source_target_pairs={{0,1},{1,0},{2,3},{3,2},{4,5},{5,4},{6,7},{7,6},{8,9},{9,8},{10,11... | collective-permute-start | bytes 786440 | tf_op jit(solution)/shard_map/ppermute | solution.py:44
  32.7 5.8 %collective-permute-start.7 = (f32[2,16,2,4,128]{4,1,3,2,0:T(8,128)S(1)}, f32[2,16,2,4,128]{4,1,3,2,0:T(8,128)S(1)}, u32[]{:S(2)}, u32[]{:S(2)}) collective-permute-start(f32[2,16,2,4,128]{4,1,3,2,0:T(8,128)S(1)} %select_bitcast_fusion.1), channel_id=1, source_target_pairs={{0,4},{4,0},{8,12},{12,8},{1,5},{5,1},{9,13},{13,9},{2,6},{6,2},{1... | collective-permute-start | bytes 393224 | tf_op jit(solution)/shard_map/ppermute | solution.py:44
  38.6 5.4 %collective-permute-start.8 = (f32[1,16,2,4,128]{4,1,3,2,0:T(8,128)S(1)}, f32[1,16,2,4,128]{4,1,3,2,0:T(8,128)S(1)}, u32[]{:S(2)}, u32[]{:S(2)}) collective-permute-start(f32[1,16,2,4,128]{4,1,3,2,0:T(8,128)S(1)} %select_bitcast_fusion.2), channel_id=1, source_target_pairs={{0,8},{4,12},{8,0},{12,4},{1,9},{5,13},{9,1},{13,5},{2,10},{6,14},... | collective-permute-start | bytes 196616 | tf_op jit(solution)/shard_map/ppermute | solution.py:44

commit v15 on v13

--- a/solution.py
+++ b/solution.py
@@ -256,8 +256,9 @@
         for piece in [first] + jnp.split(product, sections - 1, 0)
     ]
     partial_news = jnp.concatenate(pieces, axis=0)
-    jacobian = diagonal_sums(partial_news)
-    return halving_scatter(jacobian)
+    merged = partial_news.reshape(horizon, output_count * input_count, horizon)
+    jacobian = halving_scatter(diagonal_sums(merged))
+    return jacobian.reshape((jacobian.shape[0], output_count, input_count, horizon))
 
 
 def solution(mesh):

time: 44.8 us -> 45.2 us (level)
  other arithmetic: 1.97 us -> 2.72 us
    reshape x1 -> x0, local copies, waits for them, and re-layouts: 0.66 us -> none  [halving_scatter(): return held.reshape(held.shape[1:])]
    add x1 -> x2, other arithmetic: 0.05 us -> 0.68 us  [halving_scatter(): held = keep + lax.ppermute(send, axis, pairs)]
    unnamed x20 -> x21, local copies, waits for them, and re-layouts: 1.55 us -> 1.85 us
where the time goes in v15:
time: 45.2 us; the launch traced here: 44.9 us
  starting transfers between devices  20.8 us (46%)
  waiting for transfers between devices  9.34 us (21%)
  matrix products  5.03 us (11%)
  local copies, waits for them, and re-layouts  3.68 us (8%)
  other arithmetic  2.72 us (6%)
  Pallas kernels  2.42 us (5%)
  between operations  0.85 us (2%)
    ppermute x3, starting transfers between devices, swap_links(): on_chip = lax.ppermute(chip_part, 'horizon', [(0, 1), (1, 0)])  13.1 us
    ppermute x3, waiting for transfers between devices, halving_scatter(): held = keep + lax.ppermute(send, axis, pairs)  7.59 us
    ppermute x3, starting transfers between devices, halving_scatter(): held = keep + lax.ppermute(send, axis, pairs)  5.76 us
    dot_general x10, matrix products, band_parts(): jnp.einsum('cru,cun->crn', rows, moves, precision=lax.Precision.HIGH)  3.92 us
    pallas_call x1, Pallas kernels, prepare(): pl.pallas_call(prepare_kernel, out_shape=(jax.ShapeDtypeStruct((block_cou...  2.42 us
    ppermute x3, starting transfers between devices, swap_links(): across = lax.ppermute(cross_part, ('state', 'horizon'), pairs)  1.99 us
    unnamed x21, local copies, waits for them, and re-layouts  1.85 us
    ppermute x3, waiting for transfers between devices, swap_links(): on_chip = lax.ppermute(chip_part, 'horizon', [(0, 1), (1, 0)])  1.74 us
  transfers between devices with their start and end apart: 9, of which 6 were waited for; matrix products, arithmetic and copies ran while one was open for 2% of the time, Pallas kernels for 0%

profile of v15, /device:TPU:0, one launch (start us, length us, event | category | flops | bytes accessed | tf_op | source)
XLA Modules:
  0.0 44.9 jit_solution(3946966987566876111)
XLA Ops:
  0.0 2.4 %shard_map.73 = (f32[4,128,384]{2,1,0:T(8,128)}, bf16[32,512]{1,0:T(8,128)(2,1)}, f32[4,32,128]{2,1,0:T(8,128)}, f32[288,128]{1,0:T(8,128)}, f32[288,128]{1,0:T(8,128)}) custom-call(s32[1]{0:T(128)} %bitcast.flip, s32[4]{0:T(128)} %counts.1, s32[4,4]{1,0:T(4,128)} %offsets.1, s32[4]{0:T(128)} %regions.1, f32[2,16]{1,0:T(2,128)} %bitcast.169, ...), custom_call_target="tpu_custom_call" | custom-call | tf_op jit(solution)/shard_map/pallas_call | solution.py:109
  2.4 0.7 %collective-permute-start = (f32[288,128]{1,0:T(8,128)}, f32[288,128]{1,0:T(8,128)S(1)}, u32[]{:S(2)}, u32[]{:S(2)}) collective-permute-start(f32[288,128]{1,0:T(8,128)} %get-tuple-element.156), channel_id=1, source_target_pairs={{1,4},{4,1},{5,8},{8,5},{9,12},{12,9},{3,6},{6,3},{7,10},{10,7},{1... | collective-permute-start | bytes 442376 | tf_op jit(solution)/shard_map/ppermute | solution.py:162
  3.1 4.4 %collective-permute-start.1 = (f32[288,128]{1,0:T(8,128)}, f32[288,128]{1,0:T(8,128)S(1)}, u32[]{:S(2)}, u32[]{:S(2)}) collective-permute-start(f32[288,128]{1,0:T(8,128)} %get-tuple-element.157), channel_id=1, source_target_pairs={{0,1},{1,0},{2,3},{3,2},{4,5},{5,4},{6,7},{7,6},{8,9},{9,8},{10,11... | collective-permute-start | bytes 442376 | tf_op jit(solution)/shard_map/ppermute | solution.py:158
  7.9 0.4 copy-done.5
  9.3 0.6 %copy-done = f32[4,128,384]{2,1,0:T(8,128)S(1)} copy-done((f32[4,128,384]{2,1,0:T(8,128)S(1)}, f32[4,128,384]{2,1,0:T(8,128)}, u32[]{:S(2)}) %copy-start) | copy-done | bytes 786456
  10.4 0.4 fusion.52
  11.4 0.7 %collective-permute-start.2 = (f32[3,32,128]{2,1,0:T(8,128)S(1)}, f32[3,32,128]{2,1,0:T(8,128)S(1)}, u32[]{:S(2)}, u32[]{:S(2)}) collective-permute-start(f32[3,32,128]{2,1,0:T(8,128)S(1)} %get-tuple-element.211), channel_id=1, source_target_pairs={{1,4},{4,1},{5,8},{8,5},{9,12},{12,9},{3,6},{6,3},{7,10},{10,7},{1... | collective-permute-start | bytes 147464 | tf_op jit(solution)/shard_map/ppermute | solution.py:162
  12.1 4.8 %collective-permute-start.3 = (f32[3,32,128]{2,1,0:T(8,128)S(1)}, f32[3,32,128]{2,1,0:T(8,128)S(1)}, u32[]{:S(2)}, u32[]{:S(2)}) collective-permute-start(f32[3,32,128]{2,1,0:T(8,128)S(1)} %get-tuple-element.210), channel_id=1, source_target_pairs={{0,1},{1,0},{2,3},{3,2},{4,5},{5,4},{6,7},{7,6},{8,9},{9,8},{10,11... | collective-permute-start | bytes 147464 | tf_op jit(solution)/shard_map/ppermute | solution.py:158
  17.0 0.8 %collective-permute-done.3 = f32[3,32,128]{2,1,0:T(8,128)S(1)} collective-permute-done((f32[3,32,128]{2,1,0:T(8,128)S(1)}, f32[3,32,128]{2,1,0:T(8,128)S(1)}, u32[]{:S(2)}, u32[]{:S(2)}) %collective-permute-start.3) | collective-permute-done | bytes 49184 | tf_op jit(solution)/shard_map/ppermute | solution.py:158
  18.6 0.5 %slice-done.1 = f32[6,32,128]{2,1,0:T(8,128)S(1)} async-done(((f32[6,32,384]{2,1,0:T(8,128)}), f32[6,32,128]{2,1,0:T(8,128)S(1)}, s32[]{:S(2)}) %slice-start.1) | async-done | bytes 98328 | tf_op jit(solution)/shard_map/slice | solution.py:169
  19.1 0.4 fusion.17
  19.6 0.4 fusion.50
  20.1 0.4 fusion.49
  20.6 0.7 %collective-permute-start.4 = (f32[3,32,128]{2,1,0:T(8,128)S(1)}, f32[3,32,128]{2,1,0:T(8,128)S(1)}, u32[]{:S(2)}, u32[]{:S(2)}) collective-permute-start(f32[3,32,128]{2,1,0:T(8,128)S(1)} %get-tuple-element.207), channel_id=1, source_target_pairs={{1,4},{4,1},{5,8},{8,5},{9,12},{12,9},{3,6},{6,3},{7,10},{10,7},{1... | collective-permute-start | bytes 147464 | tf_op jit(solution)/shard_map/ppermute | solution.py:162
  21.3 3.9 %collective-permute-start.5 = (f32[3,32,128]{2,1,0:T(8,128)S(1)}, f32[3,32,128]{2,1,0:T(8,128)S(1)}, u32[]{:S(2)}, u32[]{:S(2)}) collective-permute-start(f32[3,32,128]{2,1,0:T(8,128)S(1)} %get-tuple-element.206), channel_id=1, source_target_pairs={{0,1},{1,0},{2,3},{3,2},{4,5},{5,4},{6,7},{7,6},{8,9},{9,8},{10,11... | collective-permute-start | bytes 147464 | tf_op jit(solution)/shard_map/ppermute | solution.py:158
  25.2 0.8 %collective-permute-done.5 = f32[3,32,128]{2,1,0:T(8,128)S(1)} collective-permute-done((f32[3,32,128]{2,1,0:T(8,128)S(1)}, f32[3,32,128]{2,1,0:T(8,128)S(1)}, u32[]{:S(2)}, u32[]{:S(2)}) %collective-permute-start.5) | collective-permute-done | bytes 49184 | tf_op jit(solution)/shard_map/ppermute | solution.py:158
  27.0 0.5 %slice-done = f32[6,32,128]{2,1,0:T(8,128)S(1)} async-done(((f32[6,32,384]{2,1,0:T(8,128)}), f32[6,32,128]{2,1,0:T(8,128)S(1)}, s32[]{:S(2)}) %slice-start) | async-done | bytes 98328 | tf_op jit(solution)/shard_map/slice | solution.py:169
  30.8 0.9 %collective-permute-start.6 = (f32[4,16,8,128]{3,2,1,0:T(8,128)S(1)}, f32[4,16,8,128]{3,2,1,0:T(8,128)S(1)}, u32[]{:S(2)}, u32[]{:S(2)}) collective-permute-start(f32[4,16,8,128]{3,2,1,0:T(8,128)S(1)} %select_bitcast_fusion), channel_id=1, source_target_pairs={{0,1},{1,0},{2,3},{3,2},{4,5},{5,4},{6,7},{7,6},{8,9},{9,8},{10,11... | collective-permute-start | bytes 786440 | tf_op jit(solution)/shard_map/ppermute | solution.py:44
  31.6 1.2 %collective-permute-done.6 = f32[4,16,8,128]{3,2,1,0:T(8,128)S(1)} collective-permute-done((f32[4,16,8,128]{3,2,1,0:T(8,128)S(1)}, f32[4,16,8,128]{3,2,1,0:T(8,128)S(1)}, u32[]{:S(2)}, u32[]{:S(2)}) %collective-permute-start.6) | collective-permute-done | bytes 262176 | tf_op jit(solution)/shard_map/ppermute | solution.py:44
  32.9 2.1 %collective-permute-start.7 = (f32[2,16,8,128]{3,2,1,0:T(8,128)S(1)}, f32[2,16,8,128]{3,2,1,0:T(8,128)S(1)}, u32[]{:S(2)}, u32[]{:S(2)}) collective-permute-start(f32[2,16,8,128]{3,2,1,0:T(8,128)S(1)} %select_bitcast_fusion.1), channel_id=1, source_target_pairs={{0,4},{4,0},{8,12},{12,8},{1,5},{5,1},{9,13},{13,9},{2,6},{6,2},{1... | collective-permute-start | bytes 393224 | tf_op jit(solution)/shard_map/ppermute | solution.py:44
  34.9 3.8 %collective-permute-done.7 = f32[2,16,8,128]{3,2,1,0:T(8,128)S(1)} collective-permute-done((f32[2,16,8,128]{3,2,1,0:T(8,128)S(1)}, f32[2,16,8,128]{3,2,1,0:T(8,128)S(1)}, u32[]{:S(2)}, u32[]{:S(2)}) %collective-permute-start.7) | collective-permute-done | bytes 131104 | tf_op jit(solution)/shard_map/ppermute | solution.py:44
  38.8 2.8 %collective-permute-start.8 = (f32[1,16,8,128]{3,2,1,0:T(8,128)S(1)}, f32[1,16,8,128]{3,2,1,0:T(8,128)S(1)}, u32[]{:S(2)}, u32[]{:S(2)}) collective-permute-start(f32[1,16,8,128]{3,2,1,0:T(8,128)S(1)} %select_bitcast_fusion.2), channel_id=1, source_target_pairs={{0,8},{4,12},{8,0},{12,4},{1,9},{5,13},{9,1},{13,5},{2,10},{6,14},... | collective-permute-start | bytes 196616 | tf_op jit(solution)/shard_map/ppermute | solution.py:44
  41.6 2.6 %collective-permute-done.8 = f32[1,16,8,128]{3,2,1,0:T(8,128)S(1)} collective-permute-done((f32[1,16,8,128]{3,2,1,0:T(8,128)S(1)}, f32[1,16,8,128]{3,2,1,0:T(8,128)S(1)}, u32[]{:S(2)}, u32[]{:S(2)}) %collective-permute-start.8) | collective-permute-done | bytes 65568 | tf_op jit(solution)/shard_map/ppermute | solution.py:44
  44.2 0.6 %bitcast_add_fusion = f32[1,16,8,128]{3,2,1,0:T(8,128)} fusion(f32[1,16,8,128]{3,2,1,0:T(8,128)S(1)} %collective-permute-done.8, f32[1,2,16,8,128]{4,3,2,1,0:T(8,128)S(1)} %fusion.15, pred[]{:T(512)S(6)} %eq.12), kind=kLoop, calls=%fused_computation.84 | loop fusion | flops 32768 | bytes 262145 | tf_op jit(solution)/shard_map/add | solution.py:44
  (121 shorter events, 7.2 us)
Async XLA Ops:
  0.0 7.5 %copy-start.1 = (bf16[512,4,128]{2,1,0:T(4,128)(2,1)S(1)}, bf16[512,4,128]{2,1,0:T(4,128)(2,1)}, u32[]{:S(2)}) copy-start(bf16[512,4,128]{2,1,0:T(4,128)(2,1)} %param.31) | copy-start | bytes 1572868
  2.4 6.2 %collective-permute-start = (f32[288,128]{1,0:T(8,128)}, f32[288,128]{1,0:T(8,128)S(1)}, u32[]{:S(2)}, u32[]{:S(2)}) collective-permute-start(f32[288,128]{1,0:T(8,128)} %get-tuple-element.156), channel_id=1, source_target_pairs={{1,4},{4,1},{5,8},{8,5},{9,12},{12,9},{3,6},{6,3},{7,10},{10,7},{1... | collective-permute-start | bytes 442376 | tf_op jit(solution)/shard_map/ppermute | solution.py:162
  3.1 5.7 %collective-permute-start.1 = (f32[288,128]{1,0:T(8,128)}, f32[288,128]{1,0:T(8,128)S(1)}, u32[]{:S(2)}, u32[]{:S(2)}) collective-permute-start(f32[288,128]{1,0:T(8,128)} %get-tuple-element.157), channel_id=1, source_target_pairs={{0,1},{1,0},{2,3},{3,2},{4,5},{5,4},{6,7},{7,6},{8,9},{9,8},{10,11... | collective-permute-start | bytes 442376 | tf_op jit(solution)/shard_map/ppermute | solution.py:158
  7.6 0.8 %copy-start.5 = (bf16[32,512]{1,0:T(8,128)(2,1)S(1)}, bf16[32,512]{1,0:T(8,128)(2,1)}, u32[]{:S(2)}) copy-start(bf16[32,512]{1,0:T(8,128)(2,1)} %get-tuple-element.154) | copy-start | bytes 98308
  8.4 0.8 %copy-start.4 = (f32[4,32,128]{2,1,0:T(8,128)S(1)}, f32[4,32,128]{2,1,0:T(8,128)}, u32[]{:S(2)}) copy-start(f32[4,32,128]{2,1,0:T(8,128)} %get-tuple-element.155) | copy-start | bytes 196612
  8.8 1.1 %copy-start = (f32[4,128,384]{2,1,0:T(8,128)S(1)}, f32[4,128,384]{2,1,0:T(8,128)}, u32[]{:S(2)}) copy-start(f32[4,128,384]{2,1,0:T(8,128)} %get-tuple-element.158) | copy-start | bytes 2359300
  11.4 6.8 %copy-start.3 = (f32[6,32,384]{2,1,0:T(8,128)}, f32[6,32,384]{2,1,0:T(8,128)S(1)}, u32[]{:S(2)}) copy-start(f32[6,32,384]{2,1,0:T(8,128)S(1)} %fusion.51) | copy-start | bytes 884740
  11.4 5.5 %collective-permute-start.2 = (f32[3,32,128]{2,1,0:T(8,128)S(1)}, f32[3,32,128]{2,1,0:T(8,128)S(1)}, u32[]{:S(2)}, u32[]{:S(2)}) collective-permute-start(f32[3,32,128]{2,1,0:T(8,128)S(1)} %get-tuple-element.211), channel_id=1, source_target_pairs={{1,4},{4,1},{5,8},{8,5},{9,12},{12,9},{3,6},{6,3},{7,10},{10,7},{1... | collective-permute-start | bytes 147464 | tf_op jit(solution)/shard_map/ppermute | solution.py:162
  12.1 5.7 %collective-permute-start.3 = (f32[3,32,128]{2,1,0:T(8,128)S(1)}, f32[3,32,128]{2,1,0:T(8,128)S(1)}, u32[]{:S(2)}, u32[]{:S(2)}) collective-permute-start(f32[3,32,128]{2,1,0:T(8,128)S(1)} %get-tuple-element.210), channel_id=1, source_target_pairs={{0,1},{1,0},{2,3},{3,2},{4,5},{5,4},{6,7},{7,6},{8,9},{9,8},{10,11... | collective-permute-start | bytes 147464 | tf_op jit(solution)/shard_map/ppermute | solution.py:158
  18.2 0.9 %slice-start.1 = ((f32[6,32,384]{2,1,0:T(8,128)}), f32[6,32,128]{2,1,0:T(8,128)S(1)}, s32[]{:S(2)}) async-start(f32[6,32,384]{2,1,0:T(8,128)} %copy-done.3), calls=%async_computation.1 | async-start | bytes 196608 | tf_op jit(solution)/shard_map/slice | solution.py:169
  20.6 5.5 %copy-start.2 = (f32[6,32,384]{2,1,0:T(8,128)}, f32[6,32,384]{2,1,0:T(8,128)S(1)}, u32[]{:S(2)}) copy-start(f32[6,32,384]{2,1,0:T(8,128)S(1)} %fusion.49) | copy-start | bytes 884740
  20.6 4.6 %collective-permute-start.4 = (f32[3,32,128]{2,1,0:T(8,128)S(1)}, f32[3,32,128]{2,1,0:T(8,128)S(1)}, u32[]{:S(2)}, u32[]{:S(2)}) collective-permute-start(f32[3,32,128]{2,1,0:T(8,128)S(1)} %get-tuple-element.207), channel_id=1, source_target_pairs={{1,4},{4,1},{5,8},{8,5},{9,12},{12,9},{3,6},{6,3},{7,10},{10,7},{1... | collective-permute-start | bytes 147464 | tf_op jit(solution)/shard_map/ppermute | solution.py:162
  21.3 4.7 %collective-permute-start.5 = (f32[3,32,128]{2,1,0:T(8,128)S(1)}, f32[3,32,128]{2,1,0:T(8,128)S(1)}, u32[]{:S(2)}, u32[]{:S(2)}) collective-permute-start(f32[3,32,128]{2,1,0:T(8,128)S(1)} %get-tuple-element.206), channel_id=1, source_target_pairs={{0,1},{1,0},{2,3},{3,2},{4,5},{5,4},{6,7},{7,6},{8,9},{9,8},{10,11... | collective-permute-start | bytes 147464 | tf_op jit(solution)/shard_map/ppermute | solution.py:158
  26.5 0.9 %slice-start = ((f32[6,32,384]{2,1,0:T(8,128)}), f32[6,32,128]{2,1,0:T(8,128)S(1)}, s32[]{:S(2)}) async-start(f32[6,32,384]{2,1,0:T(8,128)} %copy-done.2), calls=%async_computation | async-start | bytes 196608 | tf_op jit(solution)/shard_map/slice | solution.py:169
  30.8 2.0 %collective-permute-start.6 = (f32[4,16,8,128]{3,2,1,0:T(8,128)S(1)}, f32[4,16,8,128]{3,2,1,0:T(8,128)S(1)}, u32[]{:S(2)}, u32[]{:S(2)}) collective-permute-start(f32[4,16,8,128]{3,2,1,0:T(8,128)S(1)} %select_bitcast_fusion), channel_id=1, source_target_pairs={{0,1},{1,0},{2,3},{3,2},{4,5},{5,4},{6,7},{7,6},{8,9},{9,8},{10,11... | collective-permute-start | bytes 786440 | tf_op jit(solution)/shard_map/ppermute | solution.py:44
  32.9 5.9 %collective-permute-start.7 = (f32[2,16,8,128]{3,2,1,0:T(8,128)S(1)}, f32[2,16,8,128]{3,2,1,0:T(8,128)S(1)}, u32[]{:S(2)}, u32[]{:S(2)}) collective-permute-start(f32[2,16,8,128]{3,2,1,0:T(8,128)S(1)} %select_bitcast_fusion.1), channel_id=1, source_target_pairs={{0,4},{4,0},{8,12},{12,8},{1,5},{5,1},{9,13},{13,9},{2,6},{6,2},{1... | collective-permute-start | bytes 393224 | tf_op jit(solution)/shard_map/ppermute | solution.py:44
  38.8 5.4 %collective-permute-start.8 = (f32[1,16,8,128]{3,2,1,0:T(8,128)S(1)}, f32[1,16,8,128]{3,2,1,0:T(8,128)S(1)}, u32[]{:S(2)}, u32[]{:S(2)}) collective-permute-start(f32[1,16,8,128]{3,2,1,0:T(8,128)S(1)} %select_bitcast_fusion.2), channel_id=1, source_target_pairs={{0,8},{4,12},{8,0},{12,4},{1,9},{5,13},{9,1},{13,5},{2,10},{6,14},... | collective-permute-start | bytes 196616 | tf_op jit(solution)/shard_map/ppermute | solution.py:44

commit v16 on v13

--- a/solution.py
+++ b/solution.py
@@ -249,7 +249,12 @@
     stacked = jnp.concatenate(
         [level.transpose(1, 0, 2).reshape(row_count, state_count) for level in levels], 0
     )
-    product = split_product(stacked, flat_start)
+    product = jnp.dot(
+        stacked,
+        flat_start.astype(jnp.float32),
+        precision=lax.Precision.HIGH,
+        preferred_element_type=jnp.float32,
+    )
     first = jnp.dot(rows, flat_start, preferred_element_type=jnp.float32)
     pieces = [
         piece.reshape(output_count, expect_rows, input_count, horizon).transpose(1, 0, 2, 3)

time: 44.8 us -> 44.3 us (0.989)
  matrix products: 5.04 us -> 4.58 us
    dot_general x3 -> x1, matrix products: 0.87 us -> 0.41 us  [shards(): jnp.dot(stacked, flat_start.astype(jnp.float32), precision=lax.Precision....]
where the time goes in v16:
time: 44.3 us; the launch traced here: 43.9 us
  starting transfers between devices  20.8 us (47%)
  waiting for transfers between devices  9.34 us (21%)
  matrix products  4.58 us (10%)
  local copies, waits for them, and re-layouts  4.01 us (9%)
  Pallas kernels  2.41 us (5%)
  other arithmetic  1.97 us (4%)
  between operations  0.81 us (2%)
    ppermute x3, starting transfers between devices, swap_links(): on_chip = lax.ppermute(chip_part, 'horizon', [(0, 1), (1, 0)])  13.1 us
    ppermute x3, waiting for transfers between devices, halving_scatter(): held = keep + lax.ppermute(send, axis, pairs)  7.59 us
    ppermute x3, starting transfers between devices, halving_scatter(): held = keep + lax.ppermute(send, axis, pairs)  5.75 us
    dot_general x10, matrix products, band_parts(): jnp.einsum('cru,cun->crn', rows, moves, precision=lax.Precision.HIGH)  3.93 us
    pallas_call x1, Pallas kernels, prepare(): pl.pallas_call(prepare_kernel, out_shape=(jax.ShapeDtypeStruct((block_cou...  2.41 us
    ppermute x3, starting transfers between devices, swap_links(): across = lax.ppermute(cross_part, ('state', 'horizon'), pairs)  1.99 us
    ppermute x3, waiting for transfers between devices, swap_links(): on_chip = lax.ppermute(chip_part, 'horizon', [(0, 1), (1, 0)])  1.74 us
    unnamed x20, local copies, waits for them, and re-layouts  1.55 us
  transfers between devices with their start and end apart: 9, of which 6 were waited for; matrix products, arithmetic and copies ran while one was open for 2% of the time, Pallas kernels for 0%

profile of v16, /device:TPU:0, one launch (start us, length us, event | category | flops | bytes accessed | tf_op | source)
XLA Modules:
  0.0 43.9 jit_solution(13178986269964011780)
XLA Ops:
  0.0 2.4 %shard_map.73 = (f32[4,128,384]{2,1,0:T(8,128)}, bf16[32,512]{1,0:T(8,128)(2,1)}, f32[4,32,128]{2,1,0:T(8,128)}, f32[288,128]{1,0:T(8,128)}, f32[288,128]{1,0:T(8,128)}) custom-call(s32[1]{0:T(128)} %bitcast.flip, s32[4]{0:T(128)} %counts.1, s32[4,4]{1,0:T(4,128)} %offsets.1, s32[4]{0:T(128)} %regions.1, f32[2,16]{1,0:T(2,128)} %bitcast.154, ...), custom_call_target="tpu_custom_call" | custom-call | tf_op jit(solution)/shard_map/pallas_call | solution.py:109
  2.4 0.7 %collective-permute-start = (f32[288,128]{1,0:T(8,128)}, f32[288,128]{1,0:T(8,128)S(1)}, u32[]{:S(2)}, u32[]{:S(2)}) collective-permute-start(f32[288,128]{1,0:T(8,128)} %get-tuple-element.156), channel_id=1, source_target_pairs={{1,4},{4,1},{5,8},{8,5},{9,12},{12,9},{3,6},{6,3},{7,10},{10,7},{1... | collective-permute-start | bytes 442376 | tf_op jit(solution)/shard_map/ppermute | solution.py:162
  3.1 4.4 %collective-permute-start.1 = (f32[288,128]{1,0:T(8,128)}, f32[288,128]{1,0:T(8,128)S(1)}, u32[]{:S(2)}, u32[]{:S(2)}) collective-permute-start(f32[288,128]{1,0:T(8,128)} %get-tuple-element.157), channel_id=1, source_target_pairs={{0,1},{1,0},{2,3},{3,2},{4,5},{5,4},{6,7},{7,6},{8,9},{9,8},{10,11... | collective-permute-start | bytes 442376 | tf_op jit(solution)/shard_map/ppermute | solution.py:158
  9.3 0.6 %copy-done = f32[4,128,384]{2,1,0:T(8,128)S(1)} copy-done((f32[4,128,384]{2,1,0:T(8,128)S(1)}, f32[4,128,384]{2,1,0:T(8,128)}, u32[]{:S(2)}) %copy-start) | copy-done | bytes 786456
  10.4 0.4 fusion.44
  10.9 0.4 fusion.43
  11.4 0.7 %collective-permute-start.2 = (f32[3,32,128]{2,1,0:T(8,128)S(1)}, f32[3,32,128]{2,1,0:T(8,128)S(1)}, u32[]{:S(2)}, u32[]{:S(2)}) collective-permute-start(f32[3,32,128]{2,1,0:T(8,128)S(1)} %get-tuple-element.213), channel_id=1, source_target_pairs={{1,4},{4,1},{5,8},{8,5},{9,12},{12,9},{3,6},{6,3},{7,10},{10,7},{1... | collective-permute-start | bytes 147464 | tf_op jit(solution)/shard_map/ppermute | solution.py:162
  12.1 4.8 %collective-permute-start.3 = (f32[3,32,128]{2,1,0:T(8,128)S(1)}, f32[3,32,128]{2,1,0:T(8,128)S(1)}, u32[]{:S(2)}, u32[]{:S(2)}) collective-permute-start(f32[3,32,128]{2,1,0:T(8,128)S(1)} %get-tuple-element.212), channel_id=1, source_target_pairs={{0,1},{1,0},{2,3},{3,2},{4,5},{5,4},{6,7},{7,6},{8,9},{9,8},{10,11... | collective-permute-start | bytes 147464 | tf_op jit(solution)/shard_map/ppermute | solution.py:158
  16.9 0.8 %collective-permute-done.3 = f32[3,32,128]{2,1,0:T(8,128)S(1)} collective-permute-done((f32[3,32,128]{2,1,0:T(8,128)S(1)}, f32[3,32,128]{2,1,0:T(8,128)S(1)}, u32[]{:S(2)}, u32[]{:S(2)}) %collective-permute-start.3) | collective-permute-done | bytes 49184 | tf_op jit(solution)/shard_map/ppermute | solution.py:158
  18.6 0.5 %slice-done.1 = f32[6,32,128]{2,1,0:T(8,128)S(1)} async-done(((f32[6,32,384]{2,1,0:T(8,128)}), f32[6,32,128]{2,1,0:T(8,128)S(1)}, s32[]{:S(2)}) %slice-start.1) | async-done | bytes 98328 | tf_op jit(solution)/shard_map/slice | solution.py:169
  19.1 0.4 fusion.8
  19.6 0.4 %fusion.42 = f32[6,32,384]{2,1,0:T(8,128)S(1)} fusion(f32[6,32,128]{2,1,0:T(8,128)S(1)} %fusion.10, f32[1,128,384]{2,1,0:T(8,128)S(1)} %get-tuple-element.215, f32[4,128,384]{2,1,0:T(8,128)S(1)} %copy-done, f32[1,128,384]{2,1,0:T(8,128)S(1)} %get-tuple-element.214), kind=kOutput, calls=%fused_computation.117 | convolution fusion | flops 57212928 | bytes 1572864 | tf_op jit(solution)/shard_map/cru,cun->crn/dot_general | solution.py:167
  20.1 0.4 %fusion.41 = f32[6,32,384]{2,1,0:T(8,128)S(1)} fusion(f32[6,32,128]{2,1,0:T(8,128)S(1)} %fusion.9, f32[1,128,384]{2,1,0:T(8,128)S(1)} %get-tuple-element.215, f32[4,128,384]{2,1,0:T(8,128)S(1)} %copy-done, f32[1,128,384]{2,1,0:T(8,128)S(1)} %get-tuple-element.214), kind=kOutput, calls=%fused_computation.116 | convolution fusion | flops 57212928 | bytes 1572864 | tf_op jit(solution)/shard_map/cru,cun->crn/dot_general | solution.py:167
  20.6 0.7 %collective-permute-start.4 = (f32[3,32,128]{2,1,0:T(8,128)S(1)}, f32[3,32,128]{2,1,0:T(8,128)S(1)}, u32[]{:S(2)}, u32[]{:S(2)}) collective-permute-start(f32[3,32,128]{2,1,0:T(8,128)S(1)} %get-tuple-element.209), channel_id=1, source_target_pairs={{1,4},{4,1},{5,8},{8,5},{9,12},{12,9},{3,6},{6,3},{7,10},{10,7},{1... | collective-permute-start | bytes 147464 | tf_op jit(solution)/shard_map/ppermute | solution.py:162
  21.3 3.9 %collective-permute-start.5 = (f32[3,32,128]{2,1,0:T(8,128)S(1)}, f32[3,32,128]{2,1,0:T(8,128)S(1)}, u32[]{:S(2)}, u32[]{:S(2)}) collective-permute-start(f32[3,32,128]{2,1,0:T(8,128)S(1)} %get-tuple-element.208), channel_id=1, source_target_pairs={{0,1},{1,0},{2,3},{3,2},{4,5},{5,4},{6,7},{7,6},{8,9},{9,8},{10,11... | collective-permute-start | bytes 147464 | tf_op jit(solution)/shard_map/ppermute | solution.py:158
  25.2 0.8 %collective-permute-done.5 = f32[3,32,128]{2,1,0:T(8,128)S(1)} collective-permute-done((f32[3,32,128]{2,1,0:T(8,128)S(1)}, f32[3,32,128]{2,1,0:T(8,128)S(1)}, u32[]{:S(2)}, u32[]{:S(2)}) %collective-permute-start.5) | collective-permute-done | bytes 49184 | tf_op jit(solution)/shard_map/ppermute | solution.py:158
  26.9 0.5 %slice-done = f32[6,32,128]{2,1,0:T(8,128)S(1)} async-done(((f32[6,32,384]{2,1,0:T(8,128)}), f32[6,32,128]{2,1,0:T(8,128)S(1)}, s32[]{:S(2)}) %slice-start) | async-done | bytes 98328 | tf_op jit(solution)/shard_map/slice | solution.py:169
  29.8 0.9 %collective-permute-start.6 = (f32[4,16,2,4,128]{4,1,3,2,0:T(8,128)S(1)}, f32[4,16,2,4,128]{4,1,3,2,0:T(8,128)S(1)}, u32[]{:S(2)}, u32[]{:S(2)}) collective-permute-start(f32[4,16,2,4,128]{4,1,3,2,0:T(8,128)S(1)} %select_bitcast_fusion), channel_id=1, source_target_pairs={{0,1},{1,0},{2,3},{3,2},{4,5},{5,4},{6,7},{7,6},{8,9},{9,8},{10,11... | collective-permute-start | bytes 786440 | tf_op jit(solution)/shard_map/ppermute | solution.py:44
  30.7 1.2 %collective-permute-done.6 = f32[4,16,2,4,128]{4,1,3,2,0:T(8,128)S(1)} collective-permute-done((f32[4,16,2,4,128]{4,1,3,2,0:T(8,128)S(1)}, f32[4,16,2,4,128]{4,1,3,2,0:T(8,128)S(1)}, u32[]{:S(2)}, u32[]{:S(2)}) %collective-permute-start.6) | collective-permute-done | bytes 262176 | tf_op jit(solution)/shard_map/ppermute | solution.py:44
  31.9 2.1 %collective-permute-start.7 = (f32[2,16,2,4,128]{4,1,3,2,0:T(8,128)S(1)}, f32[2,16,2,4,128]{4,1,3,2,0:T(8,128)S(1)}, u32[]{:S(2)}, u32[]{:S(2)}) collective-permute-start(f32[2,16,2,4,128]{4,1,3,2,0:T(8,128)S(1)} %select_bitcast_fusion.1), channel_id=1, source_target_pairs={{0,4},{4,0},{8,12},{12,8},{1,5},{5,1},{9,13},{13,9},{2,6},{6,2},{1... | collective-permute-start | bytes 393224 | tf_op jit(solution)/shard_map/ppermute | solution.py:44
  34.0 3.8 %collective-permute-done.7 = f32[2,16,2,4,128]{4,1,3,2,0:T(8,128)S(1)} collective-permute-done((f32[2,16,2,4,128]{4,1,3,2,0:T(8,128)S(1)}, f32[2,16,2,4,128]{4,1,3,2,0:T(8,128)S(1)}, u32[]{:S(2)}, u32[]{:S(2)}) %collective-permute-start.7) | collective-permute-done | bytes 131104 | tf_op jit(solution)/shard_map/ppermute | solution.py:44
  37.8 2.8 %collective-permute-start.8 = (f32[1,16,2,4,128]{4,1,3,2,0:T(8,128)S(1)}, f32[1,16,2,4,128]{4,1,3,2,0:T(8,128)S(1)}, u32[]{:S(2)}, u32[]{:S(2)}) collective-permute-start(f32[1,16,2,4,128]{4,1,3,2,0:T(8,128)S(1)} %select_bitcast_fusion.2), channel_id=1, source_target_pairs={{0,8},{4,12},{8,0},{12,4},{1,9},{5,13},{9,1},{13,5},{2,10},{6,14},... | collective-permute-start | bytes 196616 | tf_op jit(solution)/shard_map/ppermute | solution.py:44
  40.6 2.6 %collective-permute-done.8 = f32[1,16,2,4,128]{4,1,3,2,0:T(8,128)S(1)} collective-permute-done((f32[1,16,2,4,128]{4,1,3,2,0:T(8,128)S(1)}, f32[1,16,2,4,128]{4,1,3,2,0:T(8,128)S(1)}, u32[]{:S(2)}, u32[]{:S(2)}) %collective-permute-start.8) | collective-permute-done | bytes 65568 | tf_op jit(solution)/shard_map/ppermute | solution.py:44
  43.3 0.7 %copy.34 = f32[16,2,4,128]{3,2,1,0:T(4,128)} copy(f32[16,2,4,128]{3,0,2,1:T(8,128)S(1)} %fusion.26) | data formatting | bytes 131072 | tf_op jit(solution)/shard_map/reshape | solution.py:46
  (118 shorter events, 6.3 us)
Async XLA Ops:
  0.0 7.5 %copy-start.1 = (bf16[512,4,128]{2,1,0:T(4,128)(2,1)S(1)}, bf16[512,4,128]{2,1,0:T(4,128)(2,1)}, u32[]{:S(2)}) copy-start(bf16[512,4,128]{2,1,0:T(4,128)(2,1)} %param.31) | copy-start | bytes 1572868
  2.4 6.2 %collective-permute-start = (f32[288,128]{1,0:T(8,128)}, f32[288,128]{1,0:T(8,128)S(1)}, u32[]{:S(2)}, u32[]{:S(2)}) collective-permute-start(f32[288,128]{1,0:T(8,128)} %get-tuple-element.156), channel_id=1, source_target_pairs={{1,4},{4,1},{5,8},{8,5},{9,12},{12,9},{3,6},{6,3},{7,10},{10,7},{1... | collective-permute-start | bytes 442376 | tf_op jit(solution)/shard_map/ppermute | solution.py:162
  3.1 5.7 %collective-permute-start.1 = (f32[288,128]{1,0:T(8,128)}, f32[288,128]{1,0:T(8,128)S(1)}, u32[]{:S(2)}, u32[]{:S(2)}) collective-permute-start(f32[288,128]{1,0:T(8,128)} %get-tuple-element.157), channel_id=1, source_target_pairs={{0,1},{1,0},{2,3},{3,2},{4,5},{5,4},{6,7},{7,6},{8,9},{9,8},{10,11... | collective-permute-start | bytes 442376 | tf_op jit(solution)/shard_map/ppermute | solution.py:158
  7.6 0.8 %copy-start.5 = (bf16[32,512]{1,0:T(8,128)(2,1)S(1)}, bf16[32,512]{1,0:T(8,128)(2,1)}, u32[]{:S(2)}) copy-start(bf16[32,512]{1,0:T(8,128)(2,1)} %get-tuple-element.154) | copy-start | bytes 98308
  8.4 0.8 %copy-start.4 = (f32[4,32,128]{2,1,0:T(8,128)S(1)}, f32[4,32,128]{2,1,0:T(8,128)}, u32[]{:S(2)}) copy-start(f32[4,32,128]{2,1,0:T(8,128)} %get-tuple-element.155) | copy-start | bytes 196612
  8.8 1.1 %copy-start = (f32[4,128,384]{2,1,0:T(8,128)S(1)}, f32[4,128,384]{2,1,0:T(8,128)}, u32[]{:S(2)}) copy-start(f32[4,128,384]{2,1,0:T(8,128)} %get-tuple-element.158) | copy-start | bytes 2359300
  11.4 6.8 %copy-start.3 = (f32[6,32,384]{2,1,0:T(8,128)}, f32[6,32,384]{2,1,0:T(8,128)S(1)}, u32[]{:S(2)}) copy-start(f32[6,32,384]{2,1,0:T(8,128)S(1)} %fusion.43) | copy-start | bytes 884740
  11.4 5.5 %collective-permute-start.2 = (f32[3,32,128]{2,1,0:T(8,128)S(1)}, f32[3,32,128]{2,1,0:T(8,128)S(1)}, u32[]{:S(2)}, u32[]{:S(2)}) collective-permute-start(f32[3,32,128]{2,1,0:T(8,128)S(1)} %get-tuple-element.213), channel_id=1, source_target_pairs={{1,4},{4,1},{5,8},{8,5},{9,12},{12,9},{3,6},{6,3},{7,10},{10,7},{1... | collective-permute-start | bytes 147464 | tf_op jit(solution)/shard_map/ppermute | solution.py:162
  12.1 5.7 %collective-permute-start.3 = (f32[3,32,128]{2,1,0:T(8,128)S(1)}, f32[3,32,128]{2,1,0:T(8,128)S(1)}, u32[]{:S(2)}, u32[]{:S(2)}) collective-permute-start(f32[3,32,128]{2,1,0:T(8,128)S(1)} %get-tuple-element.212), channel_id=1, source_target_pairs={{0,1},{1,0},{2,3},{3,2},{4,5},{5,4},{6,7},{7,6},{8,9},{9,8},{10,11... | collective-permute-start | bytes 147464 | tf_op jit(solution)/shard_map/ppermute | solution.py:158
  18.2 0.9 %slice-start.1 = ((f32[6,32,384]{2,1,0:T(8,128)}), f32[6,32,128]{2,1,0:T(8,128)S(1)}, s32[]{:S(2)}) async-start(f32[6,32,384]{2,1,0:T(8,128)} %copy-done.3), calls=%async_computation.1 | async-start | bytes 196608 | tf_op jit(solution)/shard_map/slice | solution.py:169
  20.6 5.5 %copy-start.2 = (f32[6,32,384]{2,1,0:T(8,128)}, f32[6,32,384]{2,1,0:T(8,128)S(1)}, u32[]{:S(2)}) copy-start(f32[6,32,384]{2,1,0:T(8,128)S(1)} %fusion.41) | copy-start | bytes 884740
  20.6 4.6 %collective-permute-start.4 = (f32[3,32,128]{2,1,0:T(8,128)S(1)}, f32[3,32,128]{2,1,0:T(8,128)S(1)}, u32[]{:S(2)}, u32[]{:S(2)}) collective-permute-start(f32[3,32,128]{2,1,0:T(8,128)S(1)} %get-tuple-element.209), channel_id=1, source_target_pairs={{1,4},{4,1},{5,8},{8,5},{9,12},{12,9},{3,6},{6,3},{7,10},{10,7},{1... | collective-permute-start | bytes 147464 | tf_op jit(solution)/shard_map/ppermute | solution.py:162
  21.3 4.7 %collective-permute-start.5 = (f32[3,32,128]{2,1,0:T(8,128)S(1)}, f32[3,32,128]{2,1,0:T(8,128)S(1)}, u32[]{:S(2)}, u32[]{:S(2)}) collective-permute-start(f32[3,32,128]{2,1,0:T(8,128)S(1)} %get-tuple-element.208), channel_id=1, source_target_pairs={{0,1},{1,0},{2,3},{3,2},{4,5},{5,4},{6,7},{7,6},{8,9},{9,8},{10,11... | collective-permute-start | bytes 147464 | tf_op jit(solution)/shard_map/ppermute | solution.py:158
  26.5 0.9 %slice-start = ((f32[6,32,384]{2,1,0:T(8,128)}), f32[6,32,128]{2,1,0:T(8,128)S(1)}, s32[]{:S(2)}) async-start(f32[6,32,384]{2,1,0:T(8,128)} %copy-done.2), calls=%async_computation | async-start | bytes 196608 | tf_op jit(solution)/shard_map/slice | solution.py:169
  29.8 2.0 %collective-permute-start.6 = (f32[4,16,2,4,128]{4,1,3,2,0:T(8,128)S(1)}, f32[4,16,2,4,128]{4,1,3,2,0:T(8,128)S(1)}, u32[]{:S(2)}, u32[]{:S(2)}) collective-permute-start(f32[4,16,2,4,128]{4,1,3,2,0:T(8,128)S(1)} %select_bitcast_fusion), channel_id=1, source_target_pairs={{0,1},{1,0},{2,3},{3,2},{4,5},{5,4},{6,7},{7,6},{8,9},{9,8},{10,11... | collective-permute-start | bytes 786440 | tf_op jit(solution)/shard_map/ppermute | solution.py:44
  31.9 5.9 %collective-permute-start.7 = (f32[2,16,2,4,128]{4,1,3,2,0:T(8,128)S(1)}, f32[2,16,2,4,128]{4,1,3,2,0:T(8,128)S(1)}, u32[]{:S(2)}, u32[]{:S(2)}) collective-permute-start(f32[2,16,2,4,128]{4,1,3,2,0:T(8,128)S(1)} %select_bitcast_fusion.1), channel_id=1, source_target_pairs={{0,4},{4,0},{8,12},{12,8},{1,5},{5,1},{9,13},{13,9},{2,6},{6,2},{1... | collective-permute-start | bytes 393224 | tf_op jit(solution)/shard_map/ppermute | solution.py:44
  37.8 5.4 %collective-permute-start.8 = (f32[1,16,2,4,128]{4,1,3,2,0:T(8,128)S(1)}, f32[1,16,2,4,128]{4,1,3,2,0:T(8,128)S(1)}, u32[]{:S(2)}, u32[]{:S(2)}) collective-permute-start(f32[1,16,2,4,128]{4,1,3,2,0:T(8,128)S(1)} %select_bitcast_fusion.2), channel_id=1, source_target_pairs={{0,8},{4,12},{8,0},{12,4},{1,9},{5,13},{9,1},{13,5},{2,10},{6,14},... | collective-permute-start | bytes 196616 | tf_op jit(solution)/shard_map/ppermute | solution.py:44

commit v17 on v16

--- a/solution.py
+++ b/solution.py
@@ -247,7 +247,9 @@
         levels += exchange_round(levels[-1], moves, wide, steps)
         remaining -= steps
     stacked = jnp.concatenate(
-        [level.transpose(1, 0, 2).reshape(row_count, state_count) for level in levels], 0
+        [rows.astype(jnp.float32)]
+        + [level.transpose(1, 0, 2).reshape(row_count, state_count) for level in levels],
+        0,
     )
     product = jnp.dot(
         stacked,
@@ -255,10 +257,9 @@
         precision=lax.Precision.HIGH,
         preferred_element_type=jnp.float32,
     )
-    first = jnp.dot(rows, flat_start, preferred_element_type=jnp.float32)
     pieces = [
         piece.reshape(output_count, expect_rows, input_count, horizon).transpose(1, 0, 2, 3)
-        for piece in [first] + jnp.split(product, sections - 1, 0)
+        for piece in jnp.split(product, sections, 0)
     ]
     partial_news = jnp.concatenate(pieces, axis=0)
     jacobian = diagonal_sums(partial_news)

time: 44.3 us -> 45.5 us (1.027)
  starting transfers between devices: 20.8 us -> 22.9 us
  waiting for transfers between devices: 9.34 us -> 8.28 us
  other arithmetic: 1.97 us -> 2.75 us
    ppermute x3, starting transfers between devices: 5.75 us -> 9.84 us  [halving_scatter(): held = keep + lax.ppermute(send, axis, pairs)]
    ppermute x3, starting transfers between devices: 13.1 us -> 10.9 us  [swap_links(): on_chip = lax.ppermute(chip_part, 'horizon', [(0, 1), (1, 0)])]
    ppermute x3, waiting for transfers between devices: 1.74 us -> 0.68 us  [swap_links(): on_chip = lax.ppermute(chip_part, 'horizon', [(0, 1), (1, 0)])]
    unnamed x5 -> x6, other arithmetic: 0.11 us -> 0.88 us
    unnamed x20 -> x18, local copies, waits for them, and re-layouts: 1.55 us -> 1.5 us
where the time goes in v17:
time: 45.5 us; the launch traced here: 45.2 us
  starting transfers between devices  22.9 us (50%)
  waiting for transfers between devices  8.28 us (18%)
  matrix products  4.37 us (10%)
  local copies, waits for them, and re-layouts  3.75 us (8%)
  other arithmetic  2.75 us (6%)
  Pallas kernels  2.34 us (5%)
  between operations  0.79 us (2%)
    ppermute x3, starting transfers between devices, swap_links(): on_chip = lax.ppermute(chip_part, 'horizon', [(0, 1), (1, 0)])  10.9 us
    ppermute x3, starting transfers between devices, halving_scatter(): held = keep + lax.ppermute(send, axis, pairs)  9.84 us
    ppermute x3, waiting for transfers between devices, halving_scatter(): held = keep + lax.ppermute(send, axis, pairs)  7.59 us
    dot_general x10, matrix products, band_parts(): jnp.einsum('cru,cun->crn', rows, moves, precision=lax.Precision.HIGH)  3.92 us
    pallas_call x1, Pallas kernels, prepare(): pl.pallas_call(prepare_kernel, out_shape=(jax.ShapeDtypeStruct((block_cou...  2.34 us
    ppermute x3, starting transfers between devices, swap_links(): across = lax.ppermute(cross_part, ('state', 'horizon'), pairs)  2.09 us
    unnamed x18, local copies, waits for them, and re-layouts  1.5 us
    add x7, other arithmetic, diagonal_sums(): total = total + moved  1.31 us
  transfers between devices with their start and end apart: 9, of which 6 were waited for; matrix products, arithmetic and copies ran while one was open for 2% of the time, Pallas kernels for 0%

profile of v17, /device:TPU:0, one launch (start us, length us, event | category | flops | bytes accessed | tf_op | source)
XLA Modules:
  0.0 45.2 jit_solution(12364164344262990271)
XLA Ops:
  0.0 2.3 %shard_map.73 = (f32[4,128,384]{2,1,0:T(8,128)}, bf16[32,512]{1,0:T(8,128)(2,1)}, f32[4,32,128]{2,1,0:T(8,128)}, f32[288,128]{1,0:T(8,128)}, f32[288,128]{1,0:T(8,128)}) custom-call(s32[1]{0:T(128)} %bitcast.flip, s32[4]{0:T(128)} %counts.1, s32[4,4]{1,0:T(4,128)} %offsets.1, s32[4]{0:T(128)} %regions.1, f32[2,16]{1,0:T(2,128)} %bitcast.145, ...), custom_call_target="tpu_custom_call" | custom-call | tf_op jit(solution)/shard_map/pallas_call | solution.py:109
  2.3 0.8 %collective-permute-start = (f32[288,128]{1,0:T(8,128)}, f32[288,128]{1,0:T(8,128)S(1)}, u32[]{:S(2)}, u32[]{:S(2)}) collective-permute-start(f32[288,128]{1,0:T(8,128)} %get-tuple-element.156), channel_id=1, source_target_pairs={{1,4},{4,1},{5,8},{8,5},{9,12},{12,9},{3,6},{6,3},{7,10},{10,7},{1... | collective-permute-start | bytes 442376 | tf_op jit(solution)/shard_map/ppermute | solution.py:162
  3.1 4.4 %collective-permute-start.1 = (f32[288,128]{1,0:T(8,128)}, f32[288,128]{1,0:T(8,128)S(1)}, u32[]{:S(2)}, u32[]{:S(2)}) collective-permute-start(f32[288,128]{1,0:T(8,128)} %get-tuple-element.157), channel_id=1, source_target_pairs={{0,1},{1,0},{2,3},{3,2},{4,5},{5,4},{6,7},{7,6},{8,9},{9,8},{10,11... | collective-permute-start | bytes 442376 | tf_op jit(solution)/shard_map/ppermute | solution.py:158
  7.7 0.8 %convert_dynamic-update-slice_fusion = f32[256,512]{1,0:T(8,128)S(1)} fusion(bf16[32,512]{1,0:T(8,128)(2,1)} %get-tuple-element.154), kind=kLoop, calls=%fused_computation.82 | loop fusion | flops 16383 | bytes 98304
  9.0 0.9 %copy-done = f32[4,128,384]{2,1,0:T(8,128)S(1)} copy-done((f32[4,128,384]{2,1,0:T(8,128)S(1)}, f32[4,128,384]{2,1,0:T(8,128)}, u32[]{:S(2)}) %copy-start) | copy-done | bytes 786456
  10.5 0.4 fusion.44
  11.0 0.4 fusion.43
  11.5 1.8 %collective-permute-start.3 = (f32[3,32,128]{2,1,0:T(8,128)S(1)}, f32[3,32,128]{2,1,0:T(8,128)S(1)}, u32[]{:S(2)}, u32[]{:S(2)}) collective-permute-start(f32[3,32,128]{2,1,0:T(8,128)S(1)} %get-tuple-element.211), channel_id=1, source_target_pairs={{0,1},{1,0},{2,3},{3,2},{4,5},{5,4},{6,7},{7,6},{8,9},{9,8},{10,11... | collective-permute-start | bytes 147464 | tf_op jit(solution)/shard_map/ppermute | solution.py:158
  13.3 0.7 %collective-permute-start.2 = (f32[3,32,128]{2,1,0:T(8,128)S(1)}, f32[3,32,128]{2,1,0:T(8,128)S(1)}, u32[]{:S(2)}, u32[]{:S(2)}) collective-permute-start(f32[3,32,128]{2,1,0:T(8,128)S(1)} %get-tuple-element.212), channel_id=1, source_target_pairs={{1,4},{4,1},{5,8},{8,5},{9,12},{12,9},{3,6},{6,3},{7,10},{10,7},{1... | collective-permute-start | bytes 147464 | tf_op jit(solution)/shard_map/ppermute | solution.py:162
  15.0 0.5 %slice-done.1 = f32[6,32,128]{2,1,0:T(8,128)S(1)} async-done(((f32[6,32,384]{2,1,0:T(8,128)}), f32[6,32,128]{2,1,0:T(8,128)S(1)}, s32[]{:S(2)}) %slice-start.1) | async-done | bytes 98328 | tf_op jit(solution)/shard_map/slice | solution.py:169
  15.5 0.4 fusion.8
  16.0 0.4 fusion.42
  17.1 4.7 %collective-permute-start.5 = (f32[3,32,128]{2,1,0:T(8,128)S(1)}, f32[3,32,128]{2,1,0:T(8,128)S(1)}, u32[]{:S(2)}, u32[]{:S(2)}) collective-permute-start(f32[3,32,128]{2,1,0:T(8,128)S(1)} %get-tuple-element.207), channel_id=1, source_target_pairs={{0,1},{1,0},{2,3},{3,2},{4,5},{5,4},{6,7},{7,6},{8,9},{9,8},{10,11... | collective-permute-start | bytes 147464 | tf_op jit(solution)/shard_map/ppermute | solution.py:158
  21.8 0.7 %collective-permute-start.4 = (f32[3,32,128]{2,1,0:T(8,128)S(1)}, f32[3,32,128]{2,1,0:T(8,128)S(1)}, u32[]{:S(2)}, u32[]{:S(2)}) collective-permute-start(f32[3,32,128]{2,1,0:T(8,128)S(1)} %get-tuple-element.208), channel_id=1, source_target_pairs={{1,4},{4,1},{5,8},{8,5},{9,12},{12,9},{3,6},{6,3},{7,10},{10,7},{1... | collective-permute-start | bytes 147464 | tf_op jit(solution)/shard_map/ppermute | solution.py:162
  23.5 0.4 slice-done
  24.0 0.5 %copy-done.3 = bf16[512,4,128]{2,1,0:T(4,128)(2,1)S(1)} copy-done((bf16[512,4,128]{2,1,0:T(4,128)(2,1)S(1)}, bf16[512,4,128]{2,1,0:T(4,128)(2,1)}, u32[]{:S(2)}) %copy-start.3) | copy-done | bytes 524312
  24.5 0.4 fusion
  26.9 5.0 %collective-permute-start.6 = (f32[4,16,2,4,128]{4,1,0,3,2:T(8,128)S(1)}, f32[4,16,2,4,128]{4,1,0,3,2:T(8,128)S(1)}, u32[]{:S(2)}, u32[]{:S(2)}) collective-permute-start(f32[4,16,2,4,128]{4,1,0,3,2:T(8,128)S(1)} %select_bitcast_fusion), channel_id=1, source_target_pairs={{0,1},{1,0},{2,3},{3,2},{4,5},{5,4},{6,7},{7,6},{8,9},{9,8},{10,11... | collective-permute-start | bytes 786440 | tf_op jit(solution)/shard_map/ppermute | solution.py:44
  31.9 1.2 %collective-permute-done.6 = f32[4,16,2,4,128]{4,1,0,3,2:T(8,128)S(1)} collective-permute-done((f32[4,16,2,4,128]{4,1,0,3,2:T(8,128)S(1)}, f32[4,16,2,4,128]{4,1,0,3,2:T(8,128)S(1)}, u32[]{:S(2)}, u32[]{:S(2)}) %collective-permute-start.6) | collective-permute-done | bytes 262176 | tf_op jit(solution)/shard_map/ppermute | solution.py:44
  33.1 2.1 %collective-permute-start.7 = (f32[2,16,2,4,128]{4,1,3,2,0:T(8,128)S(1)}, f32[2,16,2,4,128]{4,1,3,2,0:T(8,128)S(1)}, u32[]{:S(2)}, u32[]{:S(2)}) collective-permute-start(f32[2,16,2,4,128]{4,1,3,2,0:T(8,128)S(1)} %fusion.5), channel_id=1, source_target_pairs={{0,4},{4,0},{8,12},{12,8},{1,5},{5,1},{9,13},{13,9},{2,6},{6,2},{1... | collective-permute-start | bytes 393224 | tf_op jit(solution)/shard_map/ppermute | solution.py:44
  35.2 3.8 %collective-permute-done.7 = f32[2,16,2,4,128]{4,1,3,2,0:T(8,128)S(1)} collective-permute-done((f32[2,16,2,4,128]{4,1,3,2,0:T(8,128)S(1)}, f32[2,16,2,4,128]{4,1,3,2,0:T(8,128)S(1)}, u32[]{:S(2)}, u32[]{:S(2)}) %collective-permute-start.7) | collective-permute-done | bytes 131104 | tf_op jit(solution)/shard_map/ppermute | solution.py:44
  39.0 2.8 %collective-permute-start.8 = (f32[1,16,2,4,128]{4,1,3,2,0:T(8,128)S(1)}, f32[1,16,2,4,128]{4,1,3,2,0:T(8,128)S(1)}, u32[]{:S(2)}, u32[]{:S(2)}) collective-permute-start(f32[1,16,2,4,128]{4,1,3,2,0:T(8,128)S(1)} %select_bitcast_fusion.1), channel_id=1, source_target_pairs={{0,8},{4,12},{8,0},{12,4},{1,9},{5,13},{9,1},{13,5},{2,10},{6,14},... | collective-permute-start | bytes 196616 | tf_op jit(solution)/shard_map/ppermute | solution.py:44
  41.9 2.6 %collective-permute-done.8 = f32[1,16,2,4,128]{4,1,3,2,0:T(8,128)S(1)} collective-permute-done((f32[1,16,2,4,128]{4,1,3,2,0:T(8,128)S(1)}, f32[1,16,2,4,128]{4,1,3,2,0:T(8,128)S(1)}, u32[]{:S(2)}, u32[]{:S(2)}) %collective-permute-start.8) | collective-permute-done | bytes 65568 | tf_op jit(solution)/shard_map/ppermute | solution.py:44
  44.5 0.7 %copy.54 = f32[16,2,4,128]{3,2,1,0:T(4,128)} copy(f32[16,2,4,128]{3,0,2,1:T(8,128)S(1)} %fusion.26) | data formatting | bytes 131072 | tf_op jit(solution)/shard_map/reshape | solution.py:46
  (116 shorter events, 5.6 us)
Async XLA Ops:
  2.3 6.5 %copy-start.4 = (f32[4,32,128]{2,1,0:T(8,128)S(1)}, f32[4,32,128]{2,1,0:T(8,128)}, u32[]{:S(2)}) copy-start(f32[4,32,128]{2,1,0:T(8,128)} %get-tuple-element.155) | copy-start | bytes 196612
  2.3 6.1 %collective-permute-start = (f32[288,128]{1,0:T(8,128)}, f32[288,128]{1,0:T(8,128)S(1)}, u32[]{:S(2)}, u32[]{:S(2)}) collective-permute-start(f32[288,128]{1,0:T(8,128)} %get-tuple-element.156), channel_id=1, source_target_pairs={{1,4},{4,1},{5,8},{8,5},{9,12},{12,9},{3,6},{6,3},{7,10},{10,7},{1... | collective-permute-start | bytes 442376 | tf_op jit(solution)/shard_map/ppermute | solution.py:162
  3.1 5.7 %collective-permute-start.1 = (f32[288,128]{1,0:T(8,128)}, f32[288,128]{1,0:T(8,128)S(1)}, u32[]{:S(2)}, u32[]{:S(2)}) collective-permute-start(f32[288,128]{1,0:T(8,128)} %get-tuple-element.157), channel_id=1, source_target_pairs={{0,1},{1,0},{2,3},{3,2},{4,5},{5,4},{6,7},{7,6},{8,9},{9,8},{10,11... | collective-permute-start | bytes 442376 | tf_op jit(solution)/shard_map/ppermute | solution.py:158
  8.8 1.1 %copy-start = (f32[4,128,384]{2,1,0:T(8,128)S(1)}, f32[4,128,384]{2,1,0:T(8,128)}, u32[]{:S(2)}) copy-start(f32[4,128,384]{2,1,0:T(8,128)} %get-tuple-element.158) | copy-start | bytes 2359300
  11.4 3.1 %copy-start.2 = (f32[6,32,384]{2,1,0:T(8,128)}, f32[6,32,384]{2,1,0:T(8,128)S(1)}, u32[]{:S(2)}) copy-start(f32[6,32,384]{2,1,0:T(8,128)S(1)} %fusion.43) | copy-start | bytes 884740
  11.5 2.7 %collective-permute-start.3 = (f32[3,32,128]{2,1,0:T(8,128)S(1)}, f32[3,32,128]{2,1,0:T(8,128)S(1)}, u32[]{:S(2)}, u32[]{:S(2)}) collective-permute-start(f32[3,32,128]{2,1,0:T(8,128)S(1)} %get-tuple-element.211), channel_id=1, source_target_pairs={{0,1},{1,0},{2,3},{3,2},{4,5},{5,4},{6,7},{7,6},{8,9},{9,8},{10,11... | collective-permute-start | bytes 147464 | tf_op jit(solution)/shard_map/ppermute | solution.py:158
  13.3 0.9 %collective-permute-start.2 = (f32[3,32,128]{2,1,0:T(8,128)S(1)}, f32[3,32,128]{2,1,0:T(8,128)S(1)}, u32[]{:S(2)}, u32[]{:S(2)}) collective-permute-start(f32[3,32,128]{2,1,0:T(8,128)S(1)} %get-tuple-element.212), channel_id=1, source_target_pairs={{1,4},{4,1},{5,8},{8,5},{9,12},{12,9},{3,6},{6,3},{7,10},{10,7},{1... | collective-permute-start | bytes 147464 | tf_op jit(solution)/shard_map/ppermute | solution.py:162
  14.6 0.9 %slice-start.1 = ((f32[6,32,384]{2,1,0:T(8,128)}), f32[6,32,128]{2,1,0:T(8,128)S(1)}, s32[]{:S(2)}) async-start(f32[6,32,384]{2,1,0:T(8,128)} %copy-done.2), calls=%async_computation.1 | async-start | bytes 196608 | tf_op jit(solution)/shard_map/slice | solution.py:169
  17.0 5.7 %copy-start.1 = (f32[6,32,384]{2,1,0:T(8,128)}, f32[6,32,384]{2,1,0:T(8,128)S(1)}, u32[]{:S(2)}) copy-start(f32[6,32,384]{2,1,0:T(8,128)S(1)} %fusion.41) | copy-start | bytes 884740
  17.1 5.6 %collective-permute-start.5 = (f32[3,32,128]{2,1,0:T(8,128)S(1)}, f32[3,32,128]{2,1,0:T(8,128)S(1)}, u32[]{:S(2)}, u32[]{:S(2)}) collective-permute-start(f32[3,32,128]{2,1,0:T(8,128)S(1)} %get-tuple-element.207), channel_id=1, source_target_pairs={{0,1},{1,0},{2,3},{3,2},{4,5},{5,4},{6,7},{7,6},{8,9},{9,8},{10,11... | collective-permute-start | bytes 147464 | tf_op jit(solution)/shard_map/ppermute | solution.py:158
  21.8 0.9 %collective-permute-start.4 = (f32[3,32,128]{2,1,0:T(8,128)S(1)}, f32[3,32,128]{2,1,0:T(8,128)S(1)}, u32[]{:S(2)}, u32[]{:S(2)}) collective-permute-start(f32[3,32,128]{2,1,0:T(8,128)S(1)} %get-tuple-element.208), channel_id=1, source_target_pairs={{1,4},{4,1},{5,8},{8,5},{9,12},{12,9},{3,6},{6,3},{7,10},{10,7},{1... | collective-permute-start | bytes 147464 | tf_op jit(solution)/shard_map/ppermute | solution.py:162
  23.1 0.9 %slice-start = ((f32[6,32,384]{2,1,0:T(8,128)}), f32[6,32,128]{2,1,0:T(8,128)S(1)}, s32[]{:S(2)}) async-start(f32[6,32,384]{2,1,0:T(8,128)} %copy-done.1), calls=%async_computation | async-start | bytes 196608 | tf_op jit(solution)/shard_map/slice | solution.py:169
  23.4 1.1 %copy-start.3 = (bf16[512,4,128]{2,1,0:T(4,128)(2,1)S(1)}, bf16[512,4,128]{2,1,0:T(4,128)(2,1)}, u32[]{:S(2)}) copy-start(bf16[512,4,128]{2,1,0:T(4,128)(2,1)} %param.31) | copy-start | bytes 1572868
  26.9 6.1 %collective-permute-start.6 = (f32[4,16,2,4,128]{4,1,0,3,2:T(8,128)S(1)}, f32[4,16,2,4,128]{4,1,0,3,2:T(8,128)S(1)}, u32[]{:S(2)}, u32[]{:S(2)}) collective-permute-start(f32[4,16,2,4,128]{4,1,0,3,2:T(8,128)S(1)} %select_bitcast_fusion), channel_id=1, source_target_pairs={{0,1},{1,0},{2,3},{3,2},{4,5},{5,4},{6,7},{7,6},{8,9},{9,8},{10,11... | collective-permute-start | bytes 786440 | tf_op jit(solution)/shard_map/ppermute | solution.py:44
  33.1 5.9 %collective-permute-start.7 = (f32[2,16,2,4,128]{4,1,3,2,0:T(8,128)S(1)}, f32[2,16,2,4,128]{4,1,3,2,0:T(8,128)S(1)}, u32[]{:S(2)}, u32[]{:S(2)}) collective-permute-start(f32[2,16,2,4,128]{4,1,3,2,0:T(8,128)S(1)} %fusion.5), channel_id=1, source_target_pairs={{0,4},{4,0},{8,12},{12,8},{1,5},{5,1},{9,13},{13,9},{2,6},{6,2},{1... | collective-permute-start | bytes 393224 | tf_op jit(solution)/shard_map/ppermute | solution.py:44
  39.0 5.4 %collective-permute-start.8 = (f32[1,16,2,4,128]{4,1,3,2,0:T(8,128)S(1)}, f32[1,16,2,4,128]{4,1,3,2,0:T(8,128)S(1)}, u32[]{:S(2)}, u32[]{:S(2)}) collective-permute-start(f32[1,16,2,4,128]{4,1,3,2,0:T(8,128)S(1)} %select_bitcast_fusion.1), channel_id=1, source_target_pairs={{0,8},{4,12},{8,0},{12,4},{1,9},{5,13},{9,1},{13,5},{2,10},{6,14},... | collective-permute-start | bytes 196616 | tf_op jit(solution)/shard_map/ppermute | solution.py:44

commit v18 on v16

--- a/solution.py
+++ b/solution.py
@@ -51,6 +51,8 @@
     output_count, expect_rows, _ = expect.shape
     row_count = output_count * expect_rows
     parts = []
+    moves[0] = jnp.zeros(moves.shape[1:], jnp.float32)
+    moves[block_count + 1] = jnp.zeros(moves.shape[1:], jnp.float32)
     for block in range(block_count):
         count = counts[block]
         scale = lax.rsqrt(jnp.full((1, tile_size), count.astype(jnp.float32), jnp.float32))
@@ -76,7 +78,7 @@
                 total = total + weight * wide[slot]
                 flow = flow + weight * carried[slot]
             total = total * scale
-            moves[block, :, shift * tile_size : (shift + 1) * tile_size] = total
+            moves[block + 1, :, shift * tile_size : (shift + 1) * tile_size] = total
             block_parts.append(flow * scale)
             if block == block_count - 1 and shift > 0:
                 up[row_count + (shift - 1) * tile_size : row_count + shift * tile_size, :] = total
@@ -109,7 +111,7 @@
     return pl.pallas_call(
         prepare_kernel,
         out_shape=(
-            jax.ShapeDtypeStruct((block_count, tile_size, 3 * tile_size), jnp.float32),
+            jax.ShapeDtypeStruct((block_count + 2, tile_size, 3 * tile_size), jnp.float32),
             jax.ShapeDtypeStruct((row_count, block_count * tile_size), jnp.bfloat16),
             jax.ShapeDtypeStruct((block_count, row_count, tile_size), jnp.float32),
             edge,
@@ -182,7 +184,7 @@
     return inner, down[1], up[-2]
 
 
-def exchange_round(rows, moves, wide, steps):
+def exchange_round(rows, wide, steps):
     zero = jnp.zeros_like(rows[:1])
     held = jnp.concatenate([zero, rows, zero], 0)
     to_low, to_high, mine = [], [], []
@@ -198,7 +200,9 @@
         if carried is None:
             carried = jnp.zeros_like(rows)
         else:
-            carried, _, _ = band_step(carried, moves)
+            edge = jnp.zeros_like(carried[:1])
+            carried, _, _ = ext_step(jnp.concatenate([edge, carried, edge], 0), wide)
+            carried = carried[1:-1]
         carried = carried.at[0].add(from_low[step]).at[-1].add(from_high[step])
         levels.append(mine[step] + carried)
     return levels
@@ -232,19 +236,13 @@
     left_up = from_low[row_count + tile_size :]
     right_down = from_high[row_count : row_count + tile_size]
     right_self = from_high[row_count + tile_size :]
-    blank = jnp.zeros_like(left_self)
-    wide = jnp.concatenate(
-        [
-            jnp.concatenate([blank, left_self, left_up], 1)[None],
-            moves,
-            jnp.concatenate([right_down, right_self, blank], 1)[None],
-        ],
-        0,
-    )
+    size = tile_size
+    wide = moves.at[0, :, size : 2 * size].set(left_self).at[0, :, 2 * size :].set(left_up)
+    wide = wide.at[-1, :, :size].set(right_down).at[-1, :, size : 2 * size].set(right_self)
     remaining = sections - 2
     while remaining > 0:
         steps = min(3, remaining)
-        levels += exchange_round(levels[-1], moves, wide, steps)
+        levels += exchange_round(levels[-1], wide, steps)
         remaining -= steps
     stacked = jnp.concatenate(
         [level.transpose(1, 0, 2).reshape(row_count, state_count) for level in levels], 0

time: 44.3 us -> 54.7 us (1.23)
  other arithmetic: 1.97 us -> 9.18 us
  local copies, waits for them, and re-layouts: 4.01 us -> 8.25 us
  starting transfers between devices: 20.8 us -> 19.1 us
    another operation x0 -> x5, other arithmetic: none -> 7.23 us
    scatter x0 -> x4, local copies, waits for them, and re-layouts: none -> 3.56 us  [the longest x2 3.55 us: shards(): moves.at[0, :, size:2 * size].set(left_self).at[0, :, 2 * size:]]
    ppermute x3, starting transfers between devices: 13.1 us -> 11.3 us  [swap_links(): on_chip = lax.ppermute(chip_part, 'horizon', [(0, 1), (1, 0)])]
    another operation x1 -> x2, local copies, waits for them, and re-layouts: 0.01 us -> 0.68 us
    unnamed x20 -> x22, local copies, waits for them, and re-layouts: 1.55 us -> 1.82 us
  transfers between devices with their start and end apart: 9 -> 9, of which waited for: 6 -> 5; matrix products, arithmetic and copies ran while one was open for 2% -> 11% of each run, Pallas kernels for 0% -> 0%
where the time goes in v18:
time: 54.7 us; the launch traced here: 54.3 us
  starting transfers between devices  19.1 us (35%)
  waiting for transfers between devices  9.29 us (17%)
  other arithmetic  9.18 us (17%)
  local copies, waits for them, and re-layouts  8.25 us (15%)
  matrix products  5.06 us (9%)
  Pallas kernels  2.54 us (5%)
  between operations  0.87 us (2%)
    ppermute x3, starting transfers between devices, swap_links(): on_chip = lax.ppermute(chip_part, 'horizon', [(0, 1), (1, 0)])  11.3 us
    ppermute x3, waiting for transfers between devices, halving_scatter(): held = keep + lax.ppermute(send, axis, pairs)  7.65 us
    another operation x5, other arithmetic  7.23 us
    ppermute x3, starting transfers between devices, halving_scatter(): held = keep + lax.ppermute(send, axis, pairs)  5.7 us
    dot_general x10, matrix products, band_parts(): jnp.einsum('cru,cun->crn', rows, moves, precision=lax.Precision.HIGH)  4.41 us
    scatter x2, local copies, waits for them, and re-layouts, shards(): moves.at[0, :, size:2 * size].set(left_self).at[0, :, 2 * size:]  3.55 us
    pallas_call x1, Pallas kernels, prepare(): pl.pallas_call(prepare_kernel, out_shape=(jax.ShapeDtypeStruct((block_cou...  2.54 us
    ppermute x3, starting transfers between devices, swap_links(): across = lax.ppermute(cross_part, ('state', 'horizon'), pairs)  2.12 us
  transfers between devices with their start and end apart: 9, of which 5 were waited for; matrix products, arithmetic and copies ran while one was open for 11% of the time, Pallas kernels for 0%

profile of v18, /device:TPU:0, one launch (start us, length us, event | category | flops | bytes accessed | tf_op | source)
XLA Modules:
  0.0 54.3 jit_solution(8695421759727436933)
XLA Ops:
  0.0 2.5 %shard_map.73 = (f32[6,128,384]{2,1,0:T(8,128)}, bf16[32,512]{1,0:T(8,128)(2,1)}, f32[4,32,128]{2,1,0:T(8,128)}, f32[288,128]{1,0:T(8,128)}, f32[288,128]{1,0:T(8,128)}) custom-call(s32[1]{0:T(128)} %bitcast.flip, s32[4]{0:T(128)} %counts.1, s32[4,4]{1,0:T(4,128)} %offsets.1, s32[4]{0:T(128)} %regions.1, f32[2,16]{1,0:T(2,128)} %bitcast.172, ...), custom_call_target="tpu_custom_call" | custom-call | tf_op jit(solution)/shard_map/pallas_call | solution.py:111
  2.5 0.8 %collective-permute-start = (f32[288,128]{1,0:T(8,128)}, f32[288,128]{1,0:T(8,128)S(1)}, u32[]{:S(2)}, u32[]{:S(2)}) collective-permute-start(f32[288,128]{1,0:T(8,128)} %get-tuple-element.204), channel_id=1, source_target_pairs={{1,4},{4,1},{5,8},{8,5},{9,12},{12,9},{3,6},{6,3},{7,10},{10,7},{1... | collective-permute-start | bytes 442376 | tf_op jit(solution)/shard_map/ppermute | solution.py:164
  3.3 4.4 %collective-permute-start.1 = (f32[288,128]{1,0:T(8,128)}, f32[288,128]{1,0:T(8,128)S(1)}, u32[]{:S(2)}, u32[]{:S(2)}) collective-permute-start(f32[288,128]{1,0:T(8,128)} %get-tuple-element.205), channel_id=1, source_target_pairs={{0,1},{1,0},{2,3},{3,2},{4,5},{5,4},{6,7},{7,6},{8,9},{9,8},{10,11... | collective-permute-start | bytes 442376 | tf_op jit(solution)/shard_map/ppermute | solution.py:160
  7.8 1.1 %copy.70 = bf16[64,8,4,128]{3,1,2,0:T(8,128)(2,1)S(1)} copy(bf16[64,8,4,128]{3,2,1,0:T(4,128)(2,1)} %bitcast.169) | data formatting | bytes 1048576
  9.4 0.7 %fusion.77 = (s32[1]{0:T(128)}, s32[1]{0:T(128)}, s32[1]{0:T(128)}, s32[1]{0:T(128)}) fusion(s32[2]{0:T(128)S(1)} %iota_multiply_fusion, s32[2]{0:T(128)S(1)} %iota_multiply_fusion.1), kind=kLoop, calls=%fused_computation.167 | loop fusion | bytes 32 | tf_op jit(solution)/shard_map/slice.430
  10.2 3.3 %and_reduce_fusion = (pred[]{:T(512)}, pred[]{:T(512)}) fusion(s32[3]{0:T(128)S(1)} %copy-done.6, s32[1]{0:T(128)} %get-tuple-element.261, s32[1]{0:T(128)} %constant.426.clone.1, s32[1]{0:T(128)} %get-tuple-element.260, s32[1]{0:T(128)} %get-tuple-element.267, s32[1]{0:T(128)} %get-tuple-element.266), kind=kLoop, calls=%fused_computation.135 | loop fusion | flops 34 | bytes 34 | tf_op jit(solution)/shard_map/reduce.17
  13.5 2.0 %fusion.37 = f32[1,128,128]{2,1,0:T(8,128)S(1)} fusion(f32[288,128]{1,0:T(8,128)S(1)} %get-tuple-element.250, f32[6,128,384]{2,1,0:T(8,128)S(1)} %copy-done, s32[]{:T(128)} %bitcast.13, s32[]{:T(128)} %bitcast.14, pred[]{:T(512)} %get-tuple-element.208), kind=kLoop, calls=%fused_computation.91 | loop fusion | flops 16384 | bytes 196617 | tf_op jit(solution)/shard_map/select.16
  15.5 1.9 %scatter.14 = f32[6,128,384]{2,1,0:T(8,128)S(1)} dynamic-update-slice(f32[6,128,384]{2,1,0:T(8,128)S(1)} %copy-done, f32[1,128,128]{2,1,0:T(8,128)S(1)} %fusion.37, s32[]{:T(128)} %bitcast.13, s32[]{:T(128)} %constant.421.clone.1, s32[]{:T(128)} %bitcast.14) | dynamic-update-slice | bytes 131076 | tf_op jit(solution)/shard_map/scatter | solution.py:240
  17.4 2.0 %fusion.36 = f32[1,128,128]{2,1,0:T(8,128)S(1)} fusion(f32[288,128]{1,0:T(8,128)S(1)} %get-tuple-element.250, f32[6,128,384]{2,1,0:T(8,128)S(1)} %scatter.14, s32[]{:T(128)} %bitcast.16, s32[]{:T(128)} %bitcast.17, pred[]{:T(512)} %get-tuple-element.207), kind=kLoop, calls=%fused_computation.89 | loop fusion | flops 16384 | bytes 196617 | tf_op jit(solution)/shard_map/select.17
  19.4 1.7 %scatter.15 = f32[6,128,384]{2,1,0:T(8,128)S(1)} dynamic-update-slice(f32[6,128,384]{2,1,0:T(8,128)S(1)} %scatter.14, f32[1,128,128]{2,1,0:T(8,128)S(1)} %fusion.36, s32[]{:T(128)} %bitcast.16, s32[]{:T(128)} %constant.421.clone.1, s32[]{:T(128)} %bitcast.17) | dynamic-update-slice | bytes 131076 | tf_op jit(solution)/shard_map/scatter | solution.py:240
  22.7 0.7 %collective-permute-start.2 = (f32[3,32,128]{2,1,0:T(8,128)S(1)}, f32[3,32,128]{2,1,0:T(8,128)S(1)}, u32[]{:S(2)}, u32[]{:S(2)}) collective-permute-start(f32[3,32,128]{2,1,0:T(8,128)S(1)} %get-tuple-element.259), channel_id=1, source_target_pairs={{1,4},{4,1},{5,8},{8,5},{9,12},{12,9},{3,6},{6,3},{7,10},{10,7},{1... | collective-permute-start | bytes 147464 | tf_op jit(solution)/shard_map/ppermute | solution.py:164
  23.4 3.0 %collective-permute-start.3 = (f32[3,32,128]{2,1,0:T(8,128)S(1)}, f32[3,32,128]{2,1,0:T(8,128)S(1)}, u32[]{:S(2)}, u32[]{:S(2)}) collective-permute-start(f32[3,32,128]{2,1,0:T(8,128)S(1)} %get-tuple-element.258), channel_id=1, source_target_pairs={{0,1},{1,0},{2,3},{3,2},{4,5},{5,4},{6,7},{7,6},{8,9},{9,8},{10,11... | collective-permute-start | bytes 147464 | tf_op jit(solution)/shard_map/ppermute | solution.py:160
  26.4 0.8 %collective-permute-done.3 = f32[3,32,128]{2,1,0:T(8,128)S(1)} collective-permute-done((f32[3,32,128]{2,1,0:T(8,128)S(1)}, f32[3,32,128]{2,1,0:T(8,128)S(1)}, u32[]{:S(2)}, u32[]{:S(2)}) %collective-permute-start.3) | collective-permute-done | bytes 49184 | tf_op jit(solution)/shard_map/ppermute | solution.py:160
  30.3 0.7 %collective-permute-start.4 = (f32[3,32,128]{2,1,0:T(8,128)S(1)}, f32[3,32,128]{2,1,0:T(8,128)S(1)}, u32[]{:S(2)}, u32[]{:S(2)}) collective-permute-start(f32[3,32,128]{2,1,0:T(8,128)S(1)} %get-tuple-element.255), channel_id=1, source_target_pairs={{1,4},{4,1},{5,8},{8,5},{9,12},{12,9},{3,6},{6,3},{7,10},{10,7},{1... | collective-permute-start | bytes 147464 | tf_op jit(solution)/shard_map/ppermute | solution.py:164
  30.9 3.9 %collective-permute-start.5 = (f32[3,32,128]{2,1,0:T(8,128)S(1)}, f32[3,32,128]{2,1,0:T(8,128)S(1)}, u32[]{:S(2)}, u32[]{:S(2)}) collective-permute-start(f32[3,32,128]{2,1,0:T(8,128)S(1)} %get-tuple-element.254), channel_id=1, source_target_pairs={{0,1},{1,0},{2,3},{3,2},{4,5},{5,4},{6,7},{7,6},{8,9},{9,8},{10,11... | collective-permute-start | bytes 147464 | tf_op jit(solution)/shard_map/ppermute | solution.py:160
  34.9 0.8 %collective-permute-done.5 = f32[3,32,128]{2,1,0:T(8,128)S(1)} collective-permute-done((f32[3,32,128]{2,1,0:T(8,128)S(1)}, f32[3,32,128]{2,1,0:T(8,128)S(1)}, u32[]{:S(2)}, u32[]{:S(2)}) %collective-permute-start.5) | collective-permute-done | bytes 49184 | tf_op jit(solution)/shard_map/ppermute | solution.py:160
  37.2 0.6 %copy-done.1 = bf16[512,4,128]{2,1,0:T(4,128)(2,1)S(1)} copy-done((bf16[512,4,128]{2,1,0:T(4,128)(2,1)S(1)}, bf16[512,4,128]{2,1,0:T(4,128)(2,1)}, u32[]{:S(2)}) %copy-start.1) | copy-done | bytes 524312
  40.2 1.0 %collective-permute-start.6 = (f32[4,16,2,4,128]{4,1,3,2,0:T(8,128)S(1)}, f32[4,16,2,4,128]{4,1,3,2,0:T(8,128)S(1)}, u32[]{:S(2)}, u32[]{:S(2)}) collective-permute-start(f32[4,16,2,4,128]{4,1,3,2,0:T(8,128)S(1)} %select_bitcast_fusion), channel_id=1, source_target_pairs={{0,1},{1,0},{2,3},{3,2},{4,5},{5,4},{6,7},{7,6},{8,9},{9,8},{10,11... | collective-permute-start | bytes 786440 | tf_op jit(solution)/shard_map/ppermute | solution.py:44
  41.1 1.2 %collective-permute-done.6 = f32[4,16,2,4,128]{4,1,3,2,0:T(8,128)S(1)} collective-permute-done((f32[4,16,2,4,128]{4,1,3,2,0:T(8,128)S(1)}, f32[4,16,2,4,128]{4,1,3,2,0:T(8,128)S(1)}, u32[]{:S(2)}, u32[]{:S(2)}) %collective-permute-start.6) | collective-permute-done | bytes 262176 | tf_op jit(solution)/shard_map/ppermute | solution.py:44
  42.4 2.0 %collective-permute-start.7 = (f32[2,16,2,4,128]{4,1,3,2,0:T(8,128)S(1)}, f32[2,16,2,4,128]{4,1,3,2,0:T(8,128)S(1)}, u32[]{:S(2)}, u32[]{:S(2)}) collective-permute-start(f32[2,16,2,4,128]{4,1,3,2,0:T(8,128)S(1)} %select_bitcast_fusion.1), channel_id=1, source_target_pairs={{0,4},{4,0},{8,12},{12,8},{1,5},{5,1},{9,13},{13,9},{2,6},{6,2},{1... | collective-permute-start | bytes 393224 | tf_op jit(solution)/shard_map/ppermute | solution.py:44
  44.3 3.9 %collective-permute-done.7 = f32[2,16,2,4,128]{4,1,3,2,0:T(8,128)S(1)} collective-permute-done((f32[2,16,2,4,128]{4,1,3,2,0:T(8,128)S(1)}, f32[2,16,2,4,128]{4,1,3,2,0:T(8,128)S(1)}, u32[]{:S(2)}, u32[]{:S(2)}) %collective-permute-start.7) | collective-permute-done | bytes 131104 | tf_op jit(solution)/shard_map/ppermute | solution.py:44
  48.2 2.8 %collective-permute-start.8 = (f32[1,16,2,4,128]{4,1,3,2,0:T(8,128)S(1)}, f32[1,16,2,4,128]{4,1,3,2,0:T(8,128)S(1)}, u32[]{:S(2)}, u32[]{:S(2)}) collective-permute-start(f32[1,16,2,4,128]{4,1,3,2,0:T(8,128)S(1)} %select_bitcast_fusion.2), channel_id=1, source_target_pairs={{0,8},{4,12},{8,0},{12,4},{1,9},{5,13},{9,1},{13,5},{2,10},{6,14},... | collective-permute-start | bytes 196616 | tf_op jit(solution)/shard_map/ppermute | solution.py:44
  51.0 2.6 %collective-permute-done.8 = f32[1,16,2,4,128]{4,1,3,2,0:T(8,128)S(1)} collective-permute-done((f32[1,16,2,4,128]{4,1,3,2,0:T(8,128)S(1)}, f32[1,16,2,4,128]{4,1,3,2,0:T(8,128)S(1)}, u32[]{:S(2)}, u32[]{:S(2)}) %collective-permute-start.8) | collective-permute-done | bytes 65568 | tf_op jit(solution)/shard_map/ppermute | solution.py:44
  53.7 0.7 %copy.34 = f32[16,2,4,128]{3,2,1,0:T(4,128)} copy(f32[16,2,4,128]{3,0,2,1:T(8,128)S(1)} %fusion.38) | data formatting | bytes 131072 | tf_op jit(solution)/shard_map/reshape | solution.py:46
  (131 shorter events, 8.7 us)
Async XLA Ops:
  2.5 6.6 %copy-start.5 = (bf16[32,512]{1,0:T(8,128)(2,1)S(1)}, bf16[32,512]{1,0:T(8,128)(2,1)}, u32[]{:S(2)}) copy-start(bf16[32,512]{1,0:T(8,128)(2,1)} %get-tuple-element.202) | copy-start | bytes 98308
  2.5 10.9 %collective-permute-start = (f32[288,128]{1,0:T(8,128)}, f32[288,128]{1,0:T(8,128)S(1)}, u32[]{:S(2)}, u32[]{:S(2)}) collective-permute-start(f32[288,128]{1,0:T(8,128)} %get-tuple-element.204), channel_id=1, source_target_pairs={{1,4},{4,1},{5,8},{8,5},{9,12},{12,9},{3,6},{6,3},{7,10},{10,7},{1... | collective-permute-start | bytes 442376 | tf_op jit(solution)/shard_map/ppermute | solution.py:164
  3.3 10.1 %collective-permute-start.1 = (f32[288,128]{1,0:T(8,128)}, f32[288,128]{1,0:T(8,128)S(1)}, u32[]{:S(2)}, u32[]{:S(2)}) collective-permute-start(f32[288,128]{1,0:T(8,128)} %get-tuple-element.205), channel_id=1, source_target_pairs={{0,1},{1,0},{2,3},{3,2},{4,5},{5,4},{6,7},{7,6},{8,9},{9,8},{10,11... | collective-permute-start | bytes 442376 | tf_op jit(solution)/shard_map/ppermute | solution.py:160
  7.8 2.4 %copy-start.6 = (s32[3]{0:T(128)S(1)}, s32[3]{0:T(128)}, u32[]{:S(2)}) copy-start(s32[3]{0:T(128)} %constant.427.clone.1) | copy-start | bytes 40
  8.9 4.6 %copy-start = (f32[6,128,384]{2,1,0:T(8,128)S(1)}, f32[6,128,384]{2,1,0:T(8,128)}, u32[]{:S(2)}) copy-start(f32[6,128,384]{2,1,0:T(8,128)} %get-tuple-element.206) | copy-start | bytes 3538948
  9.2 11.9 %copy-start.4 = (f32[4,32,128]{2,1,0:T(8,128)S(1)}, f32[4,32,128]{2,1,0:T(8,128)}, u32[]{:S(2)}) copy-start(f32[4,32,128]{2,1,0:T(8,128)} %get-tuple-element.203) | copy-start | bytes 196612
  22.6 5.1 %copy-start.3 = (f32[6,32,384]{2,1,0:T(8,128)}, f32[6,32,384]{2,1,0:T(8,128)S(1)}, u32[]{:S(2)}) copy-start(f32[6,32,384]{2,1,0:T(8,128)S(1)} %fusion.80) | copy-start | bytes 884740
  22.7 3.8 %collective-permute-start.2 = (f32[3,32,128]{2,1,0:T(8,128)S(1)}, f32[3,32,128]{2,1,0:T(8,128)S(1)}, u32[]{:S(2)}, u32[]{:S(2)}) collective-permute-start(f32[3,32,128]{2,1,0:T(8,128)S(1)} %get-tuple-element.259), channel_id=1, source_target_pairs={{1,4},{4,1},{5,8},{8,5},{9,12},{12,9},{3,6},{6,3},{7,10},{10,7},{1... | collective-permute-start | bytes 147464 | tf_op jit(solution)/shard_map/ppermute | solution.py:164
  23.4 3.9 %collective-permute-start.3 = (f32[3,32,128]{2,1,0:T(8,128)S(1)}, f32[3,32,128]{2,1,0:T(8,128)S(1)}, u32[]{:S(2)}, u32[]{:S(2)}) collective-permute-start(f32[3,32,128]{2,1,0:T(8,128)S(1)} %get-tuple-element.258), channel_id=1, source_target_pairs={{0,1},{1,0},{2,3},{3,2},{4,5},{5,4},{6,7},{7,6},{8,9},{9,8},{10,11... | collective-permute-start | bytes 147464 | tf_op jit(solution)/shard_map/ppermute | solution.py:160
  27.8 0.9 %slice-start.1 = ((f32[6,32,384]{2,1,0:T(8,128)}), f32[6,32,128]{2,1,0:T(8,128)S(1)}, s32[]{:S(2)}) async-start(f32[6,32,384]{2,1,0:T(8,128)} %copy-done.3), calls=%async_computation.1 | async-start | bytes 196608 | tf_op jit(solution)/shard_map/slice | solution.py:171
  30.2 6.0 %copy-start.2 = (f32[6,32,384]{2,1,0:T(8,128)}, f32[6,32,384]{2,1,0:T(8,128)S(1)}, u32[]{:S(2)}) copy-start(f32[6,32,384]{2,1,0:T(8,128)S(1)} %fusion.82) | copy-start | bytes 884740
  30.3 4.6 %collective-permute-start.4 = (f32[3,32,128]{2,1,0:T(8,128)S(1)}, f32[3,32,128]{2,1,0:T(8,128)S(1)}, u32[]{:S(2)}, u32[]{:S(2)}) collective-permute-start(f32[3,32,128]{2,1,0:T(8,128)S(1)} %get-tuple-element.255), channel_id=1, source_target_pairs={{1,4},{4,1},{5,8},{8,5},{9,12},{12,9},{3,6},{6,3},{7,10},{10,7},{1... | collective-permute-start | bytes 147464 | tf_op jit(solution)/shard_map/ppermute | solution.py:164
  30.9 4.7 %collective-permute-start.5 = (f32[3,32,128]{2,1,0:T(8,128)S(1)}, f32[3,32,128]{2,1,0:T(8,128)S(1)}, u32[]{:S(2)}, u32[]{:S(2)}) collective-permute-start(f32[3,32,128]{2,1,0:T(8,128)S(1)} %get-tuple-element.254), channel_id=1, source_target_pairs={{0,1},{1,0},{2,3},{3,2},{4,5},{5,4},{6,7},{7,6},{8,9},{9,8},{10,11... | collective-permute-start | bytes 147464 | tf_op jit(solution)/shard_map/ppermute | solution.py:160
  36.3 0.9 %slice-start = ((f32[6,32,384]{2,1,0:T(8,128)}), f32[6,32,128]{2,1,0:T(8,128)S(1)}, s32[]{:S(2)}) async-start(f32[6,32,384]{2,1,0:T(8,128)} %copy-done.2), calls=%async_computation | async-start | bytes 196608 | tf_op jit(solution)/shard_map/slice | solution.py:171
  36.7 1.1 %copy-start.1 = (bf16[512,4,128]{2,1,0:T(4,128)(2,1)S(1)}, bf16[512,4,128]{2,1,0:T(4,128)(2,1)}, u32[]{:S(2)}) copy-start(bf16[512,4,128]{2,1,0:T(4,128)(2,1)} %param.39) | copy-start | bytes 1572868
  40.2 2.1 %collective-permute-start.6 = (f32[4,16,2,4,128]{4,1,3,2,0:T(8,128)S(1)}, f32[4,16,2,4,128]{4,1,3,2,0:T(8,128)S(1)}, u32[]{:S(2)}, u32[]{:S(2)}) collective-permute-start(f32[4,16,2,4,128]{4,1,3,2,0:T(8,128)S(1)} %select_bitcast_fusion), channel_id=1, source_target_pairs={{0,1},{1,0},{2,3},{3,2},{4,5},{5,4},{6,7},{7,6},{8,9},{9,8},{10,11... | collective-permute-start | bytes 786440 | tf_op jit(solution)/shard_map/ppermute | solution.py:44
  42.4 5.8 %collective-permute-start.7 = (f32[2,16,2,4,128]{4,1,3,2,0:T(8,128)S(1)}, f32[2,16,2,4,128]{4,1,3,2,0:T(8,128)S(1)}, u32[]{:S(2)}, u32[]{:S(2)}) collective-permute-start(f32[2,16,2,4,128]{4,1,3,2,0:T(8,128)S(1)} %select_bitcast_fusion.1), channel_id=1, source_target_pairs={{0,4},{4,0},{8,12},{12,8},{1,5},{5,1},{9,13},{13,9},{2,6},{6,2},{1... | collective-permute-start | bytes 393224 | tf_op jit(solution)/shard_map/ppermute | solution.py:44
  48.2 5.4 %collective-permute-start.8 = (f32[1,16,2,4,128]{4,1,3,2,0:T(8,128)S(1)}, f32[1,16,2,4,128]{4,1,3,2,0:T(8,128)S(1)}, u32[]{:S(2)}, u32[]{:S(2)}) collective-permute-start(f32[1,16,2,4,128]{4,1,3,2,0:T(8,128)S(1)} %select_bitcast_fusion.2), channel_id=1, source_target_pairs={{0,8},{4,12},{8,0},{12,4},{1,9},{5,13},{9,1},{13,5},{2,10},{6,14},... | collective-permute-start | bytes 196616 | tf_op jit(solution)/shard_map/ppermute | solution.py:44

commit v19 on v16

--- a/solution.py
+++ b/solution.py
@@ -39,8 +39,8 @@
         pairs = [(member, member ^ flip) for member in range(size)]
         bit = (index // step) % 2
         halves = held.reshape((held.shape[0] // 2, 2) + held.shape[1:])
-        keep = jnp.where(bit == 1, halves[:, 1], halves[:, 0])
-        send = jnp.where(bit == 1, halves[:, 0], halves[:, 1])
+        keep = lax.dynamic_index_in_dim(halves, bit, axis=1, keepdims=False)
+        send = lax.dynamic_index_in_dim(halves, 1 - bit, axis=1, keepdims=False)
         held = keep + lax.ppermute(send, axis, pairs)
         step *= 2
     return held.reshape(held.shape[1:])

time: 44.3 us -> 44.2 us (level)
  no operation moved by 1% of the time
where the time goes in v19:
time: 44.2 us; the launch traced here: 43.9 us
  starting transfers between devices  20.8 us (47%)
  waiting for transfers between devices  9.34 us (21%)
  matrix products  4.58 us (10%)
  local copies, waits for them, and re-layouts  4.06 us (9%)
  Pallas kernels  2.41 us (5%)
  other arithmetic  1.87 us (4%)
  between operations  0.81 us (2%)
    ppermute x3, starting transfers between devices, swap_links(): on_chip = lax.ppermute(chip_part, 'horizon', [(0, 1), (1, 0)])  13.1 us
    ppermute x3, waiting for transfers between devices, halving_scatter(): held = keep + lax.ppermute(send, axis, pairs)  7.59 us
    ppermute x3, starting transfers between devices, halving_scatter(): held = keep + lax.ppermute(send, axis, pairs)  5.75 us
    dot_general x10, matrix products, band_parts(): jnp.einsum('cru,cun->crn', rows, moves, precision=lax.Precision.HIGH)  3.93 us
    pallas_call x1, Pallas kernels, prepare(): pl.pallas_call(prepare_kernel, out_shape=(jax.ShapeDtypeStruct((block_cou...  2.41 us
    ppermute x3, starting transfers between devices, swap_links(): across = lax.ppermute(cross_part, ('state', 'horizon'), pairs)  1.99 us
    ppermute x3, waiting for transfers between devices, swap_links(): on_chip = lax.ppermute(chip_part, 'horizon', [(0, 1), (1, 0)])  1.74 us
    unnamed x20, local copies, waits for them, and re-layouts  1.55 us
  transfers between devices with their start and end apart: 9, of which 6 were waited for; matrix products, arithmetic and copies ran while one was open for 2% of the time, Pallas kernels for 0%

profile of v19, /device:TPU:0, one launch (start us, length us, event | category | flops | bytes accessed | tf_op | source)
XLA Modules:
  0.0 43.9 jit_solution(11991034688579699957)
XLA Ops:
  0.0 2.4 %shard_map.73 = (f32[4,128,384]{2,1,0:T(8,128)}, bf16[32,512]{1,0:T(8,128)(2,1)}, f32[4,32,128]{2,1,0:T(8,128)}, f32[288,128]{1,0:T(8,128)}, f32[288,128]{1,0:T(8,128)}) custom-call(s32[1]{0:T(128)} %bitcast.flip, s32[4]{0:T(128)} %counts.1, s32[4,4]{1,0:T(4,128)} %offsets.1, s32[4]{0:T(128)} %regions.1, f32[2,16]{1,0:T(2,128)} %bitcast.130, ...), custom_call_target="tpu_custom_call" | custom-call | tf_op jit(solution)/shard_map/pallas_call | solution.py:109
  2.4 0.7 %collective-permute-start = (f32[288,128]{1,0:T(8,128)}, f32[288,128]{1,0:T(8,128)S(1)}, u32[]{:S(2)}, u32[]{:S(2)}) collective-permute-start(f32[288,128]{1,0:T(8,128)} %get-tuple-element.156), channel_id=1, source_target_pairs={{1,4},{4,1},{5,8},{8,5},{9,12},{12,9},{3,6},{6,3},{7,10},{10,7},{1... | collective-permute-start | bytes 442376 | tf_op jit(solution)/shard_map/ppermute | solution.py:162
  3.1 4.4 %collective-permute-start.1 = (f32[288,128]{1,0:T(8,128)}, f32[288,128]{1,0:T(8,128)S(1)}, u32[]{:S(2)}, u32[]{:S(2)}) collective-permute-start(f32[288,128]{1,0:T(8,128)} %get-tuple-element.157), channel_id=1, source_target_pairs={{0,1},{1,0},{2,3},{3,2},{4,5},{5,4},{6,7},{7,6},{8,9},{9,8},{10,11... | collective-permute-start | bytes 442376 | tf_op jit(solution)/shard_map/ppermute | solution.py:158
  7.9 0.4 %copy-done.5 = bf16[32,512]{1,0:T(8,128)(2,1)S(1)} copy-done((bf16[32,512]{1,0:T(8,128)(2,1)S(1)}, bf16[32,512]{1,0:T(8,128)(2,1)}, u32[]{:S(2)}) %copy-start.5) | copy-done | bytes 32792
  9.3 0.6 %copy-done = f32[4,128,384]{2,1,0:T(8,128)S(1)} copy-done((f32[4,128,384]{2,1,0:T(8,128)S(1)}, f32[4,128,384]{2,1,0:T(8,128)}, u32[]{:S(2)}) %copy-start) | copy-done | bytes 786456
  10.4 0.4 fusion.40
  10.9 0.4 fusion.39
  11.4 0.7 %collective-permute-start.2 = (f32[3,32,128]{2,1,0:T(8,128)S(1)}, f32[3,32,128]{2,1,0:T(8,128)S(1)}, u32[]{:S(2)}, u32[]{:S(2)}) collective-permute-start(f32[3,32,128]{2,1,0:T(8,128)S(1)} %get-tuple-element.213), channel_id=1, source_target_pairs={{1,4},{4,1},{5,8},{8,5},{9,12},{12,9},{3,6},{6,3},{7,10},{10,7},{1... | collective-permute-start | bytes 147464 | tf_op jit(solution)/shard_map/ppermute | solution.py:162
  12.1 4.8 %collective-permute-start.3 = (f32[3,32,128]{2,1,0:T(8,128)S(1)}, f32[3,32,128]{2,1,0:T(8,128)S(1)}, u32[]{:S(2)}, u32[]{:S(2)}) collective-permute-start(f32[3,32,128]{2,1,0:T(8,128)S(1)} %get-tuple-element.212), channel_id=1, source_target_pairs={{0,1},{1,0},{2,3},{3,2},{4,5},{5,4},{6,7},{7,6},{8,9},{9,8},{10,11... | collective-permute-start | bytes 147464 | tf_op jit(solution)/shard_map/ppermute | solution.py:158
  16.9 0.8 %collective-permute-done.3 = f32[3,32,128]{2,1,0:T(8,128)S(1)} collective-permute-done((f32[3,32,128]{2,1,0:T(8,128)S(1)}, f32[3,32,128]{2,1,0:T(8,128)S(1)}, u32[]{:S(2)}, u32[]{:S(2)}) %collective-permute-start.3) | collective-permute-done | bytes 49184 | tf_op jit(solution)/shard_map/ppermute | solution.py:158
  18.6 0.5 %slice-done.1 = f32[6,32,128]{2,1,0:T(8,128)S(1)} async-done(((f32[6,32,384]{2,1,0:T(8,128)}), f32[6,32,128]{2,1,0:T(8,128)S(1)}, s32[]{:S(2)}) %slice-start.1) | async-done | bytes 98328 | tf_op jit(solution)/shard_map/slice | solution.py:169
  19.6 0.4 %fusion.38 = f32[6,32,384]{2,1,0:T(8,128)S(1)} fusion(f32[6,32,128]{2,1,0:T(8,128)S(1)} %fusion.7, f32[1,128,384]{2,1,0:T(8,128)S(1)} %get-tuple-element.215, f32[4,128,384]{2,1,0:T(8,128)S(1)} %copy-done, f32[1,128,384]{2,1,0:T(8,128)S(1)} %get-tuple-element.214), kind=kOutput, calls=%fused_computation.115 | convolution fusion | flops 57212928 | bytes 1572864 | tf_op jit(solution)/shard_map/cru,cun->crn/dot_general | solution.py:167
  20.1 0.4 %fusion.37 = f32[6,32,384]{2,1,0:T(8,128)S(1)} fusion(f32[6,32,128]{2,1,0:T(8,128)S(1)} %fusion.6, f32[1,128,384]{2,1,0:T(8,128)S(1)} %get-tuple-element.215, f32[4,128,384]{2,1,0:T(8,128)S(1)} %copy-done, f32[1,128,384]{2,1,0:T(8,128)S(1)} %get-tuple-element.214), kind=kOutput, calls=%fused_computation.114 | convolution fusion | flops 57212928 | bytes 1572864 | tf_op jit(solution)/shard_map/cru,cun->crn/dot_general | solution.py:167
  20.6 0.7 %collective-permute-start.4 = (f32[3,32,128]{2,1,0:T(8,128)S(1)}, f32[3,32,128]{2,1,0:T(8,128)S(1)}, u32[]{:S(2)}, u32[]{:S(2)}) collective-permute-start(f32[3,32,128]{2,1,0:T(8,128)S(1)} %get-tuple-element.209), channel_id=1, source_target_pairs={{1,4},{4,1},{5,8},{8,5},{9,12},{12,9},{3,6},{6,3},{7,10},{10,7},{1... | collective-permute-start | bytes 147464 | tf_op jit(solution)/shard_map/ppermute | solution.py:162
  21.3 3.9 %collective-permute-start.5 = (f32[3,32,128]{2,1,0:T(8,128)S(1)}, f32[3,32,128]{2,1,0:T(8,128)S(1)}, u32[]{:S(2)}, u32[]{:S(2)}) collective-permute-start(f32[3,32,128]{2,1,0:T(8,128)S(1)} %get-tuple-element.208), channel_id=1, source_target_pairs={{0,1},{1,0},{2,3},{3,2},{4,5},{5,4},{6,7},{7,6},{8,9},{9,8},{10,11... | collective-permute-start | bytes 147464 | tf_op jit(solution)/shard_map/ppermute | solution.py:158
  25.2 0.8 %collective-permute-done.5 = f32[3,32,128]{2,1,0:T(8,128)S(1)} collective-permute-done((f32[3,32,128]{2,1,0:T(8,128)S(1)}, f32[3,32,128]{2,1,0:T(8,128)S(1)}, u32[]{:S(2)}, u32[]{:S(2)}) %collective-permute-start.5) | collective-permute-done | bytes 49184 | tf_op jit(solution)/shard_map/ppermute | solution.py:158
  26.9 0.5 %slice-done = f32[6,32,128]{2,1,0:T(8,128)S(1)} async-done(((f32[6,32,384]{2,1,0:T(8,128)}), f32[6,32,128]{2,1,0:T(8,128)S(1)}, s32[]{:S(2)}) %slice-start) | async-done | bytes 98328 | tf_op jit(solution)/shard_map/slice | solution.py:169
  29.8 0.9 %collective-permute-start.6 = (f32[4,16,2,4,128]{4,1,3,2,0:T(8,128)S(1)}, f32[4,16,2,4,128]{4,1,3,2,0:T(8,128)S(1)}, u32[]{:S(2)}, u32[]{:S(2)}) collective-permute-start(f32[4,16,2,4,128]{4,1,3,2,0:T(8,128)S(1)} %bitcast.128), channel_id=1, source_target_pairs={{0,1},{1,0},{2,3},{3,2},{4,5},{5,4},{6,7},{7,6},{8,9},{9,8},{10,11... | collective-permute-start | bytes 786440 | tf_op jit(solution)/shard_map/ppermute | solution.py:44
  30.7 1.2 %collective-permute-done.6 = f32[4,16,2,4,128]{4,1,3,2,0:T(8,128)S(1)} collective-permute-done((f32[4,16,2,4,128]{4,1,3,2,0:T(8,128)S(1)}, f32[4,16,2,4,128]{4,1,3,2,0:T(8,128)S(1)}, u32[]{:S(2)}, u32[]{:S(2)}) %collective-permute-start.6) | collective-permute-done | bytes 262176 | tf_op jit(solution)/shard_map/ppermute | solution.py:44
  31.9 2.1 %collective-permute-start.7 = (f32[2,16,2,4,128]{4,1,3,2,0:T(8,128)S(1)}, f32[2,16,2,4,128]{4,1,3,2,0:T(8,128)S(1)}, u32[]{:S(2)}, u32[]{:S(2)}) collective-permute-start(f32[2,16,2,4,128]{4,1,3,2,0:T(8,128)S(1)} %dynamic-slice_bitcast_fusion), channel_id=1, source_target_pairs={{0,4},{4,0},{8,12},{12,8},{1,5},{5,1},{9,13},{13,9},{2,6},{6,2},{1... | collective-permute-start | bytes 393224 | tf_op jit(solution)/shard_map/ppermute | solution.py:44
  33.9 3.8 %collective-permute-done.7 = f32[2,16,2,4,128]{4,1,3,2,0:T(8,128)S(1)} collective-permute-done((f32[2,16,2,4,128]{4,1,3,2,0:T(8,128)S(1)}, f32[2,16,2,4,128]{4,1,3,2,0:T(8,128)S(1)}, u32[]{:S(2)}, u32[]{:S(2)}) %collective-permute-start.7) | collective-permute-done | bytes 131104 | tf_op jit(solution)/shard_map/ppermute | solution.py:44
  37.8 2.8 %collective-permute-start.8 = (f32[1,16,2,4,128]{4,1,3,2,0:T(8,128)S(1)}, f32[1,16,2,4,128]{4,1,3,2,0:T(8,128)S(1)}, u32[]{:S(2)}, u32[]{:S(2)}) collective-permute-start(f32[1,16,2,4,128]{4,1,3,2,0:T(8,128)S(1)} %constant_dynamic-slice_fusion), channel_id=1, source_target_pairs={{0,8},{4,12},{8,0},{12,4},{1,9},{5,13},{9,1},{13,5},{2,10},{6,14},... | collective-permute-start | bytes 196616 | tf_op jit(solution)/shard_map/ppermute | solution.py:44
  40.6 2.6 %collective-permute-done.8 = f32[1,16,2,4,128]{4,1,3,2,0:T(8,128)S(1)} collective-permute-done((f32[1,16,2,4,128]{4,1,3,2,0:T(8,128)S(1)}, f32[1,16,2,4,128]{4,1,3,2,0:T(8,128)S(1)}, u32[]{:S(2)}, u32[]{:S(2)}) %collective-permute-start.8) | collective-permute-done | bytes 65568 | tf_op jit(solution)/shard_map/ppermute | solution.py:44
  43.2 0.7 %copy.43 = f32[16,2,4,128]{3,2,1,0:T(4,128)} copy(f32[16,2,4,128]{3,0,2,1:T(8,128)S(1)} %add_bitcast_fusion) | data formatting | bytes 131072 | tf_op jit(solution)/shard_map/reshape | solution.py:46
  (118 shorter events, 6.3 us)
Async XLA Ops:
  0.0 7.5 %copy-start.1 = (bf16[512,4,128]{2,1,0:T(4,128)(2,1)S(1)}, bf16[512,4,128]{2,1,0:T(4,128)(2,1)}, u32[]{:S(2)}) copy-start(bf16[512,4,128]{2,1,0:T(4,128)(2,1)} %param.31) | copy-start | bytes 1572868
  2.4 6.2 %collective-permute-start = (f32[288,128]{1,0:T(8,128)}, f32[288,128]{1,0:T(8,128)S(1)}, u32[]{:S(2)}, u32[]{:S(2)}) collective-permute-start(f32[288,128]{1,0:T(8,128)} %get-tuple-element.156), channel_id=1, source_target_pairs={{1,4},{4,1},{5,8},{8,5},{9,12},{12,9},{3,6},{6,3},{7,10},{10,7},{1... | collective-permute-start | bytes 442376 | tf_op jit(solution)/shard_map/ppermute | solution.py:162
  3.1 5.7 %collective-permute-start.1 = (f32[288,128]{1,0:T(8,128)}, f32[288,128]{1,0:T(8,128)S(1)}, u32[]{:S(2)}, u32[]{:S(2)}) collective-permute-start(f32[288,128]{1,0:T(8,128)} %get-tuple-element.157), channel_id=1, source_target_pairs={{0,1},{1,0},{2,3},{3,2},{4,5},{5,4},{6,7},{7,6},{8,9},{9,8},{10,11... | collective-permute-start | bytes 442376 | tf_op jit(solution)/shard_map/ppermute | solution.py:158
  7.6 0.8 %copy-start.5 = (bf16[32,512]{1,0:T(8,128)(2,1)S(1)}, bf16[32,512]{1,0:T(8,128)(2,1)}, u32[]{:S(2)}) copy-start(bf16[32,512]{1,0:T(8,128)(2,1)} %get-tuple-element.154) | copy-start | bytes 98308
  8.4 0.8 %copy-start.4 = (f32[4,32,128]{2,1,0:T(8,128)S(1)}, f32[4,32,128]{2,1,0:T(8,128)}, u32[]{:S(2)}) copy-start(f32[4,32,128]{2,1,0:T(8,128)} %get-tuple-element.155) | copy-start | bytes 196612
  8.8 1.1 %copy-start = (f32[4,128,384]{2,1,0:T(8,128)S(1)}, f32[4,128,384]{2,1,0:T(8,128)}, u32[]{:S(2)}) copy-start(f32[4,128,384]{2,1,0:T(8,128)} %get-tuple-element.158) | copy-start | bytes 2359300
  11.4 6.8 %copy-start.3 = (f32[6,32,384]{2,1,0:T(8,128)}, f32[6,32,384]{2,1,0:T(8,128)S(1)}, u32[]{:S(2)}) copy-start(f32[6,32,384]{2,1,0:T(8,128)S(1)} %fusion.39) | copy-start | bytes 884740
  11.4 5.5 %collective-permute-start.2 = (f32[3,32,128]{2,1,0:T(8,128)S(1)}, f32[3,32,128]{2,1,0:T(8,128)S(1)}, u32[]{:S(2)}, u32[]{:S(2)}) collective-permute-start(f32[3,32,128]{2,1,0:T(8,128)S(1)} %get-tuple-element.213), channel_id=1, source_target_pairs={{1,4},{4,1},{5,8},{8,5},{9,12},{12,9},{3,6},{6,3},{7,10},{10,7},{1... | collective-permute-start | bytes 147464 | tf_op jit(solution)/shard_map/ppermute | solution.py:162
  12.1 5.7 %collective-permute-start.3 = (f32[3,32,128]{2,1,0:T(8,128)S(1)}, f32[3,32,128]{2,1,0:T(8,128)S(1)}, u32[]{:S(2)}, u32[]{:S(2)}) collective-permute-start(f32[3,32,128]{2,1,0:T(8,128)S(1)} %get-tuple-element.212), channel_id=1, source_target_pairs={{0,1},{1,0},{2,3},{3,2},{4,5},{5,4},{6,7},{7,6},{8,9},{9,8},{10,11... | collective-permute-start | bytes 147464 | tf_op jit(solution)/shard_map/ppermute | solution.py:158
  18.2 0.9 %slice-start.1 = ((f32[6,32,384]{2,1,0:T(8,128)}), f32[6,32,128]{2,1,0:T(8,128)S(1)}, s32[]{:S(2)}) async-start(f32[6,32,384]{2,1,0:T(8,128)} %copy-done.3), calls=%async_computation.1 | async-start | bytes 196608 | tf_op jit(solution)/shard_map/slice | solution.py:169
  20.6 5.5 %copy-start.2 = (f32[6,32,384]{2,1,0:T(8,128)}, f32[6,32,384]{2,1,0:T(8,128)S(1)}, u32[]{:S(2)}) copy-start(f32[6,32,384]{2,1,0:T(8,128)S(1)} %fusion.37) | copy-start | bytes 884740
  20.6 4.6 %collective-permute-start.4 = (f32[3,32,128]{2,1,0:T(8,128)S(1)}, f32[3,32,128]{2,1,0:T(8,128)S(1)}, u32[]{:S(2)}, u32[]{:S(2)}) collective-permute-start(f32[3,32,128]{2,1,0:T(8,128)S(1)} %get-tuple-element.209), channel_id=1, source_target_pairs={{1,4},{4,1},{5,8},{8,5},{9,12},{12,9},{3,6},{6,3},{7,10},{10,7},{1... | collective-permute-start | bytes 147464 | tf_op jit(solution)/shard_map/ppermute | solution.py:162
  21.3 4.7 %collective-permute-start.5 = (f32[3,32,128]{2,1,0:T(8,128)S(1)}, f32[3,32,128]{2,1,0:T(8,128)S(1)}, u32[]{:S(2)}, u32[]{:S(2)}) collective-permute-start(f32[3,32,128]{2,1,0:T(8,128)S(1)} %get-tuple-element.208), channel_id=1, source_target_pairs={{0,1},{1,0},{2,3},{3,2},{4,5},{5,4},{6,7},{7,6},{8,9},{9,8},{10,11... | collective-permute-start | bytes 147464 | tf_op jit(solution)/shard_map/ppermute | solution.py:158
  26.5 0.9 %slice-start = ((f32[6,32,384]{2,1,0:T(8,128)}), f32[6,32,128]{2,1,0:T(8,128)S(1)}, s32[]{:S(2)}) async-start(f32[6,32,384]{2,1,0:T(8,128)} %copy-done.2), calls=%async_computation | async-start | bytes 196608 | tf_op jit(solution)/shard_map/slice | solution.py:169
  29.8 2.0 %collective-permute-start.6 = (f32[4,16,2,4,128]{4,1,3,2,0:T(8,128)S(1)}, f32[4,16,2,4,128]{4,1,3,2,0:T(8,128)S(1)}, u32[]{:S(2)}, u32[]{:S(2)}) collective-permute-start(f32[4,16,2,4,128]{4,1,3,2,0:T(8,128)S(1)} %bitcast.128), channel_id=1, source_target_pairs={{0,1},{1,0},{2,3},{3,2},{4,5},{5,4},{6,7},{7,6},{8,9},{9,8},{10,11... | collective-permute-start | bytes 786440 | tf_op jit(solution)/shard_map/ppermute | solution.py:44
  31.9 5.9 %collective-permute-start.7 = (f32[2,16,2,4,128]{4,1,3,2,0:T(8,128)S(1)}, f32[2,16,2,4,128]{4,1,3,2,0:T(8,128)S(1)}, u32[]{:S(2)}, u32[]{:S(2)}) collective-permute-start(f32[2,16,2,4,128]{4,1,3,2,0:T(8,128)S(1)} %dynamic-slice_bitcast_fusion), channel_id=1, source_target_pairs={{0,4},{4,0},{8,12},{12,8},{1,5},{5,1},{9,13},{13,9},{2,6},{6,2},{1... | collective-permute-start | bytes 393224 | tf_op jit(solution)/shard_map/ppermute | solution.py:44
  37.8 5.4 %collective-permute-start.8 = (f32[1,16,2,4,128]{4,1,3,2,0:T(8,128)S(1)}, f32[1,16,2,4,128]{4,1,3,2,0:T(8,128)S(1)}, u32[]{:S(2)}, u32[]{:S(2)}) collective-permute-start(f32[1,16,2,4,128]{4,1,3,2,0:T(8,128)S(1)} %constant_dynamic-slice_fusion), channel_id=1, source_target_pairs={{0,8},{4,12},{8,0},{12,4},{1,9},{5,13},{9,1},{13,5},{2,10},{6,14},... | collective-permute-start | bytes 196616 | tf_op jit(solution)/shard_map/ppermute | solution.py:44

commit v20 on v19

--- a/solution.py
+++ b/solution.py
@@ -148,8 +148,11 @@
 def swap_edges(to_low, to_high):
     if lax.axis_size("horizon") != 2:
         return to_right(to_high), to_left(to_low)
-    first = lax.axis_index("horizon") == 0
-    return swap_links(jnp.where(first, to_high, to_low), jnp.where(first, to_low, to_high))
+    pair = jnp.stack([to_low, to_high])
+    core = lax.axis_index("horizon")
+    chip_part = lax.dynamic_index_in_dim(pair, 1 - core, 0, keepdims=False)
+    cross_part = lax.dynamic_index_in_dim(pair, core, 0, keepdims=False)
+    return swap_links(chip_part, cross_part)
 
 
 def swap_links(chip_part, cross_part):
@@ -160,7 +163,12 @@
     for chip in range(count // 2 - 1):
         pairs += [(2 * chip + 1, 2 * chip + 2), (2 * chip + 2, 2 * chip + 1)]
     across = lax.ppermute(cross_part, ("state", "horizon"), pairs)
-    return jnp.where(first, across, on_chip), jnp.where(first, on_chip, across)
+    got = jnp.stack([across, on_chip])
+    core = lax.axis_index("horizon")
+    return (
+        lax.dynamic_index_in_dim(got, core, 0, keepdims=False),
+        lax.dynamic_index_in_dim(got, 1 - core, 0, keepdims=False),
+    )
 
 
 def band_parts(rows, moves):

time: 44.2 us -> 45 us (1.018)
    ppermute x3, waiting for transfers between devices: 7.59 us -> 8.06 us  [halving_scatter(): held = keep + lax.ppermute(send, axis, pairs)]
  transfers between devices with their start and end apart: 9 -> 9, of which waited for: 6 -> 5; matrix products, arithmetic and copies ran while one was open for 2% -> 2% of each run, Pallas kernels for 0% -> 0%
where the time goes in v20:
time: 45 us; the launch traced here: 44.7 us
  starting transfers between devices  21 us (47%)
  waiting for transfers between devices  9.71 us (22%)
  matrix products  4.58 us (10%)
  local copies, waits for them, and re-layouts  4.06 us (9%)
  Pallas kernels  2.42 us (5%)
  other arithmetic  2.02 us (4%)
  between operations  0.89 us (2%)
    ppermute x3, starting transfers between devices, swap_links(): on_chip = lax.ppermute(chip_part, 'horizon', [(0, 1), (1, 0)])  13.1 us
    ppermute x3, waiting for transfers between devices, halving_scatter(): held = keep + lax.ppermute(send, axis, pairs)  8.06 us
    ppermute x3, starting transfers between devices, halving_scatter(): held = keep + lax.ppermute(send, axis, pairs)  5.9 us
    dot_general x10, matrix products, band_parts(): jnp.einsum('cru,cun->crn', rows, moves, precision=lax.Precision.HIGH)  3.93 us
    pallas_call x1, Pallas kernels, prepare(): pl.pallas_call(prepare_kernel, out_shape=(jax.ShapeDtypeStruct((block_cou...  2.42 us
    ppermute x3, starting transfers between devices, swap_links(): across = lax.ppermute(cross_part, ('state', 'horizon'), pairs)  1.99 us
    ppermute x3, waiting for transfers between devices, swap_links(): on_chip = lax.ppermute(chip_part, 'horizon', [(0, 1), (1, 0)])  1.63 us
    unnamed x20, local copies, waits for them, and re-layouts  1.54 us
  transfers between devices with their start and end apart: 9, of which 5 were waited for; matrix products, arithmetic and copies ran while one was open for 2% of the time, Pallas kernels for 0%

profile of v20, /device:TPU:0, one launch (start us, length us, event | category | flops | bytes accessed | tf_op | source)
XLA Modules:
  0.0 44.7 jit_solution(10699660676108046917)
XLA Ops:
  0.0 2.4 %shard_map.73 = (f32[4,128,384]{2,1,0:T(8,128)}, bf16[32,512]{1,0:T(8,128)(2,1)}, f32[4,32,128]{2,1,0:T(8,128)}, f32[288,128]{1,0:T(8,128)}, f32[288,128]{1,0:T(8,128)}) custom-call(s32[1]{0:T(128)} %bitcast.flip, s32[4]{0:T(128)} %counts.1, s32[4,4]{1,0:T(4,128)} %offsets.1, s32[4]{0:T(128)} %regions.1, f32[2,16]{1,0:T(2,128)} %bitcast.222, ...), custom_call_target="tpu_custom_call" | custom-call | tf_op jit(solution)/shard_map/pallas_call | solution.py:109
  2.4 0.5 %collective-permute-start.1 = (f32[288,128]{1,0:T(8,128)}, f32[288,128]{1,0:T(8,128)S(1)}, u32[]{:S(2)}, u32[]{:S(2)}) collective-permute-start(f32[288,128]{1,0:T(8,128)} %get-tuple-element.157), channel_id=1, source_target_pairs={{0,1},{1,0},{2,3},{3,2},{4,5},{5,4},{6,7},{7,6},{8,9},{9,8},{10,11... | collective-permute-start | bytes 442376 | tf_op jit(solution)/shard_map/ppermute | solution.py:161
  2.9 0.7 %collective-permute-start = (f32[288,128]{1,0:T(8,128)}, f32[288,128]{1,0:T(8,128)S(1)}, u32[]{:S(2)}, u32[]{:S(2)}) collective-permute-start(f32[288,128]{1,0:T(8,128)} %get-tuple-element.156), channel_id=1, source_target_pairs={{1,4},{4,1},{5,8},{8,5},{9,12},{12,9},{3,6},{6,3},{7,10},{10,7},{1... | collective-permute-start | bytes 442376 | tf_op jit(solution)/shard_map/ppermute | solution.py:165
  4.0 0.4 copy-done.5
  5.4 0.5 %copy-done = f32[4,128,384]{2,1,0:T(8,128)S(1)} copy-done((f32[4,128,384]{2,1,0:T(8,128)S(1)}, f32[4,128,384]{2,1,0:T(8,128)}, u32[]{:S(2)}) %copy-start) | copy-done | bytes 786456
  6.4 0.4 fusion.60
  6.9 0.4 fusion.59
  7.5 0.7 %collective-permute-start.2 = (f32[3,32,128]{2,1,0:T(8,128)S(1)}, f32[3,32,128]{2,1,0:T(8,128)S(1)}, u32[]{:S(2)}, u32[]{:S(2)}) collective-permute-start(f32[3,32,128]{2,1,0:T(8,128)S(1)} %get-tuple-element.213), channel_id=1, source_target_pairs={{1,4},{4,1},{5,8},{8,5},{9,12},{12,9},{3,6},{6,3},{7,10},{10,7},{1... | collective-permute-start | bytes 147464 | tf_op jit(solution)/shard_map/ppermute | solution.py:165
  8.1 8.8 %collective-permute-start.3 = (f32[3,32,128]{2,1,0:T(8,128)S(1)}, f32[3,32,128]{2,1,0:T(8,128)S(1)}, u32[]{:S(2)}, u32[]{:S(2)}) collective-permute-start(f32[3,32,128]{2,1,0:T(8,128)S(1)} %get-tuple-element.212), channel_id=1, source_target_pairs={{0,1},{1,0},{2,3},{3,2},{4,5},{5,4},{6,7},{7,6},{8,9},{9,8},{10,11... | collective-permute-start | bytes 147464 | tf_op jit(solution)/shard_map/ppermute | solution.py:161
  17.0 0.8 %collective-permute-done.3 = f32[3,32,128]{2,1,0:T(8,128)S(1)} collective-permute-done((f32[3,32,128]{2,1,0:T(8,128)S(1)}, f32[3,32,128]{2,1,0:T(8,128)S(1)}, u32[]{:S(2)}, u32[]{:S(2)}) %collective-permute-start.3) | collective-permute-done | bytes 49184 | tf_op jit(solution)/shard_map/ppermute | solution.py:161
  18.7 0.5 %slice-done.1 = f32[6,32,128]{2,1,0:T(8,128)S(1)} async-done(((f32[6,32,384]{2,1,0:T(8,128)}), f32[6,32,128]{2,1,0:T(8,128)S(1)}, s32[]{:S(2)}) %slice-start.1) | async-done | bytes 98328 | tf_op jit(solution)/shard_map/slice | solution.py:177
  19.7 0.4 fusion.58
  20.2 0.4 fusion.57
  20.8 0.7 %collective-permute-start.4 = (f32[3,32,128]{2,1,0:T(8,128)S(1)}, f32[3,32,128]{2,1,0:T(8,128)S(1)}, u32[]{:S(2)}, u32[]{:S(2)}) collective-permute-start(f32[3,32,128]{2,1,0:T(8,128)S(1)} %get-tuple-element.209), channel_id=1, source_target_pairs={{1,4},{4,1},{5,8},{8,5},{9,12},{12,9},{3,6},{6,3},{7,10},{10,7},{1... | collective-permute-start | bytes 147464 | tf_op jit(solution)/shard_map/ppermute | solution.py:165
  21.5 3.9 %collective-permute-start.5 = (f32[3,32,128]{2,1,0:T(8,128)S(1)}, f32[3,32,128]{2,1,0:T(8,128)S(1)}, u32[]{:S(2)}, u32[]{:S(2)}) collective-permute-start(f32[3,32,128]{2,1,0:T(8,128)S(1)} %get-tuple-element.208), channel_id=1, source_target_pairs={{0,1},{1,0},{2,3},{3,2},{4,5},{5,4},{6,7},{7,6},{8,9},{9,8},{10,11... | collective-permute-start | bytes 147464 | tf_op jit(solution)/shard_map/ppermute | solution.py:161
  25.4 0.8 %collective-permute-done.5 = f32[3,32,128]{2,1,0:T(8,128)S(1)} collective-permute-done((f32[3,32,128]{2,1,0:T(8,128)S(1)}, f32[3,32,128]{2,1,0:T(8,128)S(1)}, u32[]{:S(2)}, u32[]{:S(2)}) %collective-permute-start.5) | collective-permute-done | bytes 49184 | tf_op jit(solution)/shard_map/ppermute | solution.py:161
  27.1 0.5 %slice-done = f32[6,32,128]{2,1,0:T(8,128)S(1)} async-done(((f32[6,32,384]{2,1,0:T(8,128)}), f32[6,32,128]{2,1,0:T(8,128)S(1)}, s32[]{:S(2)}) %slice-start) | async-done | bytes 98328 | tf_op jit(solution)/shard_map/slice | solution.py:177
  29.9 0.9 %collective-permute-start.6 = (f32[4,16,2,4,128]{4,1,3,2,0:T(8,128)S(1)}, f32[4,16,2,4,128]{4,1,3,2,0:T(8,128)S(1)}, u32[]{:S(2)}, u32[]{:S(2)}) collective-permute-start(f32[4,16,2,4,128]{4,1,3,2,0:T(8,128)S(1)} %bitcast.214), channel_id=1, source_target_pairs={{0,1},{1,0},{2,3},{3,2},{4,5},{5,4},{6,7},{7,6},{8,9},{9,8},{10,11... | collective-permute-start | bytes 786440 | tf_op jit(solution)/shard_map/ppermute | solution.py:44
  30.8 1.2 %collective-permute-done.6 = f32[4,16,2,4,128]{4,1,3,2,0:T(8,128)S(1)} collective-permute-done((f32[4,16,2,4,128]{4,1,3,2,0:T(8,128)S(1)}, f32[4,16,2,4,128]{4,1,3,2,0:T(8,128)S(1)}, u32[]{:S(2)}, u32[]{:S(2)}) %collective-permute-start.6) | collective-permute-done | bytes 262176 | tf_op jit(solution)/shard_map/ppermute | solution.py:44
  32.1 2.2 %collective-permute-start.7 = (f32[2,16,2,4,128]{4,1,3,2,0:T(8,128)S(1)}, f32[2,16,2,4,128]{4,1,3,2,0:T(8,128)S(1)}, u32[]{:S(2)}, u32[]{:S(2)}) collective-permute-start(f32[2,16,2,4,128]{4,1,3,2,0:T(8,128)S(1)} %dynamic-slice_bitcast_fusion), channel_id=1, source_target_pairs={{0,4},{4,0},{8,12},{12,8},{1,5},{5,1},{9,13},{13,9},{2,6},{6,2},{1... | collective-permute-start | bytes 393224 | tf_op jit(solution)/shard_map/ppermute | solution.py:44
  34.3 4.0 %collective-permute-done.7 = f32[2,16,2,4,128]{4,1,3,2,0:T(8,128)S(1)} collective-permute-done((f32[2,16,2,4,128]{4,1,3,2,0:T(8,128)S(1)}, f32[2,16,2,4,128]{4,1,3,2,0:T(8,128)S(1)}, u32[]{:S(2)}, u32[]{:S(2)}) %collective-permute-start.7) | collective-permute-done | bytes 131104 | tf_op jit(solution)/shard_map/ppermute | solution.py:44
  38.3 2.8 %collective-permute-start.8 = (f32[1,16,2,4,128]{4,1,3,2,0:T(8,128)S(1)}, f32[1,16,2,4,128]{4,1,3,2,0:T(8,128)S(1)}, u32[]{:S(2)}, u32[]{:S(2)}) collective-permute-start(f32[1,16,2,4,128]{4,1,3,2,0:T(8,128)S(1)} %constant_dynamic-slice_fusion), channel_id=1, source_target_pairs={{0,8},{4,12},{8,0},{12,4},{1,9},{5,13},{9,1},{13,5},{2,10},{6,14},... | collective-permute-start | bytes 196616 | tf_op jit(solution)/shard_map/ppermute | solution.py:44
  41.1 2.9 %collective-permute-done.8 = f32[1,16,2,4,128]{4,1,3,2,0:T(8,128)S(1)} collective-permute-done((f32[1,16,2,4,128]{4,1,3,2,0:T(8,128)S(1)}, f32[1,16,2,4,128]{4,1,3,2,0:T(8,128)S(1)}, u32[]{:S(2)}, u32[]{:S(2)}) %collective-permute-start.8) | collective-permute-done | bytes 65568 | tf_op jit(solution)/shard_map/ppermute | solution.py:44
  44.0 0.7 %copy.43 = f32[16,2,4,128]{3,2,1,0:T(4,128)} copy(f32[16,2,4,128]{3,0,2,1:T(8,128)S(1)} %add_bitcast_fusion) | data formatting | bytes 131072 | tf_op jit(solution)/shard_map/reshape | solution.py:46
  (123 shorter events, 6.3 us)
Async XLA Ops:
  0.0 3.6 %copy-start.1 = (bf16[512,4,128]{2,1,0:T(4,128)(2,1)S(1)}, bf16[512,4,128]{2,1,0:T(4,128)(2,1)}, u32[]{:S(2)}) copy-start(bf16[512,4,128]{2,1,0:T(4,128)(2,1)} %param.31) | copy-start | bytes 1572868
  2.4 2.2 %collective-permute-start.1 = (f32[288,128]{1,0:T(8,128)}, f32[288,128]{1,0:T(8,128)S(1)}, u32[]{:S(2)}, u32[]{:S(2)}) collective-permute-start(f32[288,128]{1,0:T(8,128)} %get-tuple-element.157), channel_id=1, source_target_pairs={{0,1},{1,0},{2,3},{3,2},{4,5},{5,4},{6,7},{7,6},{8,9},{9,8},{10,11... | collective-permute-start | bytes 442376 | tf_op jit(solution)/shard_map/ppermute | solution.py:161
  2.9 1.8 %collective-permute-start = (f32[288,128]{1,0:T(8,128)}, f32[288,128]{1,0:T(8,128)S(1)}, u32[]{:S(2)}, u32[]{:S(2)}) collective-permute-start(f32[288,128]{1,0:T(8,128)} %get-tuple-element.156), channel_id=1, source_target_pairs={{1,4},{4,1},{5,8},{8,5},{9,12},{12,9},{3,6},{6,3},{7,10},{10,7},{1... | collective-permute-start | bytes 442376 | tf_op jit(solution)/shard_map/ppermute | solution.py:165
  3.7 0.8 %copy-start.5 = (bf16[32,512]{1,0:T(8,128)(2,1)S(1)}, bf16[32,512]{1,0:T(8,128)(2,1)}, u32[]{:S(2)}) copy-start(bf16[32,512]{1,0:T(8,128)(2,1)} %get-tuple-element.154) | copy-start | bytes 98308
  4.4 0.8 %copy-start.4 = (f32[4,32,128]{2,1,0:T(8,128)S(1)}, f32[4,32,128]{2,1,0:T(8,128)}, u32[]{:S(2)}) copy-start(f32[4,32,128]{2,1,0:T(8,128)} %get-tuple-element.155) | copy-start | bytes 196612
  4.8 1.1 %copy-start = (f32[4,128,384]{2,1,0:T(8,128)S(1)}, f32[4,128,384]{2,1,0:T(8,128)}, u32[]{:S(2)}) copy-start(f32[4,128,384]{2,1,0:T(8,128)} %get-tuple-element.158) | copy-start | bytes 2359300
  7.4 10.9 %copy-start.3 = (f32[6,32,384]{2,1,0:T(8,128)}, f32[6,32,384]{2,1,0:T(8,128)S(1)}, u32[]{:S(2)}) copy-start(f32[6,32,384]{2,1,0:T(8,128)S(1)} %fusion.59) | copy-start | bytes 884740
  7.5 9.6 %collective-permute-start.2 = (f32[3,32,128]{2,1,0:T(8,128)S(1)}, f32[3,32,128]{2,1,0:T(8,128)S(1)}, u32[]{:S(2)}, u32[]{:S(2)}) collective-permute-start(f32[3,32,128]{2,1,0:T(8,128)S(1)} %get-tuple-element.213), channel_id=1, source_target_pairs={{1,4},{4,1},{5,8},{8,5},{9,12},{12,9},{3,6},{6,3},{7,10},{10,7},{1... | collective-permute-start | bytes 147464 | tf_op jit(solution)/shard_map/ppermute | solution.py:165
  8.1 9.7 %collective-permute-start.3 = (f32[3,32,128]{2,1,0:T(8,128)S(1)}, f32[3,32,128]{2,1,0:T(8,128)S(1)}, u32[]{:S(2)}, u32[]{:S(2)}) collective-permute-start(f32[3,32,128]{2,1,0:T(8,128)S(1)} %get-tuple-element.212), channel_id=1, source_target_pairs={{0,1},{1,0},{2,3},{3,2},{4,5},{5,4},{6,7},{7,6},{8,9},{9,8},{10,11... | collective-permute-start | bytes 147464 | tf_op jit(solution)/shard_map/ppermute | solution.py:161
  18.3 0.9 %slice-start.1 = ((f32[6,32,384]{2,1,0:T(8,128)}), f32[6,32,128]{2,1,0:T(8,128)S(1)}, s32[]{:S(2)}) async-start(f32[6,32,384]{2,1,0:T(8,128)} %copy-done.3), calls=%async_computation.1 | async-start | bytes 196608 | tf_op jit(solution)/shard_map/slice | solution.py:177
  20.7 5.6 %copy-start.2 = (f32[6,32,384]{2,1,0:T(8,128)}, f32[6,32,384]{2,1,0:T(8,128)S(1)}, u32[]{:S(2)}) copy-start(f32[6,32,384]{2,1,0:T(8,128)S(1)} %fusion.57) | copy-start | bytes 884740
  20.8 4.6 %collective-permute-start.4 = (f32[3,32,128]{2,1,0:T(8,128)S(1)}, f32[3,32,128]{2,1,0:T(8,128)S(1)}, u32[]{:S(2)}, u32[]{:S(2)}) collective-permute-start(f32[3,32,128]{2,1,0:T(8,128)S(1)} %get-tuple-element.209), channel_id=1, source_target_pairs={{1,4},{4,1},{5,8},{8,5},{9,12},{12,9},{3,6},{6,3},{7,10},{10,7},{1... | collective-permute-start | bytes 147464 | tf_op jit(solution)/shard_map/ppermute | solution.py:165
  21.5 4.7 %collective-permute-start.5 = (f32[3,32,128]{2,1,0:T(8,128)S(1)}, f32[3,32,128]{2,1,0:T(8,128)S(1)}, u32[]{:S(2)}, u32[]{:S(2)}) collective-permute-start(f32[3,32,128]{2,1,0:T(8,128)S(1)} %get-tuple-element.208), channel_id=1, source_target_pairs={{0,1},{1,0},{2,3},{3,2},{4,5},{5,4},{6,7},{7,6},{8,9},{9,8},{10,11... | collective-permute-start | bytes 147464 | tf_op jit(solution)/shard_map/ppermute | solution.py:161
  26.7 0.9 %slice-start = ((f32[6,32,384]{2,1,0:T(8,128)}), f32[6,32,128]{2,1,0:T(8,128)S(1)}, s32[]{:S(2)}) async-start(f32[6,32,384]{2,1,0:T(8,128)} %copy-done.2), calls=%async_computation | async-start | bytes 196608 | tf_op jit(solution)/shard_map/slice | solution.py:177
  29.9 2.0 %collective-permute-start.6 = (f32[4,16,2,4,128]{4,1,3,2,0:T(8,128)S(1)}, f32[4,16,2,4,128]{4,1,3,2,0:T(8,128)S(1)}, u32[]{:S(2)}, u32[]{:S(2)}) collective-permute-start(f32[4,16,2,4,128]{4,1,3,2,0:T(8,128)S(1)} %bitcast.214), channel_id=1, source_target_pairs={{0,1},{1,0},{2,3},{3,2},{4,5},{5,4},{6,7},{7,6},{8,9},{9,8},{10,11... | collective-permute-start | bytes 786440 | tf_op jit(solution)/shard_map/ppermute | solution.py:44
  32.1 6.2 %collective-permute-start.7 = (f32[2,16,2,4,128]{4,1,3,2,0:T(8,128)S(1)}, f32[2,16,2,4,128]{4,1,3,2,0:T(8,128)S(1)}, u32[]{:S(2)}, u32[]{:S(2)}) collective-permute-start(f32[2,16,2,4,128]{4,1,3,2,0:T(8,128)S(1)} %dynamic-slice_bitcast_fusion), channel_id=1, source_target_pairs={{0,4},{4,0},{8,12},{12,8},{1,5},{5,1},{9,13},{13,9},{2,6},{6,2},{1... | collective-permute-start | bytes 393224 | tf_op jit(solution)/shard_map/ppermute | solution.py:44
  38.3 5.7 %collective-permute-start.8 = (f32[1,16,2,4,128]{4,1,3,2,0:T(8,128)S(1)}, f32[1,16,2,4,128]{4,1,3,2,0:T(8,128)S(1)}, u32[]{:S(2)}, u32[]{:S(2)}) collective-permute-start(f32[1,16,2,4,128]{4,1,3,2,0:T(8,128)S(1)} %constant_dynamic-slice_fusion), channel_id=1, source_target_pairs={{0,8},{4,12},{8,0},{12,4},{1,9},{5,13},{9,1},{13,5},{2,10},{6,14},... | collective-permute-start | bytes 196616 | tf_op jit(solution)/shard_map/ppermute | solution.py:44
